TPU v7x, 512 devices: a whole 4x4x16 slice. The times are simulated.
512 devices in a mesh: row: 32 (over x, y, core), col: 16 (over z).
Axes of the slice: x: 4, y: 4, z: 16, core: 2. Of those that a mesh axis runs over, the one named last changes fastest.
Arguments:
- panel: float32 [65536, 256], P('row', 'col'), may hold values from -210 to 210
- slab: float32 [65536, 4096], P('row', 'col'), may hold values from -6 to 6
Outputs:
- triangle: float32 [256, 256], P(None, 'col')
- projected: float32 [256, 4096], P(None, 'col')
- residual: float32 [65536, 4096], P('row', 'col')
All inputs are finite; a program needn't handle non-finite values.
Results may differ from a plain program's by a relative error of at most 0.0003.
Values sent between devices are 32-bit elements; how exact they have to be, the bound alone decides.
No kernel may reach another device: no remote copies, remote signals or barrier semaphores. Data moves between devices by JAX's collectives and lax.ppermute only.
A program may use at most 64 MiB of HBM per device.

v0:
```python
import math

import jax
import jax.numpy as jnp
from jax import lax
from jax.sharding import PartitionSpec as P

contract_rows = (((0,), (0,)), ((), ()))


def per_device(panel, slab):
    highest = lax.Precision.HIGHEST
    gathered = lax.all_gather(panel, "col", axis=1, tiled=True)
    cross_local = lax.dot_general(gathered, slab, contract_rows, precision=highest)
    gram_local = lax.dot_general(gathered, gathered, contract_rows, precision=highest)
    gram_total, totals = lax.psum((gram_local, cross_local), "row")
    lower_factor = jnp.linalg.cholesky(gram_total)
    projected = lax.linalg.triangular_solve(
        lower_factor, totals, left_side=True, lower=True, transpose_a=False
    )
    basis_rows = lax.linalg.triangular_solve(
        lower_factor, gathered, left_side=False, lower=True, transpose_a=True
    )
    residual = slab - jnp.dot(basis_rows, projected, precision=highest)
    col_width = panel.shape[1]
    rows_total = gathered.shape[0] * lax.axis_size("row")
    scaled = lower_factor.T * (1.0 / math.sqrt(rows_total))
    triangle = lax.dynamic_slice_in_dim(scaled, lax.axis_index("col") * col_width, col_width, 1)
    return (triangle, projected, residual)


def solution(mesh):
    placed = (P("row", "col"), P("row", "col"))
    return jax.shard_map(
        per_device,
        mesh=mesh,
        in_specs=placed,
        out_specs=(P(None, "col"), P(None, "col"), P("row", "col")),
        check_vma=False,
    )
```

profile of v0, /device:TPU:1, one launch (start us, length us, event | category | flops | bytes accessed | tf_op | source)
XLA Modules:
  0.0 307.3 jit_solution(13206898415730622074)
XLA Ops:
  7.2 0.0 all-gather.2.cloned.1.call-start
  7.2 0.7 all-gather.2.cloned.1.call-update
  7.9 0.0 all-reduce.4.cloned.1.call-start
  7.9 71.5 %all-gather.2.cloned.1.call-done = f32[2048,256]{0,1:T(8,128)} async-done(((f32[2048,16]{0,1:T(8,128)}), f32[2048,256]{0,1:T(8,128)}) %all-gather.2.cloned.1.call-update) | async-done | bytes 2097168 | tf_op jit(solution)/shard_map/all_gather | solution.py:13
  79.5 0.0 copy-start
  79.5 4.9 %fusion.19 = f32[256,256]{0,1:T(8,128)} fusion(f32[2048,256]{0,1:T(8,128)} %all-gather.2.cloned.1.call-done), kind=kOutput, calls=%fused_computation.42 | convolution fusion | flops 1610612736 | bytes 2359296 | tf_op jit(solution)/shard_map/dot_general | solution.py:15
  84.4 0.0 copy-done
  84.4 4.2 %fusion.20 = f32[256,256]{1,0:T(8,128)} fusion(f32[2048,256]{0,1:T(8,128)S(1)} %copy-done, f32[2048,256]{1,0:T(8,128)} %param.3), kind=kOutput, calls=%fused_computation.43 | convolution fusion | flops 1610612736 | bytes 4456448 | tf_op jit(solution)/shard_map/dot_general | solution.py:14
  88.6 0.0 all-reduce.4.cloned.1.call-update
  88.6 140.3 %all-reduce.4.cloned.1.call-done = (f32[256,256]{0,1:T(8,128)}, f32[256,256]{1,0:T(8,128)}) async-done(((f32[256,256]{0,1:T(8,128)}, f32[256,256]{1,0:T(8,128)}), (f32[256,256]{0,1:T(8,128)}, f32[256,256]{1,0:T(8,128)})) %all-reduce.4.cloned.1.call-update) | async-done | bytes 524304 | tf_op jit(solution)/shard_map/psum | solution.py:16
  228.9 0.0 copy-start.3
  228.9 1.1 copy.6
  230.1 1.0 fusion.5
  231.1 11.7 %cholesky.50 = f32[128,128]{1,0:T(8,128)S(1)} custom-call(f32[128,128]{1,0:T(8,128)S(1)} %cholesky.118), custom_call_target="Cholesky" | custom-call | tf_op jit(solution)/shard_map/jit(cholesky)/cholesky | solution.py:17
  242.8 9.8 %custom-call.16 = f32[1,128,128]{1,2,0:T(8,128)S(1)} custom-call(f32[1,128,128]{2,1,0:T(8,128)S(1)} %get-tuple-element.28), custom_call_target="InvertDiagBlocksLowerTriangular" | custom-call | tf_op jit(solution)/shard_map/jit(cholesky)/cholesky | solution.py:17
  252.7 0.2 constant_dynamic-update-slice_fusion
  252.9 0.3 convolution_subtract_fusion.3
  253.2 11.9 %cholesky.105 = f32[128,128]{1,0:T(8,128)S(1)} custom-call(f32[128,128]{1,0:T(8,128)S(1)} %convolution_subtract_fusion.3), custom_call_target="Cholesky" | custom-call | tf_op jit(solution)/shard_map/jit(cholesky)/cholesky | solution.py:17
  265.1 0.6 compare_reduce_fusion
  267.1 0.1 triangular_solve.59
  267.1 4.0 %while.1 = (s32[]{:T(128)}, f32[256,256]{1,0:T(8,128)S(1)}, s32[2,2]{1,0:T(2,128)S(1)}, f32[2,128,128]{2,1,0:T(8,128)S(1)}, s32[]{:T(128)}) while((s32[]{:T(128)}, f32[256,256]{1,0:T(8,128)S(1)}, s32[2,2]{1,0:T(2,128)S(1)}, f32[2,128,128]{2,1,0:T(8,128)S(1)}, s32[]{:T(128)}) %tuple.28), condition=%wide.while_cond, body=%wide.while_body.sunk | while | flops 2 | bytes 131189 | solution.py:18
  267.1 0.6 fusion.33
  267.7 1.4 bitcast_dynamic-update-slice_fusion.2
  269.1 0.6 fusion.33
  269.7 1.4 bitcast_dynamic-update-slice_fusion.2
  271.1 19.7 %custom-call.17 = f32[2,128,128]{1,2,0:T(8,128)S(1)} custom-call(f32[2,128,128]{2,1,0:T(8,128)S(1)} %get-tuple-element.10), custom_call_target="InvertDiagBlocksLowerTriangular" | custom-call | tf_op jit(solution)/shard_map/triangular_solve | solution.py:18
  290.8 0.0 copy-done.3
  290.8 0.3 fusion.7
  291.1 0.3 convolution_subtract_fusion.2
  291.4 0.3 fusion.13
  291.8 0.0 copy-start.2
  291.8 1.0 fusion.3
  292.8 0.0 copy-start.1
  292.8 1.1 convolution_subtract_fusion.1
  293.9 1.1 fusion.12
  295.0 0.6 fusion.16
  295.6 0.0 copy-done.2
  295.6 0.0 copy-done.1
  295.6 4.9 %convolution_subtract_fusion = f32[2048,256]{1,0:T(8,128)} fusion(f32[2048,256]{1,0:T(8,128)S(1)} %copy-done.1, f32[256,256]{1,0:T(8,128)S(1)} %pad_maximum_fusion, f32[2048,128]{0,1:T(8,128)S(1)} %fusion.12, f32[2048,128]{0,1:T(8,128)S(1)} %bitcast.43), kind=kOutput, calls=%fused_computation.2 | convolution fusion | flops 1611661312 | bytes 6553600 | tf_op jit(solution)/shard_map/dot_general | solution.py:24
  (10 shorter events, 0.2 us)
Async XLA Ops:
  7.2 72.3 %all-gather.2.cloned.1.call-start = ((), (), s32[]{:S(2)}) async-start(), calls=%async_computation | async-start | bytes 2228224 | tf_op jit(solution)/shard_map/all_gather | solution.py:13
  7.9 221.0 %all-reduce.4.cloned.1.call-start = ((), (), s32[]{:S(2)}) async-start(), calls=%async_computation.1 | async-start | bytes 1048576 | tf_op jit(solution)/shard_map/psum | solution.py:16
  79.5 4.9 %copy-start = (f32[2048,256]{0,1:T(8,128)S(1)}, f32[2048,256]{0,1:T(8,128)}, u32[]{:S(2)}) copy-start(f32[2048,256]{0,1:T(8,128)} %all-gather.2.cloned.1.call-done) | copy-start | bytes 6291460
  228.9 61.9 %copy-start.3 = (f32[256,256]{1,0:T(8,128)S(1)}, f32[256,256]{1,0:T(8,128)}, u32[]{:S(2)}) copy-start(f32[256,256]{1,0:T(8,128)} %get-tuple-element.20) | copy-start | bytes 786436
  291.8 3.9 %copy-start.2 = (f32[256,256]{1,0:T(8,128)}, f32[256,256]{1,0:T(8,128)S(1)}, u32[]{:S(2)}) copy-start(f32[256,256]{1,0:T(8,128)S(1)} %pad_maximum_fusion) | copy-start | bytes 786436
  292.8 2.8 copy-start.1
Sparse Core Ops, SparseCore 0:
  10.1 69.3 all-gather.1
  88.7 140.1 all-reduce.3
where the time goes:
time: 308 us; the launch traced here: 307 us
  waiting for transfers between devices  213 us (69%)
  other arithmetic  55.5 us (18%)
  matrix products  18.5 us (6%)
  between operations  15.5 us (5%)
  local copies, waits for them, and re-layouts  5.19 us (2%)
    psum x1, waiting for transfers between devices, per_device(): gram_total, totals = lax.psum((gram_local, cross_local), 'row')  140 us
    all_gather x1, waiting for transfers between devices, per_device(): gathered = lax.all_gather(panel, 'col', axis=1, tiled=True)  71.5 us
    another operation x6, other arithmetic, per_device(): lower_factor = jnp.linalg.cholesky(gram_total)  34.1 us
    another operation x4, other arithmetic, per_device(): lax.linalg.triangular_solve(lower_factor, totals, left_side=True, lower=T...  19.7 us
  transfers between devices with their start and end apart: 2, of which 2 were waited for; matrix products, arithmetic and copies ran while one was open for 0% of the time, Pallas kernels for 0%

commit v1 on v0

--- a/solution.py
+++ b/solution.py
@@ -8,20 +8,31 @@
 contract_rows = (((0,), (0,)), ((), ()))
 
 
+def row_sum(x):
+    n = lax.axis_size("row")
+    rows, cols = x.shape
+    parts = x.reshape(n, rows // n, cols)
+    mine = lax.all_to_all(parts, "row", 0, 0, tiled=False).sum(0)
+    copies = jnp.broadcast_to(mine[None], (n, rows // n, cols))
+    return lax.all_to_all(copies, "row", 0, 0, tiled=False).reshape(rows, cols)
+
+
 def per_device(panel, slab):
     highest = lax.Precision.HIGHEST
     gathered = lax.all_gather(panel, "col", axis=1, tiled=True)
     cross_local = lax.dot_general(gathered, slab, contract_rows, precision=highest)
     gram_local = lax.dot_general(gathered, gathered, contract_rows, precision=highest)
-    gram_total, totals = lax.psum((gram_local, cross_local), "row")
+    width = gram_local.shape[1]
+    summed = row_sum(jnp.concatenate([gram_local, cross_local], axis=1))
+    gram_total, totals = summed[:, :width], summed[:, width:]
     lower_factor = jnp.linalg.cholesky(gram_total)
     projected = lax.linalg.triangular_solve(
         lower_factor, totals, left_side=True, lower=True, transpose_a=False
     )
-    basis_rows = lax.linalg.triangular_solve(
-        lower_factor, gathered, left_side=False, lower=True, transpose_a=True
+    coefficients = lax.linalg.triangular_solve(
+        lower_factor, projected, left_side=True, lower=True, transpose_a=True
     )
-    residual = slab - jnp.dot(basis_rows, projected, precision=highest)
+    residual = slab - jnp.dot(gathered, coefficients, precision=highest)
     col_width = panel.shape[1]
     rows_total = gathered.shape[0] * lax.axis_size("row")
     scaled = lower_factor.T * (1.0 / math.sqrt(rows_total))

time: 308 us -> 208 us (0.68)
  waiting for transfers between devices: 213 us -> 80.7 us
  blocking collectives: 0 us -> 28 us
  local copies, waits for them, and re-layouts: 5.19 us -> 11 us
  matrix products: 18.5 us -> 13.3 us
  starting transfers between devices: 0.08 us -> 3.89 us
    psum x1 -> x0, waiting for transfers between devices: 140 us -> none  [per_device(): gram_total, totals = lax.psum((gram_local, cross_local), 'row')]
    all_to_all x0 -> x1, blocking collectives: none -> 28 us  [row_sum(): mine = lax.all_to_all(parts, 'row', 0, 0, tiled=False).sum(0)]
    all_to_all x0 -> x1, waiting for transfers between devices: none -> 8.49 us  [row_sum(): return lax.all_to_all(copies, 'row', 0, 0, tiled=False).reshape(rows, cols)]
    unnamed x8 -> x9, local copies, waits for them, and re-layouts: 0.02 us -> 5.91 us
    all_to_all x0 -> x1, starting transfers between devices: none -> 3.85 us  [row_sum(): return lax.all_to_all(copies, 'row', 0, 0, tiled=False).reshape(rows, cols)]
  transfers between devices with their start and end apart: 2 -> 2, of which waited for: 2 -> 2; matrix products, arithmetic and copies ran while one was open for 0% -> 1% of each run, Pallas kernels for 0% -> 0%
where the time goes in v1:
time: 208 us
  waiting for transfers between devices  80.7 us (39%)
  other arithmetic  55.3 us (27%)
  blocking collectives  28 us (13%)
  between operations  15.5 us (7%)
  matrix products  13.3 us (6%)
  local copies, waits for them, and re-layouts  11 us (5%)
  starting transfers between devices  3.89 us (2%)
    all_gather x1, waiting for transfers between devices, per_device(): gathered = lax.all_gather(panel, 'col', axis=1, tiled=True)  71.6 us
    another operation x6, other arithmetic, per_device(): lower_factor = jnp.linalg.cholesky(gram_total)  33.9 us
    all_to_all x1, blocking collectives, row_sum(): mine = lax.all_to_all(parts, 'row', 0, 0, tiled=False).sum(0)  28 us
    another operation x4, other arithmetic, per_device(): lax.linalg.triangular_solve(lower_factor, totals, left_side=True, lower=T...  20.7 us
    all_to_all x1, waiting for transfers between devices, row_sum(): return lax.all_to_all(copies, 'row', 0, 0, tiled=False).reshape(rows, cols)  8.49 us
    unnamed x9, local copies, waits for them, and re-layouts  5.91 us
    dot_general x1, matrix products, per_device(): lax.dot_general(gathered, gathered, contract_rows, precision=highest)  4.23 us
  transfers between devices with their start and end apart: 2, of which 2 were waited for; matrix products, arithmetic and copies ran while one was open for 1% of the time, Pallas kernels for 0%

profile of v1, /device:TPU:1, one launch (start us, length us, event | category | flops | bytes accessed | tf_op | source)
XLA Modules:
  0.0 207.8 jit_solution(18180346574200016031)
XLA Ops:
  7.2 0.0 all-gather.2.cloned.1.call-start
  7.2 0.7 all-gather.2.cloned.1.call-update
  7.9 71.6 %all-gather.2.cloned.1.call-done = f32[2048,256]{0,1:T(8,128)} async-done(((f32[2048,16]{0,1:T(8,128)}), f32[2048,256]{0,1:T(8,128)}) %all-gather.2.cloned.1.call-update) | async-done | bytes 2097168 | tf_op jit(solution)/shard_map/all_gather | solution.py:22
  79.5 0.0 copy-start
  79.5 0.0 copy-start.2
  79.5 4.2 %fusion.19 = f32[256,256]{0,1:T(8,128)S(1)} fusion(f32[2048,256]{0,1:T(8,128)} %all-gather.2.cloned.1.call-done), kind=kOutput, calls=%fused_computation.43 | convolution fusion | flops 1610612736 | bytes 2359296 | tf_op jit(solution)/shard_map/dot_general | solution.py:24
  83.7 0.0 copy-done
  83.7 0.0 copy-done.2
  83.7 3.6 %fusion.20 = f32[256,256]{0,1:T(8,128)S(1)} fusion(f32[2048,256]{0,1:T(8,128)S(1)} %copy-done, f32[2048,256]{1,0:T(8,128)S(1)} %copy-done.2), kind=kOutput, calls=%fused_computation.44 | convolution fusion | flops 1610612736 | bytes 4456448 | tf_op jit(solution)/shard_map/dot_general | solution.py:23
  87.3 0.2 copy.8
  87.5 28.0 %all_to_all.10 = f32[32,8,512]{2,1,0:T(8,128)S(1)} all-to-all(f32[32,8,512]{2,1,0:T(8,128)S(1)} %bitcast.53), channel_id=1, replica_groups=mesh['row'=32,'col'=16] {'row'}, dimensions={0} | all-to-all | bytes 1048576 | tf_op jit(solution)/shard_map/all_to_all | solution.py:15
  115.6 0.8 broadcast_in_dim.3
  116.4 3.9 %all-to-all-start.1 = ((f32[32,8,512]{2,1,0:T(8,128)}), f32[32,8,512]{2,1,0:T(8,128)S(1)}, u32[]{:S(2)}, u32[]{:S(2)}) async-start(f32[32,8,512]{2,1,0:T(8,128)} %broadcast_in_dim.3), calls=%async_computation.1 | async-start | bytes 1048576 | tf_op jit(solution)/shard_map/all_to_all | solution.py:17
  120.3 2.9 %copy.11 = f32[2048,256]{0,1:T(8,128)} copy(f32[2048,256]{1,0:T(8,128)} %param.3) | data formatting | bytes 4194304 | tf_op args[1]
  123.2 8.5 %all-to-all-done.1 = f32[32,8,512]{2,1,0:T(8,128)S(1)} async-done(((f32[32,8,512]{2,1,0:T(8,128)}), f32[32,8,512]{2,1,0:T(8,128)S(1)}, u32[]{:S(2)}, u32[]{:S(2)}) %all-to-all-start.1) | async-done | bytes 524320 | tf_op jit(solution)/shard_map/all_to_all | solution.py:17
  131.7 0.1 copy.13
  131.9 11.7 %cholesky.50 = f32[128,128]{1,0:T(8,128)S(1)} custom-call(f32[128,128]{1,0:T(8,128)S(1)} %cholesky.118), custom_call_target="Cholesky" | custom-call | tf_op jit(solution)/shard_map/jit(cholesky)/cholesky | solution.py:28
  143.7 9.8 %custom-call.16 = f32[1,128,128]{1,2,0:T(8,128)S(1)} custom-call(f32[1,128,128]{2,1,0:T(8,128)S(1)} %get-tuple-element.32), custom_call_target="InvertDiagBlocksLowerTriangular" | custom-call | tf_op jit(solution)/shard_map/jit(cholesky)/cholesky | solution.py:28
  153.5 0.2 constant_dynamic-update-slice_fusion
  153.7 0.3 convolution_subtract_fusion.2
  154.0 11.7 %cholesky.105 = f32[128,128]{1,0:T(8,128)S(1)} custom-call(f32[128,128]{1,0:T(8,128)S(1)} %convolution_subtract_fusion.2), custom_call_target="Cholesky" | custom-call | tf_op jit(solution)/shard_map/jit(cholesky)/cholesky | solution.py:28
  165.7 0.6 compare_reduce_fusion
  167.7 0.1 triangular_solve.53
  167.8 4.0 %while.1 = (s32[]{:T(128)}, f32[256,256]{1,0:T(8,128)S(1)}, s32[2,2]{1,0:T(2,128)S(1)}, f32[2,128,128]{2,1,0:T(8,128)S(1)}, s32[]{:T(128)}) while((s32[]{:T(128)}, f32[256,256]{1,0:T(8,128)S(1)}, s32[2,2]{1,0:T(2,128)S(1)}, f32[2,128,128]{2,1,0:T(8,128)S(1)}, s32[]{:T(128)}) %tuple.30), condition=%wide.while_cond, body=%wide.while_body.sunk | while | flops 2 | bytes 131189 | solution.py:29
  167.8 0.6 fusion.34
  168.4 1.4 bitcast_dynamic-update-slice_fusion.2
  169.8 0.6 fusion.34
  170.4 1.4 bitcast_dynamic-update-slice_fusion.2
  171.8 19.9 %custom-call.17 = f32[2,128,128]{1,2,0:T(8,128)S(1)} custom-call(f32[2,128,128]{2,1,0:T(8,128)S(1)} %get-tuple-element.10), custom_call_target="InvertDiagBlocksLowerTriangular" | custom-call | tf_op jit(solution)/shard_map/triangular_solve | solution.py:29
  191.7 0.0 copy-start.1
  191.7 0.3 fusion.6
  192.0 0.3 convolution_subtract_fusion.1
  192.3 0.3 fusion.13
  192.6 0.3 fusion.12
  192.9 0.7 pad_maximum_fusion.1
  193.6 0.3 convolution_subtract_fusion
  193.9 0.3 fusion.11
  194.2 0.0 copy-done.1
  194.2 3.3 %fusion = f32[2048,256]{0,1:T(8,128)} fusion(f32[2048,256]{0,1:T(8,128)S(1)} %copy-done.1, f32[2048,256]{0,1:T(8,128)S(1)} %copy-done, f32[128,256]{1,0:T(8,128)S(1)} %fusion.12, f32[128,256]{1,0:T(8,128)S(1)} %fusion.11), kind=kOutput, calls=%fused_computation.3 | convolution fusion | flops 1611202560 | bytes 6553600 | tf_op jit(solution)/shard_map/dot_general | solution.py:35
  197.5 2.9 %copy.12 = f32[2048,256]{1,0:T(8,128)} copy(f32[2048,256]{0,1:T(8,128)} %fusion) | data formatting | bytes 4194304
  200.4 0.6 fusion.16
  (13 shorter events, 0.3 us)
Async XLA Ops:
  7.2 72.3 %all-gather.2.cloned.1.call-start = ((), (), s32[]{:S(2)}) async-start(), calls=%async_computation.2 | async-start | bytes 2228224 | tf_op jit(solution)/shard_map/all_gather | solution.py:22
  79.5 4.2 %copy-start = (f32[2048,256]{0,1:T(8,128)S(1)}, f32[2048,256]{0,1:T(8,128)}, u32[]{:S(2)}) copy-start(f32[2048,256]{0,1:T(8,128)} %all-gather.2.cloned.1.call-done) | copy-start | bytes 6291460
  79.5 4.2 %copy-start.2 = (f32[2048,256]{1,0:T(8,128)S(1)}, f32[2048,256]{1,0:T(8,128)}, u32[]{:S(2)}) copy-start(f32[2048,256]{1,0:T(8,128)} %param.3) | copy-start | bytes 6291460
  116.4 15.3 %all-to-all-start.1 = ((f32[32,8,512]{2,1,0:T(8,128)}), f32[32,8,512]{2,1,0:T(8,128)S(1)}, u32[]{:S(2)}, u32[]{:S(2)}) async-start(f32[32,8,512]{2,1,0:T(8,128)} %broadcast_in_dim.3), calls=%async_computation.1 | async-start | bytes 1048576 | tf_op jit(solution)/shard_map/all_to_all | solution.py:17
  191.7 2.5 %copy-start.1 = (f32[2048,256]{0,1:T(8,128)S(1)}, f32[2048,256]{0,1:T(8,128)}, u32[]{:S(2)}) copy-start(f32[2048,256]{0,1:T(8,128)} %copy.11) | copy-start | bytes 6291460
Sparse Core Ops, SparseCore 0:
  10.1 69.3 all-gather.1

commit v2 on v1

--- a/solution.py
+++ b/solution.py
@@ -26,12 +26,12 @@
     summed = row_sum(jnp.concatenate([gram_local, cross_local], axis=1))
     gram_total, totals = summed[:, :width], summed[:, width:]
     lower_factor = jnp.linalg.cholesky(gram_total)
-    projected = lax.linalg.triangular_solve(
-        lower_factor, totals, left_side=True, lower=True, transpose_a=False
+    eye = jnp.eye(lower_factor.shape[0], dtype=lower_factor.dtype)
+    lower_inverse = lax.linalg.triangular_solve(
+        lower_factor, eye, left_side=True, lower=True, transpose_a=False
     )
-    coefficients = lax.linalg.triangular_solve(
-        lower_factor, projected, left_side=True, lower=True, transpose_a=True
-    )
+    projected = jnp.dot(lower_inverse, totals, precision=highest)
+    coefficients = lax.dot_general(lower_inverse, projected, contract_rows, precision=highest)
     residual = slab - jnp.dot(gathered, coefficients, precision=highest)
     col_width = panel.shape[1]
     rows_total = gathered.shape[0] * lax.axis_size("row")

time: 208 us -> 209 us (level)
    another operation x4 -> x3, other arithmetic: 20.7 us -> 20.5 us  [per_device(): lax.linalg.triangular_solve(lower_factor, eye, left_side=True, lower=True...]
    unnamed x9 -> x11, local copies, waits for them, and re-layouts: 5.91 us -> 5.91 us
where the time goes in v2:
time: 209 us
  waiting for transfers between devices  80.7 us (39%)
  other arithmetic  55.3 us (26%)
  blocking collectives  28 us (13%)
  between operations  15.5 us (7%)
  matrix products  13.4 us (6%)
  local copies, waits for them, and re-layouts  12.3 us (6%)
  starting transfers between devices  3.89 us (2%)
    all_gather x1, waiting for transfers between devices, per_device(): gathered = lax.all_gather(panel, 'col', axis=1, tiled=True)  71.6 us
    another operation x6, other arithmetic, per_device(): lower_factor = jnp.linalg.cholesky(gram_total)  34 us
    all_to_all x1, blocking collectives, row_sum(): mine = lax.all_to_all(parts, 'row', 0, 0, tiled=False).sum(0)  28 us
    another operation x3, other arithmetic, per_device(): lax.linalg.triangular_solve(lower_factor, eye, left_side=True, lower=True...  20.5 us
    all_to_all x1, waiting for transfers between devices, row_sum(): return lax.all_to_all(copies, 'row', 0, 0, tiled=False).reshape(rows, cols)  8.46 us
    unnamed x11, local copies, waits for them, and re-layouts  5.91 us
    another operation x6, local copies, waits for them, and re-layouts  5.19 us
    dot_general x1, matrix products, per_device(): lax.dot_general(gathered, gathered, contract_rows, precision=highest)  4.23 us
  transfers between devices with their start and end apart: 2, of which 2 were waited for; matrix products, arithmetic and copies ran while one was open for 1% of the time, Pallas kernels for 0%

profile of v2, /device:TPU:1, one launch (start us, length us, event | category | flops | bytes accessed | tf_op | source)
XLA Modules:
  0.0 209.0 jit_solution(15957067106627559851)
XLA Ops:
  7.2 0.0 all-gather.2.cloned.1.call-start
  7.2 0.7 all-gather.2.cloned.1.call-update
  7.9 71.6 %all-gather.2.cloned.1.call-done = f32[2048,256]{0,1:T(8,128)} async-done(((f32[2048,16]{0,1:T(8,128)}), f32[2048,256]{0,1:T(8,128)}) %all-gather.2.cloned.1.call-update) | async-done | bytes 2097168 | tf_op jit(solution)/shard_map/all_gather | solution.py:22
  79.5 0.0 copy-start
  79.5 0.0 copy-start.2
  79.5 4.2 %fusion.17 = f32[256,256]{0,1:T(8,128)S(1)} fusion(f32[2048,256]{0,1:T(8,128)} %all-gather.2.cloned.1.call-done), kind=kOutput, calls=%fused_computation.41 | convolution fusion | flops 1610612736 | bytes 2359296 | tf_op jit(solution)/shard_map/dot_general | solution.py:24
  83.7 0.0 copy-done
  83.7 0.0 copy-done.2
  83.7 3.6 %fusion.18 = f32[256,256]{0,1:T(8,128)S(1)} fusion(f32[2048,256]{0,1:T(8,128)S(1)} %copy-done, f32[2048,256]{1,0:T(8,128)S(1)} %copy-done.2), kind=kOutput, calls=%fused_computation.42 | convolution fusion | flops 1610612736 | bytes 4456448 | tf_op jit(solution)/shard_map/dot_general | solution.py:23
  87.3 0.2 copy.8
  87.5 28.0 %all_to_all.10 = f32[32,8,512]{2,1,0:T(8,128)S(1)} all-to-all(f32[32,8,512]{2,1,0:T(8,128)S(1)} %bitcast.49), channel_id=1, replica_groups=mesh['row'=32,'col'=16] {'row'}, dimensions={0} | all-to-all | bytes 1048576 | tf_op jit(solution)/shard_map/all_to_all | solution.py:15
  115.6 0.8 broadcast_in_dim.3
  116.4 3.9 %all-to-all-start.1 = ((f32[32,8,512]{2,1,0:T(8,128)}), f32[32,8,512]{2,1,0:T(8,128)S(1)}, u32[]{:S(2)}, u32[]{:S(2)}) async-start(f32[32,8,512]{2,1,0:T(8,128)} %broadcast_in_dim.3), calls=%async_computation.1 | async-start | bytes 1048576 | tf_op jit(solution)/shard_map/all_to_all | solution.py:17
  120.3 2.9 %copy.11 = f32[2048,256]{0,1:T(8,128)} copy(f32[2048,256]{1,0:T(8,128)} %param.3) | data formatting | bytes 4194304 | tf_op args[1]
  123.2 8.5 %all-to-all-done.1 = f32[32,8,512]{2,1,0:T(8,128)S(1)} async-done(((f32[32,8,512]{2,1,0:T(8,128)}), f32[32,8,512]{2,1,0:T(8,128)S(1)}, u32[]{:S(2)}, u32[]{:S(2)}) %all-to-all-start.1) | async-done | bytes 524320 | tf_op jit(solution)/shard_map/all_to_all | solution.py:17
  131.7 0.1 copy.13
  131.8 0.1 fusion.3
  131.9 11.7 %cholesky.50 = f32[128,128]{1,0:T(8,128)S(1)} custom-call(f32[128,128]{1,0:T(8,128)S(1)} %cholesky.118), custom_call_target="Cholesky" | custom-call | tf_op jit(solution)/shard_map/jit(cholesky)/cholesky | solution.py:28
  143.7 9.8 %custom-call.14 = f32[1,128,128]{1,2,0:T(8,128)S(1)} custom-call(f32[1,128,128]{2,1,0:T(8,128)S(1)} %get-tuple-element.32), custom_call_target="InvertDiagBlocksLowerTriangular" | custom-call | tf_op jit(solution)/shard_map/jit(cholesky)/cholesky | solution.py:28
  153.5 0.2 constant_dynamic-update-slice_fusion
  153.7 0.3 convolution_subtract_fusion.1
  154.0 11.7 %cholesky.105 = f32[128,128]{1,0:T(8,128)S(1)} custom-call(f32[128,128]{1,0:T(8,128)S(1)} %convolution_subtract_fusion.1), custom_call_target="Cholesky" | custom-call | tf_op jit(solution)/shard_map/jit(cholesky)/cholesky | solution.py:28
  165.7 0.7 compare_reduce_fusion
  167.7 0.1 triangular_solve.44
  167.8 5.2 %while.1 = (s32[]{:T(128)}, f32[256,256]{1,0:T(8,128)S(1)}, s32[2,2]{1,0:T(2,128)S(1)}, f32[2,128,128]{2,1,0:T(8,128)}, s32[]{:T(128)}) while((s32[]{:T(128)}, f32[256,256]{1,0:T(8,128)S(1)}, s32[2,2]{1,0:T(2,128)S(1)}, f32[2,128,128]{2,1,0:T(8,128)}, s32[]{:T(128)}) %tuple.30), condition=%wide.while_cond, body=%wide.while_body.sunk | while | flops 2 | bytes 132205 | solution.py:30
  167.8 0.6 fusion.31
  168.4 2.0 bitcast_dynamic-update-slice_fusion.2
  170.4 0.6 fusion.31
  171.0 2.0 bitcast_dynamic-update-slice_fusion.2
  173.0 20.5 %custom-call.15 = f32[2,128,128]{1,2,0:T(8,128)S(1)} custom-call(f32[2,128,128]{2,1,0:T(8,128)} %get-tuple-element.10), custom_call_target="InvertDiagBlocksLowerTriangular" | custom-call | tf_op jit(solution)/shard_map/triangular_solve | solution.py:30
  193.5 0.0 copy-start.1
  193.5 0.3 fusion.6
  193.8 0.3 convolution_subtract_fusion
  194.0 0.3 fusion.9
  194.4 0.4 fusion.1
  194.7 0.0 copy-start.3
  194.8 0.6 fusion.5
  195.4 0.0 copy-done.1
  195.4 3.3 %fusion = f32[2048,256]{0,1:T(8,128)} fusion(f32[2048,256]{0,1:T(8,128)S(1)} %copy-done.1, f32[256,256]{1,0:T(8,128)S(1)} %fusion.5, f32[2048,256]{0,1:T(8,128)S(1)} %copy-done), kind=kOutput, calls=%fused_computation.3 | convolution fusion | flops 1611137024 | bytes 6553600 | tf_op jit(solution)/shard_map/dot_general | solution.py:35
  198.7 0.0 copy-done.3
  198.7 2.9 %copy.12 = f32[2048,256]{1,0:T(8,128)} copy(f32[2048,256]{0,1:T(8,128)} %fusion) | data formatting | bytes 4194304
  201.6 0.6 fusion.13
  (13 shorter events, 0.3 us)
Async XLA Ops:
  7.2 72.3 %all-gather.2.cloned.1.call-start = ((), (), s32[]{:S(2)}) async-start(), calls=%async_computation.2 | async-start | bytes 2228224 | tf_op jit(solution)/shard_map/all_gather | solution.py:22
  79.5 4.2 %copy-start = (f32[2048,256]{0,1:T(8,128)S(1)}, f32[2048,256]{0,1:T(8,128)}, u32[]{:S(2)}) copy-start(f32[2048,256]{0,1:T(8,128)} %all-gather.2.cloned.1.call-done) | copy-start | bytes 6291460
  79.5 4.2 %copy-start.2 = (f32[2048,256]{1,0:T(8,128)S(1)}, f32[2048,256]{1,0:T(8,128)}, u32[]{:S(2)}) copy-start(f32[2048,256]{1,0:T(8,128)} %param.3) | copy-start | bytes 6291460
  116.4 15.3 %all-to-all-start.1 = ((f32[32,8,512]{2,1,0:T(8,128)}), f32[32,8,512]{2,1,0:T(8,128)S(1)}, u32[]{:S(2)}, u32[]{:S(2)}) async-start(f32[32,8,512]{2,1,0:T(8,128)} %broadcast_in_dim.3), calls=%async_computation.1 | async-start | bytes 1048576 | tf_op jit(solution)/shard_map/all_to_all | solution.py:17
  193.5 1.9 copy-start.1
  194.7 3.9 %copy-start.3 = (f32[256,256]{1,0:T(8,128)}, f32[256,256]{1,0:T(8,128)S(1)}, u32[]{:S(2)}) copy-start(f32[256,256]{1,0:T(8,128)S(1)} %fusion.1) | copy-start | bytes 786436
Sparse Core Ops, SparseCore 0:
  10.1 69.3 all-gather.1

commit v3 on v2

--- a/solution.py
+++ b/solution.py
@@ -3,9 +3,55 @@
 import jax
 import jax.numpy as jnp
 from jax import lax
+from jax.experimental import pallas as pl
+from jax.experimental.pallas import tpu as pltpu
 from jax.sharding import PartitionSpec as P
 
 contract_rows = (((0,), (0,)), ((), ()))
+HIGHEST = lax.Precision.HIGHEST
+
+
+def factor_kernel(gram_ref, upper_ref, inverse_ref, work_ref):
+    n = gram_ref.shape[0]
+    rows = lax.broadcasted_iota(jnp.int32, (n, n), 0)
+    cols = lax.broadcasted_iota(jnp.int32, (n, n), 1)
+    work_ref[:, :n] = gram_ref[...]
+    work_ref[:, n:] = jnp.where(rows == cols, 1.0, 0.0).astype(jnp.float32)
+    lane = lax.broadcasted_iota(jnp.int32, (8, 2 * n), 1)
+    sub = lax.broadcasted_iota(jnp.int32, (8, 2 * n), 0)
+    sub_col = lax.broadcasted_iota(jnp.int32, (8, 1), 0)
+
+    def block(b, carry):
+        base = pl.multiple_of(b * 8, 8)
+        strip = work_ref[pl.ds(base, 8), :]
+        for t in range(8):
+            col = jnp.sum(jnp.where(lane == base + t, strip, 0.0), axis=1, keepdims=True)
+            scale = 1.0 / jnp.sqrt(col[t:t + 1, :])
+            pivot = strip[t:t + 1, :] * scale
+            mult = jnp.where(sub_col > t, col * scale, 0.0)
+            strip = jnp.where(sub == t, pivot, strip - mult * pivot)
+        work_ref[pl.ds(base, 8), :] = strip
+        left = jnp.where(lane[:, :n] > base + 7, strip[:, :n], 0.0)
+        update = lax.dot_general(left, strip, contract_rows,
+                                 precision=HIGHEST, preferred_element_type=jnp.float32)
+        work_ref[...] = work_ref[...] - update
+        return carry
+
+    lax.fori_loop(0, n // 8, block, 0)
+    done = work_ref[...]
+    upper_ref[...] = jnp.where(cols >= rows, done[:, :n], 0.0)
+    inverse_ref[...] = jnp.where(cols <= rows, done[:, n:], 0.0)
+
+
+def factor(gram):
+    n = gram.shape[0]
+    return pl.pallas_call(
+        factor_kernel,
+        out_shape=(jax.ShapeDtypeStruct((n, n), jnp.float32),) * 2,
+        in_specs=[pl.BlockSpec(memory_space=pltpu.VMEM)],
+        out_specs=(pl.BlockSpec(memory_space=pltpu.VMEM),) * 2,
+        scratch_shapes=[pltpu.VMEM((n, 2 * n), jnp.float32)],
+    )(gram)
 
 
 def row_sum(x):
@@ -25,17 +71,13 @@
     width = gram_local.shape[1]
     summed = row_sum(jnp.concatenate([gram_local, cross_local], axis=1))
     gram_total, totals = summed[:, :width], summed[:, width:]
-    lower_factor = jnp.linalg.cholesky(gram_total)
-    eye = jnp.eye(lower_factor.shape[0], dtype=lower_factor.dtype)
-    lower_inverse = lax.linalg.triangular_solve(
-        lower_factor, eye, left_side=True, lower=True, transpose_a=False
-    )
+    upper_factor, lower_inverse = factor(gram_total)
     projected = jnp.dot(lower_inverse, totals, precision=highest)
     coefficients = lax.dot_general(lower_inverse, projected, contract_rows, precision=highest)
     residual = slab - jnp.dot(gathered, coefficients, precision=highest)
     col_width = panel.shape[1]
     rows_total = gathered.shape[0] * lax.axis_size("row")
-    scaled = lower_factor.T * (1.0 / math.sqrt(rows_total))
+    scaled = upper_factor * (1.0 / math.sqrt(rows_total))
     triangle = lax.dynamic_slice_in_dim(scaled, lax.axis_index("col") * col_width, col_width, 1)
     return (triangle, projected, residual)
 

time: 209 us -> 199 us (0.952)
  other arithmetic: 55.3 us -> 1.18 us
  Pallas kernels: 0 us -> 46.6 us
  local copies, waits for them, and re-layouts: 12.3 us -> 8.23 us
  matrix products: 13.4 us -> 15.5 us
    another operation x9 -> x0, other arithmetic: 54.5 us -> none  [the longest x6 34 us: per_device(): lower_factor = jnp.linalg.cholesky(gram_total)]
    pallas_call x0 -> x1, Pallas kernels: none -> 46.6 us  [factor(): pl.pallas_call(factor_kernel, out_shape=(jax.ShapeDtypeStruct((n, n), jnp...]
    another operation x9 -> x0, local copies, waits for them, and re-layouts: 5.29 us -> none
    unnamed x11 -> x9, local copies, waits for them, and re-layouts: 5.91 us -> 6.46 us
where the time goes in v3:
time: 199 us; the launch traced here: 198 us
  waiting for transfers between devices  80.9 us (41%)
  Pallas kernels  46.6 us (23%)
  blocking collectives  28 us (14%)
  matrix products  15.5 us (8%)
  between operations  14.1 us (7%)
  local copies, waits for them, and re-layouts  8.23 us (4%)
  starting transfers between devices  3.71 us (2%)
    all_gather x1, waiting for transfers between devices, per_device(): gathered = lax.all_gather(panel, 'col', axis=1, tiled=True)  71.6 us
    pallas_call x1, Pallas kernels, factor(): pl.pallas_call(factor_kernel, out_shape=(jax.ShapeDtypeStruct((n, n), jnp...  46.6 us
    all_to_all x1, blocking collectives, row_sum(): mine = lax.all_to_all(parts, 'row', 0, 0, tiled=False).sum(0)  28 us
    all_to_all x1, waiting for transfers between devices, row_sum(): return lax.all_to_all(copies, 'row', 0, 0, tiled=False).reshape(rows, cols)  8.68 us
    unnamed x9, local copies, waits for them, and re-layouts  6.46 us
    dot_general x1, matrix products, per_device(): residual = slab - jnp.dot(gathered, coefficients, precision=highest)  4.88 us
    dot_general x1, matrix products, per_device(): lax.dot_general(gathered, gathered, contract_rows, precision=highest)  4.23 us
  transfers between devices with their start and end apart: 2, of which 2 were waited for; matrix products, arithmetic and copies ran while one was open for 1% of the time, Pallas kernels for 0%

profile of v3, /device:TPU:1, one launch (start us, length us, event | category | flops | bytes accessed | tf_op | source)
XLA Modules:
  0.0 198.3 jit_solution(3790255430281744886)
XLA Ops:
  7.2 0.0 all-gather.2.cloned.1.call-start
  7.2 0.7 all-gather.2.cloned.1.call-update
  7.9 71.6 %all-gather.2.cloned.1.call-done = f32[2048,256]{0,1:T(8,128)} async-done(((f32[2048,16]{0,1:T(8,128)}), f32[2048,256]{0,1:T(8,128)}) %all-gather.2.cloned.1.call-update) | async-done | bytes 2097168 | tf_op jit(solution)/shard_map/all_gather | solution.py:68
  79.5 0.0 copy-start
  79.5 0.0 copy-start.1
  79.5 4.2 %fusion.3 = f32[256,256]{0,1:T(8,128)S(1)} fusion(f32[2048,256]{0,1:T(8,128)} %all-gather.2.cloned.1.call-done), kind=kOutput, calls=%fused_computation.6 | convolution fusion | flops 1610612736 | bytes 2359296 | tf_op jit(solution)/shard_map/dot_general | solution.py:70
  83.7 0.0 copy-done
  83.7 0.0 copy-done.1
  83.7 3.6 %fusion.4 = f32[256,256]{0,1:T(8,128)S(1)} fusion(f32[2048,256]{0,1:T(8,128)S(1)} %copy-done, f32[2048,256]{1,0:T(8,128)S(1)} %copy-done.1), kind=kOutput, calls=%fused_computation.7 | convolution fusion | flops 1610612736 | bytes 4456448 | tf_op jit(solution)/shard_map/dot_general | solution.py:69
  87.3 0.2 copy.8
  87.5 28.0 %all_to_all.10 = f32[32,8,512]{2,1,0:T(8,128)S(1)} all-to-all(f32[32,8,512]{2,1,0:T(8,128)S(1)} %bitcast.17), channel_id=1, replica_groups=mesh['row'=32,'col'=16] {'row'}, dimensions={0} | all-to-all | bytes 1048576 | tf_op jit(solution)/shard_map/all_to_all | solution.py:61
  115.6 0.9 broadcast_in_dim.2
  116.4 3.7 %all-to-all-start.1 = ((f32[32,8,512]{2,1,0:T(8,128)}), f32[32,8,512]{2,1,0:T(8,128)S(1)}, u32[]{:S(2)}, u32[]{:S(2)}) async-start(f32[32,8,512]{2,1,0:T(8,128)} %broadcast_in_dim.2), calls=%async_computation.1 | async-start | bytes 1048576 | tf_op jit(solution)/shard_map/all_to_all | solution.py:63
  120.1 2.9 %copy.9 = f32[2048,256]{0,1:T(8,128)} copy(f32[2048,256]{1,0:T(8,128)} %param.3) | data formatting | bytes 4194304 | tf_op args[1]
  123.0 8.7 %all-to-all-done.1 = f32[32,8,512]{2,1,0:T(8,128)S(1)} async-done(((f32[32,8,512]{2,1,0:T(8,128)}), f32[32,8,512]{2,1,0:T(8,128)S(1)}, u32[]{:S(2)}, u32[]{:S(2)}) %all-to-all-start.1) | async-done | bytes 524320 | tf_op jit(solution)/shard_map/all_to_all | solution.py:63
  131.7 0.7 slice.8.gram_ref
  132.4 46.6 %shard_map.49 = (f32[256,256]{1,0:T(8,128)}, f32[256,256]{1,0:T(8,128)}) custom-call(f32[256,256]{1,0:T(8,128)} %slice.8.gram_ref), custom_call_target="tpu_custom_call" | custom-call | tf_op jit(solution)/shard_map/pallas_call | solution.py:48
  179.0 1.3 fusion.1
  180.3 0.0 copy-start.2
  180.3 1.1 dynamic-slice_multiply_fusion
  181.4 0.7 copy.10
  182.1 1.5 fusion.5
  183.6 4.9 %fusion = f32[2048,256]{0,1:T(8,128)} fusion(f32[2048,256]{0,1:T(8,128)} %copy.9, f32[256,256]{1,0:T(8,128)S(1)} %fusion.5, f32[2048,256]{0,1:T(8,128)S(1)} %copy-done), kind=kOutput, calls=%fused_computation.1 | convolution fusion | flops 1611137024 | bytes 6553600 | tf_op jit(solution)/shard_map/dot_general | solution.py:77
  188.5 0.0 copy-done.2
  188.5 2.9 %copy.11 = f32[2048,256]{1,0:T(8,128)} copy(f32[2048,256]{0,1:T(8,128)} %fusion) | data formatting | bytes 4194304
  (2 shorter events, 0.1 us)
Async XLA Ops:
  7.2 72.3 %all-gather.2.cloned.1.call-start = ((), (), s32[]{:S(2)}) async-start(), calls=%async_computation.2 | async-start | bytes 2228224 | tf_op jit(solution)/shard_map/all_gather | solution.py:68
  79.5 4.2 %copy-start = (f32[2048,256]{0,1:T(8,128)S(1)}, f32[2048,256]{0,1:T(8,128)}, u32[]{:S(2)}) copy-start(f32[2048,256]{0,1:T(8,128)} %all-gather.2.cloned.1.call-done) | copy-start | bytes 6291460
  79.5 4.2 %copy-start.1 = (f32[2048,256]{1,0:T(8,128)S(1)}, f32[2048,256]{1,0:T(8,128)}, u32[]{:S(2)}) copy-start(f32[2048,256]{1,0:T(8,128)} %param.3) | copy-start | bytes 6291460
  116.4 15.3 %all-to-all-start.1 = ((f32[32,8,512]{2,1,0:T(8,128)}), f32[32,8,512]{2,1,0:T(8,128)S(1)}, u32[]{:S(2)}, u32[]{:S(2)}) async-start(f32[32,8,512]{2,1,0:T(8,128)} %broadcast_in_dim.2), calls=%async_computation.1 | async-start | bytes 1048576 | tf_op jit(solution)/shard_map/all_to_all | solution.py:63
  180.3 8.2 %copy-start.2 = (f32[256,256]{1,0:T(8,128)}, f32[256,256]{1,0:T(8,128)S(1)}, u32[]{:S(2)}) copy-start(f32[256,256]{1,0:T(8,128)S(1)} %fusion.1) | copy-start | bytes 786436
Sparse Core Ops, SparseCore 0:
  10.1 69.3 all-gather.1

commit v4 on v3

--- a/solution.py
+++ b/solution.py
@@ -17,27 +17,36 @@
     cols = lax.broadcasted_iota(jnp.int32, (n, n), 1)
     work_ref[:, :n] = gram_ref[...]
     work_ref[:, n:] = jnp.where(rows == cols, 1.0, 0.0).astype(jnp.float32)
-    lane = lax.broadcasted_iota(jnp.int32, (8, 2 * n), 1)
-    sub = lax.broadcasted_iota(jnp.int32, (8, 2 * n), 0)
     sub_col = lax.broadcasted_iota(jnp.int32, (8, 1), 0)
+    half = n // 2
 
-    def block(b, carry):
-        base = pl.multiple_of(b * 8, 8)
-        strip = work_ref[pl.ds(base, 8), :]
-        for t in range(8):
-            col = jnp.sum(jnp.where(lane == base + t, strip, 0.0), axis=1, keepdims=True)
-            scale = 1.0 / jnp.sqrt(col[t:t + 1, :])
-            pivot = strip[t:t + 1, :] * scale
-            mult = jnp.where(sub_col > t, col * scale, 0.0)
-            strip = jnp.where(sub == t, pivot, strip - mult * pivot)
-        work_ref[pl.ds(base, 8), :] = strip
-        left = jnp.where(lane[:, :n] > base + 7, strip[:, :n], 0.0)
-        update = lax.dot_general(left, strip, contract_rows,
-                                 precision=HIGHEST, preferred_element_type=jnp.float32)
-        work_ref[...] = work_ref[...] - update
-        return carry
+    def phase(first, last, lo, hi):
+        width = hi - lo
+        lane = lax.broadcasted_iota(jnp.int32, (8, width), 1) + lo
+        sub = lax.broadcasted_iota(jnp.int32, (8, width), 0)
+        key = n - lo
 
-    lax.fori_loop(0, n // 8, block, 0)
+        def block(b, carry):
+            base = pl.multiple_of(b * 8, 8)
+            strip = work_ref[pl.ds(base, 8), lo:hi]
+            for t in range(8):
+                col = jnp.sum(jnp.where(lane[:, :key] == base + t, strip[:, :key], 0.0),
+                              axis=1, keepdims=True)
+                scale = 1.0 / jnp.sqrt(col[t:t + 1, :])
+                pivot = strip[t:t + 1, :] * scale
+                mult = jnp.where(sub_col > t, col * scale, 0.0)
+                strip = jnp.where(sub == t, pivot, strip - mult * pivot)
+            work_ref[pl.ds(base, 8), lo:hi] = strip
+            left = jnp.where(lane[:, :key] > base + 7, strip[:, :key], 0.0)
+            update = lax.dot_general(left, strip, contract_rows,
+                                     precision=HIGHEST, preferred_element_type=jnp.float32)
+            work_ref[lo:n, lo:hi] = work_ref[lo:n, lo:hi] - update
+            return carry
+
+        lax.fori_loop(first, last, block, 0)
+
+    phase(0, half // 8, 0, n + half)
+    phase(half // 8, n // 8, half, 2 * n)
     done = work_ref[...]
     upper_ref[...] = jnp.where(cols >= rows, done[:, :n], 0.0)
     inverse_ref[...] = jnp.where(cols <= rows, done[:, n:], 0.0)

time: 199 us -> 192 us (0.965)
  Pallas kernels: 46.6 us -> 40.2 us
    pallas_call x1, Pallas kernels: 46.6 us -> 40.2 us  [factor(): pl.pallas_call(factor_kernel, out_shape=(jax.ShapeDtypeStruct((n, n), jnp...]
  transfers between devices with their start and end apart: 2 -> 2, of which waited for: 2 -> 2; matrix products, arithmetic and copies ran while one was open for 1% -> 2% of each run, Pallas kernels for 0% -> 0%
where the time goes in v4:
time: 192 us
  waiting for transfers between devices  80.9 us (42%)
  Pallas kernels  40.2 us (21%)
  blocking collectives  28 us (15%)
  matrix products  15.5 us (8%)
  between operations  14.1 us (7%)
  local copies, waits for them, and re-layouts  8.23 us (4%)
  starting transfers between devices  3.71 us (2%)
    all_gather x1, waiting for transfers between devices, per_device(): gathered = lax.all_gather(panel, 'col', axis=1, tiled=True)  71.6 us
    pallas_call x1, Pallas kernels, factor(): pl.pallas_call(factor_kernel, out_shape=(jax.ShapeDtypeStruct((n, n), jnp...  40.2 us
    all_to_all x1, blocking collectives, row_sum(): mine = lax.all_to_all(parts, 'row', 0, 0, tiled=False).sum(0)  28 us
    all_to_all x1, waiting for transfers between devices, row_sum(): return lax.all_to_all(copies, 'row', 0, 0, tiled=False).reshape(rows, cols)  8.68 us
    unnamed x9, local copies, waits for them, and re-layouts  6.46 us
    dot_general x1, matrix products, per_device(): residual = slab - jnp.dot(gathered, coefficients, precision=highest)  4.88 us
    dot_general x1, matrix products, per_device(): lax.dot_general(gathered, gathered, contract_rows, precision=highest)  4.23 us
  transfers between devices with their start and end apart: 2, of which 2 were waited for; matrix products, arithmetic and copies ran while one was open for 2% of the time, Pallas kernels for 0%

profile of v4, /device:TPU:1, one launch (start us, length us, event | category | flops | bytes accessed | tf_op | source)
XLA Modules:
  0.0 191.9 jit_solution(10023881378898932530)
XLA Ops:
  7.2 0.0 all-gather.2.cloned.1.call-start
  7.2 0.7 all-gather.2.cloned.1.call-update
  7.9 71.6 %all-gather.2.cloned.1.call-done = f32[2048,256]{0,1:T(8,128)} async-done(((f32[2048,16]{0,1:T(8,128)}), f32[2048,256]{0,1:T(8,128)}) %all-gather.2.cloned.1.call-update) | async-done | bytes 2097168 | tf_op jit(solution)/shard_map/all_gather | solution.py:77
  79.5 0.0 copy-start
  79.5 0.0 copy-start.1
  79.5 4.2 %fusion.3 = f32[256,256]{0,1:T(8,128)S(1)} fusion(f32[2048,256]{0,1:T(8,128)} %all-gather.2.cloned.1.call-done), kind=kOutput, calls=%fused_computation.6 | convolution fusion | flops 1610612736 | bytes 2359296 | tf_op jit(solution)/shard_map/dot_general | solution.py:79
  83.7 0.0 copy-done
  83.7 0.0 copy-done.1
  83.7 3.6 %fusion.4 = f32[256,256]{0,1:T(8,128)S(1)} fusion(f32[2048,256]{0,1:T(8,128)S(1)} %copy-done, f32[2048,256]{1,0:T(8,128)S(1)} %copy-done.1), kind=kOutput, calls=%fused_computation.7 | convolution fusion | flops 1610612736 | bytes 4456448 | tf_op jit(solution)/shard_map/dot_general | solution.py:78
  87.3 0.2 copy.8
  87.5 28.0 %all_to_all.10 = f32[32,8,512]{2,1,0:T(8,128)S(1)} all-to-all(f32[32,8,512]{2,1,0:T(8,128)S(1)} %bitcast.17), channel_id=1, replica_groups=mesh['row'=32,'col'=16] {'row'}, dimensions={0} | all-to-all | bytes 1048576 | tf_op jit(solution)/shard_map/all_to_all | solution.py:70
  115.6 0.9 broadcast_in_dim.2
  116.4 3.7 %all-to-all-start.1 = ((f32[32,8,512]{2,1,0:T(8,128)}), f32[32,8,512]{2,1,0:T(8,128)S(1)}, u32[]{:S(2)}, u32[]{:S(2)}) async-start(f32[32,8,512]{2,1,0:T(8,128)} %broadcast_in_dim.2), calls=%async_computation.1 | async-start | bytes 1048576 | tf_op jit(solution)/shard_map/all_to_all | solution.py:72
  120.1 2.9 %copy.9 = f32[2048,256]{0,1:T(8,128)} copy(f32[2048,256]{1,0:T(8,128)} %param.3) | data formatting | bytes 4194304 | tf_op args[1]
  123.0 8.7 %all-to-all-done.1 = f32[32,8,512]{2,1,0:T(8,128)S(1)} async-done(((f32[32,8,512]{2,1,0:T(8,128)}), f32[32,8,512]{2,1,0:T(8,128)S(1)}, u32[]{:S(2)}, u32[]{:S(2)}) %all-to-all-start.1) | async-done | bytes 524320 | tf_op jit(solution)/shard_map/all_to_all | solution.py:72
  131.7 0.7 slice.8.gram_ref
  132.4 40.2 %shard_map.49 = (f32[256,256]{1,0:T(8,128)}, f32[256,256]{1,0:T(8,128)}) custom-call(f32[256,256]{1,0:T(8,128)} %slice.8.gram_ref), custom_call_target="tpu_custom_call" | custom-call | tf_op jit(solution)/shard_map/pallas_call | solution.py:57
  172.6 1.3 fusion.1
  173.9 0.0 copy-start.2
  173.9 1.1 dynamic-slice_multiply_fusion
  175.0 0.7 copy.10
  175.7 1.5 fusion.5
  177.2 4.9 %fusion = f32[2048,256]{0,1:T(8,128)} fusion(f32[2048,256]{0,1:T(8,128)} %copy.9, f32[256,256]{1,0:T(8,128)S(1)} %fusion.5, f32[2048,256]{0,1:T(8,128)S(1)} %copy-done), kind=kOutput, calls=%fused_computation.1 | convolution fusion | flops 1611137024 | bytes 6553600 | tf_op jit(solution)/shard_map/dot_general | solution.py:86
  182.1 0.0 copy-done.2
  182.1 2.9 %copy.11 = f32[2048,256]{1,0:T(8,128)} copy(f32[2048,256]{0,1:T(8,128)} %fusion) | data formatting | bytes 4194304
  (2 shorter events, 0.1 us)
Async XLA Ops:
  7.2 72.3 %all-gather.2.cloned.1.call-start = ((), (), s32[]{:S(2)}) async-start(), calls=%async_computation.2 | async-start | bytes 2228224 | tf_op jit(solution)/shard_map/all_gather | solution.py:77
  79.5 4.2 %copy-start = (f32[2048,256]{0,1:T(8,128)S(1)}, f32[2048,256]{0,1:T(8,128)}, u32[]{:S(2)}) copy-start(f32[2048,256]{0,1:T(8,128)} %all-gather.2.cloned.1.call-done) | copy-start | bytes 6291460
  79.5 4.2 %copy-start.1 = (f32[2048,256]{1,0:T(8,128)S(1)}, f32[2048,256]{1,0:T(8,128)}, u32[]{:S(2)}) copy-start(f32[2048,256]{1,0:T(8,128)} %param.3) | copy-start | bytes 6291460
  116.4 15.3 %all-to-all-start.1 = ((f32[32,8,512]{2,1,0:T(8,128)}), f32[32,8,512]{2,1,0:T(8,128)S(1)}, u32[]{:S(2)}, u32[]{:S(2)}) async-start(f32[32,8,512]{2,1,0:T(8,128)} %broadcast_in_dim.2), calls=%async_computation.1 | async-start | bytes 1048576 | tf_op jit(solution)/shard_map/all_to_all | solution.py:72
  173.9 8.2 %copy-start.2 = (f32[256,256]{1,0:T(8,128)}, f32[256,256]{1,0:T(8,128)S(1)}, u32[]{:S(2)}) copy-start(f32[256,256]{1,0:T(8,128)S(1)} %fusion.1) | copy-start | bytes 786436
Sparse Core Ops, SparseCore 0:
  10.1 69.3 all-gather.1

commit v5 on v4

--- a/solution.py
+++ b/solution.py
@@ -63,6 +63,21 @@
     )(gram)
 
 
+def col_gather(x):
+    n = lax.axis_size("col")
+    ahead, behind = x, x
+    got = {0: x}
+    for step in range(1, n // 2 + 1):
+        ahead = lax.ppermute(ahead, "col", [(i, (i + 1) % n) for i in range(n)])
+        got[-step] = ahead
+        if step < n // 2:
+            behind = lax.ppermute(behind, "col", [(i, (i - 1) % n) for i in range(n)])
+            got[step] = behind
+    rotated = jnp.concatenate([got[k] for k in range(-(n // 2), n - n // 2)], axis=1)
+    shift = (lax.axis_index("col") - n // 2) * x.shape[1]
+    return jnp.roll(rotated, shift, axis=1)
+
+
 def row_sum(x):
     n = lax.axis_size("row")
     rows, cols = x.shape
@@ -74,7 +89,7 @@
 
 def per_device(panel, slab):
     highest = lax.Precision.HIGHEST
-    gathered = lax.all_gather(panel, "col", axis=1, tiled=True)
+    gathered = col_gather(panel)
     cross_local = lax.dot_general(gathered, slab, contract_rows, precision=highest)
     gram_local = lax.dot_general(gathered, gathered, contract_rows, precision=highest)
     width = gram_local.shape[1]

time: 192 us -> 174 us (0.906)
  waiting for transfers between devices: 80.9 us -> 25.7 us
  starting transfers between devices: 3.71 us -> 55.3 us
  between operations: 14.1 us -> 1.17 us
    all_gather x1 -> x0, waiting for transfers between devices: 71.6 us -> none  [per_device(): gathered = lax.all_gather(panel, 'col', axis=1, tiled=True)]
    ppermute x0 -> x15, starting transfers between devices: none -> 51.4 us  [the longest x7 33.6 us: col_gather(): behind = lax.ppermute(behind, 'col', [(i, (i - 1) % n) for i in range(n)])]
    ppermute x0 -> x15, waiting for transfers between devices: none -> 14.3 us  [the longest x8 14.3 us: col_gather(): ahead = lax.ppermute(ahead, 'col', [(i, (i + 1) % n) for i in range(n)])]
    all_to_all x1, waiting for transfers between devices: 8.68 us -> 11.4 us  [row_sum(): return lax.all_to_all(copies, 'row', 0, 0, tiled=False).reshape(rows, cols)]
    dot_general x1, matrix products: 4.23 us -> 1.87 us  [per_device(): lax.dot_general(gathered, gathered, contract_rows, precision=highest)]
    unnamed x9 -> x48, local copies, waits for them, and re-layouts: 6.46 us -> 7.15 us
  transfers between devices with their start and end apart: 2 -> 16, of which waited for: 2 -> 9; matrix products, arithmetic and copies ran while one was open for 2% -> 1% of each run, Pallas kernels for 0% -> 0%
where the time goes in v5:
time: 174 us
  starting transfers between devices  55.3 us (32%)
  Pallas kernels  40.2 us (23%)
  blocking collectives  27.4 us (16%)
  waiting for transfers between devices  25.7 us (15%)
  matrix products  14.7 us (8%)
  local copies, waits for them, and re-layouts  8.93 us (5%)
    pallas_call x1, Pallas kernels, factor(): pl.pallas_call(factor_kernel, out_shape=(jax.ShapeDtypeStruct((n, n), jnp...  40.2 us
    ppermute x7, starting transfers between devices, col_gather(): behind = lax.ppermute(behind, 'col', [(i, (i - 1) % n) for i in range(n)])  33.6 us
    all_to_all x1, blocking collectives, row_sum(): mine = lax.all_to_all(parts, 'row', 0, 0, tiled=False).sum(0)  27.4 us
    ppermute x8, starting transfers between devices, col_gather(): ahead = lax.ppermute(ahead, 'col', [(i, (i + 1) % n) for i in range(n)])  17.9 us
    ppermute x8, waiting for transfers between devices, col_gather(): ahead = lax.ppermute(ahead, 'col', [(i, (i + 1) % n) for i in range(n)])  14.3 us
    all_to_all x1, waiting for transfers between devices, row_sum(): return lax.all_to_all(copies, 'row', 0, 0, tiled=False).reshape(rows, cols)  11.4 us
    unnamed x48, local copies, waits for them, and re-layouts  7.15 us
    dot_general x1, matrix products, per_device(): residual = slab - jnp.dot(gathered, coefficients, precision=highest)  6.36 us
  transfers between devices with their start and end apart: 16, of which 9 were waited for; matrix products, arithmetic and copies ran while one was open for 1% of the time, Pallas kernels for 0%

profile of v5, /device:TPU:1, one launch (start us, length us, event | category | flops | bytes accessed | tf_op | source)
XLA Modules:
  0.0 173.6 jit_solution(10316970231818611729)
XLA Ops:
  0.6 0.0 copy-start.3
  0.6 4.5 %collective-permute-start = (f32[2048,16]{0,1:T(8,128)}, f32[2048,16]{0,1:T(8,128)S(1)}, u32[]{:S(2)}, u32[]{:S(2)}) collective-permute-start(f32[2048,16]{0,1:T(8,128)} %param.2), channel_id=1, source_target_pairs={{0,1},{1,2},{2,3},{3,4},{4,5},{5,6},{6,7},{7,8},{8,9},{9,10},{10,1... | collective-permute-start | bytes 393224 | tf_op jit(solution)/shard_map/ppermute | solution.py:71
  5.2 11.0 %collective-permute-done = f32[2048,16]{0,1:T(8,128)S(1)} collective-permute-done((f32[2048,16]{0,1:T(8,128)}, f32[2048,16]{0,1:T(8,128)S(1)}, u32[]{:S(2)}, u32[]{:S(2)}) %collective-permute-start) | collective-permute-done | bytes 131104 | tf_op jit(solution)/shard_map/ppermute | solution.py:71
  16.2 1.9 %collective-permute-start.1 = (f32[2048,16]{0,1:T(8,128)S(1)}, f32[2048,16]{0,1:T(8,128)S(1)}, u32[]{:S(2)}, u32[]{:S(2)}) collective-permute-start(f32[2048,16]{0,1:T(8,128)S(1)} %collective-permute-done), channel_id=1, source_target_pairs={{0,1},{1,2},{2,3},{3,4},{4,5},{5,6},{6,7},{7,8},{8,9},{9,10},{10,1... | collective-permute-start | bytes 393224 | tf_op jit(solution)/shard_map/ppermute | solution.py:71
  18.1 4.6 %collective-permute-start.8 = (f32[2048,16]{0,1:T(8,128)}, f32[2048,16]{0,1:T(8,128)S(1)}, u32[]{:S(2)}, u32[]{:S(2)}) collective-permute-start(f32[2048,16]{0,1:T(8,128)} %param.2), channel_id=1, source_target_pairs={{0,15},{1,0},{2,1},{3,2},{4,3},{5,4},{6,5},{7,6},{8,7},{9,8},{10,9... | collective-permute-start | bytes 393224 | tf_op jit(solution)/shard_map/ppermute | solution.py:74
  22.7 0.4 collective-permute-done.1
  23.1 1.9 %collective-permute-start.2 = (f32[2048,16]{0,1:T(8,128)S(1)}, f32[2048,16]{0,1:T(8,128)S(1)}, u32[]{:S(2)}, u32[]{:S(2)}) collective-permute-start(f32[2048,16]{0,1:T(8,128)S(1)} %collective-permute-done.1), channel_id=1, source_target_pairs={{0,1},{1,2},{2,3},{3,4},{4,5},{5,6},{6,7},{7,8},{8,9},{9,10},{10,1... | collective-permute-start | bytes 393224 | tf_op jit(solution)/shard_map/ppermute | solution.py:71
  25.0 0.0 collective-permute-done.8
  25.0 4.8 %collective-permute-start.9 = (f32[2048,16]{0,1:T(8,128)S(1)}, f32[2048,16]{0,1:T(8,128)S(1)}, u32[]{:S(2)}, u32[]{:S(2)}) collective-permute-start(f32[2048,16]{0,1:T(8,128)S(1)} %collective-permute-done.8), channel_id=1, source_target_pairs={{0,15},{1,0},{2,1},{3,2},{4,3},{5,4},{6,5},{7,6},{8,7},{9,8},{10,9... | collective-permute-start | bytes 393224 | tf_op jit(solution)/shard_map/ppermute | solution.py:74
  29.8 0.2 collective-permute-done.2
  30.0 1.9 %collective-permute-start.3 = (f32[2048,16]{0,1:T(8,128)S(1)}, f32[2048,16]{0,1:T(8,128)S(1)}, u32[]{:S(2)}, u32[]{:S(2)}) collective-permute-start(f32[2048,16]{0,1:T(8,128)S(1)} %collective-permute-done.2), channel_id=1, source_target_pairs={{0,1},{1,2},{2,3},{3,4},{4,5},{5,6},{6,7},{7,8},{8,9},{9,10},{10,1... | collective-permute-start | bytes 393224 | tf_op jit(solution)/shard_map/ppermute | solution.py:71
  31.9 0.0 collective-permute-done.9
  31.9 4.8 %collective-permute-start.10 = (f32[2048,16]{0,1:T(8,128)S(1)}, f32[2048,16]{0,1:T(8,128)S(1)}, u32[]{:S(2)}, u32[]{:S(2)}) collective-permute-start(f32[2048,16]{0,1:T(8,128)S(1)} %collective-permute-done.9), channel_id=1, source_target_pairs={{0,15},{1,0},{2,1},{3,2},{4,3},{5,4},{6,5},{7,6},{8,7},{9,8},{10,9... | collective-permute-start | bytes 393224 | tf_op jit(solution)/shard_map/ppermute | solution.py:74
  36.7 0.2 collective-permute-done.3
  36.9 1.9 %collective-permute-start.4 = (f32[2048,16]{0,1:T(8,128)S(1)}, f32[2048,16]{0,1:T(8,128)S(1)}, u32[]{:S(2)}, u32[]{:S(2)}) collective-permute-start(f32[2048,16]{0,1:T(8,128)S(1)} %collective-permute-done.3), channel_id=1, source_target_pairs={{0,1},{1,2},{2,3},{3,4},{4,5},{5,6},{6,7},{7,8},{8,9},{9,10},{10,1... | collective-permute-start | bytes 393224 | tf_op jit(solution)/shard_map/ppermute | solution.py:71
  38.8 0.0 collective-permute-done.10
  38.8 4.8 %collective-permute-start.11 = (f32[2048,16]{0,1:T(8,128)S(1)}, f32[2048,16]{0,1:T(8,128)S(1)}, u32[]{:S(2)}, u32[]{:S(2)}) collective-permute-start(f32[2048,16]{0,1:T(8,128)S(1)} %collective-permute-done.10), channel_id=1, source_target_pairs={{0,15},{1,0},{2,1},{3,2},{4,3},{5,4},{6,5},{7,6},{8,7},{9,8},{10,9... | collective-permute-start | bytes 393224 | tf_op jit(solution)/shard_map/ppermute | solution.py:74
  43.6 0.2 collective-permute-done.4
  43.8 1.9 %collective-permute-start.5 = (f32[2048,16]{0,1:T(8,128)S(1)}, f32[2048,16]{0,1:T(8,128)S(1)}, u32[]{:S(2)}, u32[]{:S(2)}) collective-permute-start(f32[2048,16]{0,1:T(8,128)S(1)} %collective-permute-done.4), channel_id=1, source_target_pairs={{0,1},{1,2},{2,3},{3,4},{4,5},{5,6},{6,7},{7,8},{8,9},{9,10},{10,1... | collective-permute-start | bytes 393224 | tf_op jit(solution)/shard_map/ppermute | solution.py:71
  45.7 0.0 collective-permute-done.11
  45.7 4.8 %collective-permute-start.12 = (f32[2048,16]{0,1:T(8,128)S(1)}, f32[2048,16]{0,1:T(8,128)S(1)}, u32[]{:S(2)}, u32[]{:S(2)}) collective-permute-start(f32[2048,16]{0,1:T(8,128)S(1)} %collective-permute-done.11), channel_id=1, source_target_pairs={{0,15},{1,0},{2,1},{3,2},{4,3},{5,4},{6,5},{7,6},{8,7},{9,8},{10,9... | collective-permute-start | bytes 393224 | tf_op jit(solution)/shard_map/ppermute | solution.py:74
  50.5 0.2 collective-permute-done.5
  50.7 0.0 copy-start.4
  50.7 1.9 %collective-permute-start.6 = (f32[2048,16]{0,1:T(8,128)S(1)}, f32[2048,16]{0,1:T(8,128)S(1)}, u32[]{:S(2)}, u32[]{:S(2)}) collective-permute-start(f32[2048,16]{0,1:T(8,128)S(1)} %collective-permute-done.5), channel_id=1, source_target_pairs={{0,1},{1,2},{2,3},{3,4},{4,5},{5,6},{6,7},{7,8},{8,9},{9,10},{10,1... | collective-permute-start | bytes 393224 | tf_op jit(solution)/shard_map/ppermute | solution.py:71
  52.6 0.0 collective-permute-done.12
  52.6 4.8 %collective-permute-start.13 = (f32[2048,16]{0,1:T(8,128)S(1)}, f32[2048,16]{0,1:T(8,128)}, u32[]{:S(2)}, u32[]{:S(2)}) collective-permute-start(f32[2048,16]{0,1:T(8,128)S(1)} %collective-permute-done.12), channel_id=1, source_target_pairs={{0,15},{1,0},{2,1},{3,2},{4,3},{5,4},{6,5},{7,6},{8,7},{9,8},{10,9... | collective-permute-start | bytes 393224 | tf_op jit(solution)/shard_map/ppermute | solution.py:74
  57.4 1.0 collective-permute-done.6
  58.4 1.9 %collective-permute-start.7 = (f32[2048,16]{0,1:T(8,128)S(1)}, f32[2048,16]{0,1:T(8,128)S(1)}, u32[]{:S(2)}, u32[]{:S(2)}) collective-permute-start(f32[2048,16]{0,1:T(8,128)S(1)} %collective-permute-done.6), channel_id=1, source_target_pairs={{0,1},{1,2},{2,3},{3,4},{4,5},{5,6},{6,7},{7,8},{8,9},{9,10},{10,1... | collective-permute-start | bytes 393224 | tf_op jit(solution)/shard_map/ppermute | solution.py:71
  60.3 0.0 collective-permute-done.13
  60.4 5.1 %collective-permute-start.14 = (f32[2048,16]{0,1:T(8,128)}, f32[2048,16]{0,1:T(8,128)S(1)}, u32[]{:S(2)}, u32[]{:S(2)}) collective-permute-start(f32[2048,16]{0,1:T(8,128)} %collective-permute-done.13), channel_id=1, source_target_pairs={{0,15},{1,0},{2,1},{3,2},{4,3},{5,4},{6,5},{7,6},{8,7},{9,8},{10,9... | collective-permute-start | bytes 393224 | tf_op jit(solution)/shard_map/ppermute | solution.py:74
  65.5 1.1 collective-permute-done.7
  66.6 0.0 copy-start.6
  66.7 0.0 copy-done.4
  66.7 0.0 copy-done.5
  66.7 0.5 copy-done.6
  67.2 0.9 constant_dynamic-update-slice_fusion.23
  68.1 0.0 copy-start.1
  68.3 1.0 constant_dynamic-update-slice_fusion.17
  69.3 0.0 collective-permute-done.14
  69.3 0.9 constant_dynamic-update-slice_fusion.15
  70.2 0.9 constant_dynamic-update-slice_fusion.14
  71.2 0.9 constant_dynamic-update-slice_fusion.13
  72.2 0.0 copy-done.3
  72.3 0.9 constant_dynamic-update-slice_fusion.1
  73.2 0.0 copy-start
  73.3 1.9 %fusion.3 = f32[256,256]{0,1:T(8,128)S(1)} fusion(f32[2048,512]{0,1:T(8,128)S(1)} %constant_dynamic-update-slice_fusion, s32[]{:T(128)S(6)} %select_n.17), kind=kOutput, calls=%fused_computation.4 | convolution fusion | flops 1610612736 | bytes 2359300 | tf_op jit(solution)/shard_map/dot_general | solution.py:94
  75.1 0.0 copy-done
  75.2 0.0 copy-done.1
  75.2 3.5 %fusion.1 = f32[256,256]{0,1:T(8,128)S(1)} fusion(f32[2048,256]{1,0:T(8,128)S(1)} %copy-done.1, f32[2048,512]{0,1:T(8,128)S(1)} %constant_dynamic-update-slice_fusion, s32[]{:T(128)S(6)} %select_n.17), kind=kOutput, calls=%fused_computation.2 | convolution fusion | flops 1610612736 | bytes 4456452 | tf_op jit(solution)/shard_map/dot_general | solution.py:93
  78.7 0.2 copy.6
  78.9 27.4 %all_to_all.10 = f32[32,8,512]{2,1,0:T(8,128)S(1)} all-to-all(f32[32,8,512]{2,1,0:T(8,128)S(1)} %bitcast.9), channel_id=1, replica_groups=mesh['row'=32,'col'=16] {'row'}, dimensions={0} | all-to-all | bytes 1048576 | tf_op jit(solution)/shard_map/all_to_all | solution.py:85
  106.4 0.9 broadcast_in_dim.2
  107.2 3.9 %all-to-all-start.1 = ((f32[32,8,512]{2,1,0:T(8,128)}), f32[32,8,512]{2,1,0:T(8,128)S(1)}, u32[]{:S(2)}, u32[]{:S(2)}) async-start(f32[32,8,512]{2,1,0:T(8,128)} %broadcast_in_dim.2), calls=%async_computation.1 | async-start | bytes 1048576 | tf_op jit(solution)/shard_map/all_to_all | solution.py:87
  111.1 11.4 %all-to-all-done.1 = f32[32,8,512]{2,1,0:T(8,128)S(1)} async-done(((f32[32,8,512]{2,1,0:T(8,128)}), f32[32,8,512]{2,1,0:T(8,128)S(1)}, u32[]{:S(2)}, u32[]{:S(2)}) %all-to-all-start.1) | async-done | bytes 524320 | tf_op jit(solution)/shard_map/all_to_all | solution.py:87
  122.5 0.7 slice.8.gram_ref
  123.2 40.2 %shard_map.49 = (f32[256,256]{1,0:T(8,128)}, f32[256,256]{1,0:T(8,128)}) custom-call(f32[256,256]{1,0:T(8,128)} %slice.8.gram_ref), custom_call_target="tpu_custom_call" | custom-call | tf_op jit(solution)/shard_map/pallas_call | solution.py:57
  163.4 1.4 fusion.5
  164.8 0.0 copy-start.2
  164.8 1.6 fusion.10
  166.4 6.4 %convolution_subtract_fusion = f32[2048,256]{1,0:T(8,128)} fusion(f32[2048,256]{1,0:T(8,128)S(1)} %copy-done.1, f32[256,256]{1,0:T(8,128)S(1)} %fusion.10, f32[2048,512]{0,1:T(8,128)} %copy-done, s32[]{:T(128)S(6)} %select_n.17), kind=kOutput, calls=%fused_computation | convolution fusion | flops 1611137024 | bytes 6553604 | tf_op jit(solution)/shard_map/dot_general | solution.py:101
  172.8 0.0 copy-done.7
  172.8 0.1 dynamic-slice_multiply_fusion
  172.9 0.7 copy.7
  173.6 0.0 copy-done.2
  (30 shorter events, 0.4 us)
Async XLA Ops:
  0.6 71.6 %copy-start.3 = (f32[2048,16]{0,1:T(8,128)S(1)}, f32[2048,16]{0,1:T(8,128)}, u32[]{:S(2)}) copy-start(f32[2048,16]{0,1:T(8,128)} %param.2) | copy-start | bytes 393220
  0.6 15.5 %collective-permute-start = (f32[2048,16]{0,1:T(8,128)}, f32[2048,16]{0,1:T(8,128)S(1)}, u32[]{:S(2)}, u32[]{:S(2)}) collective-permute-start(f32[2048,16]{0,1:T(8,128)} %param.2), channel_id=1, source_target_pairs={{0,1},{1,2},{2,3},{3,4},{4,5},{5,6},{6,7},{7,8},{8,9},{9,10},{10,1... | collective-permute-start | bytes 393224 | tf_op jit(solution)/shard_map/ppermute | solution.py:71
  16.2 6.9 %collective-permute-start.1 = (f32[2048,16]{0,1:T(8,128)S(1)}, f32[2048,16]{0,1:T(8,128)S(1)}, u32[]{:S(2)}, u32[]{:S(2)}) collective-permute-start(f32[2048,16]{0,1:T(8,128)S(1)} %collective-permute-done), channel_id=1, source_target_pairs={{0,1},{1,2},{2,3},{3,4},{4,5},{5,6},{6,7},{7,8},{8,9},{9,10},{10,1... | collective-permute-start | bytes 393224 | tf_op jit(solution)/shard_map/ppermute | solution.py:71
  18.1 6.9 %collective-permute-start.8 = (f32[2048,16]{0,1:T(8,128)}, f32[2048,16]{0,1:T(8,128)S(1)}, u32[]{:S(2)}, u32[]{:S(2)}) collective-permute-start(f32[2048,16]{0,1:T(8,128)} %param.2), channel_id=1, source_target_pairs={{0,15},{1,0},{2,1},{3,2},{4,3},{5,4},{6,5},{7,6},{8,7},{9,8},{10,9... | collective-permute-start | bytes 393224 | tf_op jit(solution)/shard_map/ppermute | solution.py:74
  23.1 6.9 %collective-permute-start.2 = (f32[2048,16]{0,1:T(8,128)S(1)}, f32[2048,16]{0,1:T(8,128)S(1)}, u32[]{:S(2)}, u32[]{:S(2)}) collective-permute-start(f32[2048,16]{0,1:T(8,128)S(1)} %collective-permute-done.1), channel_id=1, source_target_pairs={{0,1},{1,2},{2,3},{3,4},{4,5},{5,6},{6,7},{7,8},{8,9},{9,10},{10,1... | collective-permute-start | bytes 393224 | tf_op jit(solution)/shard_map/ppermute | solution.py:71
  25.0 6.9 %collective-permute-start.9 = (f32[2048,16]{0,1:T(8,128)S(1)}, f32[2048,16]{0,1:T(8,128)S(1)}, u32[]{:S(2)}, u32[]{:S(2)}) collective-permute-start(f32[2048,16]{0,1:T(8,128)S(1)} %collective-permute-done.8), channel_id=1, source_target_pairs={{0,15},{1,0},{2,1},{3,2},{4,3},{5,4},{6,5},{7,6},{8,7},{9,8},{10,9... | collective-permute-start | bytes 393224 | tf_op jit(solution)/shard_map/ppermute | solution.py:74
  30.0 6.9 %collective-permute-start.3 = (f32[2048,16]{0,1:T(8,128)S(1)}, f32[2048,16]{0,1:T(8,128)S(1)}, u32[]{:S(2)}, u32[]{:S(2)}) collective-permute-start(f32[2048,16]{0,1:T(8,128)S(1)} %collective-permute-done.2), channel_id=1, source_target_pairs={{0,1},{1,2},{2,3},{3,4},{4,5},{5,6},{6,7},{7,8},{8,9},{9,10},{10,1... | collective-permute-start | bytes 393224 | tf_op jit(solution)/shard_map/ppermute | solution.py:71
  31.9 6.9 %collective-permute-start.10 = (f32[2048,16]{0,1:T(8,128)S(1)}, f32[2048,16]{0,1:T(8,128)S(1)}, u32[]{:S(2)}, u32[]{:S(2)}) collective-permute-start(f32[2048,16]{0,1:T(8,128)S(1)} %collective-permute-done.9), channel_id=1, source_target_pairs={{0,15},{1,0},{2,1},{3,2},{4,3},{5,4},{6,5},{7,6},{8,7},{9,8},{10,9... | collective-permute-start | bytes 393224 | tf_op jit(solution)/shard_map/ppermute | solution.py:74
  36.9 6.9 %collective-permute-start.4 = (f32[2048,16]{0,1:T(8,128)S(1)}, f32[2048,16]{0,1:T(8,128)S(1)}, u32[]{:S(2)}, u32[]{:S(2)}) collective-permute-start(f32[2048,16]{0,1:T(8,128)S(1)} %collective-permute-done.3), channel_id=1, source_target_pairs={{0,1},{1,2},{2,3},{3,4},{4,5},{5,6},{6,7},{7,8},{8,9},{9,10},{10,1... | collective-permute-start | bytes 393224 | tf_op jit(solution)/shard_map/ppermute | solution.py:71
  38.8 6.9 %collective-permute-start.11 = (f32[2048,16]{0,1:T(8,128)S(1)}, f32[2048,16]{0,1:T(8,128)S(1)}, u32[]{:S(2)}, u32[]{:S(2)}) collective-permute-start(f32[2048,16]{0,1:T(8,128)S(1)} %collective-permute-done.10), channel_id=1, source_target_pairs={{0,15},{1,0},{2,1},{3,2},{4,3},{5,4},{6,5},{7,6},{8,7},{9,8},{10,9... | collective-permute-start | bytes 393224 | tf_op jit(solution)/shard_map/ppermute | solution.py:74
  43.8 6.9 %collective-permute-start.5 = (f32[2048,16]{0,1:T(8,128)S(1)}, f32[2048,16]{0,1:T(8,128)S(1)}, u32[]{:S(2)}, u32[]{:S(2)}) collective-permute-start(f32[2048,16]{0,1:T(8,128)S(1)} %collective-permute-done.4), channel_id=1, source_target_pairs={{0,1},{1,2},{2,3},{3,4},{4,5},{5,6},{6,7},{7,8},{8,9},{9,10},{10,1... | collective-permute-start | bytes 393224 | tf_op jit(solution)/shard_map/ppermute | solution.py:71
  45.7 6.9 %collective-permute-start.12 = (f32[2048,16]{0,1:T(8,128)S(1)}, f32[2048,16]{0,1:T(8,128)S(1)}, u32[]{:S(2)}, u32[]{:S(2)}) collective-permute-start(f32[2048,16]{0,1:T(8,128)S(1)} %collective-permute-done.11), channel_id=1, source_target_pairs={{0,15},{1,0},{2,1},{3,2},{4,3},{5,4},{6,5},{7,6},{8,7},{9,8},{10,9... | collective-permute-start | bytes 393224 | tf_op jit(solution)/shard_map/ppermute | solution.py:74
  50.7 16.0 %copy-start.4 = (f32[2048,16]{0,1:T(8,128)}, f32[2048,16]{0,1:T(8,128)S(1)}, u32[]{:S(2)}) copy-start(f32[2048,16]{0,1:T(8,128)S(1)} %collective-permute-done.5) | copy-start | bytes 393220
  50.7 7.7 %collective-permute-start.6 = (f32[2048,16]{0,1:T(8,128)S(1)}, f32[2048,16]{0,1:T(8,128)S(1)}, u32[]{:S(2)}, u32[]{:S(2)}) collective-permute-start(f32[2048,16]{0,1:T(8,128)S(1)} %collective-permute-done.5), channel_id=1, source_target_pairs={{0,1},{1,2},{2,3},{3,4},{4,5},{5,6},{6,7},{7,8},{8,9},{9,10},{10,1... | collective-permute-start | bytes 393224 | tf_op jit(solution)/shard_map/ppermute | solution.py:71
  52.6 7.7 %collective-permute-start.13 = (f32[2048,16]{0,1:T(8,128)S(1)}, f32[2048,16]{0,1:T(8,128)}, u32[]{:S(2)}, u32[]{:S(2)}) collective-permute-start(f32[2048,16]{0,1:T(8,128)S(1)} %collective-permute-done.12), channel_id=1, source_target_pairs={{0,15},{1,0},{2,1},{3,2},{4,3},{5,4},{6,5},{7,6},{8,7},{9,8},{10,9... | collective-permute-start | bytes 393224 | tf_op jit(solution)/shard_map/ppermute | solution.py:74
  58.4 8.3 %copy-start.5 = (f32[2048,16]{0,1:T(8,128)}, f32[2048,16]{0,1:T(8,128)S(1)}, u32[]{:S(2)}) copy-start(f32[2048,16]{0,1:T(8,128)S(1)} %collective-permute-done.6) | copy-start | bytes 393220
  58.4 8.2 %collective-permute-start.7 = (f32[2048,16]{0,1:T(8,128)S(1)}, f32[2048,16]{0,1:T(8,128)S(1)}, u32[]{:S(2)}, u32[]{:S(2)}) collective-permute-start(f32[2048,16]{0,1:T(8,128)S(1)} %collective-permute-done.6), channel_id=1, source_target_pairs={{0,1},{1,2},{2,3},{3,4},{4,5},{5,6},{6,7},{7,8},{8,9},{9,10},{10,1... | collective-permute-start | bytes 393224 | tf_op jit(solution)/shard_map/ppermute | solution.py:71
  60.4 8.9 %collective-permute-start.14 = (f32[2048,16]{0,1:T(8,128)}, f32[2048,16]{0,1:T(8,128)S(1)}, u32[]{:S(2)}, u32[]{:S(2)}) collective-permute-start(f32[2048,16]{0,1:T(8,128)} %collective-permute-done.13), channel_id=1, source_target_pairs={{0,15},{1,0},{2,1},{3,2},{4,3},{5,4},{6,5},{7,6},{8,7},{9,8},{10,9... | collective-permute-start | bytes 393224 | tf_op jit(solution)/shard_map/ppermute | solution.py:74
  66.6 0.7 copy-start.6
  68.1 7.0 %copy-start.1 = (f32[2048,256]{1,0:T(8,128)S(1)}, f32[2048,256]{1,0:T(8,128)}, u32[]{:S(2)}) copy-start(f32[2048,256]{1,0:T(8,128)} %param.3) | copy-start | bytes 6291460
  73.2 1.9 %copy-start = (f32[2048,512]{0,1:T(8,128)}, f32[2048,512]{0,1:T(8,128)S(1)}, u32[]{:S(2)}) copy-start(f32[2048,512]{0,1:T(8,128)S(1)} %constant_dynamic-update-slice_fusion) | copy-start | bytes 12582916
  107.2 15.3 %all-to-all-start.1 = ((f32[32,8,512]{2,1,0:T(8,128)}), f32[32,8,512]{2,1,0:T(8,128)S(1)}, u32[]{:S(2)}, u32[]{:S(2)}) async-start(f32[32,8,512]{2,1,0:T(8,128)} %broadcast_in_dim.2), calls=%async_computation.1 | async-start | bytes 1048576 | tf_op jit(solution)/shard_map/all_to_all | solution.py:87
  163.4 9.4 %copy-start.7 = (f32[256,256]{1,0:T(8,128)S(1)}, f32[256,256]{1,0:T(8,128)}, u32[]{:S(2)}) copy-start(f32[256,256]{1,0:T(8,128)} %get-tuple-element.5) | copy-start | bytes 786436
  164.8 8.8 %copy-start.2 = (f32[256,256]{1,0:T(8,128)}, f32[256,256]{1,0:T(8,128)S(1)}, u32[]{:S(2)}) copy-start(f32[256,256]{1,0:T(8,128)S(1)} %fusion.5) | copy-start | bytes 786436

commit v6 on v5

--- a/solution.py
+++ b/solution.py
@@ -73,9 +73,7 @@
         if step < n // 2:
             behind = lax.ppermute(behind, "col", [(i, (i - 1) % n) for i in range(n)])
             got[step] = behind
-    rotated = jnp.concatenate([got[k] for k in range(-(n // 2), n - n // 2)], axis=1)
-    shift = (lax.axis_index("col") - n // 2) * x.shape[1]
-    return jnp.roll(rotated, shift, axis=1)
+    return jnp.concatenate([got[k] for k in range(-(n // 2), n - n // 2)], axis=1)
 
 
 def row_sum(x):
@@ -90,15 +88,16 @@
 def per_device(panel, slab):
     highest = lax.Precision.HIGHEST
     gathered = col_gather(panel)
+    shift = (lax.axis_index("col") - lax.axis_size("col") // 2) * panel.shape[1]
     cross_local = lax.dot_general(gathered, slab, contract_rows, precision=highest)
     gram_local = lax.dot_general(gathered, gathered, contract_rows, precision=highest)
     width = gram_local.shape[1]
-    summed = row_sum(jnp.concatenate([gram_local, cross_local], axis=1))
-    gram_total, totals = summed[:, :width], summed[:, width:]
+    summed = jnp.roll(row_sum(jnp.concatenate([gram_local, cross_local], axis=1)), shift, axis=0)
+    gram_total, totals = jnp.roll(summed[:, :width], shift, axis=1), summed[:, width:]
     upper_factor, lower_inverse = factor(gram_total)
     projected = jnp.dot(lower_inverse, totals, precision=highest)
     coefficients = lax.dot_general(lower_inverse, projected, contract_rows, precision=highest)
-    residual = slab - jnp.dot(gathered, coefficients, precision=highest)
+    residual = slab - jnp.dot(gathered, jnp.roll(coefficients, -shift, axis=0), precision=highest)
     col_width = panel.shape[1]
     rows_total = gathered.shape[0] * lax.axis_size("row")
     scaled = upper_factor * (1.0 / math.sqrt(rows_total))

time: 174 us -> 171 us (0.983)
  local copies, waits for them, and re-layouts: 8.93 us -> 1.95 us
  other arithmetic: 0.18 us -> 2.13 us
    unnamed x48 -> x22, local copies, waits for them, and re-layouts: 7.15 us -> 0.87 us
  transfers between devices with their start and end apart: 16 -> 16, of which waited for: 9 -> 10; matrix products, arithmetic and copies ran while one was open for 1% -> 0% of each run, Pallas kernels for 0% -> 0%
where the time goes in v6:
time: 171 us; the launch traced here: 170 us
  starting transfers between devices  55.2 us (32%)
  Pallas kernels  40.1 us (23%)
  blocking collectives  27.8 us (16%)
  waiting for transfers between devices  26.8 us (16%)
  matrix products  14.7 us (9%)
  other arithmetic  2.13 us (1%)
  local copies, waits for them, and re-layouts  1.95 us (1%)
    pallas_call x1, Pallas kernels, factor(): pl.pallas_call(factor_kernel, out_shape=(jax.ShapeDtypeStruct((n, n), jnp...  40.1 us
    ppermute x7, starting transfers between devices, col_gather(): behind = lax.ppermute(behind, 'col', [(i, (i - 1) % n) for i in range(n)])  33.4 us
    all_to_all x1, blocking collectives, row_sum(): mine = lax.all_to_all(parts, 'row', 0, 0, tiled=False).sum(0)  27.8 us
    ppermute x8, starting transfers between devices, col_gather(): ahead = lax.ppermute(ahead, 'col', [(i, (i + 1) % n) for i in range(n)])  17.9 us
    ppermute x8, waiting for transfers between devices, col_gather(): ahead = lax.ppermute(ahead, 'col', [(i, (i + 1) % n) for i in range(n)])  14.3 us
    all_to_all x1, waiting for transfers between devices, row_sum(): return lax.all_to_all(copies, 'row', 0, 0, tiled=False).reshape(rows, cols)  11.3 us
    dot_general x1, matrix products, per_device(): jnp.dot(gathered, jnp.roll(coefficients, -shift, axis=0), precision=highest)  6.36 us
    all_to_all x1, starting transfers between devices, row_sum(): return lax.all_to_all(copies, 'row', 0, 0, tiled=False).reshape(rows, cols)  3.86 us
  transfers between devices with their start and end apart: 16, of which 10 were waited for; matrix products, arithmetic and copies ran while one was open for 0% of the time, Pallas kernels for 0%

profile of v6, /device:TPU:1, one launch (start us, length us, event | category | flops | bytes accessed | tf_op | source)
XLA Modules:
  0.0 169.8 jit_solution(4632637671275511690)
XLA Ops:
  0.6 0.0 copy-start.2
  0.6 4.5 %collective-permute-start = (f32[2048,16]{0,1:T(8,128)}, f32[2048,16]{0,1:T(8,128)S(1)}, u32[]{:S(2)}, u32[]{:S(2)}) collective-permute-start(f32[2048,16]{0,1:T(8,128)} %param.2), channel_id=1, source_target_pairs={{0,1},{1,2},{2,3},{3,4},{4,5},{5,6},{6,7},{7,8},{8,9},{9,10},{10,1... | collective-permute-start | bytes 393224 | tf_op jit(solution)/shard_map/ppermute | solution.py:71
  5.2 11.0 %collective-permute-done = f32[2048,16]{0,1:T(8,128)S(1)} collective-permute-done((f32[2048,16]{0,1:T(8,128)}, f32[2048,16]{0,1:T(8,128)S(1)}, u32[]{:S(2)}, u32[]{:S(2)}) %collective-permute-start) | collective-permute-done | bytes 131104 | tf_op jit(solution)/shard_map/ppermute | solution.py:71
  16.1 1.9 %collective-permute-start.1 = (f32[2048,16]{0,1:T(8,128)S(1)}, f32[2048,16]{0,1:T(8,128)S(1)}, u32[]{:S(2)}, u32[]{:S(2)}) collective-permute-start(f32[2048,16]{0,1:T(8,128)S(1)} %collective-permute-done), channel_id=1, source_target_pairs={{0,1},{1,2},{2,3},{3,4},{4,5},{5,6},{6,7},{7,8},{8,9},{9,10},{10,1... | collective-permute-start | bytes 393224 | tf_op jit(solution)/shard_map/ppermute | solution.py:71
  18.1 4.6 %collective-permute-start.8 = (f32[2048,16]{0,1:T(8,128)}, f32[2048,16]{0,1:T(8,128)S(1)}, u32[]{:S(2)}, u32[]{:S(2)}) collective-permute-start(f32[2048,16]{0,1:T(8,128)} %param.2), channel_id=1, source_target_pairs={{0,15},{1,0},{2,1},{3,2},{4,3},{5,4},{6,5},{7,6},{8,7},{9,8},{10,9... | collective-permute-start | bytes 393224 | tf_op jit(solution)/shard_map/ppermute | solution.py:74
  22.6 0.4 collective-permute-done.1
  23.1 1.9 %collective-permute-start.2 = (f32[2048,16]{0,1:T(8,128)S(1)}, f32[2048,16]{0,1:T(8,128)S(1)}, u32[]{:S(2)}, u32[]{:S(2)}) collective-permute-start(f32[2048,16]{0,1:T(8,128)S(1)} %collective-permute-done.1), channel_id=1, source_target_pairs={{0,1},{1,2},{2,3},{3,4},{4,5},{5,6},{6,7},{7,8},{8,9},{9,10},{10,1... | collective-permute-start | bytes 393224 | tf_op jit(solution)/shard_map/ppermute | solution.py:71
  25.0 0.0 collective-permute-done.8
  25.0 4.8 %collective-permute-start.9 = (f32[2048,16]{0,1:T(8,128)S(1)}, f32[2048,16]{0,1:T(8,128)S(1)}, u32[]{:S(2)}, u32[]{:S(2)}) collective-permute-start(f32[2048,16]{0,1:T(8,128)S(1)} %collective-permute-done.8), channel_id=1, source_target_pairs={{0,15},{1,0},{2,1},{3,2},{4,3},{5,4},{6,5},{7,6},{8,7},{9,8},{10,9... | collective-permute-start | bytes 393224 | tf_op jit(solution)/shard_map/ppermute | solution.py:74
  29.8 0.2 collective-permute-done.2
  30.0 1.9 %collective-permute-start.3 = (f32[2048,16]{0,1:T(8,128)S(1)}, f32[2048,16]{0,1:T(8,128)S(1)}, u32[]{:S(2)}, u32[]{:S(2)}) collective-permute-start(f32[2048,16]{0,1:T(8,128)S(1)} %collective-permute-done.2), channel_id=1, source_target_pairs={{0,1},{1,2},{2,3},{3,4},{4,5},{5,6},{6,7},{7,8},{8,9},{9,10},{10,1... | collective-permute-start | bytes 393224 | tf_op jit(solution)/shard_map/ppermute | solution.py:71
  31.9 0.0 collective-permute-done.9
  31.9 4.8 %collective-permute-start.10 = (f32[2048,16]{0,1:T(8,128)S(1)}, f32[2048,16]{0,1:T(8,128)S(1)}, u32[]{:S(2)}, u32[]{:S(2)}) collective-permute-start(f32[2048,16]{0,1:T(8,128)S(1)} %collective-permute-done.9), channel_id=1, source_target_pairs={{0,15},{1,0},{2,1},{3,2},{4,3},{5,4},{6,5},{7,6},{8,7},{9,8},{10,9... | collective-permute-start | bytes 393224 | tf_op jit(solution)/shard_map/ppermute | solution.py:74
  36.7 0.2 collective-permute-done.3
  36.9 1.9 %collective-permute-start.4 = (f32[2048,16]{0,1:T(8,128)S(1)}, f32[2048,16]{0,1:T(8,128)S(1)}, u32[]{:S(2)}, u32[]{:S(2)}) collective-permute-start(f32[2048,16]{0,1:T(8,128)S(1)} %collective-permute-done.3), channel_id=1, source_target_pairs={{0,1},{1,2},{2,3},{3,4},{4,5},{5,6},{6,7},{7,8},{8,9},{9,10},{10,1... | collective-permute-start | bytes 393224 | tf_op jit(solution)/shard_map/ppermute | solution.py:71
  38.8 0.0 collective-permute-done.10
  38.8 4.8 %collective-permute-start.11 = (f32[2048,16]{0,1:T(8,128)S(1)}, f32[2048,16]{0,1:T(8,128)S(1)}, u32[]{:S(2)}, u32[]{:S(2)}) collective-permute-start(f32[2048,16]{0,1:T(8,128)S(1)} %collective-permute-done.10), channel_id=1, source_target_pairs={{0,15},{1,0},{2,1},{3,2},{4,3},{5,4},{6,5},{7,6},{8,7},{9,8},{10,9... | collective-permute-start | bytes 393224 | tf_op jit(solution)/shard_map/ppermute | solution.py:74
  43.6 0.2 collective-permute-done.4
  43.8 1.9 %collective-permute-start.5 = (f32[2048,16]{0,1:T(8,128)S(1)}, f32[2048,16]{0,1:T(8,128)S(1)}, u32[]{:S(2)}, u32[]{:S(2)}) collective-permute-start(f32[2048,16]{0,1:T(8,128)S(1)} %collective-permute-done.4), channel_id=1, source_target_pairs={{0,1},{1,2},{2,3},{3,4},{4,5},{5,6},{6,7},{7,8},{8,9},{9,10},{10,1... | collective-permute-start | bytes 393224 | tf_op jit(solution)/shard_map/ppermute | solution.py:71
  45.7 0.0 collective-permute-done.11
  45.7 4.8 %collective-permute-start.12 = (f32[2048,16]{0,1:T(8,128)S(1)}, f32[2048,16]{0,1:T(8,128)S(1)}, u32[]{:S(2)}, u32[]{:S(2)}) collective-permute-start(f32[2048,16]{0,1:T(8,128)S(1)} %collective-permute-done.11), channel_id=1, source_target_pairs={{0,15},{1,0},{2,1},{3,2},{4,3},{5,4},{6,5},{7,6},{8,7},{9,8},{10,9... | collective-permute-start | bytes 393224 | tf_op jit(solution)/shard_map/ppermute | solution.py:74
  50.5 0.2 collective-permute-done.5
  50.7 1.9 %collective-permute-start.6 = (f32[2048,16]{0,1:T(8,128)S(1)}, f32[2048,16]{0,1:T(8,128)S(1)}, u32[]{:S(2)}, u32[]{:S(2)}) collective-permute-start(f32[2048,16]{0,1:T(8,128)S(1)} %collective-permute-done.5), channel_id=1, source_target_pairs={{0,1},{1,2},{2,3},{3,4},{4,5},{5,6},{6,7},{7,8},{8,9},{9,10},{10,1... | collective-permute-start | bytes 393224 | tf_op jit(solution)/shard_map/ppermute | solution.py:71
  52.6 0.0 collective-permute-done.12
  52.6 4.8 %collective-permute-start.13 = (f32[2048,16]{0,1:T(8,128)S(1)}, f32[2048,16]{0,1:T(8,128)S(1)}, u32[]{:S(2)}, u32[]{:S(2)}) collective-permute-start(f32[2048,16]{0,1:T(8,128)S(1)} %collective-permute-done.12), channel_id=1, source_target_pairs={{0,15},{1,0},{2,1},{3,2},{4,3},{5,4},{6,5},{7,6},{8,7},{9,8},{10,9... | collective-permute-start | bytes 393224 | tf_op jit(solution)/shard_map/ppermute | solution.py:74
  57.4 1.0 collective-permute-done.6
  58.4 1.9 %collective-permute-start.7 = (f32[2048,16]{0,1:T(8,128)S(1)}, f32[2048,16]{0,1:T(8,128)S(1)}, u32[]{:S(2)}, u32[]{:S(2)}) collective-permute-start(f32[2048,16]{0,1:T(8,128)S(1)} %collective-permute-done.6), channel_id=1, source_target_pairs={{0,1},{1,2},{2,3},{3,4},{4,5},{5,6},{6,7},{7,8},{8,9},{9,10},{10,1... | collective-permute-start | bytes 393224 | tf_op jit(solution)/shard_map/ppermute | solution.py:71
  60.3 0.0 collective-permute-done.13
  60.4 5.0 %collective-permute-start.14 = (f32[2048,16]{0,1:T(8,128)S(1)}, f32[2048,16]{0,1:T(8,128)S(1)}, u32[]{:S(2)}, u32[]{:S(2)}) collective-permute-start(f32[2048,16]{0,1:T(8,128)S(1)} %collective-permute-done.13), channel_id=1, source_target_pairs={{0,15},{1,0},{2,1},{3,2},{4,3},{5,4},{6,5},{7,6},{8,7},{9,8},{10,9... | collective-permute-start | bytes 393224 | tf_op jit(solution)/shard_map/ppermute | solution.py:74
  65.4 1.1 collective-permute-done.7
  66.6 0.0 copy-done.2
  66.7 1.2 collective-permute-done.14
  67.9 0.0 copy-start
  67.9 1.9 %fusion.8 = f32[256,256]{0,1:T(8,128)S(1)} fusion(f32[2048,256]{0,1:T(8,128)S(1)} %constant_dynamic-update-slice_fusion), kind=kOutput, calls=%fused_computation.32 | convolution fusion | flops 1610612736 | bytes 2359296 | tf_op jit(solution)/shard_map/dot_general | solution.py:93
  69.8 0.0 copy-done
  69.8 3.6 %fusion.9 = f32[256,256]{0,1:T(8,128)S(1)} fusion(f32[2048,256]{0,1:T(8,128)S(1)} %constant_dynamic-update-slice_fusion, f32[2048,256]{1,0:T(8,128)S(1)} %copy-done), kind=kOutput, calls=%fused_computation.33 | convolution fusion | flops 1610612736 | bytes 4456448 | tf_op jit(solution)/shard_map/dot_general | solution.py:92
  73.4 0.2 copy.6
  73.6 27.8 %all_to_all.10 = f32[32,8,512]{2,1,0:T(8,128)S(1)} all-to-all(f32[32,8,512]{2,1,0:T(8,128)S(1)} %bitcast.11), channel_id=1, replica_groups=mesh['row'=32,'col'=16] {'row'}, dimensions={0} | all-to-all | bytes 1048576 | tf_op jit(solution)/shard_map/all_to_all | solution.py:83
  101.4 0.9 broadcast_in_dim.2
  102.3 3.9 %all-to-all-start.1 = ((f32[32,8,512]{2,1,0:T(8,128)}), f32[32,8,512]{2,1,0:T(8,128)S(1)}, u32[]{:S(2)}, u32[]{:S(2)}) async-start(f32[32,8,512]{2,1,0:T(8,128)} %broadcast_in_dim.2), calls=%async_computation.1 | async-start | bytes 1048576 | tf_op jit(solution)/shard_map/all_to_all | solution.py:85
  106.2 11.3 %all-to-all-done.1 = f32[32,8,512]{2,1,0:T(8,128)S(1)} async-done(((f32[32,8,512]{2,1,0:T(8,128)}), f32[32,8,512]{2,1,0:T(8,128)S(1)}, u32[]{:S(2)}, u32[]{:S(2)}) %all-to-all-start.1) | async-done | bytes 524320 | tf_op jit(solution)/shard_map/all_to_all | solution.py:85
  117.6 0.1 fusion
  117.7 0.9 fusion.3.gram_ref
  118.6 40.1 %shard_map.49 = (f32[256,256]{1,0:T(8,128)}, f32[256,256]{1,0:T(8,128)}) custom-call(f32[256,256]{1,0:T(8,128)} %fusion.3.gram_ref), custom_call_target="tpu_custom_call" | custom-call | tf_op jit(solution)/shard_map/pallas_call | solution.py:57
  158.8 1.3 fusion.4
  160.1 0.0 copy-start.1
  160.1 1.6 fusion.10
  161.8 1.0 dynamic-slice_multiply_fusion
  162.8 0.7 copy.7
  163.5 6.4 %convolution_subtract_fusion = f32[2048,256]{1,0:T(8,128)} fusion(f32[2048,256]{1,0:T(8,128)} %param.3, f32[2048,256]{0,1:T(8,128)S(1)} %constant_dynamic-update-slice_fusion, s32[]{:T(128)S(6)} %select_n.36, f32[256,256]{1,0:T(8,128)S(1)} %fusion.10), kind=kOutput, calls=%fused_computation | convolution fusion | flops 1611202560 | bytes 6553604 | tf_op jit(solution)/shard_map/dot_general | solution.py:100
  169.8 0.0 copy-done.1
  (19 shorter events, 0.3 us)
Async XLA Ops:
  0.6 66.0 %copy-start.2 = (f32[2048,16]{0,1:T(8,128)S(1)}, f32[2048,16]{0,1:T(8,128)}, u32[]{:S(2)}) copy-start(f32[2048,16]{0,1:T(8,128)} %param.2) | copy-start | bytes 393220
  0.6 15.5 %collective-permute-start = (f32[2048,16]{0,1:T(8,128)}, f32[2048,16]{0,1:T(8,128)S(1)}, u32[]{:S(2)}, u32[]{:S(2)}) collective-permute-start(f32[2048,16]{0,1:T(8,128)} %param.2), channel_id=1, source_target_pairs={{0,1},{1,2},{2,3},{3,4},{4,5},{5,6},{6,7},{7,8},{8,9},{9,10},{10,1... | collective-permute-start | bytes 393224 | tf_op jit(solution)/shard_map/ppermute | solution.py:71
  16.1 6.9 %collective-permute-start.1 = (f32[2048,16]{0,1:T(8,128)S(1)}, f32[2048,16]{0,1:T(8,128)S(1)}, u32[]{:S(2)}, u32[]{:S(2)}) collective-permute-start(f32[2048,16]{0,1:T(8,128)S(1)} %collective-permute-done), channel_id=1, source_target_pairs={{0,1},{1,2},{2,3},{3,4},{4,5},{5,6},{6,7},{7,8},{8,9},{9,10},{10,1... | collective-permute-start | bytes 393224 | tf_op jit(solution)/shard_map/ppermute | solution.py:71
  18.1 6.9 %collective-permute-start.8 = (f32[2048,16]{0,1:T(8,128)}, f32[2048,16]{0,1:T(8,128)S(1)}, u32[]{:S(2)}, u32[]{:S(2)}) collective-permute-start(f32[2048,16]{0,1:T(8,128)} %param.2), channel_id=1, source_target_pairs={{0,15},{1,0},{2,1},{3,2},{4,3},{5,4},{6,5},{7,6},{8,7},{9,8},{10,9... | collective-permute-start | bytes 393224 | tf_op jit(solution)/shard_map/ppermute | solution.py:74
  23.1 6.9 %collective-permute-start.2 = (f32[2048,16]{0,1:T(8,128)S(1)}, f32[2048,16]{0,1:T(8,128)S(1)}, u32[]{:S(2)}, u32[]{:S(2)}) collective-permute-start(f32[2048,16]{0,1:T(8,128)S(1)} %collective-permute-done.1), channel_id=1, source_target_pairs={{0,1},{1,2},{2,3},{3,4},{4,5},{5,6},{6,7},{7,8},{8,9},{9,10},{10,1... | collective-permute-start | bytes 393224 | tf_op jit(solution)/shard_map/ppermute | solution.py:71
  25.0 6.9 %collective-permute-start.9 = (f32[2048,16]{0,1:T(8,128)S(1)}, f32[2048,16]{0,1:T(8,128)S(1)}, u32[]{:S(2)}, u32[]{:S(2)}) collective-permute-start(f32[2048,16]{0,1:T(8,128)S(1)} %collective-permute-done.8), channel_id=1, source_target_pairs={{0,15},{1,0},{2,1},{3,2},{4,3},{5,4},{6,5},{7,6},{8,7},{9,8},{10,9... | collective-permute-start | bytes 393224 | tf_op jit(solution)/shard_map/ppermute | solution.py:74
  30.0 6.9 %collective-permute-start.3 = (f32[2048,16]{0,1:T(8,128)S(1)}, f32[2048,16]{0,1:T(8,128)S(1)}, u32[]{:S(2)}, u32[]{:S(2)}) collective-permute-start(f32[2048,16]{0,1:T(8,128)S(1)} %collective-permute-done.2), channel_id=1, source_target_pairs={{0,1},{1,2},{2,3},{3,4},{4,5},{5,6},{6,7},{7,8},{8,9},{9,10},{10,1... | collective-permute-start | bytes 393224 | tf_op jit(solution)/shard_map/ppermute | solution.py:71
  31.9 6.9 %collective-permute-start.10 = (f32[2048,16]{0,1:T(8,128)S(1)}, f32[2048,16]{0,1:T(8,128)S(1)}, u32[]{:S(2)}, u32[]{:S(2)}) collective-permute-start(f32[2048,16]{0,1:T(8,128)S(1)} %collective-permute-done.9), channel_id=1, source_target_pairs={{0,15},{1,0},{2,1},{3,2},{4,3},{5,4},{6,5},{7,6},{8,7},{9,8},{10,9... | collective-permute-start | bytes 393224 | tf_op jit(solution)/shard_map/ppermute | solution.py:74
  36.9 6.9 %collective-permute-start.4 = (f32[2048,16]{0,1:T(8,128)S(1)}, f32[2048,16]{0,1:T(8,128)S(1)}, u32[]{:S(2)}, u32[]{:S(2)}) collective-permute-start(f32[2048,16]{0,1:T(8,128)S(1)} %collective-permute-done.3), channel_id=1, source_target_pairs={{0,1},{1,2},{2,3},{3,4},{4,5},{5,6},{6,7},{7,8},{8,9},{9,10},{10,1... | collective-permute-start | bytes 393224 | tf_op jit(solution)/shard_map/ppermute | solution.py:71
  38.8 6.9 %collective-permute-start.11 = (f32[2048,16]{0,1:T(8,128)S(1)}, f32[2048,16]{0,1:T(8,128)S(1)}, u32[]{:S(2)}, u32[]{:S(2)}) collective-permute-start(f32[2048,16]{0,1:T(8,128)S(1)} %collective-permute-done.10), channel_id=1, source_target_pairs={{0,15},{1,0},{2,1},{3,2},{4,3},{5,4},{6,5},{7,6},{8,7},{9,8},{10,9... | collective-permute-start | bytes 393224 | tf_op jit(solution)/shard_map/ppermute | solution.py:74
  43.8 6.9 %collective-permute-start.5 = (f32[2048,16]{0,1:T(8,128)S(1)}, f32[2048,16]{0,1:T(8,128)S(1)}, u32[]{:S(2)}, u32[]{:S(2)}) collective-permute-start(f32[2048,16]{0,1:T(8,128)S(1)} %collective-permute-done.4), channel_id=1, source_target_pairs={{0,1},{1,2},{2,3},{3,4},{4,5},{5,6},{6,7},{7,8},{8,9},{9,10},{10,1... | collective-permute-start | bytes 393224 | tf_op jit(solution)/shard_map/ppermute | solution.py:71
  45.7 6.9 %collective-permute-start.12 = (f32[2048,16]{0,1:T(8,128)S(1)}, f32[2048,16]{0,1:T(8,128)S(1)}, u32[]{:S(2)}, u32[]{:S(2)}) collective-permute-start(f32[2048,16]{0,1:T(8,128)S(1)} %collective-permute-done.11), channel_id=1, source_target_pairs={{0,15},{1,0},{2,1},{3,2},{4,3},{5,4},{6,5},{7,6},{8,7},{9,8},{10,9... | collective-permute-start | bytes 393224 | tf_op jit(solution)/shard_map/ppermute | solution.py:74
  50.7 7.7 %collective-permute-start.6 = (f32[2048,16]{0,1:T(8,128)S(1)}, f32[2048,16]{0,1:T(8,128)S(1)}, u32[]{:S(2)}, u32[]{:S(2)}) collective-permute-start(f32[2048,16]{0,1:T(8,128)S(1)} %collective-permute-done.5), channel_id=1, source_target_pairs={{0,1},{1,2},{2,3},{3,4},{4,5},{5,6},{6,7},{7,8},{8,9},{9,10},{10,1... | collective-permute-start | bytes 393224 | tf_op jit(solution)/shard_map/ppermute | solution.py:71
  52.6 7.7 %collective-permute-start.13 = (f32[2048,16]{0,1:T(8,128)S(1)}, f32[2048,16]{0,1:T(8,128)S(1)}, u32[]{:S(2)}, u32[]{:S(2)}) collective-permute-start(f32[2048,16]{0,1:T(8,128)S(1)} %collective-permute-done.12), channel_id=1, source_target_pairs={{0,15},{1,0},{2,1},{3,2},{4,3},{5,4},{6,5},{7,6},{8,7},{9,8},{10,9... | collective-permute-start | bytes 393224 | tf_op jit(solution)/shard_map/ppermute | solution.py:74
  58.4 8.1 %collective-permute-start.7 = (f32[2048,16]{0,1:T(8,128)S(1)}, f32[2048,16]{0,1:T(8,128)S(1)}, u32[]{:S(2)}, u32[]{:S(2)}) collective-permute-start(f32[2048,16]{0,1:T(8,128)S(1)} %collective-permute-done.6), channel_id=1, source_target_pairs={{0,1},{1,2},{2,3},{3,4},{4,5},{5,6},{6,7},{7,8},{8,9},{9,10},{10,1... | collective-permute-start | bytes 393224 | tf_op jit(solution)/shard_map/ppermute | solution.py:71
  60.4 7.5 %collective-permute-start.14 = (f32[2048,16]{0,1:T(8,128)S(1)}, f32[2048,16]{0,1:T(8,128)S(1)}, u32[]{:S(2)}, u32[]{:S(2)}) collective-permute-start(f32[2048,16]{0,1:T(8,128)S(1)} %collective-permute-done.13), channel_id=1, source_target_pairs={{0,15},{1,0},{2,1},{3,2},{4,3},{5,4},{6,5},{7,6},{8,7},{9,8},{10,9... | collective-permute-start | bytes 393224 | tf_op jit(solution)/shard_map/ppermute | solution.py:74
  67.9 1.9 %copy-start = (f32[2048,256]{1,0:T(8,128)S(1)}, f32[2048,256]{1,0:T(8,128)}, u32[]{:S(2)}) copy-start(f32[2048,256]{1,0:T(8,128)} %param.3) | copy-start | bytes 6291460
  102.3 15.3 %all-to-all-start.1 = ((f32[32,8,512]{2,1,0:T(8,128)}), f32[32,8,512]{2,1,0:T(8,128)S(1)}, u32[]{:S(2)}, u32[]{:S(2)}) async-start(f32[32,8,512]{2,1,0:T(8,128)} %broadcast_in_dim.2), calls=%async_computation.1 | async-start | bytes 1048576 | tf_op jit(solution)/shard_map/all_to_all | solution.py:85
  160.1 9.7 %copy-start.1 = (f32[256,256]{1,0:T(8,128)}, f32[256,256]{1,0:T(8,128)S(1)}, u32[]{:S(2)}) copy-start(f32[256,256]{1,0:T(8,128)S(1)} %fusion.4) | copy-start | bytes 786436

commit v7 on v6

--- a/solution.py
+++ b/solution.py
@@ -11,7 +11,7 @@
 HIGHEST = lax.Precision.HIGHEST
 
 
-def factor_kernel(gram_ref, upper_ref, inverse_ref, work_ref):
+def factor_kernel(gram_ref, upper_ref, inverse_ref, work_ref, left_ref):
     n = gram_ref.shape[0]
     rows = lax.broadcasted_iota(jnp.int32, (n, n), 0)
     cols = lax.broadcasted_iota(jnp.int32, (n, n), 1)
@@ -26,9 +26,8 @@
         sub = lax.broadcasted_iota(jnp.int32, (8, width), 0)
         key = n - lo
 
-        def block(b, carry):
+        def block(b, strip):
             base = pl.multiple_of(b * 8, 8)
-            strip = work_ref[pl.ds(base, 8), lo:hi]
             for t in range(8):
                 col = jnp.sum(jnp.where(lane[:, :key] == base + t, strip[:, :key], 0.0),
                               axis=1, keepdims=True)
@@ -38,12 +37,18 @@
                 strip = jnp.where(sub == t, pivot, strip - mult * pivot)
             work_ref[pl.ds(base, 8), lo:hi] = strip
             left = jnp.where(lane[:, :key] > base + 7, strip[:, :key], 0.0)
-            update = lax.dot_general(left, strip, contract_rows,
-                                     precision=HIGHEST, preferred_element_type=jnp.float32)
+            left_ref[lo:n, :] = jnp.transpose(left)
+            after = pl.multiple_of(jnp.minimum(base + 8, n - 8), 8)
+            nearest = left_ref[pl.ds(after, 8), :]
+            following = work_ref[pl.ds(after, 8), lo:hi] - jnp.dot(
+                nearest, strip, precision=HIGHEST, preferred_element_type=jnp.float32)
+            update = jnp.dot(left_ref[lo:n, :], strip, precision=HIGHEST,
+                             preferred_element_type=jnp.float32)
             work_ref[lo:n, lo:hi] = work_ref[lo:n, lo:hi] - update
-            return carry
+            return following
 
-        lax.fori_loop(first, last, block, 0)
+        start = work_ref[first * 8:first * 8 + 8, lo:hi]
+        lax.fori_loop(first, last, block, start, unroll=2)
 
     phase(0, half // 8, 0, n + half)
     phase(half // 8, n // 8, half, 2 * n)
@@ -59,9 +64,8 @@
         out_shape=(jax.ShapeDtypeStruct((n, n), jnp.float32),) * 2,
         in_specs=[pl.BlockSpec(memory_space=pltpu.VMEM)],
         out_specs=(pl.BlockSpec(memory_space=pltpu.VMEM),) * 2,
-        scratch_shapes=[pltpu.VMEM((n, 2 * n), jnp.float32)],
+        scratch_shapes=[pltpu.VMEM((n, 2 * n), jnp.float32), pltpu.VMEM((n, 8), jnp.float32)],
     )(gram)
-
 
 def col_gather(x):
     n = lax.axis_size("col")

time: 171 us -> 170 us (level)
  no operation moved by 1% of the time
where the time goes in v7:
time: 170 us
  starting transfers between devices  55.2 us (32%)
  Pallas kernels  40 us (24%)
  blocking collectives  27.8 us (16%)
  waiting for transfers between devices  26.8 us (16%)
  matrix products  14.7 us (9%)
  other arithmetic  2.13 us (1%)
  local copies, waits for them, and re-layouts  1.95 us (1%)
    pallas_call x1, Pallas kernels, factor(): pl.pallas_call(factor_kernel, out_shape=(jax.ShapeDtypeStruct((n, n), jnp...  40 us
    ppermute x7, starting transfers between devices, col_gather(): behind = lax.ppermute(behind, 'col', [(i, (i - 1) % n) for i in range(n)])  33.4 us
    all_to_all x1, blocking collectives, row_sum(): mine = lax.all_to_all(parts, 'row', 0, 0, tiled=False).sum(0)  27.8 us
    ppermute x8, starting transfers between devices, col_gather(): ahead = lax.ppermute(ahead, 'col', [(i, (i + 1) % n) for i in range(n)])  17.9 us
    ppermute x8, waiting for transfers between devices, col_gather(): ahead = lax.ppermute(ahead, 'col', [(i, (i + 1) % n) for i in range(n)])  14.3 us
    all_to_all x1, waiting for transfers between devices, row_sum(): return lax.all_to_all(copies, 'row', 0, 0, tiled=False).reshape(rows, cols)  11.3 us
    dot_general x1, matrix products, per_device(): jnp.dot(gathered, jnp.roll(coefficients, -shift, axis=0), precision=highest)  6.36 us
    all_to_all x1, starting transfers between devices, row_sum(): return lax.all_to_all(copies, 'row', 0, 0, tiled=False).reshape(rows, cols)  3.86 us
  transfers between devices with their start and end apart: 16, of which 10 were waited for; matrix products, arithmetic and copies ran while one was open for 0% of the time, Pallas kernels for 0%

profile of v7, /device:TPU:1, one launch (start us, length us, event | category | flops | bytes accessed | tf_op | source)
XLA Modules:
  0.0 169.7 jit_solution(6199231353351409782)
XLA Ops:
  0.6 0.0 copy-start.2
  0.6 4.5 %collective-permute-start = (f32[2048,16]{0,1:T(8,128)}, f32[2048,16]{0,1:T(8,128)S(1)}, u32[]{:S(2)}, u32[]{:S(2)}) collective-permute-start(f32[2048,16]{0,1:T(8,128)} %param.2), channel_id=1, source_target_pairs={{0,1},{1,2},{2,3},{3,4},{4,5},{5,6},{6,7},{7,8},{8,9},{9,10},{10,1... | collective-permute-start | bytes 393224 | tf_op jit(solution)/shard_map/ppermute | solution.py:75
  5.2 11.0 %collective-permute-done = f32[2048,16]{0,1:T(8,128)S(1)} collective-permute-done((f32[2048,16]{0,1:T(8,128)}, f32[2048,16]{0,1:T(8,128)S(1)}, u32[]{:S(2)}, u32[]{:S(2)}) %collective-permute-start) | collective-permute-done | bytes 131104 | tf_op jit(solution)/shard_map/ppermute | solution.py:75
  16.1 1.9 %collective-permute-start.1 = (f32[2048,16]{0,1:T(8,128)S(1)}, f32[2048,16]{0,1:T(8,128)S(1)}, u32[]{:S(2)}, u32[]{:S(2)}) collective-permute-start(f32[2048,16]{0,1:T(8,128)S(1)} %collective-permute-done), channel_id=1, source_target_pairs={{0,1},{1,2},{2,3},{3,4},{4,5},{5,6},{6,7},{7,8},{8,9},{9,10},{10,1... | collective-permute-start | bytes 393224 | tf_op jit(solution)/shard_map/ppermute | solution.py:75
  18.1 4.6 %collective-permute-start.8 = (f32[2048,16]{0,1:T(8,128)}, f32[2048,16]{0,1:T(8,128)S(1)}, u32[]{:S(2)}, u32[]{:S(2)}) collective-permute-start(f32[2048,16]{0,1:T(8,128)} %param.2), channel_id=1, source_target_pairs={{0,15},{1,0},{2,1},{3,2},{4,3},{5,4},{6,5},{7,6},{8,7},{9,8},{10,9... | collective-permute-start | bytes 393224 | tf_op jit(solution)/shard_map/ppermute | solution.py:78
  22.6 0.4 collective-permute-done.1
  23.1 1.9 %collective-permute-start.2 = (f32[2048,16]{0,1:T(8,128)S(1)}, f32[2048,16]{0,1:T(8,128)S(1)}, u32[]{:S(2)}, u32[]{:S(2)}) collective-permute-start(f32[2048,16]{0,1:T(8,128)S(1)} %collective-permute-done.1), channel_id=1, source_target_pairs={{0,1},{1,2},{2,3},{3,4},{4,5},{5,6},{6,7},{7,8},{8,9},{9,10},{10,1... | collective-permute-start | bytes 393224 | tf_op jit(solution)/shard_map/ppermute | solution.py:75
  25.0 0.0 collective-permute-done.8
  25.0 4.8 %collective-permute-start.9 = (f32[2048,16]{0,1:T(8,128)S(1)}, f32[2048,16]{0,1:T(8,128)S(1)}, u32[]{:S(2)}, u32[]{:S(2)}) collective-permute-start(f32[2048,16]{0,1:T(8,128)S(1)} %collective-permute-done.8), channel_id=1, source_target_pairs={{0,15},{1,0},{2,1},{3,2},{4,3},{5,4},{6,5},{7,6},{8,7},{9,8},{10,9... | collective-permute-start | bytes 393224 | tf_op jit(solution)/shard_map/ppermute | solution.py:78
  29.8 0.2 collective-permute-done.2
  30.0 1.9 %collective-permute-start.3 = (f32[2048,16]{0,1:T(8,128)S(1)}, f32[2048,16]{0,1:T(8,128)S(1)}, u32[]{:S(2)}, u32[]{:S(2)}) collective-permute-start(f32[2048,16]{0,1:T(8,128)S(1)} %collective-permute-done.2), channel_id=1, source_target_pairs={{0,1},{1,2},{2,3},{3,4},{4,5},{5,6},{6,7},{7,8},{8,9},{9,10},{10,1... | collective-permute-start | bytes 393224 | tf_op jit(solution)/shard_map/ppermute | solution.py:75
  31.9 0.0 collective-permute-done.9
  31.9 4.8 %collective-permute-start.10 = (f32[2048,16]{0,1:T(8,128)S(1)}, f32[2048,16]{0,1:T(8,128)S(1)}, u32[]{:S(2)}, u32[]{:S(2)}) collective-permute-start(f32[2048,16]{0,1:T(8,128)S(1)} %collective-permute-done.9), channel_id=1, source_target_pairs={{0,15},{1,0},{2,1},{3,2},{4,3},{5,4},{6,5},{7,6},{8,7},{9,8},{10,9... | collective-permute-start | bytes 393224 | tf_op jit(solution)/shard_map/ppermute | solution.py:78
  36.7 0.2 collective-permute-done.3
  36.9 1.9 %collective-permute-start.4 = (f32[2048,16]{0,1:T(8,128)S(1)}, f32[2048,16]{0,1:T(8,128)S(1)}, u32[]{:S(2)}, u32[]{:S(2)}) collective-permute-start(f32[2048,16]{0,1:T(8,128)S(1)} %collective-permute-done.3), channel_id=1, source_target_pairs={{0,1},{1,2},{2,3},{3,4},{4,5},{5,6},{6,7},{7,8},{8,9},{9,10},{10,1... | collective-permute-start | bytes 393224 | tf_op jit(solution)/shard_map/ppermute | solution.py:75
  38.8 0.0 collective-permute-done.10
  38.8 4.8 %collective-permute-start.11 = (f32[2048,16]{0,1:T(8,128)S(1)}, f32[2048,16]{0,1:T(8,128)S(1)}, u32[]{:S(2)}, u32[]{:S(2)}) collective-permute-start(f32[2048,16]{0,1:T(8,128)S(1)} %collective-permute-done.10), channel_id=1, source_target_pairs={{0,15},{1,0},{2,1},{3,2},{4,3},{5,4},{6,5},{7,6},{8,7},{9,8},{10,9... | collective-permute-start | bytes 393224 | tf_op jit(solution)/shard_map/ppermute | solution.py:78
  43.6 0.2 collective-permute-done.4
  43.8 1.9 %collective-permute-start.5 = (f32[2048,16]{0,1:T(8,128)S(1)}, f32[2048,16]{0,1:T(8,128)S(1)}, u32[]{:S(2)}, u32[]{:S(2)}) collective-permute-start(f32[2048,16]{0,1:T(8,128)S(1)} %collective-permute-done.4), channel_id=1, source_target_pairs={{0,1},{1,2},{2,3},{3,4},{4,5},{5,6},{6,7},{7,8},{8,9},{9,10},{10,1... | collective-permute-start | bytes 393224 | tf_op jit(solution)/shard_map/ppermute | solution.py:75
  45.7 0.0 collective-permute-done.11
  45.7 4.8 %collective-permute-start.12 = (f32[2048,16]{0,1:T(8,128)S(1)}, f32[2048,16]{0,1:T(8,128)S(1)}, u32[]{:S(2)}, u32[]{:S(2)}) collective-permute-start(f32[2048,16]{0,1:T(8,128)S(1)} %collective-permute-done.11), channel_id=1, source_target_pairs={{0,15},{1,0},{2,1},{3,2},{4,3},{5,4},{6,5},{7,6},{8,7},{9,8},{10,9... | collective-permute-start | bytes 393224 | tf_op jit(solution)/shard_map/ppermute | solution.py:78
  50.5 0.2 collective-permute-done.5
  50.7 1.9 %collective-permute-start.6 = (f32[2048,16]{0,1:T(8,128)S(1)}, f32[2048,16]{0,1:T(8,128)S(1)}, u32[]{:S(2)}, u32[]{:S(2)}) collective-permute-start(f32[2048,16]{0,1:T(8,128)S(1)} %collective-permute-done.5), channel_id=1, source_target_pairs={{0,1},{1,2},{2,3},{3,4},{4,5},{5,6},{6,7},{7,8},{8,9},{9,10},{10,1... | collective-permute-start | bytes 393224 | tf_op jit(solution)/shard_map/ppermute | solution.py:75
  52.6 0.0 collective-permute-done.12
  52.6 4.8 %collective-permute-start.13 = (f32[2048,16]{0,1:T(8,128)S(1)}, f32[2048,16]{0,1:T(8,128)S(1)}, u32[]{:S(2)}, u32[]{:S(2)}) collective-permute-start(f32[2048,16]{0,1:T(8,128)S(1)} %collective-permute-done.12), channel_id=1, source_target_pairs={{0,15},{1,0},{2,1},{3,2},{4,3},{5,4},{6,5},{7,6},{8,7},{9,8},{10,9... | collective-permute-start | bytes 393224 | tf_op jit(solution)/shard_map/ppermute | solution.py:78
  57.4 1.0 collective-permute-done.6
  58.4 1.9 %collective-permute-start.7 = (f32[2048,16]{0,1:T(8,128)S(1)}, f32[2048,16]{0,1:T(8,128)S(1)}, u32[]{:S(2)}, u32[]{:S(2)}) collective-permute-start(f32[2048,16]{0,1:T(8,128)S(1)} %collective-permute-done.6), channel_id=1, source_target_pairs={{0,1},{1,2},{2,3},{3,4},{4,5},{5,6},{6,7},{7,8},{8,9},{9,10},{10,1... | collective-permute-start | bytes 393224 | tf_op jit(solution)/shard_map/ppermute | solution.py:75
  60.3 0.0 collective-permute-done.13
  60.4 5.0 %collective-permute-start.14 = (f32[2048,16]{0,1:T(8,128)S(1)}, f32[2048,16]{0,1:T(8,128)S(1)}, u32[]{:S(2)}, u32[]{:S(2)}) collective-permute-start(f32[2048,16]{0,1:T(8,128)S(1)} %collective-permute-done.13), channel_id=1, source_target_pairs={{0,15},{1,0},{2,1},{3,2},{4,3},{5,4},{6,5},{7,6},{8,7},{9,8},{10,9... | collective-permute-start | bytes 393224 | tf_op jit(solution)/shard_map/ppermute | solution.py:78
  65.4 1.1 collective-permute-done.7
  66.6 0.0 copy-done.2
  66.7 1.2 collective-permute-done.14
  67.9 0.0 copy-start
  67.9 1.9 %fusion.8 = f32[256,256]{0,1:T(8,128)S(1)} fusion(f32[2048,256]{0,1:T(8,128)S(1)} %constant_dynamic-update-slice_fusion), kind=kOutput, calls=%fused_computation.32 | convolution fusion | flops 1610612736 | bytes 2359296 | tf_op jit(solution)/shard_map/dot_general | solution.py:97
  69.8 0.0 copy-done
  69.8 3.6 %fusion.9 = f32[256,256]{0,1:T(8,128)S(1)} fusion(f32[2048,256]{0,1:T(8,128)S(1)} %constant_dynamic-update-slice_fusion, f32[2048,256]{1,0:T(8,128)S(1)} %copy-done), kind=kOutput, calls=%fused_computation.33 | convolution fusion | flops 1610612736 | bytes 4456448 | tf_op jit(solution)/shard_map/dot_general | solution.py:96
  73.4 0.2 copy.6
  73.6 27.8 %all_to_all.10 = f32[32,8,512]{2,1,0:T(8,128)S(1)} all-to-all(f32[32,8,512]{2,1,0:T(8,128)S(1)} %bitcast.11), channel_id=1, replica_groups=mesh['row'=32,'col'=16] {'row'}, dimensions={0} | all-to-all | bytes 1048576 | tf_op jit(solution)/shard_map/all_to_all | solution.py:87
  101.4 0.9 broadcast_in_dim.2
  102.3 3.9 %all-to-all-start.1 = ((f32[32,8,512]{2,1,0:T(8,128)}), f32[32,8,512]{2,1,0:T(8,128)S(1)}, u32[]{:S(2)}, u32[]{:S(2)}) async-start(f32[32,8,512]{2,1,0:T(8,128)} %broadcast_in_dim.2), calls=%async_computation.1 | async-start | bytes 1048576 | tf_op jit(solution)/shard_map/all_to_all | solution.py:89
  106.2 11.3 %all-to-all-done.1 = f32[32,8,512]{2,1,0:T(8,128)S(1)} async-done(((f32[32,8,512]{2,1,0:T(8,128)}), f32[32,8,512]{2,1,0:T(8,128)S(1)}, u32[]{:S(2)}, u32[]{:S(2)}) %all-to-all-start.1) | async-done | bytes 524320 | tf_op jit(solution)/shard_map/all_to_all | solution.py:89
  117.6 0.1 fusion
  117.7 0.9 fusion.3.gram_ref
  118.6 40.0 %shard_map.49 = (f32[256,256]{1,0:T(8,128)}, f32[256,256]{1,0:T(8,128)}) custom-call(f32[256,256]{1,0:T(8,128)} %fusion.3.gram_ref), custom_call_target="tpu_custom_call" | custom-call | tf_op jit(solution)/shard_map/pallas_call | solution.py:62
  158.7 1.3 fusion.4
  160.0 0.0 copy-start.1
  160.0 1.6 fusion.10
  161.7 1.0 dynamic-slice_multiply_fusion
  162.7 0.7 copy.7
  163.4 6.4 %convolution_subtract_fusion = f32[2048,256]{1,0:T(8,128)} fusion(f32[2048,256]{1,0:T(8,128)} %param.3, f32[2048,256]{0,1:T(8,128)S(1)} %constant_dynamic-update-slice_fusion, s32[]{:T(128)S(6)} %select_n.36, f32[256,256]{1,0:T(8,128)S(1)} %fusion.10), kind=kOutput, calls=%fused_computation | convolution fusion | flops 1611202560 | bytes 6553604 | tf_op jit(solution)/shard_map/dot_general | solution.py:104
  169.7 0.0 copy-done.1
  (19 shorter events, 0.3 us)
Async XLA Ops:
  0.6 66.0 %copy-start.2 = (f32[2048,16]{0,1:T(8,128)S(1)}, f32[2048,16]{0,1:T(8,128)}, u32[]{:S(2)}) copy-start(f32[2048,16]{0,1:T(8,128)} %param.2) | copy-start | bytes 393220
  0.6 15.5 %collective-permute-start = (f32[2048,16]{0,1:T(8,128)}, f32[2048,16]{0,1:T(8,128)S(1)}, u32[]{:S(2)}, u32[]{:S(2)}) collective-permute-start(f32[2048,16]{0,1:T(8,128)} %param.2), channel_id=1, source_target_pairs={{0,1},{1,2},{2,3},{3,4},{4,5},{5,6},{6,7},{7,8},{8,9},{9,10},{10,1... | collective-permute-start | bytes 393224 | tf_op jit(solution)/shard_map/ppermute | solution.py:75
  16.1 6.9 %collective-permute-start.1 = (f32[2048,16]{0,1:T(8,128)S(1)}, f32[2048,16]{0,1:T(8,128)S(1)}, u32[]{:S(2)}, u32[]{:S(2)}) collective-permute-start(f32[2048,16]{0,1:T(8,128)S(1)} %collective-permute-done), channel_id=1, source_target_pairs={{0,1},{1,2},{2,3},{3,4},{4,5},{5,6},{6,7},{7,8},{8,9},{9,10},{10,1... | collective-permute-start | bytes 393224 | tf_op jit(solution)/shard_map/ppermute | solution.py:75
  18.1 6.9 %collective-permute-start.8 = (f32[2048,16]{0,1:T(8,128)}, f32[2048,16]{0,1:T(8,128)S(1)}, u32[]{:S(2)}, u32[]{:S(2)}) collective-permute-start(f32[2048,16]{0,1:T(8,128)} %param.2), channel_id=1, source_target_pairs={{0,15},{1,0},{2,1},{3,2},{4,3},{5,4},{6,5},{7,6},{8,7},{9,8},{10,9... | collective-permute-start | bytes 393224 | tf_op jit(solution)/shard_map/ppermute | solution.py:78
  23.1 6.9 %collective-permute-start.2 = (f32[2048,16]{0,1:T(8,128)S(1)}, f32[2048,16]{0,1:T(8,128)S(1)}, u32[]{:S(2)}, u32[]{:S(2)}) collective-permute-start(f32[2048,16]{0,1:T(8,128)S(1)} %collective-permute-done.1), channel_id=1, source_target_pairs={{0,1},{1,2},{2,3},{3,4},{4,5},{5,6},{6,7},{7,8},{8,9},{9,10},{10,1... | collective-permute-start | bytes 393224 | tf_op jit(solution)/shard_map/ppermute | solution.py:75
  25.0 6.9 %collective-permute-start.9 = (f32[2048,16]{0,1:T(8,128)S(1)}, f32[2048,16]{0,1:T(8,128)S(1)}, u32[]{:S(2)}, u32[]{:S(2)}) collective-permute-start(f32[2048,16]{0,1:T(8,128)S(1)} %collective-permute-done.8), channel_id=1, source_target_pairs={{0,15},{1,0},{2,1},{3,2},{4,3},{5,4},{6,5},{7,6},{8,7},{9,8},{10,9... | collective-permute-start | bytes 393224 | tf_op jit(solution)/shard_map/ppermute | solution.py:78
  30.0 6.9 %collective-permute-start.3 = (f32[2048,16]{0,1:T(8,128)S(1)}, f32[2048,16]{0,1:T(8,128)S(1)}, u32[]{:S(2)}, u32[]{:S(2)}) collective-permute-start(f32[2048,16]{0,1:T(8,128)S(1)} %collective-permute-done.2), channel_id=1, source_target_pairs={{0,1},{1,2},{2,3},{3,4},{4,5},{5,6},{6,7},{7,8},{8,9},{9,10},{10,1... | collective-permute-start | bytes 393224 | tf_op jit(solution)/shard_map/ppermute | solution.py:75
  31.9 6.9 %collective-permute-start.10 = (f32[2048,16]{0,1:T(8,128)S(1)}, f32[2048,16]{0,1:T(8,128)S(1)}, u32[]{:S(2)}, u32[]{:S(2)}) collective-permute-start(f32[2048,16]{0,1:T(8,128)S(1)} %collective-permute-done.9), channel_id=1, source_target_pairs={{0,15},{1,0},{2,1},{3,2},{4,3},{5,4},{6,5},{7,6},{8,7},{9,8},{10,9... | collective-permute-start | bytes 393224 | tf_op jit(solution)/shard_map/ppermute | solution.py:78
  36.9 6.9 %collective-permute-start.4 = (f32[2048,16]{0,1:T(8,128)S(1)}, f32[2048,16]{0,1:T(8,128)S(1)}, u32[]{:S(2)}, u32[]{:S(2)}) collective-permute-start(f32[2048,16]{0,1:T(8,128)S(1)} %collective-permute-done.3), channel_id=1, source_target_pairs={{0,1},{1,2},{2,3},{3,4},{4,5},{5,6},{6,7},{7,8},{8,9},{9,10},{10,1... | collective-permute-start | bytes 393224 | tf_op jit(solution)/shard_map/ppermute | solution.py:75
  38.8 6.9 %collective-permute-start.11 = (f32[2048,16]{0,1:T(8,128)S(1)}, f32[2048,16]{0,1:T(8,128)S(1)}, u32[]{:S(2)}, u32[]{:S(2)}) collective-permute-start(f32[2048,16]{0,1:T(8,128)S(1)} %collective-permute-done.10), channel_id=1, source_target_pairs={{0,15},{1,0},{2,1},{3,2},{4,3},{5,4},{6,5},{7,6},{8,7},{9,8},{10,9... | collective-permute-start | bytes 393224 | tf_op jit(solution)/shard_map/ppermute | solution.py:78
  43.8 6.9 %collective-permute-start.5 = (f32[2048,16]{0,1:T(8,128)S(1)}, f32[2048,16]{0,1:T(8,128)S(1)}, u32[]{:S(2)}, u32[]{:S(2)}) collective-permute-start(f32[2048,16]{0,1:T(8,128)S(1)} %collective-permute-done.4), channel_id=1, source_target_pairs={{0,1},{1,2},{2,3},{3,4},{4,5},{5,6},{6,7},{7,8},{8,9},{9,10},{10,1... | collective-permute-start | bytes 393224 | tf_op jit(solution)/shard_map/ppermute | solution.py:75
  45.7 6.9 %collective-permute-start.12 = (f32[2048,16]{0,1:T(8,128)S(1)}, f32[2048,16]{0,1:T(8,128)S(1)}, u32[]{:S(2)}, u32[]{:S(2)}) collective-permute-start(f32[2048,16]{0,1:T(8,128)S(1)} %collective-permute-done.11), channel_id=1, source_target_pairs={{0,15},{1,0},{2,1},{3,2},{4,3},{5,4},{6,5},{7,6},{8,7},{9,8},{10,9... | collective-permute-start | bytes 393224 | tf_op jit(solution)/shard_map/ppermute | solution.py:78
  50.7 7.7 %collective-permute-start.6 = (f32[2048,16]{0,1:T(8,128)S(1)}, f32[2048,16]{0,1:T(8,128)S(1)}, u32[]{:S(2)}, u32[]{:S(2)}) collective-permute-start(f32[2048,16]{0,1:T(8,128)S(1)} %collective-permute-done.5), channel_id=1, source_target_pairs={{0,1},{1,2},{2,3},{3,4},{4,5},{5,6},{6,7},{7,8},{8,9},{9,10},{10,1... | collective-permute-start | bytes 393224 | tf_op jit(solution)/shard_map/ppermute | solution.py:75
  52.6 7.7 %collective-permute-start.13 = (f32[2048,16]{0,1:T(8,128)S(1)}, f32[2048,16]{0,1:T(8,128)S(1)}, u32[]{:S(2)}, u32[]{:S(2)}) collective-permute-start(f32[2048,16]{0,1:T(8,128)S(1)} %collective-permute-done.12), channel_id=1, source_target_pairs={{0,15},{1,0},{2,1},{3,2},{4,3},{5,4},{6,5},{7,6},{8,7},{9,8},{10,9... | collective-permute-start | bytes 393224 | tf_op jit(solution)/shard_map/ppermute | solution.py:78
  58.4 8.1 %collective-permute-start.7 = (f32[2048,16]{0,1:T(8,128)S(1)}, f32[2048,16]{0,1:T(8,128)S(1)}, u32[]{:S(2)}, u32[]{:S(2)}) collective-permute-start(f32[2048,16]{0,1:T(8,128)S(1)} %collective-permute-done.6), channel_id=1, source_target_pairs={{0,1},{1,2},{2,3},{3,4},{4,5},{5,6},{6,7},{7,8},{8,9},{9,10},{10,1... | collective-permute-start | bytes 393224 | tf_op jit(solution)/shard_map/ppermute | solution.py:75
  60.4 7.5 %collective-permute-start.14 = (f32[2048,16]{0,1:T(8,128)S(1)}, f32[2048,16]{0,1:T(8,128)S(1)}, u32[]{:S(2)}, u32[]{:S(2)}) collective-permute-start(f32[2048,16]{0,1:T(8,128)S(1)} %collective-permute-done.13), channel_id=1, source_target_pairs={{0,15},{1,0},{2,1},{3,2},{4,3},{5,4},{6,5},{7,6},{8,7},{9,8},{10,9... | collective-permute-start | bytes 393224 | tf_op jit(solution)/shard_map/ppermute | solution.py:78
  67.9 1.9 %copy-start = (f32[2048,256]{1,0:T(8,128)S(1)}, f32[2048,256]{1,0:T(8,128)}, u32[]{:S(2)}) copy-start(f32[2048,256]{1,0:T(8,128)} %param.3) | copy-start | bytes 6291460
  102.3 15.3 %all-to-all-start.1 = ((f32[32,8,512]{2,1,0:T(8,128)}), f32[32,8,512]{2,1,0:T(8,128)S(1)}, u32[]{:S(2)}, u32[]{:S(2)}) async-start(f32[32,8,512]{2,1,0:T(8,128)} %broadcast_in_dim.2), calls=%async_computation.1 | async-start | bytes 1048576 | tf_op jit(solution)/shard_map/all_to_all | solution.py:89
  160.0 9.7 %copy-start.1 = (f32[256,256]{1,0:T(8,128)}, f32[256,256]{1,0:T(8,128)S(1)}, u32[]{:S(2)}) copy-start(f32[256,256]{1,0:T(8,128)S(1)} %fusion.4) | copy-start | bytes 786436

commit v8 on v7

--- a/solution.py
+++ b/solution.py
@@ -29,9 +29,10 @@
         def block(b, strip):
             base = pl.multiple_of(b * 8, 8)
             for t in range(8):
-                col = jnp.sum(jnp.where(lane[:, :key] == base + t, strip[:, :key], 0.0),
-                              axis=1, keepdims=True)
-                scale = 1.0 / jnp.sqrt(col[t:t + 1, :])
+                col = pltpu.roll(strip[:, :128], (128 - (base + t - lo)) % 128, 1)[:, 0:1]
+                diag = col[t:t + 1, :]
+                guess = lax.rsqrt(diag)
+                scale = guess * (1.5 - 0.5 * diag * guess * guess)
                 pivot = strip[t:t + 1, :] * scale
                 mult = jnp.where(sub_col > t, col * scale, 0.0)
                 strip = jnp.where(sub == t, pivot, strip - mult * pivot)

time: 170 us -> 185 us (1.088)
  Pallas kernels: 40 us -> 54.2 us
    pallas_call x1, Pallas kernels: 40 us -> 54.2 us  [factor(): pl.pallas_call(factor_kernel, out_shape=(jax.ShapeDtypeStruct((n, n), jnp...]
where the time goes in v8:
time: 185 us; the launch traced here: 184 us
  starting transfers between devices  55.2 us (30%)
  Pallas kernels  54.2 us (29%)
  blocking collectives  27.8 us (15%)
  waiting for transfers between devices  26.8 us (14%)
  matrix products  14.7 us (8%)
  other arithmetic  2.13 us (1%)
  local copies, waits for them, and re-layouts  1.95 us (1%)
    pallas_call x1, Pallas kernels, factor(): pl.pallas_call(factor_kernel, out_shape=(jax.ShapeDtypeStruct((n, n), jnp...  54.2 us
    ppermute x7, starting transfers between devices, col_gather(): behind = lax.ppermute(behind, 'col', [(i, (i - 1) % n) for i in range(n)])  33.4 us
    all_to_all x1, blocking collectives, row_sum(): mine = lax.all_to_all(parts, 'row', 0, 0, tiled=False).sum(0)  27.8 us
    ppermute x8, starting transfers between devices, col_gather(): ahead = lax.ppermute(ahead, 'col', [(i, (i + 1) % n) for i in range(n)])  17.9 us
    ppermute x8, waiting for transfers between devices, col_gather(): ahead = lax.ppermute(ahead, 'col', [(i, (i + 1) % n) for i in range(n)])  14.3 us
    all_to_all x1, waiting for transfers between devices, row_sum(): return lax.all_to_all(copies, 'row', 0, 0, tiled=False).reshape(rows, cols)  11.3 us
    dot_general x1, matrix products, per_device(): jnp.dot(gathered, jnp.roll(coefficients, -shift, axis=0), precision=highest)  6.35 us
    all_to_all x1, starting transfers between devices, row_sum(): return lax.all_to_all(copies, 'row', 0, 0, tiled=False).reshape(rows, cols)  3.86 us
  transfers between devices with their start and end apart: 16, of which 10 were waited for; matrix products, arithmetic and copies ran while one was open for 0% of the time, Pallas kernels for 0%

profile of v8, /device:TPU:1, one launch (start us, length us, event | category | flops | bytes accessed | tf_op | source)
XLA Modules:
  0.0 183.8 jit_solution(2453434965181106153)
XLA Ops:
  0.6 0.0 copy-start.2
  0.6 4.5 %collective-permute-start = (f32[2048,16]{0,1:T(8,128)}, f32[2048,16]{0,1:T(8,128)S(1)}, u32[]{:S(2)}, u32[]{:S(2)}) collective-permute-start(f32[2048,16]{0,1:T(8,128)} %param.2), channel_id=1, source_target_pairs={{0,1},{1,2},{2,3},{3,4},{4,5},{5,6},{6,7},{7,8},{8,9},{9,10},{10,1... | collective-permute-start | bytes 393224 | tf_op jit(solution)/shard_map/ppermute | solution.py:76
  5.2 11.0 %collective-permute-done = f32[2048,16]{0,1:T(8,128)S(1)} collective-permute-done((f32[2048,16]{0,1:T(8,128)}, f32[2048,16]{0,1:T(8,128)S(1)}, u32[]{:S(2)}, u32[]{:S(2)}) %collective-permute-start) | collective-permute-done | bytes 131104 | tf_op jit(solution)/shard_map/ppermute | solution.py:76
  16.1 1.9 %collective-permute-start.1 = (f32[2048,16]{0,1:T(8,128)S(1)}, f32[2048,16]{0,1:T(8,128)S(1)}, u32[]{:S(2)}, u32[]{:S(2)}) collective-permute-start(f32[2048,16]{0,1:T(8,128)S(1)} %collective-permute-done), channel_id=1, source_target_pairs={{0,1},{1,2},{2,3},{3,4},{4,5},{5,6},{6,7},{7,8},{8,9},{9,10},{10,1... | collective-permute-start | bytes 393224 | tf_op jit(solution)/shard_map/ppermute | solution.py:76
  18.1 4.6 %collective-permute-start.8 = (f32[2048,16]{0,1:T(8,128)}, f32[2048,16]{0,1:T(8,128)S(1)}, u32[]{:S(2)}, u32[]{:S(2)}) collective-permute-start(f32[2048,16]{0,1:T(8,128)} %param.2), channel_id=1, source_target_pairs={{0,15},{1,0},{2,1},{3,2},{4,3},{5,4},{6,5},{7,6},{8,7},{9,8},{10,9... | collective-permute-start | bytes 393224 | tf_op jit(solution)/shard_map/ppermute | solution.py:79
  22.6 0.4 collective-permute-done.1
  23.1 1.9 %collective-permute-start.2 = (f32[2048,16]{0,1:T(8,128)S(1)}, f32[2048,16]{0,1:T(8,128)S(1)}, u32[]{:S(2)}, u32[]{:S(2)}) collective-permute-start(f32[2048,16]{0,1:T(8,128)S(1)} %collective-permute-done.1), channel_id=1, source_target_pairs={{0,1},{1,2},{2,3},{3,4},{4,5},{5,6},{6,7},{7,8},{8,9},{9,10},{10,1... | collective-permute-start | bytes 393224 | tf_op jit(solution)/shard_map/ppermute | solution.py:76
  25.0 0.0 collective-permute-done.8
  25.0 4.8 %collective-permute-start.9 = (f32[2048,16]{0,1:T(8,128)S(1)}, f32[2048,16]{0,1:T(8,128)S(1)}, u32[]{:S(2)}, u32[]{:S(2)}) collective-permute-start(f32[2048,16]{0,1:T(8,128)S(1)} %collective-permute-done.8), channel_id=1, source_target_pairs={{0,15},{1,0},{2,1},{3,2},{4,3},{5,4},{6,5},{7,6},{8,7},{9,8},{10,9... | collective-permute-start | bytes 393224 | tf_op jit(solution)/shard_map/ppermute | solution.py:79
  29.8 0.2 collective-permute-done.2
  30.0 1.9 %collective-permute-start.3 = (f32[2048,16]{0,1:T(8,128)S(1)}, f32[2048,16]{0,1:T(8,128)S(1)}, u32[]{:S(2)}, u32[]{:S(2)}) collective-permute-start(f32[2048,16]{0,1:T(8,128)S(1)} %collective-permute-done.2), channel_id=1, source_target_pairs={{0,1},{1,2},{2,3},{3,4},{4,5},{5,6},{6,7},{7,8},{8,9},{9,10},{10,1... | collective-permute-start | bytes 393224 | tf_op jit(solution)/shard_map/ppermute | solution.py:76
  31.9 0.0 collective-permute-done.9
  31.9 4.8 %collective-permute-start.10 = (f32[2048,16]{0,1:T(8,128)S(1)}, f32[2048,16]{0,1:T(8,128)S(1)}, u32[]{:S(2)}, u32[]{:S(2)}) collective-permute-start(f32[2048,16]{0,1:T(8,128)S(1)} %collective-permute-done.9), channel_id=1, source_target_pairs={{0,15},{1,0},{2,1},{3,2},{4,3},{5,4},{6,5},{7,6},{8,7},{9,8},{10,9... | collective-permute-start | bytes 393224 | tf_op jit(solution)/shard_map/ppermute | solution.py:79
  36.7 0.2 collective-permute-done.3
  36.9 1.9 %collective-permute-start.4 = (f32[2048,16]{0,1:T(8,128)S(1)}, f32[2048,16]{0,1:T(8,128)S(1)}, u32[]{:S(2)}, u32[]{:S(2)}) collective-permute-start(f32[2048,16]{0,1:T(8,128)S(1)} %collective-permute-done.3), channel_id=1, source_target_pairs={{0,1},{1,2},{2,3},{3,4},{4,5},{5,6},{6,7},{7,8},{8,9},{9,10},{10,1... | collective-permute-start | bytes 393224 | tf_op jit(solution)/shard_map/ppermute | solution.py:76
  38.8 0.0 collective-permute-done.10
  38.8 4.8 %collective-permute-start.11 = (f32[2048,16]{0,1:T(8,128)S(1)}, f32[2048,16]{0,1:T(8,128)S(1)}, u32[]{:S(2)}, u32[]{:S(2)}) collective-permute-start(f32[2048,16]{0,1:T(8,128)S(1)} %collective-permute-done.10), channel_id=1, source_target_pairs={{0,15},{1,0},{2,1},{3,2},{4,3},{5,4},{6,5},{7,6},{8,7},{9,8},{10,9... | collective-permute-start | bytes 393224 | tf_op jit(solution)/shard_map/ppermute | solution.py:79
  43.6 0.2 collective-permute-done.4
  43.8 1.9 %collective-permute-start.5 = (f32[2048,16]{0,1:T(8,128)S(1)}, f32[2048,16]{0,1:T(8,128)S(1)}, u32[]{:S(2)}, u32[]{:S(2)}) collective-permute-start(f32[2048,16]{0,1:T(8,128)S(1)} %collective-permute-done.4), channel_id=1, source_target_pairs={{0,1},{1,2},{2,3},{3,4},{4,5},{5,6},{6,7},{7,8},{8,9},{9,10},{10,1... | collective-permute-start | bytes 393224 | tf_op jit(solution)/shard_map/ppermute | solution.py:76
  45.7 0.0 collective-permute-done.11
  45.7 4.8 %collective-permute-start.12 = (f32[2048,16]{0,1:T(8,128)S(1)}, f32[2048,16]{0,1:T(8,128)S(1)}, u32[]{:S(2)}, u32[]{:S(2)}) collective-permute-start(f32[2048,16]{0,1:T(8,128)S(1)} %collective-permute-done.11), channel_id=1, source_target_pairs={{0,15},{1,0},{2,1},{3,2},{4,3},{5,4},{6,5},{7,6},{8,7},{9,8},{10,9... | collective-permute-start | bytes 393224 | tf_op jit(solution)/shard_map/ppermute | solution.py:79
  50.5 0.2 collective-permute-done.5
  50.7 1.9 %collective-permute-start.6 = (f32[2048,16]{0,1:T(8,128)S(1)}, f32[2048,16]{0,1:T(8,128)S(1)}, u32[]{:S(2)}, u32[]{:S(2)}) collective-permute-start(f32[2048,16]{0,1:T(8,128)S(1)} %collective-permute-done.5), channel_id=1, source_target_pairs={{0,1},{1,2},{2,3},{3,4},{4,5},{5,6},{6,7},{7,8},{8,9},{9,10},{10,1... | collective-permute-start | bytes 393224 | tf_op jit(solution)/shard_map/ppermute | solution.py:76
  52.6 0.0 collective-permute-done.12
  52.6 4.8 %collective-permute-start.13 = (f32[2048,16]{0,1:T(8,128)S(1)}, f32[2048,16]{0,1:T(8,128)S(1)}, u32[]{:S(2)}, u32[]{:S(2)}) collective-permute-start(f32[2048,16]{0,1:T(8,128)S(1)} %collective-permute-done.12), channel_id=1, source_target_pairs={{0,15},{1,0},{2,1},{3,2},{4,3},{5,4},{6,5},{7,6},{8,7},{9,8},{10,9... | collective-permute-start | bytes 393224 | tf_op jit(solution)/shard_map/ppermute | solution.py:79
  57.4 1.0 collective-permute-done.6
  58.4 1.9 %collective-permute-start.7 = (f32[2048,16]{0,1:T(8,128)S(1)}, f32[2048,16]{0,1:T(8,128)S(1)}, u32[]{:S(2)}, u32[]{:S(2)}) collective-permute-start(f32[2048,16]{0,1:T(8,128)S(1)} %collective-permute-done.6), channel_id=1, source_target_pairs={{0,1},{1,2},{2,3},{3,4},{4,5},{5,6},{6,7},{7,8},{8,9},{9,10},{10,1... | collective-permute-start | bytes 393224 | tf_op jit(solution)/shard_map/ppermute | solution.py:76
  60.3 0.0 collective-permute-done.13
  60.4 5.0 %collective-permute-start.14 = (f32[2048,16]{0,1:T(8,128)S(1)}, f32[2048,16]{0,1:T(8,128)S(1)}, u32[]{:S(2)}, u32[]{:S(2)}) collective-permute-start(f32[2048,16]{0,1:T(8,128)S(1)} %collective-permute-done.13), channel_id=1, source_target_pairs={{0,15},{1,0},{2,1},{3,2},{4,3},{5,4},{6,5},{7,6},{8,7},{9,8},{10,9... | collective-permute-start | bytes 393224 | tf_op jit(solution)/shard_map/ppermute | solution.py:79
  65.4 1.1 collective-permute-done.7
  66.6 0.0 copy-done.2
  66.7 1.2 collective-permute-done.14
  67.9 0.0 copy-start
  67.9 1.9 %fusion.8 = f32[256,256]{0,1:T(8,128)S(1)} fusion(f32[2048,256]{0,1:T(8,128)S(1)} %constant_dynamic-update-slice_fusion), kind=kOutput, calls=%fused_computation.32 | convolution fusion | flops 1610612736 | bytes 2359296 | tf_op jit(solution)/shard_map/dot_general | solution.py:98
  69.8 0.0 copy-done
  69.8 3.6 %fusion.9 = f32[256,256]{0,1:T(8,128)S(1)} fusion(f32[2048,256]{0,1:T(8,128)S(1)} %constant_dynamic-update-slice_fusion, f32[2048,256]{1,0:T(8,128)S(1)} %copy-done), kind=kOutput, calls=%fused_computation.33 | convolution fusion | flops 1610612736 | bytes 4456448 | tf_op jit(solution)/shard_map/dot_general | solution.py:97
  73.4 0.2 copy.6
  73.6 27.8 %all_to_all.10 = f32[32,8,512]{2,1,0:T(8,128)S(1)} all-to-all(f32[32,8,512]{2,1,0:T(8,128)S(1)} %bitcast.11), channel_id=1, replica_groups=mesh['row'=32,'col'=16] {'row'}, dimensions={0} | all-to-all | bytes 1048576 | tf_op jit(solution)/shard_map/all_to_all | solution.py:88
  101.4 0.9 broadcast_in_dim.2
  102.3 3.9 %all-to-all-start.1 = ((f32[32,8,512]{2,1,0:T(8,128)}), f32[32,8,512]{2,1,0:T(8,128)S(1)}, u32[]{:S(2)}, u32[]{:S(2)}) async-start(f32[32,8,512]{2,1,0:T(8,128)} %broadcast_in_dim.2), calls=%async_computation.1 | async-start | bytes 1048576 | tf_op jit(solution)/shard_map/all_to_all | solution.py:90
  106.2 11.3 %all-to-all-done.1 = f32[32,8,512]{2,1,0:T(8,128)S(1)} async-done(((f32[32,8,512]{2,1,0:T(8,128)}), f32[32,8,512]{2,1,0:T(8,128)S(1)}, u32[]{:S(2)}, u32[]{:S(2)}) %all-to-all-start.1) | async-done | bytes 524320 | tf_op jit(solution)/shard_map/all_to_all | solution.py:90
  117.6 0.1 fusion
  117.7 0.9 fusion.3.gram_ref
  118.6 54.2 %shard_map.49 = (f32[256,256]{1,0:T(8,128)}, f32[256,256]{1,0:T(8,128)}) custom-call(f32[256,256]{1,0:T(8,128)} %fusion.3.gram_ref), custom_call_target="tpu_custom_call" | custom-call | tf_op jit(solution)/shard_map/pallas_call | solution.py:63
  172.8 1.3 fusion.4
  174.1 0.0 copy-start.1
  174.1 1.6 fusion.10
  175.8 1.0 dynamic-slice_multiply_fusion
  176.8 0.7 copy.7
  177.5 6.4 %convolution_subtract_fusion = f32[2048,256]{1,0:T(8,128)} fusion(f32[2048,256]{1,0:T(8,128)} %param.3, f32[2048,256]{0,1:T(8,128)S(1)} %constant_dynamic-update-slice_fusion, s32[]{:T(128)S(6)} %select_n.36, f32[256,256]{1,0:T(8,128)S(1)} %fusion.10), kind=kOutput, calls=%fused_computation | convolution fusion | flops 1611202560 | bytes 6553604 | tf_op jit(solution)/shard_map/dot_general | solution.py:105
  183.8 0.0 copy-done.1
  (19 shorter events, 0.3 us)
Async XLA Ops:
  0.6 66.0 %copy-start.2 = (f32[2048,16]{0,1:T(8,128)S(1)}, f32[2048,16]{0,1:T(8,128)}, u32[]{:S(2)}) copy-start(f32[2048,16]{0,1:T(8,128)} %param.2) | copy-start | bytes 393220
  0.6 15.5 %collective-permute-start = (f32[2048,16]{0,1:T(8,128)}, f32[2048,16]{0,1:T(8,128)S(1)}, u32[]{:S(2)}, u32[]{:S(2)}) collective-permute-start(f32[2048,16]{0,1:T(8,128)} %param.2), channel_id=1, source_target_pairs={{0,1},{1,2},{2,3},{3,4},{4,5},{5,6},{6,7},{7,8},{8,9},{9,10},{10,1... | collective-permute-start | bytes 393224 | tf_op jit(solution)/shard_map/ppermute | solution.py:76
  16.1 6.9 %collective-permute-start.1 = (f32[2048,16]{0,1:T(8,128)S(1)}, f32[2048,16]{0,1:T(8,128)S(1)}, u32[]{:S(2)}, u32[]{:S(2)}) collective-permute-start(f32[2048,16]{0,1:T(8,128)S(1)} %collective-permute-done), channel_id=1, source_target_pairs={{0,1},{1,2},{2,3},{3,4},{4,5},{5,6},{6,7},{7,8},{8,9},{9,10},{10,1... | collective-permute-start | bytes 393224 | tf_op jit(solution)/shard_map/ppermute | solution.py:76
  18.1 6.9 %collective-permute-start.8 = (f32[2048,16]{0,1:T(8,128)}, f32[2048,16]{0,1:T(8,128)S(1)}, u32[]{:S(2)}, u32[]{:S(2)}) collective-permute-start(f32[2048,16]{0,1:T(8,128)} %param.2), channel_id=1, source_target_pairs={{0,15},{1,0},{2,1},{3,2},{4,3},{5,4},{6,5},{7,6},{8,7},{9,8},{10,9... | collective-permute-start | bytes 393224 | tf_op jit(solution)/shard_map/ppermute | solution.py:79
  23.1 6.9 %collective-permute-start.2 = (f32[2048,16]{0,1:T(8,128)S(1)}, f32[2048,16]{0,1:T(8,128)S(1)}, u32[]{:S(2)}, u32[]{:S(2)}) collective-permute-start(f32[2048,16]{0,1:T(8,128)S(1)} %collective-permute-done.1), channel_id=1, source_target_pairs={{0,1},{1,2},{2,3},{3,4},{4,5},{5,6},{6,7},{7,8},{8,9},{9,10},{10,1... | collective-permute-start | bytes 393224 | tf_op jit(solution)/shard_map/ppermute | solution.py:76
  25.0 6.9 %collective-permute-start.9 = (f32[2048,16]{0,1:T(8,128)S(1)}, f32[2048,16]{0,1:T(8,128)S(1)}, u32[]{:S(2)}, u32[]{:S(2)}) collective-permute-start(f32[2048,16]{0,1:T(8,128)S(1)} %collective-permute-done.8), channel_id=1, source_target_pairs={{0,15},{1,0},{2,1},{3,2},{4,3},{5,4},{6,5},{7,6},{8,7},{9,8},{10,9... | collective-permute-start | bytes 393224 | tf_op jit(solution)/shard_map/ppermute | solution.py:79
  30.0 6.9 %collective-permute-start.3 = (f32[2048,16]{0,1:T(8,128)S(1)}, f32[2048,16]{0,1:T(8,128)S(1)}, u32[]{:S(2)}, u32[]{:S(2)}) collective-permute-start(f32[2048,16]{0,1:T(8,128)S(1)} %collective-permute-done.2), channel_id=1, source_target_pairs={{0,1},{1,2},{2,3},{3,4},{4,5},{5,6},{6,7},{7,8},{8,9},{9,10},{10,1... | collective-permute-start | bytes 393224 | tf_op jit(solution)/shard_map/ppermute | solution.py:76
  31.9 6.9 %collective-permute-start.10 = (f32[2048,16]{0,1:T(8,128)S(1)}, f32[2048,16]{0,1:T(8,128)S(1)}, u32[]{:S(2)}, u32[]{:S(2)}) collective-permute-start(f32[2048,16]{0,1:T(8,128)S(1)} %collective-permute-done.9), channel_id=1, source_target_pairs={{0,15},{1,0},{2,1},{3,2},{4,3},{5,4},{6,5},{7,6},{8,7},{9,8},{10,9... | collective-permute-start | bytes 393224 | tf_op jit(solution)/shard_map/ppermute | solution.py:79
  36.9 6.9 %collective-permute-start.4 = (f32[2048,16]{0,1:T(8,128)S(1)}, f32[2048,16]{0,1:T(8,128)S(1)}, u32[]{:S(2)}, u32[]{:S(2)}) collective-permute-start(f32[2048,16]{0,1:T(8,128)S(1)} %collective-permute-done.3), channel_id=1, source_target_pairs={{0,1},{1,2},{2,3},{3,4},{4,5},{5,6},{6,7},{7,8},{8,9},{9,10},{10,1... | collective-permute-start | bytes 393224 | tf_op jit(solution)/shard_map/ppermute | solution.py:76
  38.8 6.9 %collective-permute-start.11 = (f32[2048,16]{0,1:T(8,128)S(1)}, f32[2048,16]{0,1:T(8,128)S(1)}, u32[]{:S(2)}, u32[]{:S(2)}) collective-permute-start(f32[2048,16]{0,1:T(8,128)S(1)} %collective-permute-done.10), channel_id=1, source_target_pairs={{0,15},{1,0},{2,1},{3,2},{4,3},{5,4},{6,5},{7,6},{8,7},{9,8},{10,9... | collective-permute-start | bytes 393224 | tf_op jit(solution)/shard_map/ppermute | solution.py:79
  43.8 6.9 %collective-permute-start.5 = (f32[2048,16]{0,1:T(8,128)S(1)}, f32[2048,16]{0,1:T(8,128)S(1)}, u32[]{:S(2)}, u32[]{:S(2)}) collective-permute-start(f32[2048,16]{0,1:T(8,128)S(1)} %collective-permute-done.4), channel_id=1, source_target_pairs={{0,1},{1,2},{2,3},{3,4},{4,5},{5,6},{6,7},{7,8},{8,9},{9,10},{10,1... | collective-permute-start | bytes 393224 | tf_op jit(solution)/shard_map/ppermute | solution.py:76
  45.7 6.9 %collective-permute-start.12 = (f32[2048,16]{0,1:T(8,128)S(1)}, f32[2048,16]{0,1:T(8,128)S(1)}, u32[]{:S(2)}, u32[]{:S(2)}) collective-permute-start(f32[2048,16]{0,1:T(8,128)S(1)} %collective-permute-done.11), channel_id=1, source_target_pairs={{0,15},{1,0},{2,1},{3,2},{4,3},{5,4},{6,5},{7,6},{8,7},{9,8},{10,9... | collective-permute-start | bytes 393224 | tf_op jit(solution)/shard_map/ppermute | solution.py:79
  50.7 7.7 %collective-permute-start.6 = (f32[2048,16]{0,1:T(8,128)S(1)}, f32[2048,16]{0,1:T(8,128)S(1)}, u32[]{:S(2)}, u32[]{:S(2)}) collective-permute-start(f32[2048,16]{0,1:T(8,128)S(1)} %collective-permute-done.5), channel_id=1, source_target_pairs={{0,1},{1,2},{2,3},{3,4},{4,5},{5,6},{6,7},{7,8},{8,9},{9,10},{10,1... | collective-permute-start | bytes 393224 | tf_op jit(solution)/shard_map/ppermute | solution.py:76
  52.6 7.7 %collective-permute-start.13 = (f32[2048,16]{0,1:T(8,128)S(1)}, f32[2048,16]{0,1:T(8,128)S(1)}, u32[]{:S(2)}, u32[]{:S(2)}) collective-permute-start(f32[2048,16]{0,1:T(8,128)S(1)} %collective-permute-done.12), channel_id=1, source_target_pairs={{0,15},{1,0},{2,1},{3,2},{4,3},{5,4},{6,5},{7,6},{8,7},{9,8},{10,9... | collective-permute-start | bytes 393224 | tf_op jit(solution)/shard_map/ppermute | solution.py:79
  58.4 8.1 %collective-permute-start.7 = (f32[2048,16]{0,1:T(8,128)S(1)}, f32[2048,16]{0,1:T(8,128)S(1)}, u32[]{:S(2)}, u32[]{:S(2)}) collective-permute-start(f32[2048,16]{0,1:T(8,128)S(1)} %collective-permute-done.6), channel_id=1, source_target_pairs={{0,1},{1,2},{2,3},{3,4},{4,5},{5,6},{6,7},{7,8},{8,9},{9,10},{10,1... | collective-permute-start | bytes 393224 | tf_op jit(solution)/shard_map/ppermute | solution.py:76
  60.4 7.5 %collective-permute-start.14 = (f32[2048,16]{0,1:T(8,128)S(1)}, f32[2048,16]{0,1:T(8,128)S(1)}, u32[]{:S(2)}, u32[]{:S(2)}) collective-permute-start(f32[2048,16]{0,1:T(8,128)S(1)} %collective-permute-done.13), channel_id=1, source_target_pairs={{0,15},{1,0},{2,1},{3,2},{4,3},{5,4},{6,5},{7,6},{8,7},{9,8},{10,9... | collective-permute-start | bytes 393224 | tf_op jit(solution)/shard_map/ppermute | solution.py:79
  67.9 1.9 %copy-start = (f32[2048,256]{1,0:T(8,128)S(1)}, f32[2048,256]{1,0:T(8,128)}, u32[]{:S(2)}) copy-start(f32[2048,256]{1,0:T(8,128)} %param.3) | copy-start | bytes 6291460
  102.3 15.3 %all-to-all-start.1 = ((f32[32,8,512]{2,1,0:T(8,128)}), f32[32,8,512]{2,1,0:T(8,128)S(1)}, u32[]{:S(2)}, u32[]{:S(2)}) async-start(f32[32,8,512]{2,1,0:T(8,128)} %broadcast_in_dim.2), calls=%async_computation.1 | async-start | bytes 1048576 | tf_op jit(solution)/shard_map/all_to_all | solution.py:90
  174.1 9.7 %copy-start.1 = (f32[256,256]{1,0:T(8,128)}, f32[256,256]{1,0:T(8,128)S(1)}, u32[]{:S(2)}) copy-start(f32[256,256]{1,0:T(8,128)S(1)} %fusion.4) | copy-start | bytes 786436

commit v9 on v8

--- a/solution.py
+++ b/solution.py
@@ -29,7 +29,8 @@
         def block(b, strip):
             base = pl.multiple_of(b * 8, 8)
             for t in range(8):
-                col = pltpu.roll(strip[:, :128], (128 - (base + t - lo)) % 128, 1)[:, 0:1]
+                col = jnp.sum(jnp.where(lane[:, :128] == base + t, strip[:, :128], 0.0),
+                              axis=1, keepdims=True)
                 diag = col[t:t + 1, :]
                 guess = lax.rsqrt(diag)
                 scale = guess * (1.5 - 0.5 * diag * guess * guess)

time: 185 us -> 169 us (0.914)
  Pallas kernels: 54.2 us -> 39 us
    pallas_call x1, Pallas kernels: 54.2 us -> 39 us  [factor(): pl.pallas_call(factor_kernel, out_shape=(jax.ShapeDtypeStruct((n, n), jnp...]
where the time goes in v9:
time: 169 us
  starting transfers between devices  55.2 us (33%)
  Pallas kernels  39 us (23%)
  blocking collectives  27.8 us (16%)
  waiting for transfers between devices  26.8 us (16%)
  matrix products  14.7 us (9%)
  other arithmetic  2.13 us (1%)
  local copies, waits for them, and re-layouts  1.95 us (1%)
    pallas_call x1, Pallas kernels, factor(): pl.pallas_call(factor_kernel, out_shape=(jax.ShapeDtypeStruct((n, n), jnp...  39 us
    ppermute x7, starting transfers between devices, col_gather(): behind = lax.ppermute(behind, 'col', [(i, (i - 1) % n) for i in range(n)])  33.4 us
    all_to_all x1, blocking collectives, row_sum(): mine = lax.all_to_all(parts, 'row', 0, 0, tiled=False).sum(0)  27.8 us
    ppermute x8, starting transfers between devices, col_gather(): ahead = lax.ppermute(ahead, 'col', [(i, (i + 1) % n) for i in range(n)])  17.9 us
    ppermute x8, waiting for transfers between devices, col_gather(): ahead = lax.ppermute(ahead, 'col', [(i, (i + 1) % n) for i in range(n)])  14.3 us
    all_to_all x1, waiting for transfers between devices, row_sum(): return lax.all_to_all(copies, 'row', 0, 0, tiled=False).reshape(rows, cols)  11.3 us
    dot_general x1, matrix products, per_device(): jnp.dot(gathered, jnp.roll(coefficients, -shift, axis=0), precision=highest)  6.36 us
    all_to_all x1, starting transfers between devices, row_sum(): return lax.all_to_all(copies, 'row', 0, 0, tiled=False).reshape(rows, cols)  3.86 us
  transfers between devices with their start and end apart: 16, of which 10 were waited for; matrix products, arithmetic and copies ran while one was open for 0% of the time, Pallas kernels for 0%

profile of v9, /device:TPU:1, one launch (start us, length us, event | category | flops | bytes accessed | tf_op | source)
XLA Modules:
  0.0 168.6 jit_solution(18347267746683767981)
XLA Ops:
  0.6 0.0 copy-start.2
  0.6 4.5 %collective-permute-start = (f32[2048,16]{0,1:T(8,128)}, f32[2048,16]{0,1:T(8,128)S(1)}, u32[]{:S(2)}, u32[]{:S(2)}) collective-permute-start(f32[2048,16]{0,1:T(8,128)} %param.2), channel_id=1, source_target_pairs={{0,1},{1,2},{2,3},{3,4},{4,5},{5,6},{6,7},{7,8},{8,9},{9,10},{10,1... | collective-permute-start | bytes 393224 | tf_op jit(solution)/shard_map/ppermute | solution.py:77
  5.2 11.0 %collective-permute-done = f32[2048,16]{0,1:T(8,128)S(1)} collective-permute-done((f32[2048,16]{0,1:T(8,128)}, f32[2048,16]{0,1:T(8,128)S(1)}, u32[]{:S(2)}, u32[]{:S(2)}) %collective-permute-start) | collective-permute-done | bytes 131104 | tf_op jit(solution)/shard_map/ppermute | solution.py:77
  16.1 1.9 %collective-permute-start.1 = (f32[2048,16]{0,1:T(8,128)S(1)}, f32[2048,16]{0,1:T(8,128)S(1)}, u32[]{:S(2)}, u32[]{:S(2)}) collective-permute-start(f32[2048,16]{0,1:T(8,128)S(1)} %collective-permute-done), channel_id=1, source_target_pairs={{0,1},{1,2},{2,3},{3,4},{4,5},{5,6},{6,7},{7,8},{8,9},{9,10},{10,1... | collective-permute-start | bytes 393224 | tf_op jit(solution)/shard_map/ppermute | solution.py:77
  18.1 4.6 %collective-permute-start.8 = (f32[2048,16]{0,1:T(8,128)}, f32[2048,16]{0,1:T(8,128)S(1)}, u32[]{:S(2)}, u32[]{:S(2)}) collective-permute-start(f32[2048,16]{0,1:T(8,128)} %param.2), channel_id=1, source_target_pairs={{0,15},{1,0},{2,1},{3,2},{4,3},{5,4},{6,5},{7,6},{8,7},{9,8},{10,9... | collective-permute-start | bytes 393224 | tf_op jit(solution)/shard_map/ppermute | solution.py:80
  22.6 0.4 collective-permute-done.1
  23.1 1.9 %collective-permute-start.2 = (f32[2048,16]{0,1:T(8,128)S(1)}, f32[2048,16]{0,1:T(8,128)S(1)}, u32[]{:S(2)}, u32[]{:S(2)}) collective-permute-start(f32[2048,16]{0,1:T(8,128)S(1)} %collective-permute-done.1), channel_id=1, source_target_pairs={{0,1},{1,2},{2,3},{3,4},{4,5},{5,6},{6,7},{7,8},{8,9},{9,10},{10,1... | collective-permute-start | bytes 393224 | tf_op jit(solution)/shard_map/ppermute | solution.py:77
  25.0 0.0 collective-permute-done.8
  25.0 4.8 %collective-permute-start.9 = (f32[2048,16]{0,1:T(8,128)S(1)}, f32[2048,16]{0,1:T(8,128)S(1)}, u32[]{:S(2)}, u32[]{:S(2)}) collective-permute-start(f32[2048,16]{0,1:T(8,128)S(1)} %collective-permute-done.8), channel_id=1, source_target_pairs={{0,15},{1,0},{2,1},{3,2},{4,3},{5,4},{6,5},{7,6},{8,7},{9,8},{10,9... | collective-permute-start | bytes 393224 | tf_op jit(solution)/shard_map/ppermute | solution.py:80
  29.8 0.2 collective-permute-done.2
  30.0 1.9 %collective-permute-start.3 = (f32[2048,16]{0,1:T(8,128)S(1)}, f32[2048,16]{0,1:T(8,128)S(1)}, u32[]{:S(2)}, u32[]{:S(2)}) collective-permute-start(f32[2048,16]{0,1:T(8,128)S(1)} %collective-permute-done.2), channel_id=1, source_target_pairs={{0,1},{1,2},{2,3},{3,4},{4,5},{5,6},{6,7},{7,8},{8,9},{9,10},{10,1... | collective-permute-start | bytes 393224 | tf_op jit(solution)/shard_map/ppermute | solution.py:77
  31.9 0.0 collective-permute-done.9
  31.9 4.8 %collective-permute-start.10 = (f32[2048,16]{0,1:T(8,128)S(1)}, f32[2048,16]{0,1:T(8,128)S(1)}, u32[]{:S(2)}, u32[]{:S(2)}) collective-permute-start(f32[2048,16]{0,1:T(8,128)S(1)} %collective-permute-done.9), channel_id=1, source_target_pairs={{0,15},{1,0},{2,1},{3,2},{4,3},{5,4},{6,5},{7,6},{8,7},{9,8},{10,9... | collective-permute-start | bytes 393224 | tf_op jit(solution)/shard_map/ppermute | solution.py:80
  36.7 0.2 collective-permute-done.3
  36.9 1.9 %collective-permute-start.4 = (f32[2048,16]{0,1:T(8,128)S(1)}, f32[2048,16]{0,1:T(8,128)S(1)}, u32[]{:S(2)}, u32[]{:S(2)}) collective-permute-start(f32[2048,16]{0,1:T(8,128)S(1)} %collective-permute-done.3), channel_id=1, source_target_pairs={{0,1},{1,2},{2,3},{3,4},{4,5},{5,6},{6,7},{7,8},{8,9},{9,10},{10,1... | collective-permute-start | bytes 393224 | tf_op jit(solution)/shard_map/ppermute | solution.py:77
  38.8 0.0 collective-permute-done.10
  38.8 4.8 %collective-permute-start.11 = (f32[2048,16]{0,1:T(8,128)S(1)}, f32[2048,16]{0,1:T(8,128)S(1)}, u32[]{:S(2)}, u32[]{:S(2)}) collective-permute-start(f32[2048,16]{0,1:T(8,128)S(1)} %collective-permute-done.10), channel_id=1, source_target_pairs={{0,15},{1,0},{2,1},{3,2},{4,3},{5,4},{6,5},{7,6},{8,7},{9,8},{10,9... | collective-permute-start | bytes 393224 | tf_op jit(solution)/shard_map/ppermute | solution.py:80
  43.6 0.2 collective-permute-done.4
  43.8 1.9 %collective-permute-start.5 = (f32[2048,16]{0,1:T(8,128)S(1)}, f32[2048,16]{0,1:T(8,128)S(1)}, u32[]{:S(2)}, u32[]{:S(2)}) collective-permute-start(f32[2048,16]{0,1:T(8,128)S(1)} %collective-permute-done.4), channel_id=1, source_target_pairs={{0,1},{1,2},{2,3},{3,4},{4,5},{5,6},{6,7},{7,8},{8,9},{9,10},{10,1... | collective-permute-start | bytes 393224 | tf_op jit(solution)/shard_map/ppermute | solution.py:77
  45.7 0.0 collective-permute-done.11
  45.7 4.8 %collective-permute-start.12 = (f32[2048,16]{0,1:T(8,128)S(1)}, f32[2048,16]{0,1:T(8,128)S(1)}, u32[]{:S(2)}, u32[]{:S(2)}) collective-permute-start(f32[2048,16]{0,1:T(8,128)S(1)} %collective-permute-done.11), channel_id=1, source_target_pairs={{0,15},{1,0},{2,1},{3,2},{4,3},{5,4},{6,5},{7,6},{8,7},{9,8},{10,9... | collective-permute-start | bytes 393224 | tf_op jit(solution)/shard_map/ppermute | solution.py:80
  50.5 0.2 collective-permute-done.5
  50.7 1.9 %collective-permute-start.6 = (f32[2048,16]{0,1:T(8,128)S(1)}, f32[2048,16]{0,1:T(8,128)S(1)}, u32[]{:S(2)}, u32[]{:S(2)}) collective-permute-start(f32[2048,16]{0,1:T(8,128)S(1)} %collective-permute-done.5), channel_id=1, source_target_pairs={{0,1},{1,2},{2,3},{3,4},{4,5},{5,6},{6,7},{7,8},{8,9},{9,10},{10,1... | collective-permute-start | bytes 393224 | tf_op jit(solution)/shard_map/ppermute | solution.py:77
  52.6 0.0 collective-permute-done.12
  52.6 4.8 %collective-permute-start.13 = (f32[2048,16]{0,1:T(8,128)S(1)}, f32[2048,16]{0,1:T(8,128)S(1)}, u32[]{:S(2)}, u32[]{:S(2)}) collective-permute-start(f32[2048,16]{0,1:T(8,128)S(1)} %collective-permute-done.12), channel_id=1, source_target_pairs={{0,15},{1,0},{2,1},{3,2},{4,3},{5,4},{6,5},{7,6},{8,7},{9,8},{10,9... | collective-permute-start | bytes 393224 | tf_op jit(solution)/shard_map/ppermute | solution.py:80
  57.4 1.0 collective-permute-done.6
  58.4 1.9 %collective-permute-start.7 = (f32[2048,16]{0,1:T(8,128)S(1)}, f32[2048,16]{0,1:T(8,128)S(1)}, u32[]{:S(2)}, u32[]{:S(2)}) collective-permute-start(f32[2048,16]{0,1:T(8,128)S(1)} %collective-permute-done.6), channel_id=1, source_target_pairs={{0,1},{1,2},{2,3},{3,4},{4,5},{5,6},{6,7},{7,8},{8,9},{9,10},{10,1... | collective-permute-start | bytes 393224 | tf_op jit(solution)/shard_map/ppermute | solution.py:77
  60.3 0.0 collective-permute-done.13
  60.4 5.0 %collective-permute-start.14 = (f32[2048,16]{0,1:T(8,128)S(1)}, f32[2048,16]{0,1:T(8,128)S(1)}, u32[]{:S(2)}, u32[]{:S(2)}) collective-permute-start(f32[2048,16]{0,1:T(8,128)S(1)} %collective-permute-done.13), channel_id=1, source_target_pairs={{0,15},{1,0},{2,1},{3,2},{4,3},{5,4},{6,5},{7,6},{8,7},{9,8},{10,9... | collective-permute-start | bytes 393224 | tf_op jit(solution)/shard_map/ppermute | solution.py:80
  65.4 1.1 collective-permute-done.7
  66.6 0.0 copy-done.2
  66.7 1.2 collective-permute-done.14
  67.9 0.0 copy-start
  67.9 1.9 %fusion.8 = f32[256,256]{0,1:T(8,128)S(1)} fusion(f32[2048,256]{0,1:T(8,128)S(1)} %constant_dynamic-update-slice_fusion), kind=kOutput, calls=%fused_computation.32 | convolution fusion | flops 1610612736 | bytes 2359296 | tf_op jit(solution)/shard_map/dot_general | solution.py:99
  69.8 0.0 copy-done
  69.8 3.6 %fusion.9 = f32[256,256]{0,1:T(8,128)S(1)} fusion(f32[2048,256]{0,1:T(8,128)S(1)} %constant_dynamic-update-slice_fusion, f32[2048,256]{1,0:T(8,128)S(1)} %copy-done), kind=kOutput, calls=%fused_computation.33 | convolution fusion | flops 1610612736 | bytes 4456448 | tf_op jit(solution)/shard_map/dot_general | solution.py:98
  73.4 0.2 copy.6
  73.6 27.8 %all_to_all.10 = f32[32,8,512]{2,1,0:T(8,128)S(1)} all-to-all(f32[32,8,512]{2,1,0:T(8,128)S(1)} %bitcast.11), channel_id=1, replica_groups=mesh['row'=32,'col'=16] {'row'}, dimensions={0} | all-to-all | bytes 1048576 | tf_op jit(solution)/shard_map/all_to_all | solution.py:89
  101.4 0.9 broadcast_in_dim.2
  102.3 3.9 %all-to-all-start.1 = ((f32[32,8,512]{2,1,0:T(8,128)}), f32[32,8,512]{2,1,0:T(8,128)S(1)}, u32[]{:S(2)}, u32[]{:S(2)}) async-start(f32[32,8,512]{2,1,0:T(8,128)} %broadcast_in_dim.2), calls=%async_computation.1 | async-start | bytes 1048576 | tf_op jit(solution)/shard_map/all_to_all | solution.py:91
  106.2 11.3 %all-to-all-done.1 = f32[32,8,512]{2,1,0:T(8,128)S(1)} async-done(((f32[32,8,512]{2,1,0:T(8,128)}), f32[32,8,512]{2,1,0:T(8,128)S(1)}, u32[]{:S(2)}, u32[]{:S(2)}) %all-to-all-start.1) | async-done | bytes 524320 | tf_op jit(solution)/shard_map/all_to_all | solution.py:91
  117.6 0.1 fusion
  117.7 0.9 fusion.3.gram_ref
  118.6 39.0 %shard_map.49 = (f32[256,256]{1,0:T(8,128)}, f32[256,256]{1,0:T(8,128)}) custom-call(f32[256,256]{1,0:T(8,128)} %fusion.3.gram_ref), custom_call_target="tpu_custom_call" | custom-call | tf_op jit(solution)/shard_map/pallas_call | solution.py:64
  157.6 1.3 fusion.4
  158.9 0.0 copy-start.1
  158.9 1.6 fusion.10
  160.6 1.0 dynamic-slice_multiply_fusion
  161.6 0.7 copy.7
  162.3 6.4 %convolution_subtract_fusion = f32[2048,256]{1,0:T(8,128)} fusion(f32[2048,256]{1,0:T(8,128)} %param.3, f32[2048,256]{0,1:T(8,128)S(1)} %constant_dynamic-update-slice_fusion, s32[]{:T(128)S(6)} %select_n.36, f32[256,256]{1,0:T(8,128)S(1)} %fusion.10), kind=kOutput, calls=%fused_computation | convolution fusion | flops 1611202560 | bytes 6553604 | tf_op jit(solution)/shard_map/dot_general | solution.py:106
  168.6 0.0 copy-done.1
  (19 shorter events, 0.3 us)
Async XLA Ops:
  0.6 66.0 %copy-start.2 = (f32[2048,16]{0,1:T(8,128)S(1)}, f32[2048,16]{0,1:T(8,128)}, u32[]{:S(2)}) copy-start(f32[2048,16]{0,1:T(8,128)} %param.2) | copy-start | bytes 393220
  0.6 15.5 %collective-permute-start = (f32[2048,16]{0,1:T(8,128)}, f32[2048,16]{0,1:T(8,128)S(1)}, u32[]{:S(2)}, u32[]{:S(2)}) collective-permute-start(f32[2048,16]{0,1:T(8,128)} %param.2), channel_id=1, source_target_pairs={{0,1},{1,2},{2,3},{3,4},{4,5},{5,6},{6,7},{7,8},{8,9},{9,10},{10,1... | collective-permute-start | bytes 393224 | tf_op jit(solution)/shard_map/ppermute | solution.py:77
  16.1 6.9 %collective-permute-start.1 = (f32[2048,16]{0,1:T(8,128)S(1)}, f32[2048,16]{0,1:T(8,128)S(1)}, u32[]{:S(2)}, u32[]{:S(2)}) collective-permute-start(f32[2048,16]{0,1:T(8,128)S(1)} %collective-permute-done), channel_id=1, source_target_pairs={{0,1},{1,2},{2,3},{3,4},{4,5},{5,6},{6,7},{7,8},{8,9},{9,10},{10,1... | collective-permute-start | bytes 393224 | tf_op jit(solution)/shard_map/ppermute | solution.py:77
  18.1 6.9 %collective-permute-start.8 = (f32[2048,16]{0,1:T(8,128)}, f32[2048,16]{0,1:T(8,128)S(1)}, u32[]{:S(2)}, u32[]{:S(2)}) collective-permute-start(f32[2048,16]{0,1:T(8,128)} %param.2), channel_id=1, source_target_pairs={{0,15},{1,0},{2,1},{3,2},{4,3},{5,4},{6,5},{7,6},{8,7},{9,8},{10,9... | collective-permute-start | bytes 393224 | tf_op jit(solution)/shard_map/ppermute | solution.py:80
  23.1 6.9 %collective-permute-start.2 = (f32[2048,16]{0,1:T(8,128)S(1)}, f32[2048,16]{0,1:T(8,128)S(1)}, u32[]{:S(2)}, u32[]{:S(2)}) collective-permute-start(f32[2048,16]{0,1:T(8,128)S(1)} %collective-permute-done.1), channel_id=1, source_target_pairs={{0,1},{1,2},{2,3},{3,4},{4,5},{5,6},{6,7},{7,8},{8,9},{9,10},{10,1... | collective-permute-start | bytes 393224 | tf_op jit(solution)/shard_map/ppermute | solution.py:77
  25.0 6.9 %collective-permute-start.9 = (f32[2048,16]{0,1:T(8,128)S(1)}, f32[2048,16]{0,1:T(8,128)S(1)}, u32[]{:S(2)}, u32[]{:S(2)}) collective-permute-start(f32[2048,16]{0,1:T(8,128)S(1)} %collective-permute-done.8), channel_id=1, source_target_pairs={{0,15},{1,0},{2,1},{3,2},{4,3},{5,4},{6,5},{7,6},{8,7},{9,8},{10,9... | collective-permute-start | bytes 393224 | tf_op jit(solution)/shard_map/ppermute | solution.py:80
  30.0 6.9 %collective-permute-start.3 = (f32[2048,16]{0,1:T(8,128)S(1)}, f32[2048,16]{0,1:T(8,128)S(1)}, u32[]{:S(2)}, u32[]{:S(2)}) collective-permute-start(f32[2048,16]{0,1:T(8,128)S(1)} %collective-permute-done.2), channel_id=1, source_target_pairs={{0,1},{1,2},{2,3},{3,4},{4,5},{5,6},{6,7},{7,8},{8,9},{9,10},{10,1... | collective-permute-start | bytes 393224 | tf_op jit(solution)/shard_map/ppermute | solution.py:77
  31.9 6.9 %collective-permute-start.10 = (f32[2048,16]{0,1:T(8,128)S(1)}, f32[2048,16]{0,1:T(8,128)S(1)}, u32[]{:S(2)}, u32[]{:S(2)}) collective-permute-start(f32[2048,16]{0,1:T(8,128)S(1)} %collective-permute-done.9), channel_id=1, source_target_pairs={{0,15},{1,0},{2,1},{3,2},{4,3},{5,4},{6,5},{7,6},{8,7},{9,8},{10,9... | collective-permute-start | bytes 393224 | tf_op jit(solution)/shard_map/ppermute | solution.py:80
  36.9 6.9 %collective-permute-start.4 = (f32[2048,16]{0,1:T(8,128)S(1)}, f32[2048,16]{0,1:T(8,128)S(1)}, u32[]{:S(2)}, u32[]{:S(2)}) collective-permute-start(f32[2048,16]{0,1:T(8,128)S(1)} %collective-permute-done.3), channel_id=1, source_target_pairs={{0,1},{1,2},{2,3},{3,4},{4,5},{5,6},{6,7},{7,8},{8,9},{9,10},{10,1... | collective-permute-start | bytes 393224 | tf_op jit(solution)/shard_map/ppermute | solution.py:77
  38.8 6.9 %collective-permute-start.11 = (f32[2048,16]{0,1:T(8,128)S(1)}, f32[2048,16]{0,1:T(8,128)S(1)}, u32[]{:S(2)}, u32[]{:S(2)}) collective-permute-start(f32[2048,16]{0,1:T(8,128)S(1)} %collective-permute-done.10), channel_id=1, source_target_pairs={{0,15},{1,0},{2,1},{3,2},{4,3},{5,4},{6,5},{7,6},{8,7},{9,8},{10,9... | collective-permute-start | bytes 393224 | tf_op jit(solution)/shard_map/ppermute | solution.py:80
  43.8 6.9 %collective-permute-start.5 = (f32[2048,16]{0,1:T(8,128)S(1)}, f32[2048,16]{0,1:T(8,128)S(1)}, u32[]{:S(2)}, u32[]{:S(2)}) collective-permute-start(f32[2048,16]{0,1:T(8,128)S(1)} %collective-permute-done.4), channel_id=1, source_target_pairs={{0,1},{1,2},{2,3},{3,4},{4,5},{5,6},{6,7},{7,8},{8,9},{9,10},{10,1... | collective-permute-start | bytes 393224 | tf_op jit(solution)/shard_map/ppermute | solution.py:77
  45.7 6.9 %collective-permute-start.12 = (f32[2048,16]{0,1:T(8,128)S(1)}, f32[2048,16]{0,1:T(8,128)S(1)}, u32[]{:S(2)}, u32[]{:S(2)}) collective-permute-start(f32[2048,16]{0,1:T(8,128)S(1)} %collective-permute-done.11), channel_id=1, source_target_pairs={{0,15},{1,0},{2,1},{3,2},{4,3},{5,4},{6,5},{7,6},{8,7},{9,8},{10,9... | collective-permute-start | bytes 393224 | tf_op jit(solution)/shard_map/ppermute | solution.py:80
  50.7 7.7 %collective-permute-start.6 = (f32[2048,16]{0,1:T(8,128)S(1)}, f32[2048,16]{0,1:T(8,128)S(1)}, u32[]{:S(2)}, u32[]{:S(2)}) collective-permute-start(f32[2048,16]{0,1:T(8,128)S(1)} %collective-permute-done.5), channel_id=1, source_target_pairs={{0,1},{1,2},{2,3},{3,4},{4,5},{5,6},{6,7},{7,8},{8,9},{9,10},{10,1... | collective-permute-start | bytes 393224 | tf_op jit(solution)/shard_map/ppermute | solution.py:77
  52.6 7.7 %collective-permute-start.13 = (f32[2048,16]{0,1:T(8,128)S(1)}, f32[2048,16]{0,1:T(8,128)S(1)}, u32[]{:S(2)}, u32[]{:S(2)}) collective-permute-start(f32[2048,16]{0,1:T(8,128)S(1)} %collective-permute-done.12), channel_id=1, source_target_pairs={{0,15},{1,0},{2,1},{3,2},{4,3},{5,4},{6,5},{7,6},{8,7},{9,8},{10,9... | collective-permute-start | bytes 393224 | tf_op jit(solution)/shard_map/ppermute | solution.py:80
  58.4 8.1 %collective-permute-start.7 = (f32[2048,16]{0,1:T(8,128)S(1)}, f32[2048,16]{0,1:T(8,128)S(1)}, u32[]{:S(2)}, u32[]{:S(2)}) collective-permute-start(f32[2048,16]{0,1:T(8,128)S(1)} %collective-permute-done.6), channel_id=1, source_target_pairs={{0,1},{1,2},{2,3},{3,4},{4,5},{5,6},{6,7},{7,8},{8,9},{9,10},{10,1... | collective-permute-start | bytes 393224 | tf_op jit(solution)/shard_map/ppermute | solution.py:77
  60.4 7.5 %collective-permute-start.14 = (f32[2048,16]{0,1:T(8,128)S(1)}, f32[2048,16]{0,1:T(8,128)S(1)}, u32[]{:S(2)}, u32[]{:S(2)}) collective-permute-start(f32[2048,16]{0,1:T(8,128)S(1)} %collective-permute-done.13), channel_id=1, source_target_pairs={{0,15},{1,0},{2,1},{3,2},{4,3},{5,4},{6,5},{7,6},{8,7},{9,8},{10,9... | collective-permute-start | bytes 393224 | tf_op jit(solution)/shard_map/ppermute | solution.py:80
  67.9 1.9 %copy-start = (f32[2048,256]{1,0:T(8,128)S(1)}, f32[2048,256]{1,0:T(8,128)}, u32[]{:S(2)}) copy-start(f32[2048,256]{1,0:T(8,128)} %param.3) | copy-start | bytes 6291460
  102.3 15.3 %all-to-all-start.1 = ((f32[32,8,512]{2,1,0:T(8,128)}), f32[32,8,512]{2,1,0:T(8,128)S(1)}, u32[]{:S(2)}, u32[]{:S(2)}) async-start(f32[32,8,512]{2,1,0:T(8,128)} %broadcast_in_dim.2), calls=%async_computation.1 | async-start | bytes 1048576 | tf_op jit(solution)/shard_map/all_to_all | solution.py:91
  158.9 9.7 %copy-start.1 = (f32[256,256]{1,0:T(8,128)}, f32[256,256]{1,0:T(8,128)S(1)}, u32[]{:S(2)}) copy-start(f32[256,256]{1,0:T(8,128)S(1)} %fusion.4) | copy-start | bytes 786436

commit v10 on v8

--- a/solution.py
+++ b/solution.py
@@ -28,14 +28,27 @@
 
         def block(b, strip):
             base = pl.multiple_of(b * 8, 8)
-            for t in range(8):
-                col = pltpu.roll(strip[:, :128], (128 - (base + t - lo)) % 128, 1)[:, 0:1]
-                diag = col[t:t + 1, :]
+            cols = [jnp.sum(jnp.where(lane[:, :128] == base + k, strip[:, :128], 0.0),
+                            axis=1, keepdims=True) for k in range(8)]
+            factor_cols, inverse_diag = [], []
+            for k in range(8):
+                diag = cols[k][k:k + 1, :]
                 guess = lax.rsqrt(diag)
                 scale = guess * (1.5 - 0.5 * diag * guess * guess)
-                pivot = strip[t:t + 1, :] * scale
-                mult = jnp.where(sub_col > t, col * scale, 0.0)
-                strip = jnp.where(sub == t, pivot, strip - mult * pivot)
+                column = jnp.where(sub_col >= k, cols[k] * scale, 0.0)
+                factor_cols.append(column)
+                inverse_diag.append(scale)
+                for m in range(k + 1, 8):
+                    cols[m] = cols[m] - column * column[m:m + 1, :]
+            done_rows = []
+            for k in range(8):
+                row = strip[k:k + 1, :]
+                for m in range(k):
+                    row = row - factor_cols[m][k:k + 1, :] * done_rows[m]
+                done_rows.append(row * inverse_diag[k])
+            strip = done_rows[0] + jnp.zeros_like(strip)
+            for k in range(1, 8):
+                strip = jnp.where(sub == k, done_rows[k], strip)
             work_ref[pl.ds(base, 8), lo:hi] = strip
             left = jnp.where(lane[:, :key] > base + 7, strip[:, :key], 0.0)
             left_ref[lo:n, :] = jnp.transpose(left)

time: 185 us -> 152 us (0.82)
  Pallas kernels: 54.2 us -> 22 us
    pallas_call x1, Pallas kernels: 54.2 us -> 22 us  [factor(): pl.pallas_call(factor_kernel, out_shape=(jax.ShapeDtypeStruct((n, n), jnp...]
where the time goes in v10:
time: 152 us
  starting transfers between devices  55.2 us (36%)
  blocking collectives  27.8 us (18%)
  waiting for transfers between devices  26.8 us (18%)
  Pallas kernels  22 us (14%)
  matrix products  14.7 us (10%)
  other arithmetic  2.13 us (1%)
  local copies, waits for them, and re-layouts  1.95 us (1%)
    ppermute x7, starting transfers between devices, col_gather(): behind = lax.ppermute(behind, 'col', [(i, (i - 1) % n) for i in range(n)])  33.4 us
    all_to_all x1, blocking collectives, row_sum(): mine = lax.all_to_all(parts, 'row', 0, 0, tiled=False).sum(0)  27.8 us
    pallas_call x1, Pallas kernels, factor(): pl.pallas_call(factor_kernel, out_shape=(jax.ShapeDtypeStruct((n, n), jnp...  22 us
    ppermute x8, starting transfers between devices, col_gather(): ahead = lax.ppermute(ahead, 'col', [(i, (i + 1) % n) for i in range(n)])  17.9 us
    ppermute x8, waiting for transfers between devices, col_gather(): ahead = lax.ppermute(ahead, 'col', [(i, (i + 1) % n) for i in range(n)])  14.3 us
    all_to_all x1, waiting for transfers between devices, row_sum(): return lax.all_to_all(copies, 'row', 0, 0, tiled=False).reshape(rows, cols)  11.3 us
    dot_general x1, matrix products, per_device(): jnp.dot(gathered, jnp.roll(coefficients, -shift, axis=0), precision=highest)  6.36 us
    all_to_all x1, starting transfers between devices, row_sum(): return lax.all_to_all(copies, 'row', 0, 0, tiled=False).reshape(rows, cols)  3.86 us
  transfers between devices with their start and end apart: 16, of which 10 were waited for; matrix products, arithmetic and copies ran while one was open for 0% of the time, Pallas kernels for 0%

profile of v10, /device:TPU:1, one launch (start us, length us, event | category | flops | bytes accessed | tf_op | source)
XLA Modules:
  0.0 151.7 jit_solution(5286907061476340555)
XLA Ops:
  0.6 0.0 copy-start.2
  0.6 4.5 %collective-permute-start = (f32[2048,16]{0,1:T(8,128)}, f32[2048,16]{0,1:T(8,128)S(1)}, u32[]{:S(2)}, u32[]{:S(2)}) collective-permute-start(f32[2048,16]{0,1:T(8,128)} %param.2), channel_id=1, source_target_pairs={{0,1},{1,2},{2,3},{3,4},{4,5},{5,6},{6,7},{7,8},{8,9},{9,10},{10,1... | collective-permute-start | bytes 393224 | tf_op jit(solution)/shard_map/ppermute | solution.py:89
  5.2 11.0 %collective-permute-done = f32[2048,16]{0,1:T(8,128)S(1)} collective-permute-done((f32[2048,16]{0,1:T(8,128)}, f32[2048,16]{0,1:T(8,128)S(1)}, u32[]{:S(2)}, u32[]{:S(2)}) %collective-permute-start) | collective-permute-done | bytes 131104 | tf_op jit(solution)/shard_map/ppermute | solution.py:89
  16.1 1.9 %collective-permute-start.1 = (f32[2048,16]{0,1:T(8,128)S(1)}, f32[2048,16]{0,1:T(8,128)S(1)}, u32[]{:S(2)}, u32[]{:S(2)}) collective-permute-start(f32[2048,16]{0,1:T(8,128)S(1)} %collective-permute-done), channel_id=1, source_target_pairs={{0,1},{1,2},{2,3},{3,4},{4,5},{5,6},{6,7},{7,8},{8,9},{9,10},{10,1... | collective-permute-start | bytes 393224 | tf_op jit(solution)/shard_map/ppermute | solution.py:89
  18.1 4.6 %collective-permute-start.8 = (f32[2048,16]{0,1:T(8,128)}, f32[2048,16]{0,1:T(8,128)S(1)}, u32[]{:S(2)}, u32[]{:S(2)}) collective-permute-start(f32[2048,16]{0,1:T(8,128)} %param.2), channel_id=1, source_target_pairs={{0,15},{1,0},{2,1},{3,2},{4,3},{5,4},{6,5},{7,6},{8,7},{9,8},{10,9... | collective-permute-start | bytes 393224 | tf_op jit(solution)/shard_map/ppermute | solution.py:92
  22.6 0.4 collective-permute-done.1
  23.1 1.9 %collective-permute-start.2 = (f32[2048,16]{0,1:T(8,128)S(1)}, f32[2048,16]{0,1:T(8,128)S(1)}, u32[]{:S(2)}, u32[]{:S(2)}) collective-permute-start(f32[2048,16]{0,1:T(8,128)S(1)} %collective-permute-done.1), channel_id=1, source_target_pairs={{0,1},{1,2},{2,3},{3,4},{4,5},{5,6},{6,7},{7,8},{8,9},{9,10},{10,1... | collective-permute-start | bytes 393224 | tf_op jit(solution)/shard_map/ppermute | solution.py:89
  25.0 0.0 collective-permute-done.8
  25.0 4.8 %collective-permute-start.9 = (f32[2048,16]{0,1:T(8,128)S(1)}, f32[2048,16]{0,1:T(8,128)S(1)}, u32[]{:S(2)}, u32[]{:S(2)}) collective-permute-start(f32[2048,16]{0,1:T(8,128)S(1)} %collective-permute-done.8), channel_id=1, source_target_pairs={{0,15},{1,0},{2,1},{3,2},{4,3},{5,4},{6,5},{7,6},{8,7},{9,8},{10,9... | collective-permute-start | bytes 393224 | tf_op jit(solution)/shard_map/ppermute | solution.py:92
  29.8 0.2 collective-permute-done.2
  30.0 1.9 %collective-permute-start.3 = (f32[2048,16]{0,1:T(8,128)S(1)}, f32[2048,16]{0,1:T(8,128)S(1)}, u32[]{:S(2)}, u32[]{:S(2)}) collective-permute-start(f32[2048,16]{0,1:T(8,128)S(1)} %collective-permute-done.2), channel_id=1, source_target_pairs={{0,1},{1,2},{2,3},{3,4},{4,5},{5,6},{6,7},{7,8},{8,9},{9,10},{10,1... | collective-permute-start | bytes 393224 | tf_op jit(solution)/shard_map/ppermute | solution.py:89
  31.9 0.0 collective-permute-done.9
  31.9 4.8 %collective-permute-start.10 = (f32[2048,16]{0,1:T(8,128)S(1)}, f32[2048,16]{0,1:T(8,128)S(1)}, u32[]{:S(2)}, u32[]{:S(2)}) collective-permute-start(f32[2048,16]{0,1:T(8,128)S(1)} %collective-permute-done.9), channel_id=1, source_target_pairs={{0,15},{1,0},{2,1},{3,2},{4,3},{5,4},{6,5},{7,6},{8,7},{9,8},{10,9... | collective-permute-start | bytes 393224 | tf_op jit(solution)/shard_map/ppermute | solution.py:92
  36.7 0.2 collective-permute-done.3
  36.9 1.9 %collective-permute-start.4 = (f32[2048,16]{0,1:T(8,128)S(1)}, f32[2048,16]{0,1:T(8,128)S(1)}, u32[]{:S(2)}, u32[]{:S(2)}) collective-permute-start(f32[2048,16]{0,1:T(8,128)S(1)} %collective-permute-done.3), channel_id=1, source_target_pairs={{0,1},{1,2},{2,3},{3,4},{4,5},{5,6},{6,7},{7,8},{8,9},{9,10},{10,1... | collective-permute-start | bytes 393224 | tf_op jit(solution)/shard_map/ppermute | solution.py:89
  38.8 0.0 collective-permute-done.10
  38.8 4.8 %collective-permute-start.11 = (f32[2048,16]{0,1:T(8,128)S(1)}, f32[2048,16]{0,1:T(8,128)S(1)}, u32[]{:S(2)}, u32[]{:S(2)}) collective-permute-start(f32[2048,16]{0,1:T(8,128)S(1)} %collective-permute-done.10), channel_id=1, source_target_pairs={{0,15},{1,0},{2,1},{3,2},{4,3},{5,4},{6,5},{7,6},{8,7},{9,8},{10,9... | collective-permute-start | bytes 393224 | tf_op jit(solution)/shard_map/ppermute | solution.py:92
  43.6 0.2 collective-permute-done.4
  43.8 1.9 %collective-permute-start.5 = (f32[2048,16]{0,1:T(8,128)S(1)}, f32[2048,16]{0,1:T(8,128)S(1)}, u32[]{:S(2)}, u32[]{:S(2)}) collective-permute-start(f32[2048,16]{0,1:T(8,128)S(1)} %collective-permute-done.4), channel_id=1, source_target_pairs={{0,1},{1,2},{2,3},{3,4},{4,5},{5,6},{6,7},{7,8},{8,9},{9,10},{10,1... | collective-permute-start | bytes 393224 | tf_op jit(solution)/shard_map/ppermute | solution.py:89
  45.7 0.0 collective-permute-done.11
  45.7 4.8 %collective-permute-start.12 = (f32[2048,16]{0,1:T(8,128)S(1)}, f32[2048,16]{0,1:T(8,128)S(1)}, u32[]{:S(2)}, u32[]{:S(2)}) collective-permute-start(f32[2048,16]{0,1:T(8,128)S(1)} %collective-permute-done.11), channel_id=1, source_target_pairs={{0,15},{1,0},{2,1},{3,2},{4,3},{5,4},{6,5},{7,6},{8,7},{9,8},{10,9... | collective-permute-start | bytes 393224 | tf_op jit(solution)/shard_map/ppermute | solution.py:92
  50.5 0.2 collective-permute-done.5
  50.7 1.9 %collective-permute-start.6 = (f32[2048,16]{0,1:T(8,128)S(1)}, f32[2048,16]{0,1:T(8,128)S(1)}, u32[]{:S(2)}, u32[]{:S(2)}) collective-permute-start(f32[2048,16]{0,1:T(8,128)S(1)} %collective-permute-done.5), channel_id=1, source_target_pairs={{0,1},{1,2},{2,3},{3,4},{4,5},{5,6},{6,7},{7,8},{8,9},{9,10},{10,1... | collective-permute-start | bytes 393224 | tf_op jit(solution)/shard_map/ppermute | solution.py:89
  52.6 0.0 collective-permute-done.12
  52.6 4.8 %collective-permute-start.13 = (f32[2048,16]{0,1:T(8,128)S(1)}, f32[2048,16]{0,1:T(8,128)S(1)}, u32[]{:S(2)}, u32[]{:S(2)}) collective-permute-start(f32[2048,16]{0,1:T(8,128)S(1)} %collective-permute-done.12), channel_id=1, source_target_pairs={{0,15},{1,0},{2,1},{3,2},{4,3},{5,4},{6,5},{7,6},{8,7},{9,8},{10,9... | collective-permute-start | bytes 393224 | tf_op jit(solution)/shard_map/ppermute | solution.py:92
  57.4 1.0 collective-permute-done.6
  58.4 1.9 %collective-permute-start.7 = (f32[2048,16]{0,1:T(8,128)S(1)}, f32[2048,16]{0,1:T(8,128)S(1)}, u32[]{:S(2)}, u32[]{:S(2)}) collective-permute-start(f32[2048,16]{0,1:T(8,128)S(1)} %collective-permute-done.6), channel_id=1, source_target_pairs={{0,1},{1,2},{2,3},{3,4},{4,5},{5,6},{6,7},{7,8},{8,9},{9,10},{10,1... | collective-permute-start | bytes 393224 | tf_op jit(solution)/shard_map/ppermute | solution.py:89
  60.3 0.0 collective-permute-done.13
  60.4 5.0 %collective-permute-start.14 = (f32[2048,16]{0,1:T(8,128)S(1)}, f32[2048,16]{0,1:T(8,128)S(1)}, u32[]{:S(2)}, u32[]{:S(2)}) collective-permute-start(f32[2048,16]{0,1:T(8,128)S(1)} %collective-permute-done.13), channel_id=1, source_target_pairs={{0,15},{1,0},{2,1},{3,2},{4,3},{5,4},{6,5},{7,6},{8,7},{9,8},{10,9... | collective-permute-start | bytes 393224 | tf_op jit(solution)/shard_map/ppermute | solution.py:92
  65.4 1.1 collective-permute-done.7
  66.6 0.0 copy-done.2
  66.7 1.2 collective-permute-done.14
  67.9 0.0 copy-start
  67.9 1.9 %fusion.8 = f32[256,256]{0,1:T(8,128)S(1)} fusion(f32[2048,256]{0,1:T(8,128)S(1)} %constant_dynamic-update-slice_fusion), kind=kOutput, calls=%fused_computation.32 | convolution fusion | flops 1610612736 | bytes 2359296 | tf_op jit(solution)/shard_map/dot_general | solution.py:111
  69.8 0.0 copy-done
  69.8 3.6 %fusion.9 = f32[256,256]{0,1:T(8,128)S(1)} fusion(f32[2048,256]{0,1:T(8,128)S(1)} %constant_dynamic-update-slice_fusion, f32[2048,256]{1,0:T(8,128)S(1)} %copy-done), kind=kOutput, calls=%fused_computation.33 | convolution fusion | flops 1610612736 | bytes 4456448 | tf_op jit(solution)/shard_map/dot_general | solution.py:110
  73.4 0.2 copy.6
  73.6 27.8 %all_to_all.10 = f32[32,8,512]{2,1,0:T(8,128)S(1)} all-to-all(f32[32,8,512]{2,1,0:T(8,128)S(1)} %bitcast.11), channel_id=1, replica_groups=mesh['row'=32,'col'=16] {'row'}, dimensions={0} | all-to-all | bytes 1048576 | tf_op jit(solution)/shard_map/all_to_all | solution.py:101
  101.4 0.9 broadcast_in_dim.2
  102.3 3.9 %all-to-all-start.1 = ((f32[32,8,512]{2,1,0:T(8,128)}), f32[32,8,512]{2,1,0:T(8,128)S(1)}, u32[]{:S(2)}, u32[]{:S(2)}) async-start(f32[32,8,512]{2,1,0:T(8,128)} %broadcast_in_dim.2), calls=%async_computation.1 | async-start | bytes 1048576 | tf_op jit(solution)/shard_map/all_to_all | solution.py:103
  106.2 11.3 %all-to-all-done.1 = f32[32,8,512]{2,1,0:T(8,128)S(1)} async-done(((f32[32,8,512]{2,1,0:T(8,128)}), f32[32,8,512]{2,1,0:T(8,128)S(1)}, u32[]{:S(2)}, u32[]{:S(2)}) %all-to-all-start.1) | async-done | bytes 524320 | tf_op jit(solution)/shard_map/all_to_all | solution.py:103
  117.6 0.1 fusion
  117.7 0.9 fusion.3.gram_ref
  118.6 22.0 %shard_map.49 = (f32[256,256]{1,0:T(8,128)}, f32[256,256]{1,0:T(8,128)}) custom-call(f32[256,256]{1,0:T(8,128)} %fusion.3.gram_ref), custom_call_target="tpu_custom_call" | custom-call | tf_op jit(solution)/shard_map/pallas_call | solution.py:76
  140.6 1.3 fusion.4
  142.0 0.0 copy-start.1
  142.0 1.6 %fusion.10 = f32[256,256]{1,0:T(8,128)S(1)} fusion(f32[256,256]{1,0:T(8,128)} %get-tuple-element.6, f32[256,256]{1,0:T(8,128)S(1)} %fusion.4), kind=kOutput, calls=%fused_computation.34 | convolution fusion | flops 201326592 | bytes 786432 | tf_op jit(solution)/shard_map/dot_general | solution.py:117
  143.6 1.0 dynamic-slice_multiply_fusion
  144.6 0.7 copy.7
  145.3 6.4 %convolution_subtract_fusion = f32[2048,256]{1,0:T(8,128)} fusion(f32[2048,256]{1,0:T(8,128)} %param.3, f32[2048,256]{0,1:T(8,128)S(1)} %constant_dynamic-update-slice_fusion, s32[]{:T(128)S(6)} %select_n.36, f32[256,256]{1,0:T(8,128)S(1)} %fusion.10), kind=kOutput, calls=%fused_computation | convolution fusion | flops 1611202560 | bytes 6553604 | tf_op jit(solution)/shard_map/dot_general | solution.py:118
  151.7 0.0 copy-done.1
  (19 shorter events, 0.3 us)
Async XLA Ops:
  0.6 66.0 %copy-start.2 = (f32[2048,16]{0,1:T(8,128)S(1)}, f32[2048,16]{0,1:T(8,128)}, u32[]{:S(2)}) copy-start(f32[2048,16]{0,1:T(8,128)} %param.2) | copy-start | bytes 393220
  0.6 15.5 %collective-permute-start = (f32[2048,16]{0,1:T(8,128)}, f32[2048,16]{0,1:T(8,128)S(1)}, u32[]{:S(2)}, u32[]{:S(2)}) collective-permute-start(f32[2048,16]{0,1:T(8,128)} %param.2), channel_id=1, source_target_pairs={{0,1},{1,2},{2,3},{3,4},{4,5},{5,6},{6,7},{7,8},{8,9},{9,10},{10,1... | collective-permute-start | bytes 393224 | tf_op jit(solution)/shard_map/ppermute | solution.py:89
  16.1 6.9 %collective-permute-start.1 = (f32[2048,16]{0,1:T(8,128)S(1)}, f32[2048,16]{0,1:T(8,128)S(1)}, u32[]{:S(2)}, u32[]{:S(2)}) collective-permute-start(f32[2048,16]{0,1:T(8,128)S(1)} %collective-permute-done), channel_id=1, source_target_pairs={{0,1},{1,2},{2,3},{3,4},{4,5},{5,6},{6,7},{7,8},{8,9},{9,10},{10,1... | collective-permute-start | bytes 393224 | tf_op jit(solution)/shard_map/ppermute | solution.py:89
  18.1 6.9 %collective-permute-start.8 = (f32[2048,16]{0,1:T(8,128)}, f32[2048,16]{0,1:T(8,128)S(1)}, u32[]{:S(2)}, u32[]{:S(2)}) collective-permute-start(f32[2048,16]{0,1:T(8,128)} %param.2), channel_id=1, source_target_pairs={{0,15},{1,0},{2,1},{3,2},{4,3},{5,4},{6,5},{7,6},{8,7},{9,8},{10,9... | collective-permute-start | bytes 393224 | tf_op jit(solution)/shard_map/ppermute | solution.py:92
  23.1 6.9 %collective-permute-start.2 = (f32[2048,16]{0,1:T(8,128)S(1)}, f32[2048,16]{0,1:T(8,128)S(1)}, u32[]{:S(2)}, u32[]{:S(2)}) collective-permute-start(f32[2048,16]{0,1:T(8,128)S(1)} %collective-permute-done.1), channel_id=1, source_target_pairs={{0,1},{1,2},{2,3},{3,4},{4,5},{5,6},{6,7},{7,8},{8,9},{9,10},{10,1... | collective-permute-start | bytes 393224 | tf_op jit(solution)/shard_map/ppermute | solution.py:89
  25.0 6.9 %collective-permute-start.9 = (f32[2048,16]{0,1:T(8,128)S(1)}, f32[2048,16]{0,1:T(8,128)S(1)}, u32[]{:S(2)}, u32[]{:S(2)}) collective-permute-start(f32[2048,16]{0,1:T(8,128)S(1)} %collective-permute-done.8), channel_id=1, source_target_pairs={{0,15},{1,0},{2,1},{3,2},{4,3},{5,4},{6,5},{7,6},{8,7},{9,8},{10,9... | collective-permute-start | bytes 393224 | tf_op jit(solution)/shard_map/ppermute | solution.py:92
  30.0 6.9 %collective-permute-start.3 = (f32[2048,16]{0,1:T(8,128)S(1)}, f32[2048,16]{0,1:T(8,128)S(1)}, u32[]{:S(2)}, u32[]{:S(2)}) collective-permute-start(f32[2048,16]{0,1:T(8,128)S(1)} %collective-permute-done.2), channel_id=1, source_target_pairs={{0,1},{1,2},{2,3},{3,4},{4,5},{5,6},{6,7},{7,8},{8,9},{9,10},{10,1... | collective-permute-start | bytes 393224 | tf_op jit(solution)/shard_map/ppermute | solution.py:89
  31.9 6.9 %collective-permute-start.10 = (f32[2048,16]{0,1:T(8,128)S(1)}, f32[2048,16]{0,1:T(8,128)S(1)}, u32[]{:S(2)}, u32[]{:S(2)}) collective-permute-start(f32[2048,16]{0,1:T(8,128)S(1)} %collective-permute-done.9), channel_id=1, source_target_pairs={{0,15},{1,0},{2,1},{3,2},{4,3},{5,4},{6,5},{7,6},{8,7},{9,8},{10,9... | collective-permute-start | bytes 393224 | tf_op jit(solution)/shard_map/ppermute | solution.py:92
  36.9 6.9 %collective-permute-start.4 = (f32[2048,16]{0,1:T(8,128)S(1)}, f32[2048,16]{0,1:T(8,128)S(1)}, u32[]{:S(2)}, u32[]{:S(2)}) collective-permute-start(f32[2048,16]{0,1:T(8,128)S(1)} %collective-permute-done.3), channel_id=1, source_target_pairs={{0,1},{1,2},{2,3},{3,4},{4,5},{5,6},{6,7},{7,8},{8,9},{9,10},{10,1... | collective-permute-start | bytes 393224 | tf_op jit(solution)/shard_map/ppermute | solution.py:89
  38.8 6.9 %collective-permute-start.11 = (f32[2048,16]{0,1:T(8,128)S(1)}, f32[2048,16]{0,1:T(8,128)S(1)}, u32[]{:S(2)}, u32[]{:S(2)}) collective-permute-start(f32[2048,16]{0,1:T(8,128)S(1)} %collective-permute-done.10), channel_id=1, source_target_pairs={{0,15},{1,0},{2,1},{3,2},{4,3},{5,4},{6,5},{7,6},{8,7},{9,8},{10,9... | collective-permute-start | bytes 393224 | tf_op jit(solution)/shard_map/ppermute | solution.py:92
  43.8 6.9 %collective-permute-start.5 = (f32[2048,16]{0,1:T(8,128)S(1)}, f32[2048,16]{0,1:T(8,128)S(1)}, u32[]{:S(2)}, u32[]{:S(2)}) collective-permute-start(f32[2048,16]{0,1:T(8,128)S(1)} %collective-permute-done.4), channel_id=1, source_target_pairs={{0,1},{1,2},{2,3},{3,4},{4,5},{5,6},{6,7},{7,8},{8,9},{9,10},{10,1... | collective-permute-start | bytes 393224 | tf_op jit(solution)/shard_map/ppermute | solution.py:89
  45.7 6.9 %collective-permute-start.12 = (f32[2048,16]{0,1:T(8,128)S(1)}, f32[2048,16]{0,1:T(8,128)S(1)}, u32[]{:S(2)}, u32[]{:S(2)}) collective-permute-start(f32[2048,16]{0,1:T(8,128)S(1)} %collective-permute-done.11), channel_id=1, source_target_pairs={{0,15},{1,0},{2,1},{3,2},{4,3},{5,4},{6,5},{7,6},{8,7},{9,8},{10,9... | collective-permute-start | bytes 393224 | tf_op jit(solution)/shard_map/ppermute | solution.py:92
  50.7 7.7 %collective-permute-start.6 = (f32[2048,16]{0,1:T(8,128)S(1)}, f32[2048,16]{0,1:T(8,128)S(1)}, u32[]{:S(2)}, u32[]{:S(2)}) collective-permute-start(f32[2048,16]{0,1:T(8,128)S(1)} %collective-permute-done.5), channel_id=1, source_target_pairs={{0,1},{1,2},{2,3},{3,4},{4,5},{5,6},{6,7},{7,8},{8,9},{9,10},{10,1... | collective-permute-start | bytes 393224 | tf_op jit(solution)/shard_map/ppermute | solution.py:89
  52.6 7.7 %collective-permute-start.13 = (f32[2048,16]{0,1:T(8,128)S(1)}, f32[2048,16]{0,1:T(8,128)S(1)}, u32[]{:S(2)}, u32[]{:S(2)}) collective-permute-start(f32[2048,16]{0,1:T(8,128)S(1)} %collective-permute-done.12), channel_id=1, source_target_pairs={{0,15},{1,0},{2,1},{3,2},{4,3},{5,4},{6,5},{7,6},{8,7},{9,8},{10,9... | collective-permute-start | bytes 393224 | tf_op jit(solution)/shard_map/ppermute | solution.py:92
  58.4 8.1 %collective-permute-start.7 = (f32[2048,16]{0,1:T(8,128)S(1)}, f32[2048,16]{0,1:T(8,128)S(1)}, u32[]{:S(2)}, u32[]{:S(2)}) collective-permute-start(f32[2048,16]{0,1:T(8,128)S(1)} %collective-permute-done.6), channel_id=1, source_target_pairs={{0,1},{1,2},{2,3},{3,4},{4,5},{5,6},{6,7},{7,8},{8,9},{9,10},{10,1... | collective-permute-start | bytes 393224 | tf_op jit(solution)/shard_map/ppermute | solution.py:89
  60.4 7.5 %collective-permute-start.14 = (f32[2048,16]{0,1:T(8,128)S(1)}, f32[2048,16]{0,1:T(8,128)S(1)}, u32[]{:S(2)}, u32[]{:S(2)}) collective-permute-start(f32[2048,16]{0,1:T(8,128)S(1)} %collective-permute-done.13), channel_id=1, source_target_pairs={{0,15},{1,0},{2,1},{3,2},{4,3},{5,4},{6,5},{7,6},{8,7},{9,8},{10,9... | collective-permute-start | bytes 393224 | tf_op jit(solution)/shard_map/ppermute | solution.py:92
  67.9 1.9 %copy-start = (f32[2048,256]{1,0:T(8,128)S(1)}, f32[2048,256]{1,0:T(8,128)}, u32[]{:S(2)}) copy-start(f32[2048,256]{1,0:T(8,128)} %param.3) | copy-start | bytes 6291460
  102.3 15.3 %all-to-all-start.1 = ((f32[32,8,512]{2,1,0:T(8,128)}), f32[32,8,512]{2,1,0:T(8,128)S(1)}, u32[]{:S(2)}, u32[]{:S(2)}) async-start(f32[32,8,512]{2,1,0:T(8,128)} %broadcast_in_dim.2), calls=%async_computation.1 | async-start | bytes 1048576 | tf_op jit(solution)/shard_map/all_to_all | solution.py:103
  142.0 9.7 %copy-start.1 = (f32[256,256]{1,0:T(8,128)}, f32[256,256]{1,0:T(8,128)S(1)}, u32[]{:S(2)}) copy-start(f32[256,256]{1,0:T(8,128)S(1)} %fusion.4) | copy-start | bytes 786436

commit v11 on v10

--- a/solution.py
+++ b/solution.py
@@ -17,55 +17,56 @@
     cols = lax.broadcasted_iota(jnp.int32, (n, n), 1)
     work_ref[:, :n] = gram_ref[...]
     work_ref[:, n:] = jnp.where(rows == cols, 1.0, 0.0).astype(jnp.float32)
-    sub_col = lax.broadcasted_iota(jnp.int32, (8, 1), 0)
+    depth = 16
+    sub_col = lax.broadcasted_iota(jnp.int32, (depth, 1), 0)
     half = n // 2
 
     def phase(first, last, lo, hi):
         width = hi - lo
-        lane = lax.broadcasted_iota(jnp.int32, (8, width), 1) + lo
-        sub = lax.broadcasted_iota(jnp.int32, (8, width), 0)
+        lane = lax.broadcasted_iota(jnp.int32, (depth, width), 1) + lo
+        sub = lax.broadcasted_iota(jnp.int32, (depth, width), 0)
         key = n - lo
 
         def block(b, strip):
-            base = pl.multiple_of(b * 8, 8)
+            base = pl.multiple_of(b * depth, depth)
             cols = [jnp.sum(jnp.where(lane[:, :128] == base + k, strip[:, :128], 0.0),
-                            axis=1, keepdims=True) for k in range(8)]
+                            axis=1, keepdims=True) for k in range(depth)]
             factor_cols, inverse_diag = [], []
-            for k in range(8):
+            for k in range(depth):
                 diag = cols[k][k:k + 1, :]
                 guess = lax.rsqrt(diag)
                 scale = guess * (1.5 - 0.5 * diag * guess * guess)
                 column = jnp.where(sub_col >= k, cols[k] * scale, 0.0)
                 factor_cols.append(column)
                 inverse_diag.append(scale)
-                for m in range(k + 1, 8):
+                for m in range(k + 1, depth):
                     cols[m] = cols[m] - column * column[m:m + 1, :]
             done_rows = []
-            for k in range(8):
+            for k in range(depth):
                 row = strip[k:k + 1, :]
                 for m in range(k):
                     row = row - factor_cols[m][k:k + 1, :] * done_rows[m]
                 done_rows.append(row * inverse_diag[k])
             strip = done_rows[0] + jnp.zeros_like(strip)
-            for k in range(1, 8):
+            for k in range(1, depth):
                 strip = jnp.where(sub == k, done_rows[k], strip)
-            work_ref[pl.ds(base, 8), lo:hi] = strip
-            left = jnp.where(lane[:, :key] > base + 7, strip[:, :key], 0.0)
+            work_ref[pl.ds(base, depth), lo:hi] = strip
+            left = jnp.where(lane[:, :key] > base + depth - 1, strip[:, :key], 0.0)
             left_ref[lo:n, :] = jnp.transpose(left)
-            after = pl.multiple_of(jnp.minimum(base + 8, n - 8), 8)
-            nearest = left_ref[pl.ds(after, 8), :]
-            following = work_ref[pl.ds(after, 8), lo:hi] - jnp.dot(
+            after = pl.multiple_of(jnp.minimum(base + depth, n - depth), depth)
+            nearest = left_ref[pl.ds(after, depth), :]
+            following = work_ref[pl.ds(after, depth), lo:hi] - jnp.dot(
                 nearest, strip, precision=HIGHEST, preferred_element_type=jnp.float32)
             update = jnp.dot(left_ref[lo:n, :], strip, precision=HIGHEST,
                              preferred_element_type=jnp.float32)
             work_ref[lo:n, lo:hi] = work_ref[lo:n, lo:hi] - update
             return following
 
-        start = work_ref[first * 8:first * 8 + 8, lo:hi]
+        start = work_ref[first * depth:(first + 1) * depth, lo:hi]
         lax.fori_loop(first, last, block, start, unroll=2)
 
-    phase(0, half // 8, 0, n + half)
-    phase(half // 8, n // 8, half, 2 * n)
+    phase(0, half // depth, 0, n + half)
+    phase(half // depth, n // depth, half, 2 * n)
     done = work_ref[...]
     upper_ref[...] = jnp.where(cols >= rows, done[:, :n], 0.0)
     inverse_ref[...] = jnp.where(cols <= rows, done[:, n:], 0.0)
@@ -78,7 +79,7 @@
         out_shape=(jax.ShapeDtypeStruct((n, n), jnp.float32),) * 2,
         in_specs=[pl.BlockSpec(memory_space=pltpu.VMEM)],
         out_specs=(pl.BlockSpec(memory_space=pltpu.VMEM),) * 2,
-        scratch_shapes=[pltpu.VMEM((n, 2 * n), jnp.float32), pltpu.VMEM((n, 8), jnp.float32)],
+        scratch_shapes=[pltpu.VMEM((n, 2 * n), jnp.float32), pltpu.VMEM((n, 16), jnp.float32)],
     )(gram)
 
 def col_gather(x):

time: 152 us -> 145 us (0.954)
  Pallas kernels: 22 us -> 14.4 us
    pallas_call x1, Pallas kernels: 22 us -> 14.4 us  [factor(): pl.pallas_call(factor_kernel, out_shape=(jax.ShapeDtypeStruct((n, n), jnp...]
where the time goes in v11:
time: 145 us; the launch traced here: 144 us
  starting transfers between devices  55.2 us (38%)
  blocking collectives  27.8 us (19%)
  waiting for transfers between devices  26.8 us (18%)
  matrix products  14.7 us (10%)
  Pallas kernels  14.4 us (10%)
  other arithmetic  2.13 us (1%)
  local copies, waits for them, and re-layouts  1.95 us (1%)
    ppermute x7, starting transfers between devices, col_gather(): behind = lax.ppermute(behind, 'col', [(i, (i - 1) % n) for i in range(n)])  33.4 us
    all_to_all x1, blocking collectives, row_sum(): mine = lax.all_to_all(parts, 'row', 0, 0, tiled=False).sum(0)  27.8 us
    ppermute x8, starting transfers between devices, col_gather(): ahead = lax.ppermute(ahead, 'col', [(i, (i + 1) % n) for i in range(n)])  17.9 us
    pallas_call x1, Pallas kernels, factor(): pl.pallas_call(factor_kernel, out_shape=(jax.ShapeDtypeStruct((n, n), jnp...  14.4 us
    ppermute x8, waiting for transfers between devices, col_gather(): ahead = lax.ppermute(ahead, 'col', [(i, (i + 1) % n) for i in range(n)])  14.3 us
    all_to_all x1, waiting for transfers between devices, row_sum(): return lax.all_to_all(copies, 'row', 0, 0, tiled=False).reshape(rows, cols)  11.3 us
    dot_general x1, matrix products, per_device(): jnp.dot(gathered, jnp.roll(coefficients, -shift, axis=0), precision=highest)  6.36 us
    all_to_all x1, starting transfers between devices, row_sum(): return lax.all_to_all(copies, 'row', 0, 0, tiled=False).reshape(rows, cols)  3.86 us
  transfers between devices with their start and end apart: 16, of which 10 were waited for; matrix products, arithmetic and copies ran while one was open for 0% of the time, Pallas kernels for 0%

profile of v11, /device:TPU:1, one launch (start us, length us, event | category | flops | bytes accessed | tf_op | source)
XLA Modules:
  0.0 144.0 jit_solution(17129383835442070953)
XLA Ops:
  0.6 0.0 copy-start.2
  0.6 4.5 %collective-permute-start = (f32[2048,16]{0,1:T(8,128)}, f32[2048,16]{0,1:T(8,128)S(1)}, u32[]{:S(2)}, u32[]{:S(2)}) collective-permute-start(f32[2048,16]{0,1:T(8,128)} %param.2), channel_id=1, source_target_pairs={{0,1},{1,2},{2,3},{3,4},{4,5},{5,6},{6,7},{7,8},{8,9},{9,10},{10,1... | collective-permute-start | bytes 393224 | tf_op jit(solution)/shard_map/ppermute | solution.py:90
  5.2 11.0 %collective-permute-done = f32[2048,16]{0,1:T(8,128)S(1)} collective-permute-done((f32[2048,16]{0,1:T(8,128)}, f32[2048,16]{0,1:T(8,128)S(1)}, u32[]{:S(2)}, u32[]{:S(2)}) %collective-permute-start) | collective-permute-done | bytes 131104 | tf_op jit(solution)/shard_map/ppermute | solution.py:90
  16.1 1.9 %collective-permute-start.1 = (f32[2048,16]{0,1:T(8,128)S(1)}, f32[2048,16]{0,1:T(8,128)S(1)}, u32[]{:S(2)}, u32[]{:S(2)}) collective-permute-start(f32[2048,16]{0,1:T(8,128)S(1)} %collective-permute-done), channel_id=1, source_target_pairs={{0,1},{1,2},{2,3},{3,4},{4,5},{5,6},{6,7},{7,8},{8,9},{9,10},{10,1... | collective-permute-start | bytes 393224 | tf_op jit(solution)/shard_map/ppermute | solution.py:90
  18.1 4.6 %collective-permute-start.8 = (f32[2048,16]{0,1:T(8,128)}, f32[2048,16]{0,1:T(8,128)S(1)}, u32[]{:S(2)}, u32[]{:S(2)}) collective-permute-start(f32[2048,16]{0,1:T(8,128)} %param.2), channel_id=1, source_target_pairs={{0,15},{1,0},{2,1},{3,2},{4,3},{5,4},{6,5},{7,6},{8,7},{9,8},{10,9... | collective-permute-start | bytes 393224 | tf_op jit(solution)/shard_map/ppermute | solution.py:93
  22.6 0.4 collective-permute-done.1
  23.1 1.9 %collective-permute-start.2 = (f32[2048,16]{0,1:T(8,128)S(1)}, f32[2048,16]{0,1:T(8,128)S(1)}, u32[]{:S(2)}, u32[]{:S(2)}) collective-permute-start(f32[2048,16]{0,1:T(8,128)S(1)} %collective-permute-done.1), channel_id=1, source_target_pairs={{0,1},{1,2},{2,3},{3,4},{4,5},{5,6},{6,7},{7,8},{8,9},{9,10},{10,1... | collective-permute-start | bytes 393224 | tf_op jit(solution)/shard_map/ppermute | solution.py:90
  25.0 0.0 collective-permute-done.8
  25.0 4.8 %collective-permute-start.9 = (f32[2048,16]{0,1:T(8,128)S(1)}, f32[2048,16]{0,1:T(8,128)S(1)}, u32[]{:S(2)}, u32[]{:S(2)}) collective-permute-start(f32[2048,16]{0,1:T(8,128)S(1)} %collective-permute-done.8), channel_id=1, source_target_pairs={{0,15},{1,0},{2,1},{3,2},{4,3},{5,4},{6,5},{7,6},{8,7},{9,8},{10,9... | collective-permute-start | bytes 393224 | tf_op jit(solution)/shard_map/ppermute | solution.py:93
  29.8 0.2 collective-permute-done.2
  30.0 1.9 %collective-permute-start.3 = (f32[2048,16]{0,1:T(8,128)S(1)}, f32[2048,16]{0,1:T(8,128)S(1)}, u32[]{:S(2)}, u32[]{:S(2)}) collective-permute-start(f32[2048,16]{0,1:T(8,128)S(1)} %collective-permute-done.2), channel_id=1, source_target_pairs={{0,1},{1,2},{2,3},{3,4},{4,5},{5,6},{6,7},{7,8},{8,9},{9,10},{10,1... | collective-permute-start | bytes 393224 | tf_op jit(solution)/shard_map/ppermute | solution.py:90
  31.9 0.0 collective-permute-done.9
  31.9 4.8 %collective-permute-start.10 = (f32[2048,16]{0,1:T(8,128)S(1)}, f32[2048,16]{0,1:T(8,128)S(1)}, u32[]{:S(2)}, u32[]{:S(2)}) collective-permute-start(f32[2048,16]{0,1:T(8,128)S(1)} %collective-permute-done.9), channel_id=1, source_target_pairs={{0,15},{1,0},{2,1},{3,2},{4,3},{5,4},{6,5},{7,6},{8,7},{9,8},{10,9... | collective-permute-start | bytes 393224 | tf_op jit(solution)/shard_map/ppermute | solution.py:93
  36.7 0.2 collective-permute-done.3
  36.9 1.9 %collective-permute-start.4 = (f32[2048,16]{0,1:T(8,128)S(1)}, f32[2048,16]{0,1:T(8,128)S(1)}, u32[]{:S(2)}, u32[]{:S(2)}) collective-permute-start(f32[2048,16]{0,1:T(8,128)S(1)} %collective-permute-done.3), channel_id=1, source_target_pairs={{0,1},{1,2},{2,3},{3,4},{4,5},{5,6},{6,7},{7,8},{8,9},{9,10},{10,1... | collective-permute-start | bytes 393224 | tf_op jit(solution)/shard_map/ppermute | solution.py:90
  38.8 0.0 collective-permute-done.10
  38.8 4.8 %collective-permute-start.11 = (f32[2048,16]{0,1:T(8,128)S(1)}, f32[2048,16]{0,1:T(8,128)S(1)}, u32[]{:S(2)}, u32[]{:S(2)}) collective-permute-start(f32[2048,16]{0,1:T(8,128)S(1)} %collective-permute-done.10), channel_id=1, source_target_pairs={{0,15},{1,0},{2,1},{3,2},{4,3},{5,4},{6,5},{7,6},{8,7},{9,8},{10,9... | collective-permute-start | bytes 393224 | tf_op jit(solution)/shard_map/ppermute | solution.py:93
  43.6 0.2 collective-permute-done.4
  43.8 1.9 %collective-permute-start.5 = (f32[2048,16]{0,1:T(8,128)S(1)}, f32[2048,16]{0,1:T(8,128)S(1)}, u32[]{:S(2)}, u32[]{:S(2)}) collective-permute-start(f32[2048,16]{0,1:T(8,128)S(1)} %collective-permute-done.4), channel_id=1, source_target_pairs={{0,1},{1,2},{2,3},{3,4},{4,5},{5,6},{6,7},{7,8},{8,9},{9,10},{10,1... | collective-permute-start | bytes 393224 | tf_op jit(solution)/shard_map/ppermute | solution.py:90
  45.7 0.0 collective-permute-done.11
  45.7 4.8 %collective-permute-start.12 = (f32[2048,16]{0,1:T(8,128)S(1)}, f32[2048,16]{0,1:T(8,128)S(1)}, u32[]{:S(2)}, u32[]{:S(2)}) collective-permute-start(f32[2048,16]{0,1:T(8,128)S(1)} %collective-permute-done.11), channel_id=1, source_target_pairs={{0,15},{1,0},{2,1},{3,2},{4,3},{5,4},{6,5},{7,6},{8,7},{9,8},{10,9... | collective-permute-start | bytes 393224 | tf_op jit(solution)/shard_map/ppermute | solution.py:93
  50.5 0.2 collective-permute-done.5
  50.7 1.9 %collective-permute-start.6 = (f32[2048,16]{0,1:T(8,128)S(1)}, f32[2048,16]{0,1:T(8,128)S(1)}, u32[]{:S(2)}, u32[]{:S(2)}) collective-permute-start(f32[2048,16]{0,1:T(8,128)S(1)} %collective-permute-done.5), channel_id=1, source_target_pairs={{0,1},{1,2},{2,3},{3,4},{4,5},{5,6},{6,7},{7,8},{8,9},{9,10},{10,1... | collective-permute-start | bytes 393224 | tf_op jit(solution)/shard_map/ppermute | solution.py:90
  52.6 0.0 collective-permute-done.12
  52.6 4.8 %collective-permute-start.13 = (f32[2048,16]{0,1:T(8,128)S(1)}, f32[2048,16]{0,1:T(8,128)S(1)}, u32[]{:S(2)}, u32[]{:S(2)}) collective-permute-start(f32[2048,16]{0,1:T(8,128)S(1)} %collective-permute-done.12), channel_id=1, source_target_pairs={{0,15},{1,0},{2,1},{3,2},{4,3},{5,4},{6,5},{7,6},{8,7},{9,8},{10,9... | collective-permute-start | bytes 393224 | tf_op jit(solution)/shard_map/ppermute | solution.py:93
  57.4 1.0 collective-permute-done.6
  58.4 1.9 %collective-permute-start.7 = (f32[2048,16]{0,1:T(8,128)S(1)}, f32[2048,16]{0,1:T(8,128)S(1)}, u32[]{:S(2)}, u32[]{:S(2)}) collective-permute-start(f32[2048,16]{0,1:T(8,128)S(1)} %collective-permute-done.6), channel_id=1, source_target_pairs={{0,1},{1,2},{2,3},{3,4},{4,5},{5,6},{6,7},{7,8},{8,9},{9,10},{10,1... | collective-permute-start | bytes 393224 | tf_op jit(solution)/shard_map/ppermute | solution.py:90
  60.3 0.0 collective-permute-done.13
  60.4 5.0 %collective-permute-start.14 = (f32[2048,16]{0,1:T(8,128)S(1)}, f32[2048,16]{0,1:T(8,128)S(1)}, u32[]{:S(2)}, u32[]{:S(2)}) collective-permute-start(f32[2048,16]{0,1:T(8,128)S(1)} %collective-permute-done.13), channel_id=1, source_target_pairs={{0,15},{1,0},{2,1},{3,2},{4,3},{5,4},{6,5},{7,6},{8,7},{9,8},{10,9... | collective-permute-start | bytes 393224 | tf_op jit(solution)/shard_map/ppermute | solution.py:93
  65.4 1.1 collective-permute-done.7
  66.6 0.0 copy-done.2
  66.7 1.2 collective-permute-done.14
  67.9 0.0 copy-start
  67.9 1.9 %fusion.8 = f32[256,256]{0,1:T(8,128)S(1)} fusion(f32[2048,256]{0,1:T(8,128)S(1)} %constant_dynamic-update-slice_fusion), kind=kOutput, calls=%fused_computation.32 | convolution fusion | flops 1610612736 | bytes 2359296 | tf_op jit(solution)/shard_map/dot_general | solution.py:112
  69.8 0.0 copy-done
  69.8 3.6 %fusion.9 = f32[256,256]{0,1:T(8,128)S(1)} fusion(f32[2048,256]{0,1:T(8,128)S(1)} %constant_dynamic-update-slice_fusion, f32[2048,256]{1,0:T(8,128)S(1)} %copy-done), kind=kOutput, calls=%fused_computation.33 | convolution fusion | flops 1610612736 | bytes 4456448 | tf_op jit(solution)/shard_map/dot_general | solution.py:111
  73.4 0.2 copy.6
  73.6 27.8 %all_to_all.10 = f32[32,8,512]{2,1,0:T(8,128)S(1)} all-to-all(f32[32,8,512]{2,1,0:T(8,128)S(1)} %bitcast.11), channel_id=1, replica_groups=mesh['row'=32,'col'=16] {'row'}, dimensions={0} | all-to-all | bytes 1048576 | tf_op jit(solution)/shard_map/all_to_all | solution.py:102
  101.4 0.9 broadcast_in_dim.2
  102.3 3.9 %all-to-all-start.1 = ((f32[32,8,512]{2,1,0:T(8,128)}), f32[32,8,512]{2,1,0:T(8,128)S(1)}, u32[]{:S(2)}, u32[]{:S(2)}) async-start(f32[32,8,512]{2,1,0:T(8,128)} %broadcast_in_dim.2), calls=%async_computation.1 | async-start | bytes 1048576 | tf_op jit(solution)/shard_map/all_to_all | solution.py:104
  106.2 11.3 %all-to-all-done.1 = f32[32,8,512]{2,1,0:T(8,128)S(1)} async-done(((f32[32,8,512]{2,1,0:T(8,128)}), f32[32,8,512]{2,1,0:T(8,128)S(1)}, u32[]{:S(2)}, u32[]{:S(2)}) %all-to-all-start.1) | async-done | bytes 524320 | tf_op jit(solution)/shard_map/all_to_all | solution.py:104
  117.6 0.1 fusion
  117.7 0.9 fusion.3.gram_ref
  118.6 14.4 %shard_map.49 = (f32[256,256]{1,0:T(8,128)}, f32[256,256]{1,0:T(8,128)}) custom-call(f32[256,256]{1,0:T(8,128)} %fusion.3.gram_ref), custom_call_target="tpu_custom_call" | custom-call | tf_op jit(solution)/shard_map/pallas_call | solution.py:77
  133.0 1.3 fusion.4
  134.3 0.0 copy-start.1
  134.4 1.6 %fusion.10 = f32[256,256]{1,0:T(8,128)S(1)} fusion(f32[256,256]{1,0:T(8,128)} %get-tuple-element.6, f32[256,256]{1,0:T(8,128)S(1)} %fusion.4), kind=kOutput, calls=%fused_computation.34 | convolution fusion | flops 201326592 | bytes 786432 | tf_op jit(solution)/shard_map/dot_general | solution.py:118
  136.0 1.0 dynamic-slice_multiply_fusion
  137.0 0.7 copy.7
  137.7 6.4 %convolution_subtract_fusion = f32[2048,256]{1,0:T(8,128)} fusion(f32[2048,256]{1,0:T(8,128)} %param.3, f32[2048,256]{0,1:T(8,128)S(1)} %constant_dynamic-update-slice_fusion, s32[]{:T(128)S(6)} %select_n.36, f32[256,256]{1,0:T(8,128)S(1)} %fusion.10), kind=kOutput, calls=%fused_computation | convolution fusion | flops 1611202560 | bytes 6553604 | tf_op jit(solution)/shard_map/dot_general | solution.py:119
  144.0 0.0 copy-done.1
  (19 shorter events, 0.3 us)
Async XLA Ops:
  0.6 66.0 %copy-start.2 = (f32[2048,16]{0,1:T(8,128)S(1)}, f32[2048,16]{0,1:T(8,128)}, u32[]{:S(2)}) copy-start(f32[2048,16]{0,1:T(8,128)} %param.2) | copy-start | bytes 393220
  0.6 15.5 %collective-permute-start = (f32[2048,16]{0,1:T(8,128)}, f32[2048,16]{0,1:T(8,128)S(1)}, u32[]{:S(2)}, u32[]{:S(2)}) collective-permute-start(f32[2048,16]{0,1:T(8,128)} %param.2), channel_id=1, source_target_pairs={{0,1},{1,2},{2,3},{3,4},{4,5},{5,6},{6,7},{7,8},{8,9},{9,10},{10,1... | collective-permute-start | bytes 393224 | tf_op jit(solution)/shard_map/ppermute | solution.py:90
  16.1 6.9 %collective-permute-start.1 = (f32[2048,16]{0,1:T(8,128)S(1)}, f32[2048,16]{0,1:T(8,128)S(1)}, u32[]{:S(2)}, u32[]{:S(2)}) collective-permute-start(f32[2048,16]{0,1:T(8,128)S(1)} %collective-permute-done), channel_id=1, source_target_pairs={{0,1},{1,2},{2,3},{3,4},{4,5},{5,6},{6,7},{7,8},{8,9},{9,10},{10,1... | collective-permute-start | bytes 393224 | tf_op jit(solution)/shard_map/ppermute | solution.py:90
  18.1 6.9 %collective-permute-start.8 = (f32[2048,16]{0,1:T(8,128)}, f32[2048,16]{0,1:T(8,128)S(1)}, u32[]{:S(2)}, u32[]{:S(2)}) collective-permute-start(f32[2048,16]{0,1:T(8,128)} %param.2), channel_id=1, source_target_pairs={{0,15},{1,0},{2,1},{3,2},{4,3},{5,4},{6,5},{7,6},{8,7},{9,8},{10,9... | collective-permute-start | bytes 393224 | tf_op jit(solution)/shard_map/ppermute | solution.py:93
  23.1 6.9 %collective-permute-start.2 = (f32[2048,16]{0,1:T(8,128)S(1)}, f32[2048,16]{0,1:T(8,128)S(1)}, u32[]{:S(2)}, u32[]{:S(2)}) collective-permute-start(f32[2048,16]{0,1:T(8,128)S(1)} %collective-permute-done.1), channel_id=1, source_target_pairs={{0,1},{1,2},{2,3},{3,4},{4,5},{5,6},{6,7},{7,8},{8,9},{9,10},{10,1... | collective-permute-start | bytes 393224 | tf_op jit(solution)/shard_map/ppermute | solution.py:90
  25.0 6.9 %collective-permute-start.9 = (f32[2048,16]{0,1:T(8,128)S(1)}, f32[2048,16]{0,1:T(8,128)S(1)}, u32[]{:S(2)}, u32[]{:S(2)}) collective-permute-start(f32[2048,16]{0,1:T(8,128)S(1)} %collective-permute-done.8), channel_id=1, source_target_pairs={{0,15},{1,0},{2,1},{3,2},{4,3},{5,4},{6,5},{7,6},{8,7},{9,8},{10,9... | collective-permute-start | bytes 393224 | tf_op jit(solution)/shard_map/ppermute | solution.py:93
  30.0 6.9 %collective-permute-start.3 = (f32[2048,16]{0,1:T(8,128)S(1)}, f32[2048,16]{0,1:T(8,128)S(1)}, u32[]{:S(2)}, u32[]{:S(2)}) collective-permute-start(f32[2048,16]{0,1:T(8,128)S(1)} %collective-permute-done.2), channel_id=1, source_target_pairs={{0,1},{1,2},{2,3},{3,4},{4,5},{5,6},{6,7},{7,8},{8,9},{9,10},{10,1... | collective-permute-start | bytes 393224 | tf_op jit(solution)/shard_map/ppermute | solution.py:90
  31.9 6.9 %collective-permute-start.10 = (f32[2048,16]{0,1:T(8,128)S(1)}, f32[2048,16]{0,1:T(8,128)S(1)}, u32[]{:S(2)}, u32[]{:S(2)}) collective-permute-start(f32[2048,16]{0,1:T(8,128)S(1)} %collective-permute-done.9), channel_id=1, source_target_pairs={{0,15},{1,0},{2,1},{3,2},{4,3},{5,4},{6,5},{7,6},{8,7},{9,8},{10,9... | collective-permute-start | bytes 393224 | tf_op jit(solution)/shard_map/ppermute | solution.py:93
  36.9 6.9 %collective-permute-start.4 = (f32[2048,16]{0,1:T(8,128)S(1)}, f32[2048,16]{0,1:T(8,128)S(1)}, u32[]{:S(2)}, u32[]{:S(2)}) collective-permute-start(f32[2048,16]{0,1:T(8,128)S(1)} %collective-permute-done.3), channel_id=1, source_target_pairs={{0,1},{1,2},{2,3},{3,4},{4,5},{5,6},{6,7},{7,8},{8,9},{9,10},{10,1... | collective-permute-start | bytes 393224 | tf_op jit(solution)/shard_map/ppermute | solution.py:90
  38.8 6.9 %collective-permute-start.11 = (f32[2048,16]{0,1:T(8,128)S(1)}, f32[2048,16]{0,1:T(8,128)S(1)}, u32[]{:S(2)}, u32[]{:S(2)}) collective-permute-start(f32[2048,16]{0,1:T(8,128)S(1)} %collective-permute-done.10), channel_id=1, source_target_pairs={{0,15},{1,0},{2,1},{3,2},{4,3},{5,4},{6,5},{7,6},{8,7},{9,8},{10,9... | collective-permute-start | bytes 393224 | tf_op jit(solution)/shard_map/ppermute | solution.py:93
  43.8 6.9 %collective-permute-start.5 = (f32[2048,16]{0,1:T(8,128)S(1)}, f32[2048,16]{0,1:T(8,128)S(1)}, u32[]{:S(2)}, u32[]{:S(2)}) collective-permute-start(f32[2048,16]{0,1:T(8,128)S(1)} %collective-permute-done.4), channel_id=1, source_target_pairs={{0,1},{1,2},{2,3},{3,4},{4,5},{5,6},{6,7},{7,8},{8,9},{9,10},{10,1... | collective-permute-start | bytes 393224 | tf_op jit(solution)/shard_map/ppermute | solution.py:90
  45.7 6.9 %collective-permute-start.12 = (f32[2048,16]{0,1:T(8,128)S(1)}, f32[2048,16]{0,1:T(8,128)S(1)}, u32[]{:S(2)}, u32[]{:S(2)}) collective-permute-start(f32[2048,16]{0,1:T(8,128)S(1)} %collective-permute-done.11), channel_id=1, source_target_pairs={{0,15},{1,0},{2,1},{3,2},{4,3},{5,4},{6,5},{7,6},{8,7},{9,8},{10,9... | collective-permute-start | bytes 393224 | tf_op jit(solution)/shard_map/ppermute | solution.py:93
  50.7 7.7 %collective-permute-start.6 = (f32[2048,16]{0,1:T(8,128)S(1)}, f32[2048,16]{0,1:T(8,128)S(1)}, u32[]{:S(2)}, u32[]{:S(2)}) collective-permute-start(f32[2048,16]{0,1:T(8,128)S(1)} %collective-permute-done.5), channel_id=1, source_target_pairs={{0,1},{1,2},{2,3},{3,4},{4,5},{5,6},{6,7},{7,8},{8,9},{9,10},{10,1... | collective-permute-start | bytes 393224 | tf_op jit(solution)/shard_map/ppermute | solution.py:90
  52.6 7.7 %collective-permute-start.13 = (f32[2048,16]{0,1:T(8,128)S(1)}, f32[2048,16]{0,1:T(8,128)S(1)}, u32[]{:S(2)}, u32[]{:S(2)}) collective-permute-start(f32[2048,16]{0,1:T(8,128)S(1)} %collective-permute-done.12), channel_id=1, source_target_pairs={{0,15},{1,0},{2,1},{3,2},{4,3},{5,4},{6,5},{7,6},{8,7},{9,8},{10,9... | collective-permute-start | bytes 393224 | tf_op jit(solution)/shard_map/ppermute | solution.py:93
  58.4 8.1 %collective-permute-start.7 = (f32[2048,16]{0,1:T(8,128)S(1)}, f32[2048,16]{0,1:T(8,128)S(1)}, u32[]{:S(2)}, u32[]{:S(2)}) collective-permute-start(f32[2048,16]{0,1:T(8,128)S(1)} %collective-permute-done.6), channel_id=1, source_target_pairs={{0,1},{1,2},{2,3},{3,4},{4,5},{5,6},{6,7},{7,8},{8,9},{9,10},{10,1... | collective-permute-start | bytes 393224 | tf_op jit(solution)/shard_map/ppermute | solution.py:90
  60.4 7.5 %collective-permute-start.14 = (f32[2048,16]{0,1:T(8,128)S(1)}, f32[2048,16]{0,1:T(8,128)S(1)}, u32[]{:S(2)}, u32[]{:S(2)}) collective-permute-start(f32[2048,16]{0,1:T(8,128)S(1)} %collective-permute-done.13), channel_id=1, source_target_pairs={{0,15},{1,0},{2,1},{3,2},{4,3},{5,4},{6,5},{7,6},{8,7},{9,8},{10,9... | collective-permute-start | bytes 393224 | tf_op jit(solution)/shard_map/ppermute | solution.py:93
  67.9 1.9 %copy-start = (f32[2048,256]{1,0:T(8,128)S(1)}, f32[2048,256]{1,0:T(8,128)}, u32[]{:S(2)}) copy-start(f32[2048,256]{1,0:T(8,128)} %param.3) | copy-start | bytes 6291460
  102.3 15.3 %all-to-all-start.1 = ((f32[32,8,512]{2,1,0:T(8,128)}), f32[32,8,512]{2,1,0:T(8,128)S(1)}, u32[]{:S(2)}, u32[]{:S(2)}) async-start(f32[32,8,512]{2,1,0:T(8,128)} %broadcast_in_dim.2), calls=%async_computation.1 | async-start | bytes 1048576 | tf_op jit(solution)/shard_map/all_to_all | solution.py:104
  134.3 9.7 %copy-start.1 = (f32[256,256]{1,0:T(8,128)}, f32[256,256]{1,0:T(8,128)S(1)}, u32[]{:S(2)}) copy-start(f32[256,256]{1,0:T(8,128)S(1)} %fusion.4) | copy-start | bytes 786436

commit v12 on v11

--- a/solution.py
+++ b/solution.py
@@ -17,7 +17,7 @@
     cols = lax.broadcasted_iota(jnp.int32, (n, n), 1)
     work_ref[:, :n] = gram_ref[...]
     work_ref[:, n:] = jnp.where(rows == cols, 1.0, 0.0).astype(jnp.float32)
-    depth = 16
+    depth = 32
     sub_col = lax.broadcasted_iota(jnp.int32, (depth, 1), 0)
     half = n // 2
 
@@ -79,7 +79,7 @@
         out_shape=(jax.ShapeDtypeStruct((n, n), jnp.float32),) * 2,
         in_specs=[pl.BlockSpec(memory_space=pltpu.VMEM)],
         out_specs=(pl.BlockSpec(memory_space=pltpu.VMEM),) * 2,
-        scratch_shapes=[pltpu.VMEM((n, 2 * n), jnp.float32), pltpu.VMEM((n, 16), jnp.float32)],
+        scratch_shapes=[pltpu.VMEM((n, 2 * n), jnp.float32), pltpu.VMEM((n, 32), jnp.float32)],
     )(gram)
 
 def col_gather(x):

time: 145 us -> 144 us (level)
  no operation moved by 1% of the time
where the time goes in v12:
time: 144 us
  starting transfers between devices  55.2 us (38%)
  blocking collectives  27.8 us (19%)
  waiting for transfers between devices  26.8 us (19%)
  matrix products  14.7 us (10%)
  Pallas kernels  13.9 us (10%)
  other arithmetic  2.13 us (1%)
  local copies, waits for them, and re-layouts  1.95 us (1%)
    ppermute x7, starting transfers between devices, col_gather(): behind = lax.ppermute(behind, 'col', [(i, (i - 1) % n) for i in range(n)])  33.4 us
    all_to_all x1, blocking collectives, row_sum(): mine = lax.all_to_all(parts, 'row', 0, 0, tiled=False).sum(0)  27.8 us
    ppermute x8, starting transfers between devices, col_gather(): ahead = lax.ppermute(ahead, 'col', [(i, (i + 1) % n) for i in range(n)])  17.9 us
    ppermute x8, waiting for transfers between devices, col_gather(): ahead = lax.ppermute(ahead, 'col', [(i, (i + 1) % n) for i in range(n)])  14.3 us
    pallas_call x1, Pallas kernels, factor(): pl.pallas_call(factor_kernel, out_shape=(jax.ShapeDtypeStruct((n, n), jnp...  13.9 us
    all_to_all x1, waiting for transfers between devices, row_sum(): return lax.all_to_all(copies, 'row', 0, 0, tiled=False).reshape(rows, cols)  11.3 us
    dot_general x1, matrix products, per_device(): jnp.dot(gathered, jnp.roll(coefficients, -shift, axis=0), precision=highest)  6.36 us
    all_to_all x1, starting transfers between devices, row_sum(): return lax.all_to_all(copies, 'row', 0, 0, tiled=False).reshape(rows, cols)  3.86 us
  transfers between devices with their start and end apart: 16, of which 10 were waited for; matrix products, arithmetic and copies ran while one was open for 0% of the time, Pallas kernels for 0%

profile of v12, /device:TPU:1, one launch (start us, length us, event | category | flops | bytes accessed | tf_op | source)
XLA Modules:
  0.0 143.6 jit_solution(4496153041649814673)
XLA Ops:
  0.6 0.0 copy-start.2
  0.6 4.5 %collective-permute-start = (f32[2048,16]{0,1:T(8,128)}, f32[2048,16]{0,1:T(8,128)S(1)}, u32[]{:S(2)}, u32[]{:S(2)}) collective-permute-start(f32[2048,16]{0,1:T(8,128)} %param.2), channel_id=1, source_target_pairs={{0,1},{1,2},{2,3},{3,4},{4,5},{5,6},{6,7},{7,8},{8,9},{9,10},{10,1... | collective-permute-start | bytes 393224 | tf_op jit(solution)/shard_map/ppermute | solution.py:90
  5.2 11.0 %collective-permute-done = f32[2048,16]{0,1:T(8,128)S(1)} collective-permute-done((f32[2048,16]{0,1:T(8,128)}, f32[2048,16]{0,1:T(8,128)S(1)}, u32[]{:S(2)}, u32[]{:S(2)}) %collective-permute-start) | collective-permute-done | bytes 131104 | tf_op jit(solution)/shard_map/ppermute | solution.py:90
  16.1 1.9 %collective-permute-start.1 = (f32[2048,16]{0,1:T(8,128)S(1)}, f32[2048,16]{0,1:T(8,128)S(1)}, u32[]{:S(2)}, u32[]{:S(2)}) collective-permute-start(f32[2048,16]{0,1:T(8,128)S(1)} %collective-permute-done), channel_id=1, source_target_pairs={{0,1},{1,2},{2,3},{3,4},{4,5},{5,6},{6,7},{7,8},{8,9},{9,10},{10,1... | collective-permute-start | bytes 393224 | tf_op jit(solution)/shard_map/ppermute | solution.py:90
  18.1 4.6 %collective-permute-start.8 = (f32[2048,16]{0,1:T(8,128)}, f32[2048,16]{0,1:T(8,128)S(1)}, u32[]{:S(2)}, u32[]{:S(2)}) collective-permute-start(f32[2048,16]{0,1:T(8,128)} %param.2), channel_id=1, source_target_pairs={{0,15},{1,0},{2,1},{3,2},{4,3},{5,4},{6,5},{7,6},{8,7},{9,8},{10,9... | collective-permute-start | bytes 393224 | tf_op jit(solution)/shard_map/ppermute | solution.py:93
  22.6 0.4 collective-permute-done.1
  23.1 1.9 %collective-permute-start.2 = (f32[2048,16]{0,1:T(8,128)S(1)}, f32[2048,16]{0,1:T(8,128)S(1)}, u32[]{:S(2)}, u32[]{:S(2)}) collective-permute-start(f32[2048,16]{0,1:T(8,128)S(1)} %collective-permute-done.1), channel_id=1, source_target_pairs={{0,1},{1,2},{2,3},{3,4},{4,5},{5,6},{6,7},{7,8},{8,9},{9,10},{10,1... | collective-permute-start | bytes 393224 | tf_op jit(solution)/shard_map/ppermute | solution.py:90
  25.0 0.0 collective-permute-done.8
  25.0 4.8 %collective-permute-start.9 = (f32[2048,16]{0,1:T(8,128)S(1)}, f32[2048,16]{0,1:T(8,128)S(1)}, u32[]{:S(2)}, u32[]{:S(2)}) collective-permute-start(f32[2048,16]{0,1:T(8,128)S(1)} %collective-permute-done.8), channel_id=1, source_target_pairs={{0,15},{1,0},{2,1},{3,2},{4,3},{5,4},{6,5},{7,6},{8,7},{9,8},{10,9... | collective-permute-start | bytes 393224 | tf_op jit(solution)/shard_map/ppermute | solution.py:93
  29.8 0.2 collective-permute-done.2
  30.0 1.9 %collective-permute-start.3 = (f32[2048,16]{0,1:T(8,128)S(1)}, f32[2048,16]{0,1:T(8,128)S(1)}, u32[]{:S(2)}, u32[]{:S(2)}) collective-permute-start(f32[2048,16]{0,1:T(8,128)S(1)} %collective-permute-done.2), channel_id=1, source_target_pairs={{0,1},{1,2},{2,3},{3,4},{4,5},{5,6},{6,7},{7,8},{8,9},{9,10},{10,1... | collective-permute-start | bytes 393224 | tf_op jit(solution)/shard_map/ppermute | solution.py:90
  31.9 0.0 collective-permute-done.9
  31.9 4.8 %collective-permute-start.10 = (f32[2048,16]{0,1:T(8,128)S(1)}, f32[2048,16]{0,1:T(8,128)S(1)}, u32[]{:S(2)}, u32[]{:S(2)}) collective-permute-start(f32[2048,16]{0,1:T(8,128)S(1)} %collective-permute-done.9), channel_id=1, source_target_pairs={{0,15},{1,0},{2,1},{3,2},{4,3},{5,4},{6,5},{7,6},{8,7},{9,8},{10,9... | collective-permute-start | bytes 393224 | tf_op jit(solution)/shard_map/ppermute | solution.py:93
  36.7 0.2 collective-permute-done.3
  36.9 1.9 %collective-permute-start.4 = (f32[2048,16]{0,1:T(8,128)S(1)}, f32[2048,16]{0,1:T(8,128)S(1)}, u32[]{:S(2)}, u32[]{:S(2)}) collective-permute-start(f32[2048,16]{0,1:T(8,128)S(1)} %collective-permute-done.3), channel_id=1, source_target_pairs={{0,1},{1,2},{2,3},{3,4},{4,5},{5,6},{6,7},{7,8},{8,9},{9,10},{10,1... | collective-permute-start | bytes 393224 | tf_op jit(solution)/shard_map/ppermute | solution.py:90
  38.8 0.0 collective-permute-done.10
  38.8 4.8 %collective-permute-start.11 = (f32[2048,16]{0,1:T(8,128)S(1)}, f32[2048,16]{0,1:T(8,128)S(1)}, u32[]{:S(2)}, u32[]{:S(2)}) collective-permute-start(f32[2048,16]{0,1:T(8,128)S(1)} %collective-permute-done.10), channel_id=1, source_target_pairs={{0,15},{1,0},{2,1},{3,2},{4,3},{5,4},{6,5},{7,6},{8,7},{9,8},{10,9... | collective-permute-start | bytes 393224 | tf_op jit(solution)/shard_map/ppermute | solution.py:93
  43.6 0.2 collective-permute-done.4
  43.8 1.9 %collective-permute-start.5 = (f32[2048,16]{0,1:T(8,128)S(1)}, f32[2048,16]{0,1:T(8,128)S(1)}, u32[]{:S(2)}, u32[]{:S(2)}) collective-permute-start(f32[2048,16]{0,1:T(8,128)S(1)} %collective-permute-done.4), channel_id=1, source_target_pairs={{0,1},{1,2},{2,3},{3,4},{4,5},{5,6},{6,7},{7,8},{8,9},{9,10},{10,1... | collective-permute-start | bytes 393224 | tf_op jit(solution)/shard_map/ppermute | solution.py:90
  45.7 0.0 collective-permute-done.11
  45.7 4.8 %collective-permute-start.12 = (f32[2048,16]{0,1:T(8,128)S(1)}, f32[2048,16]{0,1:T(8,128)S(1)}, u32[]{:S(2)}, u32[]{:S(2)}) collective-permute-start(f32[2048,16]{0,1:T(8,128)S(1)} %collective-permute-done.11), channel_id=1, source_target_pairs={{0,15},{1,0},{2,1},{3,2},{4,3},{5,4},{6,5},{7,6},{8,7},{9,8},{10,9... | collective-permute-start | bytes 393224 | tf_op jit(solution)/shard_map/ppermute | solution.py:93
  50.5 0.2 collective-permute-done.5
  50.7 1.9 %collective-permute-start.6 = (f32[2048,16]{0,1:T(8,128)S(1)}, f32[2048,16]{0,1:T(8,128)S(1)}, u32[]{:S(2)}, u32[]{:S(2)}) collective-permute-start(f32[2048,16]{0,1:T(8,128)S(1)} %collective-permute-done.5), channel_id=1, source_target_pairs={{0,1},{1,2},{2,3},{3,4},{4,5},{5,6},{6,7},{7,8},{8,9},{9,10},{10,1... | collective-permute-start | bytes 393224 | tf_op jit(solution)/shard_map/ppermute | solution.py:90
  52.6 0.0 collective-permute-done.12
  52.6 4.8 %collective-permute-start.13 = (f32[2048,16]{0,1:T(8,128)S(1)}, f32[2048,16]{0,1:T(8,128)S(1)}, u32[]{:S(2)}, u32[]{:S(2)}) collective-permute-start(f32[2048,16]{0,1:T(8,128)S(1)} %collective-permute-done.12), channel_id=1, source_target_pairs={{0,15},{1,0},{2,1},{3,2},{4,3},{5,4},{6,5},{7,6},{8,7},{9,8},{10,9... | collective-permute-start | bytes 393224 | tf_op jit(solution)/shard_map/ppermute | solution.py:93
  57.4 1.0 collective-permute-done.6
  58.4 1.9 %collective-permute-start.7 = (f32[2048,16]{0,1:T(8,128)S(1)}, f32[2048,16]{0,1:T(8,128)S(1)}, u32[]{:S(2)}, u32[]{:S(2)}) collective-permute-start(f32[2048,16]{0,1:T(8,128)S(1)} %collective-permute-done.6), channel_id=1, source_target_pairs={{0,1},{1,2},{2,3},{3,4},{4,5},{5,6},{6,7},{7,8},{8,9},{9,10},{10,1... | collective-permute-start | bytes 393224 | tf_op jit(solution)/shard_map/ppermute | solution.py:90
  60.3 0.0 collective-permute-done.13
  60.4 5.0 %collective-permute-start.14 = (f32[2048,16]{0,1:T(8,128)S(1)}, f32[2048,16]{0,1:T(8,128)S(1)}, u32[]{:S(2)}, u32[]{:S(2)}) collective-permute-start(f32[2048,16]{0,1:T(8,128)S(1)} %collective-permute-done.13), channel_id=1, source_target_pairs={{0,15},{1,0},{2,1},{3,2},{4,3},{5,4},{6,5},{7,6},{8,7},{9,8},{10,9... | collective-permute-start | bytes 393224 | tf_op jit(solution)/shard_map/ppermute | solution.py:93
  65.4 1.1 collective-permute-done.7
  66.6 0.0 copy-done.2
  66.7 1.2 collective-permute-done.14
  67.9 0.0 copy-start
  67.9 1.9 %fusion.8 = f32[256,256]{0,1:T(8,128)S(1)} fusion(f32[2048,256]{0,1:T(8,128)S(1)} %constant_dynamic-update-slice_fusion), kind=kOutput, calls=%fused_computation.32 | convolution fusion | flops 1610612736 | bytes 2359296 | tf_op jit(solution)/shard_map/dot_general | solution.py:112
  69.8 0.0 copy-done
  69.8 3.6 %fusion.9 = f32[256,256]{0,1:T(8,128)S(1)} fusion(f32[2048,256]{0,1:T(8,128)S(1)} %constant_dynamic-update-slice_fusion, f32[2048,256]{1,0:T(8,128)S(1)} %copy-done), kind=kOutput, calls=%fused_computation.33 | convolution fusion | flops 1610612736 | bytes 4456448 | tf_op jit(solution)/shard_map/dot_general | solution.py:111
  73.4 0.2 copy.6
  73.6 27.8 %all_to_all.10 = f32[32,8,512]{2,1,0:T(8,128)S(1)} all-to-all(f32[32,8,512]{2,1,0:T(8,128)S(1)} %bitcast.11), channel_id=1, replica_groups=mesh['row'=32,'col'=16] {'row'}, dimensions={0} | all-to-all | bytes 1048576 | tf_op jit(solution)/shard_map/all_to_all | solution.py:102
  101.4 0.9 broadcast_in_dim.2
  102.3 3.9 %all-to-all-start.1 = ((f32[32,8,512]{2,1,0:T(8,128)}), f32[32,8,512]{2,1,0:T(8,128)S(1)}, u32[]{:S(2)}, u32[]{:S(2)}) async-start(f32[32,8,512]{2,1,0:T(8,128)} %broadcast_in_dim.2), calls=%async_computation.1 | async-start | bytes 1048576 | tf_op jit(solution)/shard_map/all_to_all | solution.py:104
  106.2 11.3 %all-to-all-done.1 = f32[32,8,512]{2,1,0:T(8,128)S(1)} async-done(((f32[32,8,512]{2,1,0:T(8,128)}), f32[32,8,512]{2,1,0:T(8,128)S(1)}, u32[]{:S(2)}, u32[]{:S(2)}) %all-to-all-start.1) | async-done | bytes 524320 | tf_op jit(solution)/shard_map/all_to_all | solution.py:104
  117.6 0.1 fusion
  117.7 0.9 fusion.3.gram_ref
  118.6 13.9 %shard_map.49 = (f32[256,256]{1,0:T(8,128)}, f32[256,256]{1,0:T(8,128)}) custom-call(f32[256,256]{1,0:T(8,128)} %fusion.3.gram_ref), custom_call_target="tpu_custom_call" | custom-call | tf_op jit(solution)/shard_map/pallas_call | solution.py:77
  132.6 1.3 fusion.4
  133.9 0.0 copy-start.1
  133.9 1.6 %fusion.10 = f32[256,256]{1,0:T(8,128)S(1)} fusion(f32[256,256]{1,0:T(8,128)} %get-tuple-element.6, f32[256,256]{1,0:T(8,128)S(1)} %fusion.4), kind=kOutput, calls=%fused_computation.34 | convolution fusion | flops 201326592 | bytes 786432 | tf_op jit(solution)/shard_map/dot_general | solution.py:118
  135.6 1.0 dynamic-slice_multiply_fusion
  136.6 0.7 copy.7
  137.3 6.4 %convolution_subtract_fusion = f32[2048,256]{1,0:T(8,128)} fusion(f32[2048,256]{1,0:T(8,128)} %param.3, f32[2048,256]{0,1:T(8,128)S(1)} %constant_dynamic-update-slice_fusion, s32[]{:T(128)S(6)} %select_n.36, f32[256,256]{1,0:T(8,128)S(1)} %fusion.10), kind=kOutput, calls=%fused_computation | convolution fusion | flops 1611202560 | bytes 6553604 | tf_op jit(solution)/shard_map/dot_general | solution.py:119
  143.6 0.0 copy-done.1
  (19 shorter events, 0.3 us)
Async XLA Ops:
  0.6 66.0 %copy-start.2 = (f32[2048,16]{0,1:T(8,128)S(1)}, f32[2048,16]{0,1:T(8,128)}, u32[]{:S(2)}) copy-start(f32[2048,16]{0,1:T(8,128)} %param.2) | copy-start | bytes 393220
  0.6 15.5 %collective-permute-start = (f32[2048,16]{0,1:T(8,128)}, f32[2048,16]{0,1:T(8,128)S(1)}, u32[]{:S(2)}, u32[]{:S(2)}) collective-permute-start(f32[2048,16]{0,1:T(8,128)} %param.2), channel_id=1, source_target_pairs={{0,1},{1,2},{2,3},{3,4},{4,5},{5,6},{6,7},{7,8},{8,9},{9,10},{10,1... | collective-permute-start | bytes 393224 | tf_op jit(solution)/shard_map/ppermute | solution.py:90
  16.1 6.9 %collective-permute-start.1 = (f32[2048,16]{0,1:T(8,128)S(1)}, f32[2048,16]{0,1:T(8,128)S(1)}, u32[]{:S(2)}, u32[]{:S(2)}) collective-permute-start(f32[2048,16]{0,1:T(8,128)S(1)} %collective-permute-done), channel_id=1, source_target_pairs={{0,1},{1,2},{2,3},{3,4},{4,5},{5,6},{6,7},{7,8},{8,9},{9,10},{10,1... | collective-permute-start | bytes 393224 | tf_op jit(solution)/shard_map/ppermute | solution.py:90
  18.1 6.9 %collective-permute-start.8 = (f32[2048,16]{0,1:T(8,128)}, f32[2048,16]{0,1:T(8,128)S(1)}, u32[]{:S(2)}, u32[]{:S(2)}) collective-permute-start(f32[2048,16]{0,1:T(8,128)} %param.2), channel_id=1, source_target_pairs={{0,15},{1,0},{2,1},{3,2},{4,3},{5,4},{6,5},{7,6},{8,7},{9,8},{10,9... | collective-permute-start | bytes 393224 | tf_op jit(solution)/shard_map/ppermute | solution.py:93
  23.1 6.9 %collective-permute-start.2 = (f32[2048,16]{0,1:T(8,128)S(1)}, f32[2048,16]{0,1:T(8,128)S(1)}, u32[]{:S(2)}, u32[]{:S(2)}) collective-permute-start(f32[2048,16]{0,1:T(8,128)S(1)} %collective-permute-done.1), channel_id=1, source_target_pairs={{0,1},{1,2},{2,3},{3,4},{4,5},{5,6},{6,7},{7,8},{8,9},{9,10},{10,1... | collective-permute-start | bytes 393224 | tf_op jit(solution)/shard_map/ppermute | solution.py:90
  25.0 6.9 %collective-permute-start.9 = (f32[2048,16]{0,1:T(8,128)S(1)}, f32[2048,16]{0,1:T(8,128)S(1)}, u32[]{:S(2)}, u32[]{:S(2)}) collective-permute-start(f32[2048,16]{0,1:T(8,128)S(1)} %collective-permute-done.8), channel_id=1, source_target_pairs={{0,15},{1,0},{2,1},{3,2},{4,3},{5,4},{6,5},{7,6},{8,7},{9,8},{10,9... | collective-permute-start | bytes 393224 | tf_op jit(solution)/shard_map/ppermute | solution.py:93
  30.0 6.9 %collective-permute-start.3 = (f32[2048,16]{0,1:T(8,128)S(1)}, f32[2048,16]{0,1:T(8,128)S(1)}, u32[]{:S(2)}, u32[]{:S(2)}) collective-permute-start(f32[2048,16]{0,1:T(8,128)S(1)} %collective-permute-done.2), channel_id=1, source_target_pairs={{0,1},{1,2},{2,3},{3,4},{4,5},{5,6},{6,7},{7,8},{8,9},{9,10},{10,1... | collective-permute-start | bytes 393224 | tf_op jit(solution)/shard_map/ppermute | solution.py:90
  31.9 6.9 %collective-permute-start.10 = (f32[2048,16]{0,1:T(8,128)S(1)}, f32[2048,16]{0,1:T(8,128)S(1)}, u32[]{:S(2)}, u32[]{:S(2)}) collective-permute-start(f32[2048,16]{0,1:T(8,128)S(1)} %collective-permute-done.9), channel_id=1, source_target_pairs={{0,15},{1,0},{2,1},{3,2},{4,3},{5,4},{6,5},{7,6},{8,7},{9,8},{10,9... | collective-permute-start | bytes 393224 | tf_op jit(solution)/shard_map/ppermute | solution.py:93
  36.9 6.9 %collective-permute-start.4 = (f32[2048,16]{0,1:T(8,128)S(1)}, f32[2048,16]{0,1:T(8,128)S(1)}, u32[]{:S(2)}, u32[]{:S(2)}) collective-permute-start(f32[2048,16]{0,1:T(8,128)S(1)} %collective-permute-done.3), channel_id=1, source_target_pairs={{0,1},{1,2},{2,3},{3,4},{4,5},{5,6},{6,7},{7,8},{8,9},{9,10},{10,1... | collective-permute-start | bytes 393224 | tf_op jit(solution)/shard_map/ppermute | solution.py:90
  38.8 6.9 %collective-permute-start.11 = (f32[2048,16]{0,1:T(8,128)S(1)}, f32[2048,16]{0,1:T(8,128)S(1)}, u32[]{:S(2)}, u32[]{:S(2)}) collective-permute-start(f32[2048,16]{0,1:T(8,128)S(1)} %collective-permute-done.10), channel_id=1, source_target_pairs={{0,15},{1,0},{2,1},{3,2},{4,3},{5,4},{6,5},{7,6},{8,7},{9,8},{10,9... | collective-permute-start | bytes 393224 | tf_op jit(solution)/shard_map/ppermute | solution.py:93
  43.8 6.9 %collective-permute-start.5 = (f32[2048,16]{0,1:T(8,128)S(1)}, f32[2048,16]{0,1:T(8,128)S(1)}, u32[]{:S(2)}, u32[]{:S(2)}) collective-permute-start(f32[2048,16]{0,1:T(8,128)S(1)} %collective-permute-done.4), channel_id=1, source_target_pairs={{0,1},{1,2},{2,3},{3,4},{4,5},{5,6},{6,7},{7,8},{8,9},{9,10},{10,1... | collective-permute-start | bytes 393224 | tf_op jit(solution)/shard_map/ppermute | solution.py:90
  45.7 6.9 %collective-permute-start.12 = (f32[2048,16]{0,1:T(8,128)S(1)}, f32[2048,16]{0,1:T(8,128)S(1)}, u32[]{:S(2)}, u32[]{:S(2)}) collective-permute-start(f32[2048,16]{0,1:T(8,128)S(1)} %collective-permute-done.11), channel_id=1, source_target_pairs={{0,15},{1,0},{2,1},{3,2},{4,3},{5,4},{6,5},{7,6},{8,7},{9,8},{10,9... | collective-permute-start | bytes 393224 | tf_op jit(solution)/shard_map/ppermute | solution.py:93
  50.7 7.7 %collective-permute-start.6 = (f32[2048,16]{0,1:T(8,128)S(1)}, f32[2048,16]{0,1:T(8,128)S(1)}, u32[]{:S(2)}, u32[]{:S(2)}) collective-permute-start(f32[2048,16]{0,1:T(8,128)S(1)} %collective-permute-done.5), channel_id=1, source_target_pairs={{0,1},{1,2},{2,3},{3,4},{4,5},{5,6},{6,7},{7,8},{8,9},{9,10},{10,1... | collective-permute-start | bytes 393224 | tf_op jit(solution)/shard_map/ppermute | solution.py:90
  52.6 7.7 %collective-permute-start.13 = (f32[2048,16]{0,1:T(8,128)S(1)}, f32[2048,16]{0,1:T(8,128)S(1)}, u32[]{:S(2)}, u32[]{:S(2)}) collective-permute-start(f32[2048,16]{0,1:T(8,128)S(1)} %collective-permute-done.12), channel_id=1, source_target_pairs={{0,15},{1,0},{2,1},{3,2},{4,3},{5,4},{6,5},{7,6},{8,7},{9,8},{10,9... | collective-permute-start | bytes 393224 | tf_op jit(solution)/shard_map/ppermute | solution.py:93
  58.4 8.1 %collective-permute-start.7 = (f32[2048,16]{0,1:T(8,128)S(1)}, f32[2048,16]{0,1:T(8,128)S(1)}, u32[]{:S(2)}, u32[]{:S(2)}) collective-permute-start(f32[2048,16]{0,1:T(8,128)S(1)} %collective-permute-done.6), channel_id=1, source_target_pairs={{0,1},{1,2},{2,3},{3,4},{4,5},{5,6},{6,7},{7,8},{8,9},{9,10},{10,1... | collective-permute-start | bytes 393224 | tf_op jit(solution)/shard_map/ppermute | solution.py:90
  60.4 7.5 %collective-permute-start.14 = (f32[2048,16]{0,1:T(8,128)S(1)}, f32[2048,16]{0,1:T(8,128)S(1)}, u32[]{:S(2)}, u32[]{:S(2)}) collective-permute-start(f32[2048,16]{0,1:T(8,128)S(1)} %collective-permute-done.13), channel_id=1, source_target_pairs={{0,15},{1,0},{2,1},{3,2},{4,3},{5,4},{6,5},{7,6},{8,7},{9,8},{10,9... | collective-permute-start | bytes 393224 | tf_op jit(solution)/shard_map/ppermute | solution.py:93
  67.9 1.9 %copy-start = (f32[2048,256]{1,0:T(8,128)S(1)}, f32[2048,256]{1,0:T(8,128)}, u32[]{:S(2)}) copy-start(f32[2048,256]{1,0:T(8,128)} %param.3) | copy-start | bytes 6291460
  102.3 15.3 %all-to-all-start.1 = ((f32[32,8,512]{2,1,0:T(8,128)}), f32[32,8,512]{2,1,0:T(8,128)S(1)}, u32[]{:S(2)}, u32[]{:S(2)}) async-start(f32[32,8,512]{2,1,0:T(8,128)} %broadcast_in_dim.2), calls=%async_computation.1 | async-start | bytes 1048576 | tf_op jit(solution)/shard_map/all_to_all | solution.py:104
  133.9 9.7 %copy-start.1 = (f32[256,256]{1,0:T(8,128)}, f32[256,256]{1,0:T(8,128)S(1)}, u32[]{:S(2)}) copy-start(f32[256,256]{1,0:T(8,128)S(1)} %fusion.4) | copy-start | bytes 786436

commit v13 on v11

--- a/solution.py
+++ b/solution.py
@@ -95,13 +95,17 @@
     return jnp.concatenate([got[k] for k in range(-(n // 2), n - n // 2)], axis=1)
 
 
-def row_sum(x):
+def row_sum(x, width):
     n = lax.axis_size("row")
     rows, cols = x.shape
     parts = x.reshape(n, rows // n, cols)
     mine = lax.all_to_all(parts, "row", 0, 0, tiled=False).sum(0)
-    copies = jnp.broadcast_to(mine[None], (n, rows // n, cols))
-    return lax.all_to_all(copies, "row", 0, 0, tiled=False).reshape(rows, cols)
+
+    def spread(piece):
+        copies = jnp.broadcast_to(piece[None], (n,) + piece.shape)
+        return lax.all_to_all(copies, "row", 0, 0, tiled=False).reshape(rows, piece.shape[1])
+
+    return spread(mine[:, :width]), spread(mine[:, width:])
 
 
 def per_device(panel, slab):
@@ -111,8 +115,9 @@
     cross_local = lax.dot_general(gathered, slab, contract_rows, precision=highest)
     gram_local = lax.dot_general(gathered, gathered, contract_rows, precision=highest)
     width = gram_local.shape[1]
-    summed = jnp.roll(row_sum(jnp.concatenate([gram_local, cross_local], axis=1)), shift, axis=0)
-    gram_total, totals = jnp.roll(summed[:, :width], shift, axis=1), summed[:, width:]
+    gram_rotated, cross_rotated = row_sum(jnp.concatenate([gram_local, cross_local], axis=1), width)
+    gram_total = jnp.roll(jnp.roll(gram_rotated, shift, axis=0), shift, axis=1)
+    totals = jnp.roll(cross_rotated, shift, axis=0)
     upper_factor, lower_inverse = factor(gram_total)
     projected = jnp.dot(lower_inverse, totals, precision=highest)
     coefficients = lax.dot_general(lower_inverse, projected, contract_rows, precision=highest)

time: 145 us -> 146 us (level)
  blocking collectives: 27.8 us -> 40.2 us
  waiting for transfers between devices: 26.8 us -> 15.5 us
    all_to_all x0 -> x1, blocking collectives: none -> 12.4 us  [spread(): lax.all_to_all(copies, 'row', 0, 0, tiled=False)]
    all_to_all x1, waiting for transfers between devices: 11.3 us -> 0.01 us  [spread(): lax.all_to_all(copies, 'row', 0, 0, tiled=False)]
  transfers between devices with their start and end apart: 16 -> 16, of which waited for: 10 -> 9; matrix products, arithmetic and copies ran while one was open for 0% -> 1% of each run, Pallas kernels for 0% -> 10%
where the time goes in v13:
time: 146 us; the launch traced here: 145 us
  starting transfers between devices  55.2 us (38%)
  blocking collectives  40.2 us (28%)
  waiting for transfers between devices  15.5 us (11%)
  matrix products  14.8 us (10%)
  Pallas kernels  14.4 us (10%)
  other arithmetic  2.1 us (1%)
  local copies, waits for them, and re-layouts  1.8 us (1%)
    ppermute x7, starting transfers between devices, col_gather(): behind = lax.ppermute(behind, 'col', [(i, (i - 1) % n) for i in range(n)])  33.4 us
    all_to_all x1, blocking collectives, row_sum(): mine = lax.all_to_all(parts, 'row', 0, 0, tiled=False).sum(0)  27.8 us
    ppermute x8, starting transfers between devices, col_gather(): ahead = lax.ppermute(ahead, 'col', [(i, (i + 1) % n) for i in range(n)])  17.9 us
    pallas_call x1, Pallas kernels, factor(): pl.pallas_call(factor_kernel, out_shape=(jax.ShapeDtypeStruct((n, n), jnp...  14.4 us
    ppermute x8, waiting for transfers between devices, col_gather(): ahead = lax.ppermute(ahead, 'col', [(i, (i + 1) % n) for i in range(n)])  14.3 us
    all_to_all x1, blocking collectives, spread(): lax.all_to_all(copies, 'row', 0, 0, tiled=False)  12.4 us
    dot_general x1, matrix products, per_device(): jnp.dot(gathered, jnp.roll(coefficients, -shift, axis=0), precision=highest)  6.35 us
    all_to_all x1, starting transfers between devices, spread(): lax.all_to_all(copies, 'row', 0, 0, tiled=False)  3.84 us
  transfers between devices with their start and end apart: 16, of which 9 were waited for; matrix products, arithmetic and copies ran while one was open for 1% of the time, Pallas kernels for 10%

profile of v13, /device:TPU:1, one launch (start us, length us, event | category | flops | bytes accessed | tf_op | source)
XLA Modules:
  0.0 145.0 jit_solution(13808164427773606503)
XLA Ops:
  0.6 0.0 copy-start.2
  0.6 4.5 %collective-permute-start = (f32[2048,16]{0,1:T(8,128)}, f32[2048,16]{0,1:T(8,128)S(1)}, u32[]{:S(2)}, u32[]{:S(2)}) collective-permute-start(f32[2048,16]{0,1:T(8,128)} %param.4), channel_id=1, source_target_pairs={{0,1},{1,2},{2,3},{3,4},{4,5},{5,6},{6,7},{7,8},{8,9},{9,10},{10,1... | collective-permute-start | bytes 393224 | tf_op jit(solution)/shard_map/ppermute | solution.py:90
  5.2 11.0 %collective-permute-done = f32[2048,16]{0,1:T(8,128)S(1)} collective-permute-done((f32[2048,16]{0,1:T(8,128)}, f32[2048,16]{0,1:T(8,128)S(1)}, u32[]{:S(2)}, u32[]{:S(2)}) %collective-permute-start) | collective-permute-done | bytes 131104 | tf_op jit(solution)/shard_map/ppermute | solution.py:90
  16.1 1.9 %collective-permute-start.1 = (f32[2048,16]{0,1:T(8,128)S(1)}, f32[2048,16]{0,1:T(8,128)S(1)}, u32[]{:S(2)}, u32[]{:S(2)}) collective-permute-start(f32[2048,16]{0,1:T(8,128)S(1)} %collective-permute-done), channel_id=1, source_target_pairs={{0,1},{1,2},{2,3},{3,4},{4,5},{5,6},{6,7},{7,8},{8,9},{9,10},{10,1... | collective-permute-start | bytes 393224 | tf_op jit(solution)/shard_map/ppermute | solution.py:90
  18.1 4.6 %collective-permute-start.8 = (f32[2048,16]{0,1:T(8,128)}, f32[2048,16]{0,1:T(8,128)S(1)}, u32[]{:S(2)}, u32[]{:S(2)}) collective-permute-start(f32[2048,16]{0,1:T(8,128)} %param.4), channel_id=1, source_target_pairs={{0,15},{1,0},{2,1},{3,2},{4,3},{5,4},{6,5},{7,6},{8,7},{9,8},{10,9... | collective-permute-start | bytes 393224 | tf_op jit(solution)/shard_map/ppermute | solution.py:93
  22.6 0.4 collective-permute-done.1
  23.1 1.9 %collective-permute-start.2 = (f32[2048,16]{0,1:T(8,128)S(1)}, f32[2048,16]{0,1:T(8,128)S(1)}, u32[]{:S(2)}, u32[]{:S(2)}) collective-permute-start(f32[2048,16]{0,1:T(8,128)S(1)} %collective-permute-done.1), channel_id=1, source_target_pairs={{0,1},{1,2},{2,3},{3,4},{4,5},{5,6},{6,7},{7,8},{8,9},{9,10},{10,1... | collective-permute-start | bytes 393224 | tf_op jit(solution)/shard_map/ppermute | solution.py:90
  25.0 0.0 collective-permute-done.8
  25.0 4.8 %collective-permute-start.9 = (f32[2048,16]{0,1:T(8,128)S(1)}, f32[2048,16]{0,1:T(8,128)S(1)}, u32[]{:S(2)}, u32[]{:S(2)}) collective-permute-start(f32[2048,16]{0,1:T(8,128)S(1)} %collective-permute-done.8), channel_id=1, source_target_pairs={{0,15},{1,0},{2,1},{3,2},{4,3},{5,4},{6,5},{7,6},{8,7},{9,8},{10,9... | collective-permute-start | bytes 393224 | tf_op jit(solution)/shard_map/ppermute | solution.py:93
  29.8 0.2 collective-permute-done.2
  30.0 1.9 %collective-permute-start.3 = (f32[2048,16]{0,1:T(8,128)S(1)}, f32[2048,16]{0,1:T(8,128)S(1)}, u32[]{:S(2)}, u32[]{:S(2)}) collective-permute-start(f32[2048,16]{0,1:T(8,128)S(1)} %collective-permute-done.2), channel_id=1, source_target_pairs={{0,1},{1,2},{2,3},{3,4},{4,5},{5,6},{6,7},{7,8},{8,9},{9,10},{10,1... | collective-permute-start | bytes 393224 | tf_op jit(solution)/shard_map/ppermute | solution.py:90
  31.9 0.0 collective-permute-done.9
  31.9 4.8 %collective-permute-start.10 = (f32[2048,16]{0,1:T(8,128)S(1)}, f32[2048,16]{0,1:T(8,128)S(1)}, u32[]{:S(2)}, u32[]{:S(2)}) collective-permute-start(f32[2048,16]{0,1:T(8,128)S(1)} %collective-permute-done.9), channel_id=1, source_target_pairs={{0,15},{1,0},{2,1},{3,2},{4,3},{5,4},{6,5},{7,6},{8,7},{9,8},{10,9... | collective-permute-start | bytes 393224 | tf_op jit(solution)/shard_map/ppermute | solution.py:93
  36.7 0.2 collective-permute-done.3
  36.9 1.9 %collective-permute-start.4 = (f32[2048,16]{0,1:T(8,128)S(1)}, f32[2048,16]{0,1:T(8,128)S(1)}, u32[]{:S(2)}, u32[]{:S(2)}) collective-permute-start(f32[2048,16]{0,1:T(8,128)S(1)} %collective-permute-done.3), channel_id=1, source_target_pairs={{0,1},{1,2},{2,3},{3,4},{4,5},{5,6},{6,7},{7,8},{8,9},{9,10},{10,1... | collective-permute-start | bytes 393224 | tf_op jit(solution)/shard_map/ppermute | solution.py:90
  38.8 0.0 collective-permute-done.10
  38.8 4.8 %collective-permute-start.11 = (f32[2048,16]{0,1:T(8,128)S(1)}, f32[2048,16]{0,1:T(8,128)S(1)}, u32[]{:S(2)}, u32[]{:S(2)}) collective-permute-start(f32[2048,16]{0,1:T(8,128)S(1)} %collective-permute-done.10), channel_id=1, source_target_pairs={{0,15},{1,0},{2,1},{3,2},{4,3},{5,4},{6,5},{7,6},{8,7},{9,8},{10,9... | collective-permute-start | bytes 393224 | tf_op jit(solution)/shard_map/ppermute | solution.py:93
  43.6 0.2 collective-permute-done.4
  43.8 1.9 %collective-permute-start.5 = (f32[2048,16]{0,1:T(8,128)S(1)}, f32[2048,16]{0,1:T(8,128)S(1)}, u32[]{:S(2)}, u32[]{:S(2)}) collective-permute-start(f32[2048,16]{0,1:T(8,128)S(1)} %collective-permute-done.4), channel_id=1, source_target_pairs={{0,1},{1,2},{2,3},{3,4},{4,5},{5,6},{6,7},{7,8},{8,9},{9,10},{10,1... | collective-permute-start | bytes 393224 | tf_op jit(solution)/shard_map/ppermute | solution.py:90
  45.7 0.0 collective-permute-done.11
  45.7 4.8 %collective-permute-start.12 = (f32[2048,16]{0,1:T(8,128)S(1)}, f32[2048,16]{0,1:T(8,128)S(1)}, u32[]{:S(2)}, u32[]{:S(2)}) collective-permute-start(f32[2048,16]{0,1:T(8,128)S(1)} %collective-permute-done.11), channel_id=1, source_target_pairs={{0,15},{1,0},{2,1},{3,2},{4,3},{5,4},{6,5},{7,6},{8,7},{9,8},{10,9... | collective-permute-start | bytes 393224 | tf_op jit(solution)/shard_map/ppermute | solution.py:93
  50.5 0.2 collective-permute-done.5
  50.7 1.9 %collective-permute-start.6 = (f32[2048,16]{0,1:T(8,128)S(1)}, f32[2048,16]{0,1:T(8,128)S(1)}, u32[]{:S(2)}, u32[]{:S(2)}) collective-permute-start(f32[2048,16]{0,1:T(8,128)S(1)} %collective-permute-done.5), channel_id=1, source_target_pairs={{0,1},{1,2},{2,3},{3,4},{4,5},{5,6},{6,7},{7,8},{8,9},{9,10},{10,1... | collective-permute-start | bytes 393224 | tf_op jit(solution)/shard_map/ppermute | solution.py:90
  52.6 0.0 collective-permute-done.12
  52.6 4.8 %collective-permute-start.13 = (f32[2048,16]{0,1:T(8,128)S(1)}, f32[2048,16]{0,1:T(8,128)S(1)}, u32[]{:S(2)}, u32[]{:S(2)}) collective-permute-start(f32[2048,16]{0,1:T(8,128)S(1)} %collective-permute-done.12), channel_id=1, source_target_pairs={{0,15},{1,0},{2,1},{3,2},{4,3},{5,4},{6,5},{7,6},{8,7},{9,8},{10,9... | collective-permute-start | bytes 393224 | tf_op jit(solution)/shard_map/ppermute | solution.py:93
  57.4 1.0 collective-permute-done.6
  58.4 1.9 %collective-permute-start.7 = (f32[2048,16]{0,1:T(8,128)S(1)}, f32[2048,16]{0,1:T(8,128)S(1)}, u32[]{:S(2)}, u32[]{:S(2)}) collective-permute-start(f32[2048,16]{0,1:T(8,128)S(1)} %collective-permute-done.6), channel_id=1, source_target_pairs={{0,1},{1,2},{2,3},{3,4},{4,5},{5,6},{6,7},{7,8},{8,9},{9,10},{10,1... | collective-permute-start | bytes 393224 | tf_op jit(solution)/shard_map/ppermute | solution.py:90
  60.3 0.0 collective-permute-done.13
  60.4 5.0 %collective-permute-start.14 = (f32[2048,16]{0,1:T(8,128)S(1)}, f32[2048,16]{0,1:T(8,128)S(1)}, u32[]{:S(2)}, u32[]{:S(2)}) collective-permute-start(f32[2048,16]{0,1:T(8,128)S(1)} %collective-permute-done.13), channel_id=1, source_target_pairs={{0,15},{1,0},{2,1},{3,2},{4,3},{5,4},{6,5},{7,6},{8,7},{9,8},{10,9... | collective-permute-start | bytes 393224 | tf_op jit(solution)/shard_map/ppermute | solution.py:93
  65.4 1.1 collective-permute-done.7
  66.6 0.0 copy-done.2
  66.7 1.2 collective-permute-done.14
  67.9 0.0 copy-start
  67.9 1.9 %fusion.12 = f32[256,256]{0,1:T(8,128)S(1)} fusion(f32[2048,256]{0,1:T(8,128)S(1)} %constant_dynamic-update-slice_fusion), kind=kOutput, calls=%fused_computation.37 | convolution fusion | flops 1610612736 | bytes 2359296 | tf_op jit(solution)/shard_map/dot_general | solution.py:116
  69.8 0.0 copy-done
  69.8 3.6 %fusion.13 = f32[256,256]{0,1:T(8,128)S(1)} fusion(f32[2048,256]{0,1:T(8,128)S(1)} %constant_dynamic-update-slice_fusion, f32[2048,256]{1,0:T(8,128)S(1)} %copy-done), kind=kOutput, calls=%fused_computation.38 | convolution fusion | flops 1610612736 | bytes 4456448 | tf_op jit(solution)/shard_map/dot_general | solution.py:115
  73.4 0.2 copy.6
  73.6 27.8 %all_to_all.15 = f32[32,8,512]{2,1,0:T(8,128)S(1)} all-to-all(f32[32,8,512]{2,1,0:T(8,128)S(1)} %bitcast.11), channel_id=1, replica_groups=mesh['row'=32,'col'=16] {'row'}, dimensions={0} | all-to-all | bytes 1048576 | tf_op jit(solution)/shard_map/all_to_all | solution.py:102
  101.5 12.4 %all_to_all.16 = f32[32,8,256]{2,1,0:T(8,128)S(1)} all-to-all(f32[32,8,256]{2,1,0:T(8,128)S(1)} %broadcast_in_dim.4), channel_id=1, replica_groups=mesh['row'=32,'col'=16] {'row'}, dimensions={0} | all-to-all | bytes 524288 | tf_op jit(solution)/shard_map/all_to_all | solution.py:106
  113.9 0.7 broadcast_in_dim.5
  114.6 3.8 %all-to-all-start.2 = ((f32[32,8,256]{2,1,0:T(8,128)}), f32[32,8,256]{2,1,0:T(8,128)S(1)}, u32[]{:S(2)}, u32[]{:S(2)}) async-start(f32[32,8,256]{2,1,0:T(8,128)} %broadcast_in_dim.5), calls=%async_computation.2 | async-start | bytes 524288 | tf_op jit(solution)/shard_map/all_to_all | solution.py:106
  118.5 0.1 fusion.6
  118.6 0.9 fusion.5.gram_ref
  119.5 14.4 %shard_map.49 = (f32[256,256]{1,0:T(8,128)}, f32[256,256]{1,0:T(8,128)}) custom-call(f32[256,256]{1,0:T(8,128)} %fusion.5.gram_ref), custom_call_target="tpu_custom_call" | custom-call | tf_op jit(solution)/shard_map/pallas_call | solution.py:77
  133.9 0.0 all-to-all-done.2
  133.9 1.4 fusion.3
  135.3 0.0 copy-start.1
  135.3 1.6 %fusion.14 = f32[256,256]{1,0:T(8,128)S(1)} fusion(f32[256,256]{1,0:T(8,128)} %get-tuple-element.7, f32[256,256]{1,0:T(8,128)S(1)} %fusion.3), kind=kOutput, calls=%fused_computation.39 | convolution fusion | flops 201326592 | bytes 786432 | tf_op jit(solution)/shard_map/dot_general | solution.py:123
  136.9 1.0 dynamic-slice_multiply_fusion
  137.9 0.7 copy.7
  138.6 6.4 %convolution_subtract_fusion = f32[2048,256]{1,0:T(8,128)} fusion(f32[2048,256]{1,0:T(8,128)} %param.5, f32[2048,256]{0,1:T(8,128)S(1)} %constant_dynamic-update-slice_fusion, s32[]{:T(128)S(6)} %select_n.35, f32[256,256]{1,0:T(8,128)S(1)} %fusion.14), kind=kOutput, calls=%fused_computation | convolution fusion | flops 1611202560 | bytes 6553604 | tf_op jit(solution)/shard_map/dot_general | solution.py:124
  145.0 0.0 copy-done.1
  (20 shorter events, 0.3 us)
Async XLA Ops:
  0.6 66.0 %copy-start.2 = (f32[2048,16]{0,1:T(8,128)S(1)}, f32[2048,16]{0,1:T(8,128)}, u32[]{:S(2)}) copy-start(f32[2048,16]{0,1:T(8,128)} %param.4) | copy-start | bytes 393220
  0.6 15.5 %collective-permute-start = (f32[2048,16]{0,1:T(8,128)}, f32[2048,16]{0,1:T(8,128)S(1)}, u32[]{:S(2)}, u32[]{:S(2)}) collective-permute-start(f32[2048,16]{0,1:T(8,128)} %param.4), channel_id=1, source_target_pairs={{0,1},{1,2},{2,3},{3,4},{4,5},{5,6},{6,7},{7,8},{8,9},{9,10},{10,1... | collective-permute-start | bytes 393224 | tf_op jit(solution)/shard_map/ppermute | solution.py:90
  16.1 6.9 %collective-permute-start.1 = (f32[2048,16]{0,1:T(8,128)S(1)}, f32[2048,16]{0,1:T(8,128)S(1)}, u32[]{:S(2)}, u32[]{:S(2)}) collective-permute-start(f32[2048,16]{0,1:T(8,128)S(1)} %collective-permute-done), channel_id=1, source_target_pairs={{0,1},{1,2},{2,3},{3,4},{4,5},{5,6},{6,7},{7,8},{8,9},{9,10},{10,1... | collective-permute-start | bytes 393224 | tf_op jit(solution)/shard_map/ppermute | solution.py:90
  18.1 6.9 %collective-permute-start.8 = (f32[2048,16]{0,1:T(8,128)}, f32[2048,16]{0,1:T(8,128)S(1)}, u32[]{:S(2)}, u32[]{:S(2)}) collective-permute-start(f32[2048,16]{0,1:T(8,128)} %param.4), channel_id=1, source_target_pairs={{0,15},{1,0},{2,1},{3,2},{4,3},{5,4},{6,5},{7,6},{8,7},{9,8},{10,9... | collective-permute-start | bytes 393224 | tf_op jit(solution)/shard_map/ppermute | solution.py:93
  23.1 6.9 %collective-permute-start.2 = (f32[2048,16]{0,1:T(8,128)S(1)}, f32[2048,16]{0,1:T(8,128)S(1)}, u32[]{:S(2)}, u32[]{:S(2)}) collective-permute-start(f32[2048,16]{0,1:T(8,128)S(1)} %collective-permute-done.1), channel_id=1, source_target_pairs={{0,1},{1,2},{2,3},{3,4},{4,5},{5,6},{6,7},{7,8},{8,9},{9,10},{10,1... | collective-permute-start | bytes 393224 | tf_op jit(solution)/shard_map/ppermute | solution.py:90
  25.0 6.9 %collective-permute-start.9 = (f32[2048,16]{0,1:T(8,128)S(1)}, f32[2048,16]{0,1:T(8,128)S(1)}, u32[]{:S(2)}, u32[]{:S(2)}) collective-permute-start(f32[2048,16]{0,1:T(8,128)S(1)} %collective-permute-done.8), channel_id=1, source_target_pairs={{0,15},{1,0},{2,1},{3,2},{4,3},{5,4},{6,5},{7,6},{8,7},{9,8},{10,9... | collective-permute-start | bytes 393224 | tf_op jit(solution)/shard_map/ppermute | solution.py:93
  30.0 6.9 %collective-permute-start.3 = (f32[2048,16]{0,1:T(8,128)S(1)}, f32[2048,16]{0,1:T(8,128)S(1)}, u32[]{:S(2)}, u32[]{:S(2)}) collective-permute-start(f32[2048,16]{0,1:T(8,128)S(1)} %collective-permute-done.2), channel_id=1, source_target_pairs={{0,1},{1,2},{2,3},{3,4},{4,5},{5,6},{6,7},{7,8},{8,9},{9,10},{10,1... | collective-permute-start | bytes 393224 | tf_op jit(solution)/shard_map/ppermute | solution.py:90
  31.9 6.9 %collective-permute-start.10 = (f32[2048,16]{0,1:T(8,128)S(1)}, f32[2048,16]{0,1:T(8,128)S(1)}, u32[]{:S(2)}, u32[]{:S(2)}) collective-permute-start(f32[2048,16]{0,1:T(8,128)S(1)} %collective-permute-done.9), channel_id=1, source_target_pairs={{0,15},{1,0},{2,1},{3,2},{4,3},{5,4},{6,5},{7,6},{8,7},{9,8},{10,9... | collective-permute-start | bytes 393224 | tf_op jit(solution)/shard_map/ppermute | solution.py:93
  36.9 6.9 %collective-permute-start.4 = (f32[2048,16]{0,1:T(8,128)S(1)}, f32[2048,16]{0,1:T(8,128)S(1)}, u32[]{:S(2)}, u32[]{:S(2)}) collective-permute-start(f32[2048,16]{0,1:T(8,128)S(1)} %collective-permute-done.3), channel_id=1, source_target_pairs={{0,1},{1,2},{2,3},{3,4},{4,5},{5,6},{6,7},{7,8},{8,9},{9,10},{10,1... | collective-permute-start | bytes 393224 | tf_op jit(solution)/shard_map/ppermute | solution.py:90
  38.8 6.9 %collective-permute-start.11 = (f32[2048,16]{0,1:T(8,128)S(1)}, f32[2048,16]{0,1:T(8,128)S(1)}, u32[]{:S(2)}, u32[]{:S(2)}) collective-permute-start(f32[2048,16]{0,1:T(8,128)S(1)} %collective-permute-done.10), channel_id=1, source_target_pairs={{0,15},{1,0},{2,1},{3,2},{4,3},{5,4},{6,5},{7,6},{8,7},{9,8},{10,9... | collective-permute-start | bytes 393224 | tf_op jit(solution)/shard_map/ppermute | solution.py:93
  43.8 6.9 %collective-permute-start.5 = (f32[2048,16]{0,1:T(8,128)S(1)}, f32[2048,16]{0,1:T(8,128)S(1)}, u32[]{:S(2)}, u32[]{:S(2)}) collective-permute-start(f32[2048,16]{0,1:T(8,128)S(1)} %collective-permute-done.4), channel_id=1, source_target_pairs={{0,1},{1,2},{2,3},{3,4},{4,5},{5,6},{6,7},{7,8},{8,9},{9,10},{10,1... | collective-permute-start | bytes 393224 | tf_op jit(solution)/shard_map/ppermute | solution.py:90
  45.7 6.9 %collective-permute-start.12 = (f32[2048,16]{0,1:T(8,128)S(1)}, f32[2048,16]{0,1:T(8,128)S(1)}, u32[]{:S(2)}, u32[]{:S(2)}) collective-permute-start(f32[2048,16]{0,1:T(8,128)S(1)} %collective-permute-done.11), channel_id=1, source_target_pairs={{0,15},{1,0},{2,1},{3,2},{4,3},{5,4},{6,5},{7,6},{8,7},{9,8},{10,9... | collective-permute-start | bytes 393224 | tf_op jit(solution)/shard_map/ppermute | solution.py:93
  50.7 7.7 %collective-permute-start.6 = (f32[2048,16]{0,1:T(8,128)S(1)}, f32[2048,16]{0,1:T(8,128)S(1)}, u32[]{:S(2)}, u32[]{:S(2)}) collective-permute-start(f32[2048,16]{0,1:T(8,128)S(1)} %collective-permute-done.5), channel_id=1, source_target_pairs={{0,1},{1,2},{2,3},{3,4},{4,5},{5,6},{6,7},{7,8},{8,9},{9,10},{10,1... | collective-permute-start | bytes 393224 | tf_op jit(solution)/shard_map/ppermute | solution.py:90
  52.6 7.7 %collective-permute-start.13 = (f32[2048,16]{0,1:T(8,128)S(1)}, f32[2048,16]{0,1:T(8,128)S(1)}, u32[]{:S(2)}, u32[]{:S(2)}) collective-permute-start(f32[2048,16]{0,1:T(8,128)S(1)} %collective-permute-done.12), channel_id=1, source_target_pairs={{0,15},{1,0},{2,1},{3,2},{4,3},{5,4},{6,5},{7,6},{8,7},{9,8},{10,9... | collective-permute-start | bytes 393224 | tf_op jit(solution)/shard_map/ppermute | solution.py:93
  58.4 8.1 %collective-permute-start.7 = (f32[2048,16]{0,1:T(8,128)S(1)}, f32[2048,16]{0,1:T(8,128)S(1)}, u32[]{:S(2)}, u32[]{:S(2)}) collective-permute-start(f32[2048,16]{0,1:T(8,128)S(1)} %collective-permute-done.6), channel_id=1, source_target_pairs={{0,1},{1,2},{2,3},{3,4},{4,5},{5,6},{6,7},{7,8},{8,9},{9,10},{10,1... | collective-permute-start | bytes 393224 | tf_op jit(solution)/shard_map/ppermute | solution.py:90
  60.4 7.5 %collective-permute-start.14 = (f32[2048,16]{0,1:T(8,128)S(1)}, f32[2048,16]{0,1:T(8,128)S(1)}, u32[]{:S(2)}, u32[]{:S(2)}) collective-permute-start(f32[2048,16]{0,1:T(8,128)S(1)} %collective-permute-done.13), channel_id=1, source_target_pairs={{0,15},{1,0},{2,1},{3,2},{4,3},{5,4},{6,5},{7,6},{8,7},{9,8},{10,9... | collective-permute-start | bytes 393224 | tf_op jit(solution)/shard_map/ppermute | solution.py:93
  67.9 1.9 %copy-start = (f32[2048,256]{1,0:T(8,128)S(1)}, f32[2048,256]{1,0:T(8,128)}, u32[]{:S(2)}) copy-start(f32[2048,256]{1,0:T(8,128)} %param.5) | copy-start | bytes 6291460
  114.6 19.3 %all-to-all-start.2 = ((f32[32,8,256]{2,1,0:T(8,128)}), f32[32,8,256]{2,1,0:T(8,128)S(1)}, u32[]{:S(2)}, u32[]{:S(2)}) async-start(f32[32,8,256]{2,1,0:T(8,128)} %broadcast_in_dim.5), calls=%async_computation.2 | async-start | bytes 524288 | tf_op jit(solution)/shard_map/all_to_all | solution.py:106
  135.3 9.7 %copy-start.1 = (f32[256,256]{1,0:T(8,128)}, f32[256,256]{1,0:T(8,128)S(1)}, u32[]{:S(2)}) copy-start(f32[256,256]{1,0:T(8,128)S(1)} %fusion.3) | copy-start | bytes 786436

commit v14 on v11

--- a/solution.py
+++ b/solution.py
@@ -63,7 +63,7 @@
             return following
 
         start = work_ref[first * depth:(first + 1) * depth, lo:hi]
-        lax.fori_loop(first, last, block, start, unroll=2)
+        lax.fori_loop(first, last, block, start, unroll=True)
 
     phase(0, half // depth, 0, n + half)
     phase(half // depth, n // depth, half, 2 * n)

time: 145 us -> 142 us (0.979)
  Pallas kernels: 14.4 us -> 11.9 us
    pallas_call x1, Pallas kernels: 14.4 us -> 11.9 us  [factor(): pl.pallas_call(factor_kernel, out_shape=(jax.ShapeDtypeStruct((n, n), jnp...]
where the time goes in v14:
time: 142 us
  starting transfers between devices  55.2 us (39%)
  blocking collectives  27.8 us (20%)
  waiting for transfers between devices  26.8 us (19%)
  matrix products  14.7 us (10%)
  Pallas kernels  11.9 us (8%)
  other arithmetic  2.13 us (2%)
  local copies, waits for them, and re-layouts  1.95 us (1%)
    ppermute x7, starting transfers between devices, col_gather(): behind = lax.ppermute(behind, 'col', [(i, (i - 1) % n) for i in range(n)])  33.4 us
    all_to_all x1, blocking collectives, row_sum(): mine = lax.all_to_all(parts, 'row', 0, 0, tiled=False).sum(0)  27.8 us
    ppermute x8, starting transfers between devices, col_gather(): ahead = lax.ppermute(ahead, 'col', [(i, (i + 1) % n) for i in range(n)])  17.9 us
    ppermute x8, waiting for transfers between devices, col_gather(): ahead = lax.ppermute(ahead, 'col', [(i, (i + 1) % n) for i in range(n)])  14.3 us
    pallas_call x1, Pallas kernels, factor(): pl.pallas_call(factor_kernel, out_shape=(jax.ShapeDtypeStruct((n, n), jnp...  11.9 us
    all_to_all x1, waiting for transfers between devices, row_sum(): return lax.all_to_all(copies, 'row', 0, 0, tiled=False).reshape(rows, cols)  11.3 us
    dot_general x1, matrix products, per_device(): jnp.dot(gathered, jnp.roll(coefficients, -shift, axis=0), precision=highest)  6.35 us
    all_to_all x1, starting transfers between devices, row_sum(): return lax.all_to_all(copies, 'row', 0, 0, tiled=False).reshape(rows, cols)  3.86 us
  transfers between devices with their start and end apart: 16, of which 10 were waited for; matrix products, arithmetic and copies ran while one was open for 0% of the time, Pallas kernels for 0%

profile of v14, /device:TPU:1, one launch (start us, length us, event | category | flops | bytes accessed | tf_op | source)
XLA Modules:
  0.0 141.6 jit_solution(8383452915413579203)
XLA Ops:
  0.6 0.0 copy-start.2
  0.6 4.5 %collective-permute-start = (f32[2048,16]{0,1:T(8,128)}, f32[2048,16]{0,1:T(8,128)S(1)}, u32[]{:S(2)}, u32[]{:S(2)}) collective-permute-start(f32[2048,16]{0,1:T(8,128)} %param.2), channel_id=1, source_target_pairs={{0,1},{1,2},{2,3},{3,4},{4,5},{5,6},{6,7},{7,8},{8,9},{9,10},{10,1... | collective-permute-start | bytes 393224 | tf_op jit(solution)/shard_map/ppermute | solution.py:90
  5.2 11.0 %collective-permute-done = f32[2048,16]{0,1:T(8,128)S(1)} collective-permute-done((f32[2048,16]{0,1:T(8,128)}, f32[2048,16]{0,1:T(8,128)S(1)}, u32[]{:S(2)}, u32[]{:S(2)}) %collective-permute-start) | collective-permute-done | bytes 131104 | tf_op jit(solution)/shard_map/ppermute | solution.py:90
  16.1 1.9 %collective-permute-start.1 = (f32[2048,16]{0,1:T(8,128)S(1)}, f32[2048,16]{0,1:T(8,128)S(1)}, u32[]{:S(2)}, u32[]{:S(2)}) collective-permute-start(f32[2048,16]{0,1:T(8,128)S(1)} %collective-permute-done), channel_id=1, source_target_pairs={{0,1},{1,2},{2,3},{3,4},{4,5},{5,6},{6,7},{7,8},{8,9},{9,10},{10,1... | collective-permute-start | bytes 393224 | tf_op jit(solution)/shard_map/ppermute | solution.py:90
  18.1 4.6 %collective-permute-start.8 = (f32[2048,16]{0,1:T(8,128)}, f32[2048,16]{0,1:T(8,128)S(1)}, u32[]{:S(2)}, u32[]{:S(2)}) collective-permute-start(f32[2048,16]{0,1:T(8,128)} %param.2), channel_id=1, source_target_pairs={{0,15},{1,0},{2,1},{3,2},{4,3},{5,4},{6,5},{7,6},{8,7},{9,8},{10,9... | collective-permute-start | bytes 393224 | tf_op jit(solution)/shard_map/ppermute | solution.py:93
  22.6 0.4 collective-permute-done.1
  23.1 1.9 %collective-permute-start.2 = (f32[2048,16]{0,1:T(8,128)S(1)}, f32[2048,16]{0,1:T(8,128)S(1)}, u32[]{:S(2)}, u32[]{:S(2)}) collective-permute-start(f32[2048,16]{0,1:T(8,128)S(1)} %collective-permute-done.1), channel_id=1, source_target_pairs={{0,1},{1,2},{2,3},{3,4},{4,5},{5,6},{6,7},{7,8},{8,9},{9,10},{10,1... | collective-permute-start | bytes 393224 | tf_op jit(solution)/shard_map/ppermute | solution.py:90
  25.0 0.0 collective-permute-done.8
  25.0 4.8 %collective-permute-start.9 = (f32[2048,16]{0,1:T(8,128)S(1)}, f32[2048,16]{0,1:T(8,128)S(1)}, u32[]{:S(2)}, u32[]{:S(2)}) collective-permute-start(f32[2048,16]{0,1:T(8,128)S(1)} %collective-permute-done.8), channel_id=1, source_target_pairs={{0,15},{1,0},{2,1},{3,2},{4,3},{5,4},{6,5},{7,6},{8,7},{9,8},{10,9... | collective-permute-start | bytes 393224 | tf_op jit(solution)/shard_map/ppermute | solution.py:93
  29.8 0.2 collective-permute-done.2
  30.0 1.9 %collective-permute-start.3 = (f32[2048,16]{0,1:T(8,128)S(1)}, f32[2048,16]{0,1:T(8,128)S(1)}, u32[]{:S(2)}, u32[]{:S(2)}) collective-permute-start(f32[2048,16]{0,1:T(8,128)S(1)} %collective-permute-done.2), channel_id=1, source_target_pairs={{0,1},{1,2},{2,3},{3,4},{4,5},{5,6},{6,7},{7,8},{8,9},{9,10},{10,1... | collective-permute-start | bytes 393224 | tf_op jit(solution)/shard_map/ppermute | solution.py:90
  31.9 0.0 collective-permute-done.9
  31.9 4.8 %collective-permute-start.10 = (f32[2048,16]{0,1:T(8,128)S(1)}, f32[2048,16]{0,1:T(8,128)S(1)}, u32[]{:S(2)}, u32[]{:S(2)}) collective-permute-start(f32[2048,16]{0,1:T(8,128)S(1)} %collective-permute-done.9), channel_id=1, source_target_pairs={{0,15},{1,0},{2,1},{3,2},{4,3},{5,4},{6,5},{7,6},{8,7},{9,8},{10,9... | collective-permute-start | bytes 393224 | tf_op jit(solution)/shard_map/ppermute | solution.py:93
  36.7 0.2 collective-permute-done.3
  36.9 1.9 %collective-permute-start.4 = (f32[2048,16]{0,1:T(8,128)S(1)}, f32[2048,16]{0,1:T(8,128)S(1)}, u32[]{:S(2)}, u32[]{:S(2)}) collective-permute-start(f32[2048,16]{0,1:T(8,128)S(1)} %collective-permute-done.3), channel_id=1, source_target_pairs={{0,1},{1,2},{2,3},{3,4},{4,5},{5,6},{6,7},{7,8},{8,9},{9,10},{10,1... | collective-permute-start | bytes 393224 | tf_op jit(solution)/shard_map/ppermute | solution.py:90
  38.8 0.0 collective-permute-done.10
  38.8 4.8 %collective-permute-start.11 = (f32[2048,16]{0,1:T(8,128)S(1)}, f32[2048,16]{0,1:T(8,128)S(1)}, u32[]{:S(2)}, u32[]{:S(2)}) collective-permute-start(f32[2048,16]{0,1:T(8,128)S(1)} %collective-permute-done.10), channel_id=1, source_target_pairs={{0,15},{1,0},{2,1},{3,2},{4,3},{5,4},{6,5},{7,6},{8,7},{9,8},{10,9... | collective-permute-start | bytes 393224 | tf_op jit(solution)/shard_map/ppermute | solution.py:93
  43.6 0.2 collective-permute-done.4
  43.8 1.9 %collective-permute-start.5 = (f32[2048,16]{0,1:T(8,128)S(1)}, f32[2048,16]{0,1:T(8,128)S(1)}, u32[]{:S(2)}, u32[]{:S(2)}) collective-permute-start(f32[2048,16]{0,1:T(8,128)S(1)} %collective-permute-done.4), channel_id=1, source_target_pairs={{0,1},{1,2},{2,3},{3,4},{4,5},{5,6},{6,7},{7,8},{8,9},{9,10},{10,1... | collective-permute-start | bytes 393224 | tf_op jit(solution)/shard_map/ppermute | solution.py:90
  45.7 0.0 collective-permute-done.11
  45.7 4.8 %collective-permute-start.12 = (f32[2048,16]{0,1:T(8,128)S(1)}, f32[2048,16]{0,1:T(8,128)S(1)}, u32[]{:S(2)}, u32[]{:S(2)}) collective-permute-start(f32[2048,16]{0,1:T(8,128)S(1)} %collective-permute-done.11), channel_id=1, source_target_pairs={{0,15},{1,0},{2,1},{3,2},{4,3},{5,4},{6,5},{7,6},{8,7},{9,8},{10,9... | collective-permute-start | bytes 393224 | tf_op jit(solution)/shard_map/ppermute | solution.py:93
  50.5 0.2 collective-permute-done.5
  50.7 1.9 %collective-permute-start.6 = (f32[2048,16]{0,1:T(8,128)S(1)}, f32[2048,16]{0,1:T(8,128)S(1)}, u32[]{:S(2)}, u32[]{:S(2)}) collective-permute-start(f32[2048,16]{0,1:T(8,128)S(1)} %collective-permute-done.5), channel_id=1, source_target_pairs={{0,1},{1,2},{2,3},{3,4},{4,5},{5,6},{6,7},{7,8},{8,9},{9,10},{10,1... | collective-permute-start | bytes 393224 | tf_op jit(solution)/shard_map/ppermute | solution.py:90
  52.6 0.0 collective-permute-done.12
  52.6 4.8 %collective-permute-start.13 = (f32[2048,16]{0,1:T(8,128)S(1)}, f32[2048,16]{0,1:T(8,128)S(1)}, u32[]{:S(2)}, u32[]{:S(2)}) collective-permute-start(f32[2048,16]{0,1:T(8,128)S(1)} %collective-permute-done.12), channel_id=1, source_target_pairs={{0,15},{1,0},{2,1},{3,2},{4,3},{5,4},{6,5},{7,6},{8,7},{9,8},{10,9... | collective-permute-start | bytes 393224 | tf_op jit(solution)/shard_map/ppermute | solution.py:93
  57.4 1.0 collective-permute-done.6
  58.4 1.9 %collective-permute-start.7 = (f32[2048,16]{0,1:T(8,128)S(1)}, f32[2048,16]{0,1:T(8,128)S(1)}, u32[]{:S(2)}, u32[]{:S(2)}) collective-permute-start(f32[2048,16]{0,1:T(8,128)S(1)} %collective-permute-done.6), channel_id=1, source_target_pairs={{0,1},{1,2},{2,3},{3,4},{4,5},{5,6},{6,7},{7,8},{8,9},{9,10},{10,1... | collective-permute-start | bytes 393224 | tf_op jit(solution)/shard_map/ppermute | solution.py:90
  60.3 0.0 collective-permute-done.13
  60.4 5.0 %collective-permute-start.14 = (f32[2048,16]{0,1:T(8,128)S(1)}, f32[2048,16]{0,1:T(8,128)S(1)}, u32[]{:S(2)}, u32[]{:S(2)}) collective-permute-start(f32[2048,16]{0,1:T(8,128)S(1)} %collective-permute-done.13), channel_id=1, source_target_pairs={{0,15},{1,0},{2,1},{3,2},{4,3},{5,4},{6,5},{7,6},{8,7},{9,8},{10,9... | collective-permute-start | bytes 393224 | tf_op jit(solution)/shard_map/ppermute | solution.py:93
  65.4 1.1 collective-permute-done.7
  66.6 0.0 copy-done.2
  66.7 1.2 collective-permute-done.14
  67.9 0.0 copy-start
  67.9 1.9 %fusion.8 = f32[256,256]{0,1:T(8,128)S(1)} fusion(f32[2048,256]{0,1:T(8,128)S(1)} %constant_dynamic-update-slice_fusion), kind=kOutput, calls=%fused_computation.32 | convolution fusion | flops 1610612736 | bytes 2359296 | tf_op jit(solution)/shard_map/dot_general | solution.py:112
  69.8 0.0 copy-done
  69.8 3.6 %fusion.9 = f32[256,256]{0,1:T(8,128)S(1)} fusion(f32[2048,256]{0,1:T(8,128)S(1)} %constant_dynamic-update-slice_fusion, f32[2048,256]{1,0:T(8,128)S(1)} %copy-done), kind=kOutput, calls=%fused_computation.33 | convolution fusion | flops 1610612736 | bytes 4456448 | tf_op jit(solution)/shard_map/dot_general | solution.py:111
  73.4 0.2 copy.6
  73.6 27.8 %all_to_all.10 = f32[32,8,512]{2,1,0:T(8,128)S(1)} all-to-all(f32[32,8,512]{2,1,0:T(8,128)S(1)} %bitcast.11), channel_id=1, replica_groups=mesh['row'=32,'col'=16] {'row'}, dimensions={0} | all-to-all | bytes 1048576 | tf_op jit(solution)/shard_map/all_to_all | solution.py:102
  101.4 0.9 broadcast_in_dim.2
  102.3 3.9 %all-to-all-start.1 = ((f32[32,8,512]{2,1,0:T(8,128)}), f32[32,8,512]{2,1,0:T(8,128)S(1)}, u32[]{:S(2)}, u32[]{:S(2)}) async-start(f32[32,8,512]{2,1,0:T(8,128)} %broadcast_in_dim.2), calls=%async_computation.1 | async-start | bytes 1048576 | tf_op jit(solution)/shard_map/all_to_all | solution.py:104
  106.2 11.3 %all-to-all-done.1 = f32[32,8,512]{2,1,0:T(8,128)S(1)} async-done(((f32[32,8,512]{2,1,0:T(8,128)}), f32[32,8,512]{2,1,0:T(8,128)S(1)}, u32[]{:S(2)}, u32[]{:S(2)}) %all-to-all-start.1) | async-done | bytes 524320 | tf_op jit(solution)/shard_map/all_to_all | solution.py:104
  117.6 0.1 fusion
  117.7 0.9 fusion.3.gram_ref
  118.6 11.9 %shard_map.49 = (f32[256,256]{1,0:T(8,128)}, f32[256,256]{1,0:T(8,128)}) custom-call(f32[256,256]{1,0:T(8,128)} %fusion.3.gram_ref), custom_call_target="tpu_custom_call" | custom-call | tf_op jit(solution)/shard_map/pallas_call | solution.py:77
  130.6 1.3 fusion.4
  131.9 0.0 copy-start.1
  131.9 1.6 %fusion.10 = f32[256,256]{1,0:T(8,128)S(1)} fusion(f32[256,256]{1,0:T(8,128)} %get-tuple-element.6, f32[256,256]{1,0:T(8,128)S(1)} %fusion.4), kind=kOutput, calls=%fused_computation.34 | convolution fusion | flops 201326592 | bytes 786432 | tf_op jit(solution)/shard_map/dot_general | solution.py:118
  133.6 1.0 dynamic-slice_multiply_fusion
  134.6 0.7 copy.7
  135.2 6.4 %convolution_subtract_fusion = f32[2048,256]{1,0:T(8,128)} fusion(f32[2048,256]{1,0:T(8,128)} %param.3, f32[2048,256]{0,1:T(8,128)S(1)} %constant_dynamic-update-slice_fusion, s32[]{:T(128)S(6)} %select_n.36, f32[256,256]{1,0:T(8,128)S(1)} %fusion.10), kind=kOutput, calls=%fused_computation | convolution fusion | flops 1611202560 | bytes 6553604 | tf_op jit(solution)/shard_map/dot_general | solution.py:119
  141.6 0.0 copy-done.1
  (19 shorter events, 0.3 us)
Async XLA Ops:
  0.6 66.0 %copy-start.2 = (f32[2048,16]{0,1:T(8,128)S(1)}, f32[2048,16]{0,1:T(8,128)}, u32[]{:S(2)}) copy-start(f32[2048,16]{0,1:T(8,128)} %param.2) | copy-start | bytes 393220
  0.6 15.5 %collective-permute-start = (f32[2048,16]{0,1:T(8,128)}, f32[2048,16]{0,1:T(8,128)S(1)}, u32[]{:S(2)}, u32[]{:S(2)}) collective-permute-start(f32[2048,16]{0,1:T(8,128)} %param.2), channel_id=1, source_target_pairs={{0,1},{1,2},{2,3},{3,4},{4,5},{5,6},{6,7},{7,8},{8,9},{9,10},{10,1... | collective-permute-start | bytes 393224 | tf_op jit(solution)/shard_map/ppermute | solution.py:90
  16.1 6.9 %collective-permute-start.1 = (f32[2048,16]{0,1:T(8,128)S(1)}, f32[2048,16]{0,1:T(8,128)S(1)}, u32[]{:S(2)}, u32[]{:S(2)}) collective-permute-start(f32[2048,16]{0,1:T(8,128)S(1)} %collective-permute-done), channel_id=1, source_target_pairs={{0,1},{1,2},{2,3},{3,4},{4,5},{5,6},{6,7},{7,8},{8,9},{9,10},{10,1... | collective-permute-start | bytes 393224 | tf_op jit(solution)/shard_map/ppermute | solution.py:90
  18.1 6.9 %collective-permute-start.8 = (f32[2048,16]{0,1:T(8,128)}, f32[2048,16]{0,1:T(8,128)S(1)}, u32[]{:S(2)}, u32[]{:S(2)}) collective-permute-start(f32[2048,16]{0,1:T(8,128)} %param.2), channel_id=1, source_target_pairs={{0,15},{1,0},{2,1},{3,2},{4,3},{5,4},{6,5},{7,6},{8,7},{9,8},{10,9... | collective-permute-start | bytes 393224 | tf_op jit(solution)/shard_map/ppermute | solution.py:93
  23.1 6.9 %collective-permute-start.2 = (f32[2048,16]{0,1:T(8,128)S(1)}, f32[2048,16]{0,1:T(8,128)S(1)}, u32[]{:S(2)}, u32[]{:S(2)}) collective-permute-start(f32[2048,16]{0,1:T(8,128)S(1)} %collective-permute-done.1), channel_id=1, source_target_pairs={{0,1},{1,2},{2,3},{3,4},{4,5},{5,6},{6,7},{7,8},{8,9},{9,10},{10,1... | collective-permute-start | bytes 393224 | tf_op jit(solution)/shard_map/ppermute | solution.py:90
  25.0 6.9 %collective-permute-start.9 = (f32[2048,16]{0,1:T(8,128)S(1)}, f32[2048,16]{0,1:T(8,128)S(1)}, u32[]{:S(2)}, u32[]{:S(2)}) collective-permute-start(f32[2048,16]{0,1:T(8,128)S(1)} %collective-permute-done.8), channel_id=1, source_target_pairs={{0,15},{1,0},{2,1},{3,2},{4,3},{5,4},{6,5},{7,6},{8,7},{9,8},{10,9... | collective-permute-start | bytes 393224 | tf_op jit(solution)/shard_map/ppermute | solution.py:93
  30.0 6.9 %collective-permute-start.3 = (f32[2048,16]{0,1:T(8,128)S(1)}, f32[2048,16]{0,1:T(8,128)S(1)}, u32[]{:S(2)}, u32[]{:S(2)}) collective-permute-start(f32[2048,16]{0,1:T(8,128)S(1)} %collective-permute-done.2), channel_id=1, source_target_pairs={{0,1},{1,2},{2,3},{3,4},{4,5},{5,6},{6,7},{7,8},{8,9},{9,10},{10,1... | collective-permute-start | bytes 393224 | tf_op jit(solution)/shard_map/ppermute | solution.py:90
  31.9 6.9 %collective-permute-start.10 = (f32[2048,16]{0,1:T(8,128)S(1)}, f32[2048,16]{0,1:T(8,128)S(1)}, u32[]{:S(2)}, u32[]{:S(2)}) collective-permute-start(f32[2048,16]{0,1:T(8,128)S(1)} %collective-permute-done.9), channel_id=1, source_target_pairs={{0,15},{1,0},{2,1},{3,2},{4,3},{5,4},{6,5},{7,6},{8,7},{9,8},{10,9... | collective-permute-start | bytes 393224 | tf_op jit(solution)/shard_map/ppermute | solution.py:93
  36.9 6.9 %collective-permute-start.4 = (f32[2048,16]{0,1:T(8,128)S(1)}, f32[2048,16]{0,1:T(8,128)S(1)}, u32[]{:S(2)}, u32[]{:S(2)}) collective-permute-start(f32[2048,16]{0,1:T(8,128)S(1)} %collective-permute-done.3), channel_id=1, source_target_pairs={{0,1},{1,2},{2,3},{3,4},{4,5},{5,6},{6,7},{7,8},{8,9},{9,10},{10,1... | collective-permute-start | bytes 393224 | tf_op jit(solution)/shard_map/ppermute | solution.py:90
  38.8 6.9 %collective-permute-start.11 = (f32[2048,16]{0,1:T(8,128)S(1)}, f32[2048,16]{0,1:T(8,128)S(1)}, u32[]{:S(2)}, u32[]{:S(2)}) collective-permute-start(f32[2048,16]{0,1:T(8,128)S(1)} %collective-permute-done.10), channel_id=1, source_target_pairs={{0,15},{1,0},{2,1},{3,2},{4,3},{5,4},{6,5},{7,6},{8,7},{9,8},{10,9... | collective-permute-start | bytes 393224 | tf_op jit(solution)/shard_map/ppermute | solution.py:93
  43.8 6.9 %collective-permute-start.5 = (f32[2048,16]{0,1:T(8,128)S(1)}, f32[2048,16]{0,1:T(8,128)S(1)}, u32[]{:S(2)}, u32[]{:S(2)}) collective-permute-start(f32[2048,16]{0,1:T(8,128)S(1)} %collective-permute-done.4), channel_id=1, source_target_pairs={{0,1},{1,2},{2,3},{3,4},{4,5},{5,6},{6,7},{7,8},{8,9},{9,10},{10,1... | collective-permute-start | bytes 393224 | tf_op jit(solution)/shard_map/ppermute | solution.py:90
  45.7 6.9 %collective-permute-start.12 = (f32[2048,16]{0,1:T(8,128)S(1)}, f32[2048,16]{0,1:T(8,128)S(1)}, u32[]{:S(2)}, u32[]{:S(2)}) collective-permute-start(f32[2048,16]{0,1:T(8,128)S(1)} %collective-permute-done.11), channel_id=1, source_target_pairs={{0,15},{1,0},{2,1},{3,2},{4,3},{5,4},{6,5},{7,6},{8,7},{9,8},{10,9... | collective-permute-start | bytes 393224 | tf_op jit(solution)/shard_map/ppermute | solution.py:93
  50.7 7.7 %collective-permute-start.6 = (f32[2048,16]{0,1:T(8,128)S(1)}, f32[2048,16]{0,1:T(8,128)S(1)}, u32[]{:S(2)}, u32[]{:S(2)}) collective-permute-start(f32[2048,16]{0,1:T(8,128)S(1)} %collective-permute-done.5), channel_id=1, source_target_pairs={{0,1},{1,2},{2,3},{3,4},{4,5},{5,6},{6,7},{7,8},{8,9},{9,10},{10,1... | collective-permute-start | bytes 393224 | tf_op jit(solution)/shard_map/ppermute | solution.py:90
  52.6 7.7 %collective-permute-start.13 = (f32[2048,16]{0,1:T(8,128)S(1)}, f32[2048,16]{0,1:T(8,128)S(1)}, u32[]{:S(2)}, u32[]{:S(2)}) collective-permute-start(f32[2048,16]{0,1:T(8,128)S(1)} %collective-permute-done.12), channel_id=1, source_target_pairs={{0,15},{1,0},{2,1},{3,2},{4,3},{5,4},{6,5},{7,6},{8,7},{9,8},{10,9... | collective-permute-start | bytes 393224 | tf_op jit(solution)/shard_map/ppermute | solution.py:93
  58.4 8.1 %collective-permute-start.7 = (f32[2048,16]{0,1:T(8,128)S(1)}, f32[2048,16]{0,1:T(8,128)S(1)}, u32[]{:S(2)}, u32[]{:S(2)}) collective-permute-start(f32[2048,16]{0,1:T(8,128)S(1)} %collective-permute-done.6), channel_id=1, source_target_pairs={{0,1},{1,2},{2,3},{3,4},{4,5},{5,6},{6,7},{7,8},{8,9},{9,10},{10,1... | collective-permute-start | bytes 393224 | tf_op jit(solution)/shard_map/ppermute | solution.py:90
  60.4 7.5 %collective-permute-start.14 = (f32[2048,16]{0,1:T(8,128)S(1)}, f32[2048,16]{0,1:T(8,128)S(1)}, u32[]{:S(2)}, u32[]{:S(2)}) collective-permute-start(f32[2048,16]{0,1:T(8,128)S(1)} %collective-permute-done.13), channel_id=1, source_target_pairs={{0,15},{1,0},{2,1},{3,2},{4,3},{5,4},{6,5},{7,6},{8,7},{9,8},{10,9... | collective-permute-start | bytes 393224 | tf_op jit(solution)/shard_map/ppermute | solution.py:93
  67.9 1.9 %copy-start = (f32[2048,256]{1,0:T(8,128)S(1)}, f32[2048,256]{1,0:T(8,128)}, u32[]{:S(2)}) copy-start(f32[2048,256]{1,0:T(8,128)} %param.3) | copy-start | bytes 6291460
  102.3 15.3 %all-to-all-start.1 = ((f32[32,8,512]{2,1,0:T(8,128)}), f32[32,8,512]{2,1,0:T(8,128)S(1)}, u32[]{:S(2)}, u32[]{:S(2)}) async-start(f32[32,8,512]{2,1,0:T(8,128)} %broadcast_in_dim.2), calls=%async_computation.1 | async-start | bytes 1048576 | tf_op jit(solution)/shard_map/all_to_all | solution.py:104
  131.9 9.7 %copy-start.1 = (f32[256,256]{1,0:T(8,128)}, f32[256,256]{1,0:T(8,128)S(1)}, u32[]{:S(2)}) copy-start(f32[256,256]{1,0:T(8,128)S(1)} %fusion.4) | copy-start | bytes 786436

commit v15 on v12

--- a/solution.py
+++ b/solution.py
@@ -63,7 +63,7 @@
             return following
 
         start = work_ref[first * depth:(first + 1) * depth, lo:hi]
-        lax.fori_loop(first, last, block, start, unroll=2)
+        lax.fori_loop(first, last, block, start, unroll=True)
 
     phase(0, half // depth, 0, n + half)
     phase(half // depth, n // depth, half, 2 * n)

time: 144 us -> 144 us (level)
  no operation moved by 1% of the time
where the time goes in v15:
time: 144 us; the launch traced here: 143 us
  starting transfers between devices  55.2 us (38%)
  blocking collectives  27.8 us (19%)
  waiting for transfers between devices  26.8 us (19%)
  matrix products  14.7 us (10%)
  Pallas kernels  13.2 us (9%)
  other arithmetic  2.13 us (1%)
  local copies, waits for them, and re-layouts  2.12 us (1%)
    ppermute x7, starting transfers between devices, col_gather(): behind = lax.ppermute(behind, 'col', [(i, (i - 1) % n) for i in range(n)])  33.4 us
    all_to_all x1, blocking collectives, row_sum(): mine = lax.all_to_all(parts, 'row', 0, 0, tiled=False).sum(0)  27.8 us
    ppermute x8, starting transfers between devices, col_gather(): ahead = lax.ppermute(ahead, 'col', [(i, (i + 1) % n) for i in range(n)])  17.9 us
    ppermute x8, waiting for transfers between devices, col_gather(): ahead = lax.ppermute(ahead, 'col', [(i, (i + 1) % n) for i in range(n)])  14.3 us
    pallas_call x1, Pallas kernels, factor(): pl.pallas_call(factor_kernel, out_shape=(jax.ShapeDtypeStruct((n, n), jnp...  13.2 us
    all_to_all x1, waiting for transfers between devices, row_sum(): return lax.all_to_all(copies, 'row', 0, 0, tiled=False).reshape(rows, cols)  11.3 us
    dot_general x1, matrix products, per_device(): jnp.dot(gathered, jnp.roll(coefficients, -shift, axis=0), precision=highest)  6.36 us
    all_to_all x1, starting transfers between devices, row_sum(): return lax.all_to_all(copies, 'row', 0, 0, tiled=False).reshape(rows, cols)  3.86 us
  transfers between devices with their start and end apart: 16, of which 10 were waited for; matrix products, arithmetic and copies ran while one was open for 0% of the time, Pallas kernels for 0%

profile of v15, /device:TPU:1, one launch (start us, length us, event | category | flops | bytes accessed | tf_op | source)
XLA Modules:
  0.0 143.0 jit_solution(18115477260119675400)
XLA Ops:
  0.6 0.0 copy-start.2
  0.6 4.5 %collective-permute-start = (f32[2048,16]{0,1:T(8,128)}, f32[2048,16]{0,1:T(8,128)S(1)}, u32[]{:S(2)}, u32[]{:S(2)}) collective-permute-start(f32[2048,16]{0,1:T(8,128)} %param.2), channel_id=1, source_target_pairs={{0,1},{1,2},{2,3},{3,4},{4,5},{5,6},{6,7},{7,8},{8,9},{9,10},{10,1... | collective-permute-start | bytes 393224 | tf_op jit(solution)/shard_map/ppermute | solution.py:90
  5.2 11.0 %collective-permute-done = f32[2048,16]{0,1:T(8,128)S(1)} collective-permute-done((f32[2048,16]{0,1:T(8,128)}, f32[2048,16]{0,1:T(8,128)S(1)}, u32[]{:S(2)}, u32[]{:S(2)}) %collective-permute-start) | collective-permute-done | bytes 131104 | tf_op jit(solution)/shard_map/ppermute | solution.py:90
  16.1 1.9 %collective-permute-start.1 = (f32[2048,16]{0,1:T(8,128)S(1)}, f32[2048,16]{0,1:T(8,128)S(1)}, u32[]{:S(2)}, u32[]{:S(2)}) collective-permute-start(f32[2048,16]{0,1:T(8,128)S(1)} %collective-permute-done), channel_id=1, source_target_pairs={{0,1},{1,2},{2,3},{3,4},{4,5},{5,6},{6,7},{7,8},{8,9},{9,10},{10,1... | collective-permute-start | bytes 393224 | tf_op jit(solution)/shard_map/ppermute | solution.py:90
  18.1 4.6 %collective-permute-start.8 = (f32[2048,16]{0,1:T(8,128)}, f32[2048,16]{0,1:T(8,128)S(1)}, u32[]{:S(2)}, u32[]{:S(2)}) collective-permute-start(f32[2048,16]{0,1:T(8,128)} %param.2), channel_id=1, source_target_pairs={{0,15},{1,0},{2,1},{3,2},{4,3},{5,4},{6,5},{7,6},{8,7},{9,8},{10,9... | collective-permute-start | bytes 393224 | tf_op jit(solution)/shard_map/ppermute | solution.py:93
  22.6 0.4 collective-permute-done.1
  23.1 1.9 %collective-permute-start.2 = (f32[2048,16]{0,1:T(8,128)S(1)}, f32[2048,16]{0,1:T(8,128)S(1)}, u32[]{:S(2)}, u32[]{:S(2)}) collective-permute-start(f32[2048,16]{0,1:T(8,128)S(1)} %collective-permute-done.1), channel_id=1, source_target_pairs={{0,1},{1,2},{2,3},{3,4},{4,5},{5,6},{6,7},{7,8},{8,9},{9,10},{10,1... | collective-permute-start | bytes 393224 | tf_op jit(solution)/shard_map/ppermute | solution.py:90
  25.0 0.0 collective-permute-done.8
  25.0 4.8 %collective-permute-start.9 = (f32[2048,16]{0,1:T(8,128)S(1)}, f32[2048,16]{0,1:T(8,128)S(1)}, u32[]{:S(2)}, u32[]{:S(2)}) collective-permute-start(f32[2048,16]{0,1:T(8,128)S(1)} %collective-permute-done.8), channel_id=1, source_target_pairs={{0,15},{1,0},{2,1},{3,2},{4,3},{5,4},{6,5},{7,6},{8,7},{9,8},{10,9... | collective-permute-start | bytes 393224 | tf_op jit(solution)/shard_map/ppermute | solution.py:93
  29.8 0.2 collective-permute-done.2
  30.0 1.9 %collective-permute-start.3 = (f32[2048,16]{0,1:T(8,128)S(1)}, f32[2048,16]{0,1:T(8,128)S(1)}, u32[]{:S(2)}, u32[]{:S(2)}) collective-permute-start(f32[2048,16]{0,1:T(8,128)S(1)} %collective-permute-done.2), channel_id=1, source_target_pairs={{0,1},{1,2},{2,3},{3,4},{4,5},{5,6},{6,7},{7,8},{8,9},{9,10},{10,1... | collective-permute-start | bytes 393224 | tf_op jit(solution)/shard_map/ppermute | solution.py:90
  31.9 0.0 collective-permute-done.9
  31.9 4.8 %collective-permute-start.10 = (f32[2048,16]{0,1:T(8,128)S(1)}, f32[2048,16]{0,1:T(8,128)S(1)}, u32[]{:S(2)}, u32[]{:S(2)}) collective-permute-start(f32[2048,16]{0,1:T(8,128)S(1)} %collective-permute-done.9), channel_id=1, source_target_pairs={{0,15},{1,0},{2,1},{3,2},{4,3},{5,4},{6,5},{7,6},{8,7},{9,8},{10,9... | collective-permute-start | bytes 393224 | tf_op jit(solution)/shard_map/ppermute | solution.py:93
  36.7 0.2 collective-permute-done.3
  36.9 1.9 %collective-permute-start.4 = (f32[2048,16]{0,1:T(8,128)S(1)}, f32[2048,16]{0,1:T(8,128)S(1)}, u32[]{:S(2)}, u32[]{:S(2)}) collective-permute-start(f32[2048,16]{0,1:T(8,128)S(1)} %collective-permute-done.3), channel_id=1, source_target_pairs={{0,1},{1,2},{2,3},{3,4},{4,5},{5,6},{6,7},{7,8},{8,9},{9,10},{10,1... | collective-permute-start | bytes 393224 | tf_op jit(solution)/shard_map/ppermute | solution.py:90
  38.8 0.0 collective-permute-done.10
  38.8 4.8 %collective-permute-start.11 = (f32[2048,16]{0,1:T(8,128)S(1)}, f32[2048,16]{0,1:T(8,128)S(1)}, u32[]{:S(2)}, u32[]{:S(2)}) collective-permute-start(f32[2048,16]{0,1:T(8,128)S(1)} %collective-permute-done.10), channel_id=1, source_target_pairs={{0,15},{1,0},{2,1},{3,2},{4,3},{5,4},{6,5},{7,6},{8,7},{9,8},{10,9... | collective-permute-start | bytes 393224 | tf_op jit(solution)/shard_map/ppermute | solution.py:93
  43.6 0.2 collective-permute-done.4
  43.8 1.9 %collective-permute-start.5 = (f32[2048,16]{0,1:T(8,128)S(1)}, f32[2048,16]{0,1:T(8,128)S(1)}, u32[]{:S(2)}, u32[]{:S(2)}) collective-permute-start(f32[2048,16]{0,1:T(8,128)S(1)} %collective-permute-done.4), channel_id=1, source_target_pairs={{0,1},{1,2},{2,3},{3,4},{4,5},{5,6},{6,7},{7,8},{8,9},{9,10},{10,1... | collective-permute-start | bytes 393224 | tf_op jit(solution)/shard_map/ppermute | solution.py:90
  45.7 0.0 collective-permute-done.11
  45.7 4.8 %collective-permute-start.12 = (f32[2048,16]{0,1:T(8,128)S(1)}, f32[2048,16]{0,1:T(8,128)S(1)}, u32[]{:S(2)}, u32[]{:S(2)}) collective-permute-start(f32[2048,16]{0,1:T(8,128)S(1)} %collective-permute-done.11), channel_id=1, source_target_pairs={{0,15},{1,0},{2,1},{3,2},{4,3},{5,4},{6,5},{7,6},{8,7},{9,8},{10,9... | collective-permute-start | bytes 393224 | tf_op jit(solution)/shard_map/ppermute | solution.py:93
  50.5 0.2 collective-permute-done.5
  50.7 1.9 %collective-permute-start.6 = (f32[2048,16]{0,1:T(8,128)S(1)}, f32[2048,16]{0,1:T(8,128)S(1)}, u32[]{:S(2)}, u32[]{:S(2)}) collective-permute-start(f32[2048,16]{0,1:T(8,128)S(1)} %collective-permute-done.5), channel_id=1, source_target_pairs={{0,1},{1,2},{2,3},{3,4},{4,5},{5,6},{6,7},{7,8},{8,9},{9,10},{10,1... | collective-permute-start | bytes 393224 | tf_op jit(solution)/shard_map/ppermute | solution.py:90
  52.6 0.0 collective-permute-done.12
  52.6 4.8 %collective-permute-start.13 = (f32[2048,16]{0,1:T(8,128)S(1)}, f32[2048,16]{0,1:T(8,128)S(1)}, u32[]{:S(2)}, u32[]{:S(2)}) collective-permute-start(f32[2048,16]{0,1:T(8,128)S(1)} %collective-permute-done.12), channel_id=1, source_target_pairs={{0,15},{1,0},{2,1},{3,2},{4,3},{5,4},{6,5},{7,6},{8,7},{9,8},{10,9... | collective-permute-start | bytes 393224 | tf_op jit(solution)/shard_map/ppermute | solution.py:93
  57.4 1.0 collective-permute-done.6
  58.4 1.9 %collective-permute-start.7 = (f32[2048,16]{0,1:T(8,128)S(1)}, f32[2048,16]{0,1:T(8,128)S(1)}, u32[]{:S(2)}, u32[]{:S(2)}) collective-permute-start(f32[2048,16]{0,1:T(8,128)S(1)} %collective-permute-done.6), channel_id=1, source_target_pairs={{0,1},{1,2},{2,3},{3,4},{4,5},{5,6},{6,7},{7,8},{8,9},{9,10},{10,1... | collective-permute-start | bytes 393224 | tf_op jit(solution)/shard_map/ppermute | solution.py:90
  60.3 0.0 collective-permute-done.13
  60.4 5.0 %collective-permute-start.14 = (f32[2048,16]{0,1:T(8,128)S(1)}, f32[2048,16]{0,1:T(8,128)S(1)}, u32[]{:S(2)}, u32[]{:S(2)}) collective-permute-start(f32[2048,16]{0,1:T(8,128)S(1)} %collective-permute-done.13), channel_id=1, source_target_pairs={{0,15},{1,0},{2,1},{3,2},{4,3},{5,4},{6,5},{7,6},{8,7},{9,8},{10,9... | collective-permute-start | bytes 393224 | tf_op jit(solution)/shard_map/ppermute | solution.py:93
  65.4 1.1 collective-permute-done.7
  66.6 0.0 copy-done.2
  66.7 1.2 collective-permute-done.14
  67.9 0.0 copy-start
  67.9 1.9 %fusion.8 = f32[256,256]{0,1:T(8,128)S(1)} fusion(f32[2048,256]{0,1:T(8,128)S(1)} %constant_dynamic-update-slice_fusion), kind=kOutput, calls=%fused_computation.32 | convolution fusion | flops 1610612736 | bytes 2359296 | tf_op jit(solution)/shard_map/dot_general | solution.py:112
  69.8 0.0 copy-done
  69.8 3.6 %fusion.9 = f32[256,256]{0,1:T(8,128)S(1)} fusion(f32[2048,256]{0,1:T(8,128)S(1)} %constant_dynamic-update-slice_fusion, f32[2048,256]{1,0:T(8,128)S(1)} %copy-done), kind=kOutput, calls=%fused_computation.33 | convolution fusion | flops 1610612736 | bytes 4456448 | tf_op jit(solution)/shard_map/dot_general | solution.py:111
  73.4 0.2 copy.6
  73.6 27.8 %all_to_all.10 = f32[32,8,512]{2,1,0:T(8,128)S(1)} all-to-all(f32[32,8,512]{2,1,0:T(8,128)S(1)} %bitcast.11), channel_id=1, replica_groups=mesh['row'=32,'col'=16] {'row'}, dimensions={0} | all-to-all | bytes 1048576 | tf_op jit(solution)/shard_map/all_to_all | solution.py:102
  101.4 0.9 broadcast_in_dim.2
  102.3 3.9 %all-to-all-start.1 = ((f32[32,8,512]{2,1,0:T(8,128)}), f32[32,8,512]{2,1,0:T(8,128)S(1)}, u32[]{:S(2)}, u32[]{:S(2)}) async-start(f32[32,8,512]{2,1,0:T(8,128)} %broadcast_in_dim.2), calls=%async_computation.1 | async-start | bytes 1048576 | tf_op jit(solution)/shard_map/all_to_all | solution.py:104
  106.2 11.3 %all-to-all-done.1 = f32[32,8,512]{2,1,0:T(8,128)S(1)} async-done(((f32[32,8,512]{2,1,0:T(8,128)}), f32[32,8,512]{2,1,0:T(8,128)S(1)}, u32[]{:S(2)}, u32[]{:S(2)}) %all-to-all-start.1) | async-done | bytes 524320 | tf_op jit(solution)/shard_map/all_to_all | solution.py:104
  117.6 0.1 fusion
  117.7 0.9 fusion.3.gram_ref
  118.6 13.2 %shard_map.49 = (f32[256,256]{1,0:T(8,128)}, f32[256,256]{1,0:T(8,128)}) custom-call(f32[256,256]{1,0:T(8,128)} %fusion.3.gram_ref), custom_call_target="tpu_custom_call" | custom-call | tf_op jit(solution)/shard_map/pallas_call | solution.py:77
  131.8 1.3 fusion.4
  133.1 0.0 copy-start.1
  133.2 1.6 %fusion.10 = f32[256,256]{1,0:T(8,128)S(1)} fusion(f32[256,256]{1,0:T(8,128)} %get-tuple-element.6, f32[256,256]{1,0:T(8,128)S(1)} %fusion.4), kind=kOutput, calls=%fused_computation.34 | convolution fusion | flops 201326592 | bytes 786432 | tf_op jit(solution)/shard_map/dot_general | solution.py:118
  134.8 1.0 dynamic-slice_multiply_fusion
  135.8 0.9 copy.7
  136.7 6.4 %convolution_subtract_fusion = f32[2048,256]{1,0:T(8,128)} fusion(f32[2048,256]{1,0:T(8,128)} %param.3, f32[2048,256]{0,1:T(8,128)S(1)} %constant_dynamic-update-slice_fusion, s32[]{:T(128)S(6)} %select_n.36, f32[256,256]{1,0:T(8,128)S(1)} %fusion.10), kind=kOutput, calls=%fused_computation | convolution fusion | flops 1611202560 | bytes 6553604 | tf_op jit(solution)/shard_map/dot_general | solution.py:119
  143.0 0.0 copy-done.1
  (19 shorter events, 0.3 us)
Async XLA Ops:
  0.6 66.0 %copy-start.2 = (f32[2048,16]{0,1:T(8,128)S(1)}, f32[2048,16]{0,1:T(8,128)}, u32[]{:S(2)}) copy-start(f32[2048,16]{0,1:T(8,128)} %param.2) | copy-start | bytes 393220
  0.6 15.5 %collective-permute-start = (f32[2048,16]{0,1:T(8,128)}, f32[2048,16]{0,1:T(8,128)S(1)}, u32[]{:S(2)}, u32[]{:S(2)}) collective-permute-start(f32[2048,16]{0,1:T(8,128)} %param.2), channel_id=1, source_target_pairs={{0,1},{1,2},{2,3},{3,4},{4,5},{5,6},{6,7},{7,8},{8,9},{9,10},{10,1... | collective-permute-start | bytes 393224 | tf_op jit(solution)/shard_map/ppermute | solution.py:90
  16.1 6.9 %collective-permute-start.1 = (f32[2048,16]{0,1:T(8,128)S(1)}, f32[2048,16]{0,1:T(8,128)S(1)}, u32[]{:S(2)}, u32[]{:S(2)}) collective-permute-start(f32[2048,16]{0,1:T(8,128)S(1)} %collective-permute-done), channel_id=1, source_target_pairs={{0,1},{1,2},{2,3},{3,4},{4,5},{5,6},{6,7},{7,8},{8,9},{9,10},{10,1... | collective-permute-start | bytes 393224 | tf_op jit(solution)/shard_map/ppermute | solution.py:90
  18.1 6.9 %collective-permute-start.8 = (f32[2048,16]{0,1:T(8,128)}, f32[2048,16]{0,1:T(8,128)S(1)}, u32[]{:S(2)}, u32[]{:S(2)}) collective-permute-start(f32[2048,16]{0,1:T(8,128)} %param.2), channel_id=1, source_target_pairs={{0,15},{1,0},{2,1},{3,2},{4,3},{5,4},{6,5},{7,6},{8,7},{9,8},{10,9... | collective-permute-start | bytes 393224 | tf_op jit(solution)/shard_map/ppermute | solution.py:93
  23.1 6.9 %collective-permute-start.2 = (f32[2048,16]{0,1:T(8,128)S(1)}, f32[2048,16]{0,1:T(8,128)S(1)}, u32[]{:S(2)}, u32[]{:S(2)}) collective-permute-start(f32[2048,16]{0,1:T(8,128)S(1)} %collective-permute-done.1), channel_id=1, source_target_pairs={{0,1},{1,2},{2,3},{3,4},{4,5},{5,6},{6,7},{7,8},{8,9},{9,10},{10,1... | collective-permute-start | bytes 393224 | tf_op jit(solution)/shard_map/ppermute | solution.py:90
  25.0 6.9 %collective-permute-start.9 = (f32[2048,16]{0,1:T(8,128)S(1)}, f32[2048,16]{0,1:T(8,128)S(1)}, u32[]{:S(2)}, u32[]{:S(2)}) collective-permute-start(f32[2048,16]{0,1:T(8,128)S(1)} %collective-permute-done.8), channel_id=1, source_target_pairs={{0,15},{1,0},{2,1},{3,2},{4,3},{5,4},{6,5},{7,6},{8,7},{9,8},{10,9... | collective-permute-start | bytes 393224 | tf_op jit(solution)/shard_map/ppermute | solution.py:93
  30.0 6.9 %collective-permute-start.3 = (f32[2048,16]{0,1:T(8,128)S(1)}, f32[2048,16]{0,1:T(8,128)S(1)}, u32[]{:S(2)}, u32[]{:S(2)}) collective-permute-start(f32[2048,16]{0,1:T(8,128)S(1)} %collective-permute-done.2), channel_id=1, source_target_pairs={{0,1},{1,2},{2,3},{3,4},{4,5},{5,6},{6,7},{7,8},{8,9},{9,10},{10,1... | collective-permute-start | bytes 393224 | tf_op jit(solution)/shard_map/ppermute | solution.py:90
  31.9 6.9 %collective-permute-start.10 = (f32[2048,16]{0,1:T(8,128)S(1)}, f32[2048,16]{0,1:T(8,128)S(1)}, u32[]{:S(2)}, u32[]{:S(2)}) collective-permute-start(f32[2048,16]{0,1:T(8,128)S(1)} %collective-permute-done.9), channel_id=1, source_target_pairs={{0,15},{1,0},{2,1},{3,2},{4,3},{5,4},{6,5},{7,6},{8,7},{9,8},{10,9... | collective-permute-start | bytes 393224 | tf_op jit(solution)/shard_map/ppermute | solution.py:93
  36.9 6.9 %collective-permute-start.4 = (f32[2048,16]{0,1:T(8,128)S(1)}, f32[2048,16]{0,1:T(8,128)S(1)}, u32[]{:S(2)}, u32[]{:S(2)}) collective-permute-start(f32[2048,16]{0,1:T(8,128)S(1)} %collective-permute-done.3), channel_id=1, source_target_pairs={{0,1},{1,2},{2,3},{3,4},{4,5},{5,6},{6,7},{7,8},{8,9},{9,10},{10,1... | collective-permute-start | bytes 393224 | tf_op jit(solution)/shard_map/ppermute | solution.py:90
  38.8 6.9 %collective-permute-start.11 = (f32[2048,16]{0,1:T(8,128)S(1)}, f32[2048,16]{0,1:T(8,128)S(1)}, u32[]{:S(2)}, u32[]{:S(2)}) collective-permute-start(f32[2048,16]{0,1:T(8,128)S(1)} %collective-permute-done.10), channel_id=1, source_target_pairs={{0,15},{1,0},{2,1},{3,2},{4,3},{5,4},{6,5},{7,6},{8,7},{9,8},{10,9... | collective-permute-start | bytes 393224 | tf_op jit(solution)/shard_map/ppermute | solution.py:93
  43.8 6.9 %collective-permute-start.5 = (f32[2048,16]{0,1:T(8,128)S(1)}, f32[2048,16]{0,1:T(8,128)S(1)}, u32[]{:S(2)}, u32[]{:S(2)}) collective-permute-start(f32[2048,16]{0,1:T(8,128)S(1)} %collective-permute-done.4), channel_id=1, source_target_pairs={{0,1},{1,2},{2,3},{3,4},{4,5},{5,6},{6,7},{7,8},{8,9},{9,10},{10,1... | collective-permute-start | bytes 393224 | tf_op jit(solution)/shard_map/ppermute | solution.py:90
  45.7 6.9 %collective-permute-start.12 = (f32[2048,16]{0,1:T(8,128)S(1)}, f32[2048,16]{0,1:T(8,128)S(1)}, u32[]{:S(2)}, u32[]{:S(2)}) collective-permute-start(f32[2048,16]{0,1:T(8,128)S(1)} %collective-permute-done.11), channel_id=1, source_target_pairs={{0,15},{1,0},{2,1},{3,2},{4,3},{5,4},{6,5},{7,6},{8,7},{9,8},{10,9... | collective-permute-start | bytes 393224 | tf_op jit(solution)/shard_map/ppermute | solution.py:93
  50.7 7.7 %collective-permute-start.6 = (f32[2048,16]{0,1:T(8,128)S(1)}, f32[2048,16]{0,1:T(8,128)S(1)}, u32[]{:S(2)}, u32[]{:S(2)}) collective-permute-start(f32[2048,16]{0,1:T(8,128)S(1)} %collective-permute-done.5), channel_id=1, source_target_pairs={{0,1},{1,2},{2,3},{3,4},{4,5},{5,6},{6,7},{7,8},{8,9},{9,10},{10,1... | collective-permute-start | bytes 393224 | tf_op jit(solution)/shard_map/ppermute | solution.py:90
  52.6 7.7 %collective-permute-start.13 = (f32[2048,16]{0,1:T(8,128)S(1)}, f32[2048,16]{0,1:T(8,128)S(1)}, u32[]{:S(2)}, u32[]{:S(2)}) collective-permute-start(f32[2048,16]{0,1:T(8,128)S(1)} %collective-permute-done.12), channel_id=1, source_target_pairs={{0,15},{1,0},{2,1},{3,2},{4,3},{5,4},{6,5},{7,6},{8,7},{9,8},{10,9... | collective-permute-start | bytes 393224 | tf_op jit(solution)/shard_map/ppermute | solution.py:93
  58.4 8.1 %collective-permute-start.7 = (f32[2048,16]{0,1:T(8,128)S(1)}, f32[2048,16]{0,1:T(8,128)S(1)}, u32[]{:S(2)}, u32[]{:S(2)}) collective-permute-start(f32[2048,16]{0,1:T(8,128)S(1)} %collective-permute-done.6), channel_id=1, source_target_pairs={{0,1},{1,2},{2,3},{3,4},{4,5},{5,6},{6,7},{7,8},{8,9},{9,10},{10,1... | collective-permute-start | bytes 393224 | tf_op jit(solution)/shard_map/ppermute | solution.py:90
  60.4 7.5 %collective-permute-start.14 = (f32[2048,16]{0,1:T(8,128)S(1)}, f32[2048,16]{0,1:T(8,128)S(1)}, u32[]{:S(2)}, u32[]{:S(2)}) collective-permute-start(f32[2048,16]{0,1:T(8,128)S(1)} %collective-permute-done.13), channel_id=1, source_target_pairs={{0,15},{1,0},{2,1},{3,2},{4,3},{5,4},{6,5},{7,6},{8,7},{9,8},{10,9... | collective-permute-start | bytes 393224 | tf_op jit(solution)/shard_map/ppermute | solution.py:93
  67.9 1.9 %copy-start = (f32[2048,256]{1,0:T(8,128)S(1)}, f32[2048,256]{1,0:T(8,128)}, u32[]{:S(2)}) copy-start(f32[2048,256]{1,0:T(8,128)} %param.3) | copy-start | bytes 6291460
  102.3 15.3 %all-to-all-start.1 = ((f32[32,8,512]{2,1,0:T(8,128)}), f32[32,8,512]{2,1,0:T(8,128)S(1)}, u32[]{:S(2)}, u32[]{:S(2)}) async-start(f32[32,8,512]{2,1,0:T(8,128)} %broadcast_in_dim.2), calls=%async_computation.1 | async-start | bytes 1048576 | tf_op jit(solution)/shard_map/all_to_all | solution.py:104
  133.1 9.9 %copy-start.1 = (f32[256,256]{1,0:T(8,128)}, f32[256,256]{1,0:T(8,128)S(1)}, u32[]{:S(2)}) copy-start(f32[256,256]{1,0:T(8,128)S(1)} %fusion.4) | copy-start | bytes 786436

commit v16 on v14

--- a/solution.py
+++ b/solution.py
@@ -1,3 +1,4 @@
+import functools
 import math
 
 import jax
@@ -11,7 +12,8 @@
 HIGHEST = lax.Precision.HIGHEST
 
 
-def factor_kernel(gram_ref, upper_ref, inverse_ref, work_ref, left_ref):
+def factor_kernel(gram_ref, cross_ref, upper_ref, projected_ref, coefficients_ref, work_ref, left_ref,
+                  *, rows_total):
     n = gram_ref.shape[0]
     rows = lax.broadcasted_iota(jnp.int32, (n, n), 0)
     cols = lax.broadcasted_iota(jnp.int32, (n, n), 1)
@@ -68,19 +70,26 @@
     phase(0, half // depth, 0, n + half)
     phase(half // depth, n // depth, half, 2 * n)
     done = work_ref[...]
-    upper_ref[...] = jnp.where(cols >= rows, done[:, :n], 0.0)
-    inverse_ref[...] = jnp.where(cols <= rows, done[:, n:], 0.0)
+    upper_ref[...] = jnp.where(cols >= rows, done[:, :n], 0.0) * (1.0 / math.sqrt(rows_total))
+    inverse = jnp.where(cols <= rows, done[:, n:], 0.0)
+    projected = jnp.dot(inverse, cross_ref[...], precision=HIGHEST,
+                        preferred_element_type=jnp.float32)
+    projected_ref[...] = projected
+    coefficients_ref[...] = lax.dot_general(inverse, projected, contract_rows, precision=HIGHEST,
+                                            preferred_element_type=jnp.float32)
 
 
-def factor(gram):
+def factor(gram, cross, rows_total):
     n = gram.shape[0]
     return pl.pallas_call(
-        factor_kernel,
-        out_shape=(jax.ShapeDtypeStruct((n, n), jnp.float32),) * 2,
-        in_specs=[pl.BlockSpec(memory_space=pltpu.VMEM)],
-        out_specs=(pl.BlockSpec(memory_space=pltpu.VMEM),) * 2,
+        functools.partial(factor_kernel, rows_total=rows_total),
+        out_shape=(jax.ShapeDtypeStruct((n, n), jnp.float32),
+                   jax.ShapeDtypeStruct(cross.shape, jnp.float32),
+                   jax.ShapeDtypeStruct(cross.shape, jnp.float32)),
+        in_specs=[pl.BlockSpec(memory_space=pltpu.VMEM)] * 2,
+        out_specs=(pl.BlockSpec(memory_space=pltpu.VMEM),) * 3,
         scratch_shapes=[pltpu.VMEM((n, 2 * n), jnp.float32), pltpu.VMEM((n, 16), jnp.float32)],
-    )(gram)
+    )(gram, cross)
 
 def col_gather(x):
     n = lax.axis_size("col")
@@ -113,13 +122,10 @@
     width = gram_local.shape[1]
     summed = jnp.roll(row_sum(jnp.concatenate([gram_local, cross_local], axis=1)), shift, axis=0)
     gram_total, totals = jnp.roll(summed[:, :width], shift, axis=1), summed[:, width:]
-    upper_factor, lower_inverse = factor(gram_total)
-    projected = jnp.dot(lower_inverse, totals, precision=highest)
-    coefficients = lax.dot_general(lower_inverse, projected, contract_rows, precision=highest)
+    rows_total = gathered.shape[0] * lax.axis_size("row")
+    scaled, projected, coefficients = factor(gram_total, totals, rows_total)
     residual = slab - jnp.dot(gathered, jnp.roll(coefficients, -shift, axis=0), precision=highest)
     col_width = panel.shape[1]
-    rows_total = gathered.shape[0] * lax.axis_size("row")
-    scaled = upper_factor * (1.0 / math.sqrt(rows_total))
     triangle = lax.dynamic_slice_in_dim(scaled, lax.axis_index("col") * col_width, col_width, 1)
     return (triangle, projected, residual)
 

time: 142 us -> 141 us (level)
  matrix products: 14.7 us -> 11.9 us
  local copies, waits for them, and re-layouts: 1.95 us -> 3.66 us
    dot_general x2 -> x0, matrix products: 2.97 us -> none  [the longest x1 1.64 us: per_device(): lax.dot_general(lower_inverse, projected, contract_rows, precision=highest)]
where the time goes in v16:
time: 141 us; the launch traced here: 140 us
  starting transfers between devices  55.2 us (39%)
  blocking collectives  27.8 us (20%)
  waiting for transfers between devices  26.8 us (19%)
  Pallas kernels  12.9 us (9%)
  matrix products  11.9 us (8%)
  local copies, waits for them, and re-layouts  3.66 us (3%)
    ppermute x7, starting transfers between devices, col_gather(): behind = lax.ppermute(behind, 'col', [(i, (i - 1) % n) for i in range(n)])  33.4 us
    all_to_all x1, blocking collectives, row_sum(): mine = lax.all_to_all(parts, 'row', 0, 0, tiled=False).sum(0)  27.8 us
    ppermute x8, starting transfers between devices, col_gather(): ahead = lax.ppermute(ahead, 'col', [(i, (i + 1) % n) for i in range(n)])  17.9 us
    ppermute x8, waiting for transfers between devices, col_gather(): ahead = lax.ppermute(ahead, 'col', [(i, (i + 1) % n) for i in range(n)])  14.3 us
    pallas_call x1, Pallas kernels, factor(): pl.pallas_call(functools.partial(factor_kernel, rows_total=rows_total), o...  12.9 us
    all_to_all x1, waiting for transfers between devices, row_sum(): return lax.all_to_all(copies, 'row', 0, 0, tiled=False).reshape(rows, cols)  11.3 us
    dot_general x1, matrix products, per_device(): jnp.dot(gathered, jnp.roll(coefficients, -shift, axis=0), precision=highest)  6.51 us
    all_to_all x1, starting transfers between devices, row_sum(): return lax.all_to_all(copies, 'row', 0, 0, tiled=False).reshape(rows, cols)  3.86 us
  transfers between devices with their start and end apart: 16, of which 10 were waited for; matrix products, arithmetic and copies ran while one was open for 0% of the time, Pallas kernels for 0%

profile of v16, /device:TPU:1, one launch (start us, length us, event | category | flops | bytes accessed | tf_op | source)
XLA Modules:
  0.0 140.4 jit_solution(12570100783233233048)
XLA Ops:
  0.6 0.0 copy-start.1
  0.6 4.5 %collective-permute-start = (f32[2048,16]{0,1:T(8,128)}, f32[2048,16]{0,1:T(8,128)S(1)}, u32[]{:S(2)}, u32[]{:S(2)}) collective-permute-start(f32[2048,16]{0,1:T(8,128)} %param.2), channel_id=1, source_target_pairs={{0,1},{1,2},{2,3},{3,4},{4,5},{5,6},{6,7},{7,8},{8,9},{9,10},{10,1... | collective-permute-start | bytes 393224 | tf_op jit(solution)/shard_map/ppermute | solution.py:99
  5.2 11.0 %collective-permute-done = f32[2048,16]{0,1:T(8,128)S(1)} collective-permute-done((f32[2048,16]{0,1:T(8,128)}, f32[2048,16]{0,1:T(8,128)S(1)}, u32[]{:S(2)}, u32[]{:S(2)}) %collective-permute-start) | collective-permute-done | bytes 131104 | tf_op jit(solution)/shard_map/ppermute | solution.py:99
  16.1 1.9 %collective-permute-start.1 = (f32[2048,16]{0,1:T(8,128)S(1)}, f32[2048,16]{0,1:T(8,128)S(1)}, u32[]{:S(2)}, u32[]{:S(2)}) collective-permute-start(f32[2048,16]{0,1:T(8,128)S(1)} %collective-permute-done), channel_id=1, source_target_pairs={{0,1},{1,2},{2,3},{3,4},{4,5},{5,6},{6,7},{7,8},{8,9},{9,10},{10,1... | collective-permute-start | bytes 393224 | tf_op jit(solution)/shard_map/ppermute | solution.py:99
  18.1 4.6 %collective-permute-start.8 = (f32[2048,16]{0,1:T(8,128)}, f32[2048,16]{0,1:T(8,128)S(1)}, u32[]{:S(2)}, u32[]{:S(2)}) collective-permute-start(f32[2048,16]{0,1:T(8,128)} %param.2), channel_id=1, source_target_pairs={{0,15},{1,0},{2,1},{3,2},{4,3},{5,4},{6,5},{7,6},{8,7},{9,8},{10,9... | collective-permute-start | bytes 393224 | tf_op jit(solution)/shard_map/ppermute | solution.py:102
  22.6 0.4 collective-permute-done.1
  23.1 1.9 %collective-permute-start.2 = (f32[2048,16]{0,1:T(8,128)S(1)}, f32[2048,16]{0,1:T(8,128)S(1)}, u32[]{:S(2)}, u32[]{:S(2)}) collective-permute-start(f32[2048,16]{0,1:T(8,128)S(1)} %collective-permute-done.1), channel_id=1, source_target_pairs={{0,1},{1,2},{2,3},{3,4},{4,5},{5,6},{6,7},{7,8},{8,9},{9,10},{10,1... | collective-permute-start | bytes 393224 | tf_op jit(solution)/shard_map/ppermute | solution.py:99
  25.0 0.0 collective-permute-done.8
  25.0 4.8 %collective-permute-start.9 = (f32[2048,16]{0,1:T(8,128)S(1)}, f32[2048,16]{0,1:T(8,128)S(1)}, u32[]{:S(2)}, u32[]{:S(2)}) collective-permute-start(f32[2048,16]{0,1:T(8,128)S(1)} %collective-permute-done.8), channel_id=1, source_target_pairs={{0,15},{1,0},{2,1},{3,2},{4,3},{5,4},{6,5},{7,6},{8,7},{9,8},{10,9... | collective-permute-start | bytes 393224 | tf_op jit(solution)/shard_map/ppermute | solution.py:102
  29.8 0.2 collective-permute-done.2
  30.0 1.9 %collective-permute-start.3 = (f32[2048,16]{0,1:T(8,128)S(1)}, f32[2048,16]{0,1:T(8,128)S(1)}, u32[]{:S(2)}, u32[]{:S(2)}) collective-permute-start(f32[2048,16]{0,1:T(8,128)S(1)} %collective-permute-done.2), channel_id=1, source_target_pairs={{0,1},{1,2},{2,3},{3,4},{4,5},{5,6},{6,7},{7,8},{8,9},{9,10},{10,1... | collective-permute-start | bytes 393224 | tf_op jit(solution)/shard_map/ppermute | solution.py:99
  31.9 0.0 collective-permute-done.9
  31.9 4.8 %collective-permute-start.10 = (f32[2048,16]{0,1:T(8,128)S(1)}, f32[2048,16]{0,1:T(8,128)S(1)}, u32[]{:S(2)}, u32[]{:S(2)}) collective-permute-start(f32[2048,16]{0,1:T(8,128)S(1)} %collective-permute-done.9), channel_id=1, source_target_pairs={{0,15},{1,0},{2,1},{3,2},{4,3},{5,4},{6,5},{7,6},{8,7},{9,8},{10,9... | collective-permute-start | bytes 393224 | tf_op jit(solution)/shard_map/ppermute | solution.py:102
  36.7 0.2 collective-permute-done.3
  36.9 1.9 %collective-permute-start.4 = (f32[2048,16]{0,1:T(8,128)S(1)}, f32[2048,16]{0,1:T(8,128)S(1)}, u32[]{:S(2)}, u32[]{:S(2)}) collective-permute-start(f32[2048,16]{0,1:T(8,128)S(1)} %collective-permute-done.3), channel_id=1, source_target_pairs={{0,1},{1,2},{2,3},{3,4},{4,5},{5,6},{6,7},{7,8},{8,9},{9,10},{10,1... | collective-permute-start | bytes 393224 | tf_op jit(solution)/shard_map/ppermute | solution.py:99
  38.8 0.0 collective-permute-done.10
  38.8 4.8 %collective-permute-start.11 = (f32[2048,16]{0,1:T(8,128)S(1)}, f32[2048,16]{0,1:T(8,128)S(1)}, u32[]{:S(2)}, u32[]{:S(2)}) collective-permute-start(f32[2048,16]{0,1:T(8,128)S(1)} %collective-permute-done.10), channel_id=1, source_target_pairs={{0,15},{1,0},{2,1},{3,2},{4,3},{5,4},{6,5},{7,6},{8,7},{9,8},{10,9... | collective-permute-start | bytes 393224 | tf_op jit(solution)/shard_map/ppermute | solution.py:102
  43.6 0.2 collective-permute-done.4
  43.8 1.9 %collective-permute-start.5 = (f32[2048,16]{0,1:T(8,128)S(1)}, f32[2048,16]{0,1:T(8,128)S(1)}, u32[]{:S(2)}, u32[]{:S(2)}) collective-permute-start(f32[2048,16]{0,1:T(8,128)S(1)} %collective-permute-done.4), channel_id=1, source_target_pairs={{0,1},{1,2},{2,3},{3,4},{4,5},{5,6},{6,7},{7,8},{8,9},{9,10},{10,1... | collective-permute-start | bytes 393224 | tf_op jit(solution)/shard_map/ppermute | solution.py:99
  45.7 0.0 collective-permute-done.11
  45.7 4.8 %collective-permute-start.12 = (f32[2048,16]{0,1:T(8,128)S(1)}, f32[2048,16]{0,1:T(8,128)S(1)}, u32[]{:S(2)}, u32[]{:S(2)}) collective-permute-start(f32[2048,16]{0,1:T(8,128)S(1)} %collective-permute-done.11), channel_id=1, source_target_pairs={{0,15},{1,0},{2,1},{3,2},{4,3},{5,4},{6,5},{7,6},{8,7},{9,8},{10,9... | collective-permute-start | bytes 393224 | tf_op jit(solution)/shard_map/ppermute | solution.py:102
  50.5 0.2 collective-permute-done.5
  50.7 1.9 %collective-permute-start.6 = (f32[2048,16]{0,1:T(8,128)S(1)}, f32[2048,16]{0,1:T(8,128)S(1)}, u32[]{:S(2)}, u32[]{:S(2)}) collective-permute-start(f32[2048,16]{0,1:T(8,128)S(1)} %collective-permute-done.5), channel_id=1, source_target_pairs={{0,1},{1,2},{2,3},{3,4},{4,5},{5,6},{6,7},{7,8},{8,9},{9,10},{10,1... | collective-permute-start | bytes 393224 | tf_op jit(solution)/shard_map/ppermute | solution.py:99
  52.6 0.0 collective-permute-done.12
  52.6 4.8 %collective-permute-start.13 = (f32[2048,16]{0,1:T(8,128)S(1)}, f32[2048,16]{0,1:T(8,128)S(1)}, u32[]{:S(2)}, u32[]{:S(2)}) collective-permute-start(f32[2048,16]{0,1:T(8,128)S(1)} %collective-permute-done.12), channel_id=1, source_target_pairs={{0,15},{1,0},{2,1},{3,2},{4,3},{5,4},{6,5},{7,6},{8,7},{9,8},{10,9... | collective-permute-start | bytes 393224 | tf_op jit(solution)/shard_map/ppermute | solution.py:102
  57.4 1.0 collective-permute-done.6
  58.4 1.9 %collective-permute-start.7 = (f32[2048,16]{0,1:T(8,128)S(1)}, f32[2048,16]{0,1:T(8,128)S(1)}, u32[]{:S(2)}, u32[]{:S(2)}) collective-permute-start(f32[2048,16]{0,1:T(8,128)S(1)} %collective-permute-done.6), channel_id=1, source_target_pairs={{0,1},{1,2},{2,3},{3,4},{4,5},{5,6},{6,7},{7,8},{8,9},{9,10},{10,1... | collective-permute-start | bytes 393224 | tf_op jit(solution)/shard_map/ppermute | solution.py:99
  60.3 0.0 collective-permute-done.13
  60.4 5.0 %collective-permute-start.14 = (f32[2048,16]{0,1:T(8,128)S(1)}, f32[2048,16]{0,1:T(8,128)S(1)}, u32[]{:S(2)}, u32[]{:S(2)}) collective-permute-start(f32[2048,16]{0,1:T(8,128)S(1)} %collective-permute-done.13), channel_id=1, source_target_pairs={{0,15},{1,0},{2,1},{3,2},{4,3},{5,4},{6,5},{7,6},{8,7},{9,8},{10,9... | collective-permute-start | bytes 393224 | tf_op jit(solution)/shard_map/ppermute | solution.py:102
  65.4 1.1 collective-permute-done.7
  66.6 0.0 copy-done.1
  66.7 1.2 collective-permute-done.14
  67.9 0.0 copy-start
  67.9 1.9 %fusion.7 = f32[256,256]{0,1:T(8,128)S(1)} fusion(f32[2048,256]{0,1:T(8,128)S(1)} %constant_dynamic-update-slice_fusion), kind=kOutput, calls=%fused_computation.31 | convolution fusion | flops 1610612736 | bytes 2359296 | tf_op jit(solution)/shard_map/dot_general | solution.py:121
  69.8 0.0 copy-done
  69.8 3.6 %fusion.8 = f32[256,256]{0,1:T(8,128)S(1)} fusion(f32[2048,256]{0,1:T(8,128)S(1)} %constant_dynamic-update-slice_fusion, f32[2048,256]{1,0:T(8,128)S(1)} %copy-done), kind=kOutput, calls=%fused_computation.32 | convolution fusion | flops 1610612736 | bytes 4456448 | tf_op jit(solution)/shard_map/dot_general | solution.py:120
  73.4 0.2 copy.6
  73.6 27.8 %all_to_all.10 = f32[32,8,512]{2,1,0:T(8,128)S(1)} all-to-all(f32[32,8,512]{2,1,0:T(8,128)S(1)} %bitcast.8), channel_id=1, replica_groups=mesh['row'=32,'col'=16] {'row'}, dimensions={0} | all-to-all | bytes 1048576 | tf_op jit(solution)/shard_map/all_to_all | solution.py:111
  101.4 0.9 broadcast_in_dim.2
  102.3 3.9 %all-to-all-start.1 = ((f32[32,8,512]{2,1,0:T(8,128)}), f32[32,8,512]{2,1,0:T(8,128)S(1)}, u32[]{:S(2)}, u32[]{:S(2)}) async-start(f32[32,8,512]{2,1,0:T(8,128)} %broadcast_in_dim.2), calls=%async_computation.1 | async-start | bytes 1048576 | tf_op jit(solution)/shard_map/all_to_all | solution.py:113
  106.2 11.3 %all-to-all-done.1 = f32[32,8,512]{2,1,0:T(8,128)S(1)} async-done(((f32[32,8,512]{2,1,0:T(8,128)}), f32[32,8,512]{2,1,0:T(8,128)S(1)}, u32[]{:S(2)}, u32[]{:S(2)}) %all-to-all-start.1) | async-done | bytes 524320 | tf_op jit(solution)/shard_map/all_to_all | solution.py:113
  117.6 0.1 fusion
  117.7 0.7 fusion.6
  118.4 0.9 fusion.3.gram_ref
  119.3 12.9 %shard_map.49 = (f32[256,256]{1,0:T(8,128)}, f32[256,256]{1,0:T(8,128)}, f32[256,256]{1,0:T(8,128)}) custom-call(f32[256,256]{1,0:T(8,128)} %fusion.3.gram_ref, f32[256,256]{1,0:T(8,128)} %get-tuple-element.15.cross_ref), custom_call_target="tpu_custom_call" | custom-call | tf_op jit(solution)/shard_map/pallas_call | solution.py:84
  132.2 1.0 constant_dynamic-slice_fusion
  133.2 0.7 copy.7
  133.9 6.5 %convolution_subtract_fusion = f32[2048,256]{1,0:T(8,128)} fusion(f32[2048,256]{1,0:T(8,128)} %param.3, f32[2048,256]{0,1:T(8,128)S(1)} %constant_dynamic-update-slice_fusion, s32[]{:T(128)S(6)} %select_n.36, f32[256,256]{1,0:T(8,128)} %get-tuple-element.8), kind=kOutput, calls=%fused_computation | convolution fusion | flops 1611202560 | bytes 6553604 | tf_op jit(solution)/shard_map/dot_general | solution.py:127
  (18 shorter events, 0.3 us)
Async XLA Ops:
  0.6 66.0 %copy-start.1 = (f32[2048,16]{0,1:T(8,128)S(1)}, f32[2048,16]{0,1:T(8,128)}, u32[]{:S(2)}) copy-start(f32[2048,16]{0,1:T(8,128)} %param.2) | copy-start | bytes 393220
  0.6 15.5 %collective-permute-start = (f32[2048,16]{0,1:T(8,128)}, f32[2048,16]{0,1:T(8,128)S(1)}, u32[]{:S(2)}, u32[]{:S(2)}) collective-permute-start(f32[2048,16]{0,1:T(8,128)} %param.2), channel_id=1, source_target_pairs={{0,1},{1,2},{2,3},{3,4},{4,5},{5,6},{6,7},{7,8},{8,9},{9,10},{10,1... | collective-permute-start | bytes 393224 | tf_op jit(solution)/shard_map/ppermute | solution.py:99
  16.1 6.9 %collective-permute-start.1 = (f32[2048,16]{0,1:T(8,128)S(1)}, f32[2048,16]{0,1:T(8,128)S(1)}, u32[]{:S(2)}, u32[]{:S(2)}) collective-permute-start(f32[2048,16]{0,1:T(8,128)S(1)} %collective-permute-done), channel_id=1, source_target_pairs={{0,1},{1,2},{2,3},{3,4},{4,5},{5,6},{6,7},{7,8},{8,9},{9,10},{10,1... | collective-permute-start | bytes 393224 | tf_op jit(solution)/shard_map/ppermute | solution.py:99
  18.1 6.9 %collective-permute-start.8 = (f32[2048,16]{0,1:T(8,128)}, f32[2048,16]{0,1:T(8,128)S(1)}, u32[]{:S(2)}, u32[]{:S(2)}) collective-permute-start(f32[2048,16]{0,1:T(8,128)} %param.2), channel_id=1, source_target_pairs={{0,15},{1,0},{2,1},{3,2},{4,3},{5,4},{6,5},{7,6},{8,7},{9,8},{10,9... | collective-permute-start | bytes 393224 | tf_op jit(solution)/shard_map/ppermute | solution.py:102
  23.1 6.9 %collective-permute-start.2 = (f32[2048,16]{0,1:T(8,128)S(1)}, f32[2048,16]{0,1:T(8,128)S(1)}, u32[]{:S(2)}, u32[]{:S(2)}) collective-permute-start(f32[2048,16]{0,1:T(8,128)S(1)} %collective-permute-done.1), channel_id=1, source_target_pairs={{0,1},{1,2},{2,3},{3,4},{4,5},{5,6},{6,7},{7,8},{8,9},{9,10},{10,1... | collective-permute-start | bytes 393224 | tf_op jit(solution)/shard_map/ppermute | solution.py:99
  25.0 6.9 %collective-permute-start.9 = (f32[2048,16]{0,1:T(8,128)S(1)}, f32[2048,16]{0,1:T(8,128)S(1)}, u32[]{:S(2)}, u32[]{:S(2)}) collective-permute-start(f32[2048,16]{0,1:T(8,128)S(1)} %collective-permute-done.8), channel_id=1, source_target_pairs={{0,15},{1,0},{2,1},{3,2},{4,3},{5,4},{6,5},{7,6},{8,7},{9,8},{10,9... | collective-permute-start | bytes 393224 | tf_op jit(solution)/shard_map/ppermute | solution.py:102
  30.0 6.9 %collective-permute-start.3 = (f32[2048,16]{0,1:T(8,128)S(1)}, f32[2048,16]{0,1:T(8,128)S(1)}, u32[]{:S(2)}, u32[]{:S(2)}) collective-permute-start(f32[2048,16]{0,1:T(8,128)S(1)} %collective-permute-done.2), channel_id=1, source_target_pairs={{0,1},{1,2},{2,3},{3,4},{4,5},{5,6},{6,7},{7,8},{8,9},{9,10},{10,1... | collective-permute-start | bytes 393224 | tf_op jit(solution)/shard_map/ppermute | solution.py:99
  31.9 6.9 %collective-permute-start.10 = (f32[2048,16]{0,1:T(8,128)S(1)}, f32[2048,16]{0,1:T(8,128)S(1)}, u32[]{:S(2)}, u32[]{:S(2)}) collective-permute-start(f32[2048,16]{0,1:T(8,128)S(1)} %collective-permute-done.9), channel_id=1, source_target_pairs={{0,15},{1,0},{2,1},{3,2},{4,3},{5,4},{6,5},{7,6},{8,7},{9,8},{10,9... | collective-permute-start | bytes 393224 | tf_op jit(solution)/shard_map/ppermute | solution.py:102
  36.9 6.9 %collective-permute-start.4 = (f32[2048,16]{0,1:T(8,128)S(1)}, f32[2048,16]{0,1:T(8,128)S(1)}, u32[]{:S(2)}, u32[]{:S(2)}) collective-permute-start(f32[2048,16]{0,1:T(8,128)S(1)} %collective-permute-done.3), channel_id=1, source_target_pairs={{0,1},{1,2},{2,3},{3,4},{4,5},{5,6},{6,7},{7,8},{8,9},{9,10},{10,1... | collective-permute-start | bytes 393224 | tf_op jit(solution)/shard_map/ppermute | solution.py:99
  38.8 6.9 %collective-permute-start.11 = (f32[2048,16]{0,1:T(8,128)S(1)}, f32[2048,16]{0,1:T(8,128)S(1)}, u32[]{:S(2)}, u32[]{:S(2)}) collective-permute-start(f32[2048,16]{0,1:T(8,128)S(1)} %collective-permute-done.10), channel_id=1, source_target_pairs={{0,15},{1,0},{2,1},{3,2},{4,3},{5,4},{6,5},{7,6},{8,7},{9,8},{10,9... | collective-permute-start | bytes 393224 | tf_op jit(solution)/shard_map/ppermute | solution.py:102
  43.8 6.9 %collective-permute-start.5 = (f32[2048,16]{0,1:T(8,128)S(1)}, f32[2048,16]{0,1:T(8,128)S(1)}, u32[]{:S(2)}, u32[]{:S(2)}) collective-permute-start(f32[2048,16]{0,1:T(8,128)S(1)} %collective-permute-done.4), channel_id=1, source_target_pairs={{0,1},{1,2},{2,3},{3,4},{4,5},{5,6},{6,7},{7,8},{8,9},{9,10},{10,1... | collective-permute-start | bytes 393224 | tf_op jit(solution)/shard_map/ppermute | solution.py:99
  45.7 6.9 %collective-permute-start.12 = (f32[2048,16]{0,1:T(8,128)S(1)}, f32[2048,16]{0,1:T(8,128)S(1)}, u32[]{:S(2)}, u32[]{:S(2)}) collective-permute-start(f32[2048,16]{0,1:T(8,128)S(1)} %collective-permute-done.11), channel_id=1, source_target_pairs={{0,15},{1,0},{2,1},{3,2},{4,3},{5,4},{6,5},{7,6},{8,7},{9,8},{10,9... | collective-permute-start | bytes 393224 | tf_op jit(solution)/shard_map/ppermute | solution.py:102
  50.7 7.7 %collective-permute-start.6 = (f32[2048,16]{0,1:T(8,128)S(1)}, f32[2048,16]{0,1:T(8,128)S(1)}, u32[]{:S(2)}, u32[]{:S(2)}) collective-permute-start(f32[2048,16]{0,1:T(8,128)S(1)} %collective-permute-done.5), channel_id=1, source_target_pairs={{0,1},{1,2},{2,3},{3,4},{4,5},{5,6},{6,7},{7,8},{8,9},{9,10},{10,1... | collective-permute-start | bytes 393224 | tf_op jit(solution)/shard_map/ppermute | solution.py:99
  52.6 7.7 %collective-permute-start.13 = (f32[2048,16]{0,1:T(8,128)S(1)}, f32[2048,16]{0,1:T(8,128)S(1)}, u32[]{:S(2)}, u32[]{:S(2)}) collective-permute-start(f32[2048,16]{0,1:T(8,128)S(1)} %collective-permute-done.12), channel_id=1, source_target_pairs={{0,15},{1,0},{2,1},{3,2},{4,3},{5,4},{6,5},{7,6},{8,7},{9,8},{10,9... | collective-permute-start | bytes 393224 | tf_op jit(solution)/shard_map/ppermute | solution.py:102
  58.4 8.1 %collective-permute-start.7 = (f32[2048,16]{0,1:T(8,128)S(1)}, f32[2048,16]{0,1:T(8,128)S(1)}, u32[]{:S(2)}, u32[]{:S(2)}) collective-permute-start(f32[2048,16]{0,1:T(8,128)S(1)} %collective-permute-done.6), channel_id=1, source_target_pairs={{0,1},{1,2},{2,3},{3,4},{4,5},{5,6},{6,7},{7,8},{8,9},{9,10},{10,1... | collective-permute-start | bytes 393224 | tf_op jit(solution)/shard_map/ppermute | solution.py:99
  60.4 7.5 %collective-permute-start.14 = (f32[2048,16]{0,1:T(8,128)S(1)}, f32[2048,16]{0,1:T(8,128)S(1)}, u32[]{:S(2)}, u32[]{:S(2)}) collective-permute-start(f32[2048,16]{0,1:T(8,128)S(1)} %collective-permute-done.13), channel_id=1, source_target_pairs={{0,15},{1,0},{2,1},{3,2},{4,3},{5,4},{6,5},{7,6},{8,7},{9,8},{10,9... | collective-permute-start | bytes 393224 | tf_op jit(solution)/shard_map/ppermute | solution.py:102
  67.9 1.9 %copy-start = (f32[2048,256]{1,0:T(8,128)S(1)}, f32[2048,256]{1,0:T(8,128)}, u32[]{:S(2)}) copy-start(f32[2048,256]{1,0:T(8,128)} %param.3) | copy-start | bytes 6291460
  102.3 15.3 %all-to-all-start.1 = ((f32[32,8,512]{2,1,0:T(8,128)}), f32[32,8,512]{2,1,0:T(8,128)S(1)}, u32[]{:S(2)}, u32[]{:S(2)}) async-start(f32[32,8,512]{2,1,0:T(8,128)} %broadcast_in_dim.2), calls=%async_computation.1 | async-start | bytes 1048576 | tf_op jit(solution)/shard_map/all_to_all | solution.py:113

commit v17 on v16

--- a/solution.py
+++ b/solution.py
@@ -12,7 +12,7 @@
 HIGHEST = lax.Precision.HIGHEST
 
 
-def factor_kernel(gram_ref, cross_ref, upper_ref, projected_ref, coefficients_ref, work_ref, left_ref,
+def factor_kernel(gram_ref, cross_ref, lower_ref, projected_ref, coefficients_ref, work_ref, left_ref,
                   *, rows_total):
     n = gram_ref.shape[0]
     rows = lax.broadcasted_iota(jnp.int32, (n, n), 0)
@@ -70,7 +70,8 @@
     phase(0, half // depth, 0, n + half)
     phase(half // depth, n // depth, half, 2 * n)
     done = work_ref[...]
-    upper_ref[...] = jnp.where(cols >= rows, done[:, :n], 0.0) * (1.0 / math.sqrt(rows_total))
+    lower_ref[...] = jnp.transpose(
+        jnp.where(cols >= rows, done[:, :n], 0.0) * (1.0 / math.sqrt(rows_total)))
     inverse = jnp.where(cols <= rows, done[:, n:], 0.0)
     projected = jnp.dot(inverse, cross_ref[...], precision=HIGHEST,
                         preferred_element_type=jnp.float32)
@@ -126,7 +127,7 @@
     scaled, projected, coefficients = factor(gram_total, totals, rows_total)
     residual = slab - jnp.dot(gathered, jnp.roll(coefficients, -shift, axis=0), precision=highest)
     col_width = panel.shape[1]
-    triangle = lax.dynamic_slice_in_dim(scaled, lax.axis_index("col") * col_width, col_width, 1)
+    triangle = lax.dynamic_slice_in_dim(scaled, lax.axis_index("col") * col_width, col_width, 0).T
     return (triangle, projected, residual)
 
 

time: 141 us -> 141 us (level)
  no operation moved by 1% of the time
where the time goes in v17:
time: 141 us; the launch traced here: 140 us
  starting transfers between devices  55.2 us (39%)
  blocking collectives  27.8 us (20%)
  waiting for transfers between devices  26.8 us (19%)
  Pallas kernels  12.9 us (9%)
  matrix products  11.9 us (8%)
  local copies, waits for them, and re-layouts  3.3 us (2%)
    ppermute x7, starting transfers between devices, col_gather(): behind = lax.ppermute(behind, 'col', [(i, (i - 1) % n) for i in range(n)])  33.4 us
    all_to_all x1, blocking collectives, row_sum(): mine = lax.all_to_all(parts, 'row', 0, 0, tiled=False).sum(0)  27.8 us
    ppermute x8, starting transfers between devices, col_gather(): ahead = lax.ppermute(ahead, 'col', [(i, (i + 1) % n) for i in range(n)])  17.9 us
    ppermute x8, waiting for transfers between devices, col_gather(): ahead = lax.ppermute(ahead, 'col', [(i, (i + 1) % n) for i in range(n)])  14.3 us
    pallas_call x1, Pallas kernels, factor(): pl.pallas_call(functools.partial(factor_kernel, rows_total=rows_total), o...  12.9 us
    all_to_all x1, waiting for transfers between devices, row_sum(): return lax.all_to_all(copies, 'row', 0, 0, tiled=False).reshape(rows, cols)  11.3 us
    dot_general x1, matrix products, per_device(): jnp.dot(gathered, jnp.roll(coefficients, -shift, axis=0), precision=highest)  6.51 us
    all_to_all x1, starting transfers between devices, row_sum(): return lax.all_to_all(copies, 'row', 0, 0, tiled=False).reshape(rows, cols)  3.86 us
  transfers between devices with their start and end apart: 16, of which 10 were waited for; matrix products, arithmetic and copies ran while one was open for 0% of the time, Pallas kernels for 0%

profile of v17, /device:TPU:1, one launch (start us, length us, event | category | flops | bytes accessed | tf_op | source)
XLA Modules:
  0.0 140.1 jit_solution(16095309758109961467)
XLA Ops:
  0.6 0.0 copy-start.1
  0.6 4.5 %collective-permute-start = (f32[2048,16]{0,1:T(8,128)}, f32[2048,16]{0,1:T(8,128)S(1)}, u32[]{:S(2)}, u32[]{:S(2)}) collective-permute-start(f32[2048,16]{0,1:T(8,128)} %param.2), channel_id=1, source_target_pairs={{0,1},{1,2},{2,3},{3,4},{4,5},{5,6},{6,7},{7,8},{8,9},{9,10},{10,1... | collective-permute-start | bytes 393224 | tf_op jit(solution)/shard_map/ppermute | solution.py:100
  5.2 11.0 %collective-permute-done = f32[2048,16]{0,1:T(8,128)S(1)} collective-permute-done((f32[2048,16]{0,1:T(8,128)}, f32[2048,16]{0,1:T(8,128)S(1)}, u32[]{:S(2)}, u32[]{:S(2)}) %collective-permute-start) | collective-permute-done | bytes 131104 | tf_op jit(solution)/shard_map/ppermute | solution.py:100
  16.1 1.9 %collective-permute-start.1 = (f32[2048,16]{0,1:T(8,128)S(1)}, f32[2048,16]{0,1:T(8,128)S(1)}, u32[]{:S(2)}, u32[]{:S(2)}) collective-permute-start(f32[2048,16]{0,1:T(8,128)S(1)} %collective-permute-done), channel_id=1, source_target_pairs={{0,1},{1,2},{2,3},{3,4},{4,5},{5,6},{6,7},{7,8},{8,9},{9,10},{10,1... | collective-permute-start | bytes 393224 | tf_op jit(solution)/shard_map/ppermute | solution.py:100
  18.1 4.6 %collective-permute-start.8 = (f32[2048,16]{0,1:T(8,128)}, f32[2048,16]{0,1:T(8,128)S(1)}, u32[]{:S(2)}, u32[]{:S(2)}) collective-permute-start(f32[2048,16]{0,1:T(8,128)} %param.2), channel_id=1, source_target_pairs={{0,15},{1,0},{2,1},{3,2},{4,3},{5,4},{6,5},{7,6},{8,7},{9,8},{10,9... | collective-permute-start | bytes 393224 | tf_op jit(solution)/shard_map/ppermute | solution.py:103
  22.6 0.4 collective-permute-done.1
  23.1 1.9 %collective-permute-start.2 = (f32[2048,16]{0,1:T(8,128)S(1)}, f32[2048,16]{0,1:T(8,128)S(1)}, u32[]{:S(2)}, u32[]{:S(2)}) collective-permute-start(f32[2048,16]{0,1:T(8,128)S(1)} %collective-permute-done.1), channel_id=1, source_target_pairs={{0,1},{1,2},{2,3},{3,4},{4,5},{5,6},{6,7},{7,8},{8,9},{9,10},{10,1... | collective-permute-start | bytes 393224 | tf_op jit(solution)/shard_map/ppermute | solution.py:100
  25.0 0.0 collective-permute-done.8
  25.0 4.8 %collective-permute-start.9 = (f32[2048,16]{0,1:T(8,128)S(1)}, f32[2048,16]{0,1:T(8,128)S(1)}, u32[]{:S(2)}, u32[]{:S(2)}) collective-permute-start(f32[2048,16]{0,1:T(8,128)S(1)} %collective-permute-done.8), channel_id=1, source_target_pairs={{0,15},{1,0},{2,1},{3,2},{4,3},{5,4},{6,5},{7,6},{8,7},{9,8},{10,9... | collective-permute-start | bytes 393224 | tf_op jit(solution)/shard_map/ppermute | solution.py:103
  29.8 0.2 collective-permute-done.2
  30.0 1.9 %collective-permute-start.3 = (f32[2048,16]{0,1:T(8,128)S(1)}, f32[2048,16]{0,1:T(8,128)S(1)}, u32[]{:S(2)}, u32[]{:S(2)}) collective-permute-start(f32[2048,16]{0,1:T(8,128)S(1)} %collective-permute-done.2), channel_id=1, source_target_pairs={{0,1},{1,2},{2,3},{3,4},{4,5},{5,6},{6,7},{7,8},{8,9},{9,10},{10,1... | collective-permute-start | bytes 393224 | tf_op jit(solution)/shard_map/ppermute | solution.py:100
  31.9 0.0 collective-permute-done.9
  31.9 4.8 %collective-permute-start.10 = (f32[2048,16]{0,1:T(8,128)S(1)}, f32[2048,16]{0,1:T(8,128)S(1)}, u32[]{:S(2)}, u32[]{:S(2)}) collective-permute-start(f32[2048,16]{0,1:T(8,128)S(1)} %collective-permute-done.9), channel_id=1, source_target_pairs={{0,15},{1,0},{2,1},{3,2},{4,3},{5,4},{6,5},{7,6},{8,7},{9,8},{10,9... | collective-permute-start | bytes 393224 | tf_op jit(solution)/shard_map/ppermute | solution.py:103
  36.7 0.2 collective-permute-done.3
  36.9 1.9 %collective-permute-start.4 = (f32[2048,16]{0,1:T(8,128)S(1)}, f32[2048,16]{0,1:T(8,128)S(1)}, u32[]{:S(2)}, u32[]{:S(2)}) collective-permute-start(f32[2048,16]{0,1:T(8,128)S(1)} %collective-permute-done.3), channel_id=1, source_target_pairs={{0,1},{1,2},{2,3},{3,4},{4,5},{5,6},{6,7},{7,8},{8,9},{9,10},{10,1... | collective-permute-start | bytes 393224 | tf_op jit(solution)/shard_map/ppermute | solution.py:100
  38.8 0.0 collective-permute-done.10
  38.8 4.8 %collective-permute-start.11 = (f32[2048,16]{0,1:T(8,128)S(1)}, f32[2048,16]{0,1:T(8,128)S(1)}, u32[]{:S(2)}, u32[]{:S(2)}) collective-permute-start(f32[2048,16]{0,1:T(8,128)S(1)} %collective-permute-done.10), channel_id=1, source_target_pairs={{0,15},{1,0},{2,1},{3,2},{4,3},{5,4},{6,5},{7,6},{8,7},{9,8},{10,9... | collective-permute-start | bytes 393224 | tf_op jit(solution)/shard_map/ppermute | solution.py:103
  43.6 0.2 collective-permute-done.4
  43.8 1.9 %collective-permute-start.5 = (f32[2048,16]{0,1:T(8,128)S(1)}, f32[2048,16]{0,1:T(8,128)S(1)}, u32[]{:S(2)}, u32[]{:S(2)}) collective-permute-start(f32[2048,16]{0,1:T(8,128)S(1)} %collective-permute-done.4), channel_id=1, source_target_pairs={{0,1},{1,2},{2,3},{3,4},{4,5},{5,6},{6,7},{7,8},{8,9},{9,10},{10,1... | collective-permute-start | bytes 393224 | tf_op jit(solution)/shard_map/ppermute | solution.py:100
  45.7 0.0 collective-permute-done.11
  45.7 4.8 %collective-permute-start.12 = (f32[2048,16]{0,1:T(8,128)S(1)}, f32[2048,16]{0,1:T(8,128)S(1)}, u32[]{:S(2)}, u32[]{:S(2)}) collective-permute-start(f32[2048,16]{0,1:T(8,128)S(1)} %collective-permute-done.11), channel_id=1, source_target_pairs={{0,15},{1,0},{2,1},{3,2},{4,3},{5,4},{6,5},{7,6},{8,7},{9,8},{10,9... | collective-permute-start | bytes 393224 | tf_op jit(solution)/shard_map/ppermute | solution.py:103
  50.5 0.2 collective-permute-done.5
  50.7 1.9 %collective-permute-start.6 = (f32[2048,16]{0,1:T(8,128)S(1)}, f32[2048,16]{0,1:T(8,128)S(1)}, u32[]{:S(2)}, u32[]{:S(2)}) collective-permute-start(f32[2048,16]{0,1:T(8,128)S(1)} %collective-permute-done.5), channel_id=1, source_target_pairs={{0,1},{1,2},{2,3},{3,4},{4,5},{5,6},{6,7},{7,8},{8,9},{9,10},{10,1... | collective-permute-start | bytes 393224 | tf_op jit(solution)/shard_map/ppermute | solution.py:100
  52.6 0.0 collective-permute-done.12
  52.6 4.8 %collective-permute-start.13 = (f32[2048,16]{0,1:T(8,128)S(1)}, f32[2048,16]{0,1:T(8,128)S(1)}, u32[]{:S(2)}, u32[]{:S(2)}) collective-permute-start(f32[2048,16]{0,1:T(8,128)S(1)} %collective-permute-done.12), channel_id=1, source_target_pairs={{0,15},{1,0},{2,1},{3,2},{4,3},{5,4},{6,5},{7,6},{8,7},{9,8},{10,9... | collective-permute-start | bytes 393224 | tf_op jit(solution)/shard_map/ppermute | solution.py:103
  57.4 1.0 collective-permute-done.6
  58.4 1.9 %collective-permute-start.7 = (f32[2048,16]{0,1:T(8,128)S(1)}, f32[2048,16]{0,1:T(8,128)S(1)}, u32[]{:S(2)}, u32[]{:S(2)}) collective-permute-start(f32[2048,16]{0,1:T(8,128)S(1)} %collective-permute-done.6), channel_id=1, source_target_pairs={{0,1},{1,2},{2,3},{3,4},{4,5},{5,6},{6,7},{7,8},{8,9},{9,10},{10,1... | collective-permute-start | bytes 393224 | tf_op jit(solution)/shard_map/ppermute | solution.py:100
  60.3 0.0 collective-permute-done.13
  60.4 5.0 %collective-permute-start.14 = (f32[2048,16]{0,1:T(8,128)S(1)}, f32[2048,16]{0,1:T(8,128)S(1)}, u32[]{:S(2)}, u32[]{:S(2)}) collective-permute-start(f32[2048,16]{0,1:T(8,128)S(1)} %collective-permute-done.13), channel_id=1, source_target_pairs={{0,15},{1,0},{2,1},{3,2},{4,3},{5,4},{6,5},{7,6},{8,7},{9,8},{10,9... | collective-permute-start | bytes 393224 | tf_op jit(solution)/shard_map/ppermute | solution.py:103
  65.4 1.1 collective-permute-done.7
  66.6 0.0 copy-done.1
  66.7 1.2 collective-permute-done.14
  67.9 0.0 copy-start
  67.9 1.9 %fusion.7 = f32[256,256]{0,1:T(8,128)S(1)} fusion(f32[2048,256]{0,1:T(8,128)S(1)} %constant_dynamic-update-slice_fusion), kind=kOutput, calls=%fused_computation.31 | convolution fusion | flops 1610612736 | bytes 2359296 | tf_op jit(solution)/shard_map/dot_general | solution.py:122
  69.8 0.0 copy-done
  69.8 3.6 %fusion.8 = f32[256,256]{0,1:T(8,128)S(1)} fusion(f32[2048,256]{0,1:T(8,128)S(1)} %constant_dynamic-update-slice_fusion, f32[2048,256]{1,0:T(8,128)S(1)} %copy-done), kind=kOutput, calls=%fused_computation.32 | convolution fusion | flops 1610612736 | bytes 4456448 | tf_op jit(solution)/shard_map/dot_general | solution.py:121
  73.4 0.2 copy.5
  73.6 27.8 %all_to_all.10 = f32[32,8,512]{2,1,0:T(8,128)S(1)} all-to-all(f32[32,8,512]{2,1,0:T(8,128)S(1)} %bitcast.10), channel_id=1, replica_groups=mesh['row'=32,'col'=16] {'row'}, dimensions={0} | all-to-all | bytes 1048576 | tf_op jit(solution)/shard_map/all_to_all | solution.py:112
  101.4 0.9 broadcast_in_dim.2
  102.3 3.9 %all-to-all-start.1 = ((f32[32,8,512]{2,1,0:T(8,128)}), f32[32,8,512]{2,1,0:T(8,128)S(1)}, u32[]{:S(2)}, u32[]{:S(2)}) async-start(f32[32,8,512]{2,1,0:T(8,128)} %broadcast_in_dim.2), calls=%async_computation.1 | async-start | bytes 1048576 | tf_op jit(solution)/shard_map/all_to_all | solution.py:114
  106.2 11.3 %all-to-all-done.1 = f32[32,8,512]{2,1,0:T(8,128)S(1)} async-done(((f32[32,8,512]{2,1,0:T(8,128)}), f32[32,8,512]{2,1,0:T(8,128)S(1)}, u32[]{:S(2)}, u32[]{:S(2)}) %all-to-all-start.1) | async-done | bytes 524320 | tf_op jit(solution)/shard_map/all_to_all | solution.py:114
  117.6 0.1 fusion
  117.7 0.7 fusion.6
  118.4 0.9 fusion.3.gram_ref
  119.3 12.9 %shard_map.49 = (f32[256,256]{1,0:T(8,128)}, f32[256,256]{1,0:T(8,128)}, f32[256,256]{1,0:T(8,128)}) custom-call(f32[256,256]{1,0:T(8,128)} %fusion.3.gram_ref, f32[256,256]{1,0:T(8,128)} %get-tuple-element.9.cross_ref), custom_call_target="tpu_custom_call" | custom-call | tf_op jit(solution)/shard_map/pallas_call | solution.py:85
  132.2 6.5 %convolution_subtract_fusion = f32[2048,256]{1,0:T(8,128)} fusion(f32[2048,256]{1,0:T(8,128)} %param.3, f32[2048,256]{0,1:T(8,128)S(1)} %constant_dynamic-update-slice_fusion, s32[]{:T(128)S(6)} %select_n.36, f32[256,256]{1,0:T(8,128)} %get-tuple-element.8), kind=kOutput, calls=%fused_computation | convolution fusion | flops 1611202560 | bytes 6553604 | tf_op jit(solution)/shard_map/dot_general | solution.py:128
  138.7 1.3 dynamic-slice_bitcast_fusion
  (18 shorter events, 0.3 us)
Async XLA Ops:
  0.6 66.0 %copy-start.1 = (f32[2048,16]{0,1:T(8,128)S(1)}, f32[2048,16]{0,1:T(8,128)}, u32[]{:S(2)}) copy-start(f32[2048,16]{0,1:T(8,128)} %param.2) | copy-start | bytes 393220
  0.6 15.5 %collective-permute-start = (f32[2048,16]{0,1:T(8,128)}, f32[2048,16]{0,1:T(8,128)S(1)}, u32[]{:S(2)}, u32[]{:S(2)}) collective-permute-start(f32[2048,16]{0,1:T(8,128)} %param.2), channel_id=1, source_target_pairs={{0,1},{1,2},{2,3},{3,4},{4,5},{5,6},{6,7},{7,8},{8,9},{9,10},{10,1... | collective-permute-start | bytes 393224 | tf_op jit(solution)/shard_map/ppermute | solution.py:100
  16.1 6.9 %collective-permute-start.1 = (f32[2048,16]{0,1:T(8,128)S(1)}, f32[2048,16]{0,1:T(8,128)S(1)}, u32[]{:S(2)}, u32[]{:S(2)}) collective-permute-start(f32[2048,16]{0,1:T(8,128)S(1)} %collective-permute-done), channel_id=1, source_target_pairs={{0,1},{1,2},{2,3},{3,4},{4,5},{5,6},{6,7},{7,8},{8,9},{9,10},{10,1... | collective-permute-start | bytes 393224 | tf_op jit(solution)/shard_map/ppermute | solution.py:100
  18.1 6.9 %collective-permute-start.8 = (f32[2048,16]{0,1:T(8,128)}, f32[2048,16]{0,1:T(8,128)S(1)}, u32[]{:S(2)}, u32[]{:S(2)}) collective-permute-start(f32[2048,16]{0,1:T(8,128)} %param.2), channel_id=1, source_target_pairs={{0,15},{1,0},{2,1},{3,2},{4,3},{5,4},{6,5},{7,6},{8,7},{9,8},{10,9... | collective-permute-start | bytes 393224 | tf_op jit(solution)/shard_map/ppermute | solution.py:103
  23.1 6.9 %collective-permute-start.2 = (f32[2048,16]{0,1:T(8,128)S(1)}, f32[2048,16]{0,1:T(8,128)S(1)}, u32[]{:S(2)}, u32[]{:S(2)}) collective-permute-start(f32[2048,16]{0,1:T(8,128)S(1)} %collective-permute-done.1), channel_id=1, source_target_pairs={{0,1},{1,2},{2,3},{3,4},{4,5},{5,6},{6,7},{7,8},{8,9},{9,10},{10,1... | collective-permute-start | bytes 393224 | tf_op jit(solution)/shard_map/ppermute | solution.py:100
  25.0 6.9 %collective-permute-start.9 = (f32[2048,16]{0,1:T(8,128)S(1)}, f32[2048,16]{0,1:T(8,128)S(1)}, u32[]{:S(2)}, u32[]{:S(2)}) collective-permute-start(f32[2048,16]{0,1:T(8,128)S(1)} %collective-permute-done.8), channel_id=1, source_target_pairs={{0,15},{1,0},{2,1},{3,2},{4,3},{5,4},{6,5},{7,6},{8,7},{9,8},{10,9... | collective-permute-start | bytes 393224 | tf_op jit(solution)/shard_map/ppermute | solution.py:103
  30.0 6.9 %collective-permute-start.3 = (f32[2048,16]{0,1:T(8,128)S(1)}, f32[2048,16]{0,1:T(8,128)S(1)}, u32[]{:S(2)}, u32[]{:S(2)}) collective-permute-start(f32[2048,16]{0,1:T(8,128)S(1)} %collective-permute-done.2), channel_id=1, source_target_pairs={{0,1},{1,2},{2,3},{3,4},{4,5},{5,6},{6,7},{7,8},{8,9},{9,10},{10,1... | collective-permute-start | bytes 393224 | tf_op jit(solution)/shard_map/ppermute | solution.py:100
  31.9 6.9 %collective-permute-start.10 = (f32[2048,16]{0,1:T(8,128)S(1)}, f32[2048,16]{0,1:T(8,128)S(1)}, u32[]{:S(2)}, u32[]{:S(2)}) collective-permute-start(f32[2048,16]{0,1:T(8,128)S(1)} %collective-permute-done.9), channel_id=1, source_target_pairs={{0,15},{1,0},{2,1},{3,2},{4,3},{5,4},{6,5},{7,6},{8,7},{9,8},{10,9... | collective-permute-start | bytes 393224 | tf_op jit(solution)/shard_map/ppermute | solution.py:103
  36.9 6.9 %collective-permute-start.4 = (f32[2048,16]{0,1:T(8,128)S(1)}, f32[2048,16]{0,1:T(8,128)S(1)}, u32[]{:S(2)}, u32[]{:S(2)}) collective-permute-start(f32[2048,16]{0,1:T(8,128)S(1)} %collective-permute-done.3), channel_id=1, source_target_pairs={{0,1},{1,2},{2,3},{3,4},{4,5},{5,6},{6,7},{7,8},{8,9},{9,10},{10,1... | collective-permute-start | bytes 393224 | tf_op jit(solution)/shard_map/ppermute | solution.py:100
  38.8 6.9 %collective-permute-start.11 = (f32[2048,16]{0,1:T(8,128)S(1)}, f32[2048,16]{0,1:T(8,128)S(1)}, u32[]{:S(2)}, u32[]{:S(2)}) collective-permute-start(f32[2048,16]{0,1:T(8,128)S(1)} %collective-permute-done.10), channel_id=1, source_target_pairs={{0,15},{1,0},{2,1},{3,2},{4,3},{5,4},{6,5},{7,6},{8,7},{9,8},{10,9... | collective-permute-start | bytes 393224 | tf_op jit(solution)/shard_map/ppermute | solution.py:103
  43.8 6.9 %collective-permute-start.5 = (f32[2048,16]{0,1:T(8,128)S(1)}, f32[2048,16]{0,1:T(8,128)S(1)}, u32[]{:S(2)}, u32[]{:S(2)}) collective-permute-start(f32[2048,16]{0,1:T(8,128)S(1)} %collective-permute-done.4), channel_id=1, source_target_pairs={{0,1},{1,2},{2,3},{3,4},{4,5},{5,6},{6,7},{7,8},{8,9},{9,10},{10,1... | collective-permute-start | bytes 393224 | tf_op jit(solution)/shard_map/ppermute | solution.py:100
  45.7 6.9 %collective-permute-start.12 = (f32[2048,16]{0,1:T(8,128)S(1)}, f32[2048,16]{0,1:T(8,128)S(1)}, u32[]{:S(2)}, u32[]{:S(2)}) collective-permute-start(f32[2048,16]{0,1:T(8,128)S(1)} %collective-permute-done.11), channel_id=1, source_target_pairs={{0,15},{1,0},{2,1},{3,2},{4,3},{5,4},{6,5},{7,6},{8,7},{9,8},{10,9... | collective-permute-start | bytes 393224 | tf_op jit(solution)/shard_map/ppermute | solution.py:103
  50.7 7.7 %collective-permute-start.6 = (f32[2048,16]{0,1:T(8,128)S(1)}, f32[2048,16]{0,1:T(8,128)S(1)}, u32[]{:S(2)}, u32[]{:S(2)}) collective-permute-start(f32[2048,16]{0,1:T(8,128)S(1)} %collective-permute-done.5), channel_id=1, source_target_pairs={{0,1},{1,2},{2,3},{3,4},{4,5},{5,6},{6,7},{7,8},{8,9},{9,10},{10,1... | collective-permute-start | bytes 393224 | tf_op jit(solution)/shard_map/ppermute | solution.py:100
  52.6 7.7 %collective-permute-start.13 = (f32[2048,16]{0,1:T(8,128)S(1)}, f32[2048,16]{0,1:T(8,128)S(1)}, u32[]{:S(2)}, u32[]{:S(2)}) collective-permute-start(f32[2048,16]{0,1:T(8,128)S(1)} %collective-permute-done.12), channel_id=1, source_target_pairs={{0,15},{1,0},{2,1},{3,2},{4,3},{5,4},{6,5},{7,6},{8,7},{9,8},{10,9... | collective-permute-start | bytes 393224 | tf_op jit(solution)/shard_map/ppermute | solution.py:103
  58.4 8.1 %collective-permute-start.7 = (f32[2048,16]{0,1:T(8,128)S(1)}, f32[2048,16]{0,1:T(8,128)S(1)}, u32[]{:S(2)}, u32[]{:S(2)}) collective-permute-start(f32[2048,16]{0,1:T(8,128)S(1)} %collective-permute-done.6), channel_id=1, source_target_pairs={{0,1},{1,2},{2,3},{3,4},{4,5},{5,6},{6,7},{7,8},{8,9},{9,10},{10,1... | collective-permute-start | bytes 393224 | tf_op jit(solution)/shard_map/ppermute | solution.py:100
  60.4 7.5 %collective-permute-start.14 = (f32[2048,16]{0,1:T(8,128)S(1)}, f32[2048,16]{0,1:T(8,128)S(1)}, u32[]{:S(2)}, u32[]{:S(2)}) collective-permute-start(f32[2048,16]{0,1:T(8,128)S(1)} %collective-permute-done.13), channel_id=1, source_target_pairs={{0,15},{1,0},{2,1},{3,2},{4,3},{5,4},{6,5},{7,6},{8,7},{9,8},{10,9... | collective-permute-start | bytes 393224 | tf_op jit(solution)/shard_map/ppermute | solution.py:103
  67.9 1.9 %copy-start = (f32[2048,256]{1,0:T(8,128)S(1)}, f32[2048,256]{1,0:T(8,128)}, u32[]{:S(2)}) copy-start(f32[2048,256]{1,0:T(8,128)} %param.3) | copy-start | bytes 6291460
  102.3 15.3 %all-to-all-start.1 = ((f32[32,8,512]{2,1,0:T(8,128)}), f32[32,8,512]{2,1,0:T(8,128)S(1)}, u32[]{:S(2)}, u32[]{:S(2)}) async-start(f32[32,8,512]{2,1,0:T(8,128)} %broadcast_in_dim.2), calls=%async_computation.1 | async-start | bytes 1048576 | tf_op jit(solution)/shard_map/all_to_all | solution.py:114
